TPU v7x, 32 devices: a whole 2x2x4 slice. The times are simulated.
32 devices in a mesh: member: 2 (over x), wide: 8 (over z, y), narrow: 2 (over core).
Axes of the slice: x: 2, y: 2, z: 4, core: 2. Of those that a mesh axis runs over, the one named last changes fastest.
Arguments:
- noise: bfloat16 [256, 512, 512], P('member', 'wide', 'narrow'), parts along dimension 0, may hold values from -6 to 6
- root_z: bfloat16 [128, 128], replicated, may hold values from -0.5 to 0.5
- root_x: bfloat16 [512, 512], replicated, may hold values from -0.25 to 0.25
- root_y: bfloat16 [512, 512], replicated, may hold values from -0.25 to 0.25
- pressure_start: bfloat16 [256, 512, 512], P('member', 'wide', 'narrow'), parts along dimension 0, may hold values from -4 to 4
- well_x: int32 [512], P('member'), parts along dimension 0, may hold values from 0 to 511
- well_y: int32 [512], P('member'), parts along dimension 0, may hold values from 0 to 511
- well_z: int32 [512], P('member'), parts along dimension 0, may hold values from 0 to 127
- well_rate: float32 [512], P('member'), parts along dimension 0, may hold values from -20 to 20
Outputs:
- log_perm: bfloat16 [256, 512, 512], P('member', 'wide', 'narrow'), parts along dimension 0
- pressure: float32 [256, 512, 512], P('member', 'wide', 'narrow'), parts along dimension 0
There are 2 independent parts, one for each index of `member`. A program takes and returns all parts, laid end to end along the dimension named above; an argument that names none is the same for every part. Nothing has to cross between parts.
All inputs are finite; a program needn't handle non-finite values.
Results may differ from a plain program's by a relative error of at most 0.002.
The roundings to bfloat16 on the way count: a program that leaves them out, or rounds other values in their place, can miss the bound.
Values may be sent and summed in bfloat16 or wider, within the bound.
No kernel may reach another device: no remote copies, remote signals or barrier semaphores. Data moves between devices by JAX's collectives and lax.ppermute only.
A program may use at most 128 MiB of HBM per device.

v0:
```python
import jax
import jax.numpy as jnp
from jax import lax
from jax.experimental import pallas as pl
from jax.experimental.pallas import tpu as pltpu
from jax.sharding import PartitionSpec as P

STEPS = 2


STEP_SIZE = 0.03
CAP_LOG = 1.5
CHUNK_Z = 8


def permeability(values):
    return jnp.exp(CAP_LOG * jnp.tanh(values / CAP_LOG))


def harmonic(a, b):
    return 2.0 * a * b / (a + b)


def halos(block, dtype):
    forward_w = [(i, i + 1) for i in range(lax.axis_size("wide") - 1)]
    backward_w = [(j, i) for i, j in forward_w]
    forward_n = [(i, i + 1) for i in range(lax.axis_size("narrow") - 1)]
    backward_n = [(j, i) for i, j in forward_n]
    block = block.astype(dtype)
    x_lo = lax.ppermute(block[:, -1:, :], "wide", forward_w)
    x_hi = lax.ppermute(block[:, :1, :], "wide", backward_w)
    y_lo = lax.ppermute(block[:, :, -1:], "narrow", forward_n)
    y_hi = lax.ppermute(block[:, :, :1], "narrow", backward_n)
    return x_lo, x_hi, y_lo, y_hi


def step_kernel(
    lpm_ref, lpb_ref, lpa_ref, kxl_ref, kxh_ref, kyl_ref, kyh_ref,
    pm_ref, pb_ref, pa_ref, qxl_ref, qxh_ref, qyl_ref, qyh_ref, f_ref, o_ref,
):
    c = pl.program_id(0)
    last = pl.num_programs(0) - 1
    tz, nx, ny = pm_ref.shape
    f32 = jnp.float32

    below = jnp.where(c == 0, 0.0, permeability(lpb_ref[...].astype(f32)))
    above = jnp.where(c == last, 0.0, permeability(lpa_ref[...].astype(f32)))
    centre = permeability(lpm_ref[...].astype(f32))
    ext = jnp.concatenate([below, centre, above], axis=0)
    faces = harmonic(ext[:-1], ext[1:])
    t_zm = faces[:-1]
    t_zp = faces[1:]

    xi = lax.broadcasted_iota(jnp.int32, (tz, nx, ny), 1)
    yi = lax.broadcasted_iota(jnp.int32, (tz, nx, ny), 2)

    fx = harmonic(centre, pltpu.roll(centre, nx - 1, 1))
    t_xp = jnp.where(xi == nx - 1, harmonic(centre[:, nx - 1 :, :], kxh_ref[...]), fx)
    t_xm = jnp.where(xi == 0, harmonic(centre[:, :1, :], kxl_ref[...]), pltpu.roll(fx, 1, 1))
    fy = harmonic(centre, pltpu.roll(centre, ny - 1, 2))
    t_yp = jnp.where(yi == ny - 1, harmonic(centre[:, :, ny - 1 :], kyh_ref[...]), fy)
    t_ym = jnp.where(yi == 0, harmonic(centre[:, :, :1], kyl_ref[...]), pltpu.roll(fy, 1, 2))

    p = pm_ref[...].astype(f32)
    pext = jnp.concatenate([pb_ref[...].astype(f32), p, pa_ref[...].astype(f32)], axis=0)
    n_xp = jnp.where(xi == nx - 1, qxh_ref[...].astype(f32), pltpu.roll(p, nx - 1, 1))
    n_xm = jnp.where(xi == 0, qxl_ref[...].astype(f32), pltpu.roll(p, 1, 1))
    n_yp = jnp.where(yi == ny - 1, qyh_ref[...].astype(f32), pltpu.roll(p, ny - 1, 2))
    n_ym = jnp.where(yi == 0, qyl_ref[...].astype(f32), pltpu.roll(p, 1, 2))

    flux = t_zp * (pext[2:] - p)
    flux = flux + t_zm * (pext[:-2] - p)
    flux = flux + t_xp * (n_xp - p)
    flux = flux + t_xm * (n_xm - p)
    flux = flux + t_yp * (n_yp - p)
    flux = flux + t_ym * (n_ym - p)
    o_ref[...] = p + STEP_SIZE * (flux + f_ref[...]) / (1.0 + 0.5 * p * p)


def advance(log_perm, perm_halos, pressure, pressure_halos, flow):
    depth, nx, ny = pressure.shape
    tz = CHUNK_Z
    grid = (depth // tz,)
    main = pl.BlockSpec((tz, nx, ny), lambda c: (c, 0, 0))
    below = pl.BlockSpec((1, nx, ny), lambda c: (jnp.maximum(c * tz - 1, 0), 0, 0))
    above = pl.BlockSpec((1, nx, ny), lambda c: (jnp.minimum(c * tz + tz, depth - 1), 0, 0))
    row = pl.BlockSpec((tz, 1, ny), lambda c: (c, 0, 0))
    col = pl.BlockSpec((tz, nx, 1), lambda c: (c, 0, 0))
    side = [row, row, col, col]
    return pl.pallas_call(
        step_kernel,
        out_shape=jax.ShapeDtypeStruct((depth, nx, ny), jnp.float32),
        grid=grid,
        in_specs=[main, below, above] + side + [main, below, above] + side + [main],
        out_specs=main,
        compiler_params=pltpu.CompilerParams(dimension_semantics=("arbitrary",)),
    )(log_perm, log_perm, log_perm, *perm_halos, pressure, pressure, pressure, *pressure_halos, flow)


def body(noise, root_z, root_x, root_y, pressure_start, well_x, well_y, well_z, well_rate):
    depth, rows_x, rows_y = noise.shape
    first = jnp.dot(
        root_z, noise.reshape(depth, rows_x * rows_y), preferred_element_type=jnp.float32
    )
    first = first.reshape(depth, rows_x, rows_y).astype(jnp.bfloat16)
    count_w = lax.axis_size("wide")
    count_n = lax.axis_size("narrow")
    groups = count_w * count_n
    planes = depth // groups
    gathered = lax.all_to_all(
        first.reshape(groups, planes, rows_x, rows_y),
        ("wide", "narrow"), split_axis=0, concat_axis=0, tiled=True,
    ).reshape(count_w, count_n, planes, rows_x, rows_y)
    gathered = gathered.transpose(2, 0, 3, 1, 4).reshape(planes, count_w * rows_x, count_n * rows_y)
    second = jnp.einsum(
        "ia,zay->ziy", root_x, gathered, preferred_element_type=jnp.float32
    ).astype(jnp.bfloat16)
    third = jnp.einsum(
        "zxb,jb->zxj", second, root_y, preferred_element_type=jnp.float32
    ).astype(jnp.bfloat16)
    outgoing = third.reshape(planes, count_w, rows_x, count_n, rows_y).transpose(1, 3, 0, 2, 4)
    log_perm = lax.all_to_all(
        outgoing.reshape(groups, planes, rows_x, rows_y),
        ("wide", "narrow"), split_axis=0, concat_axis=0, tiled=True,
    ).reshape(depth, rows_x, rows_y)

    wide_at = lax.axis_index("wide")
    narrow_at = lax.axis_index("narrow")
    last_w = lax.axis_size("wide") - 1
    last_n = lax.axis_size("narrow") - 1

    local_x = well_x - wide_at * rows_x
    local_y = well_y - narrow_at * rows_y
    valid = (local_x >= 0) & (local_x < rows_x) & (local_y >= 0) & (local_y < rows_y)
    rates = jnp.where(valid, well_rate, 0.0).astype(jnp.float32)
    wells = well_x.shape[0]
    cells = well_z * rows_x + local_x
    pick_rows = jnp.where(
        lax.broadcasted_iota(jnp.int32, (depth * rows_x, wells), 0) == cells[None, :],
        rates[None, :],
        0.0,
    )
    pick_cols = (
        lax.broadcasted_iota(jnp.int32, (wells, rows_y), 1) == local_y[:, None]
    ).astype(jnp.float32)
    flow = jnp.dot(
        pick_rows, pick_cols, precision=lax.Precision.HIGHEST, preferred_element_type=jnp.float32
    ).reshape(depth, rows_x, rows_y)

    x_lo, x_hi, y_lo, y_hi = halos(log_perm, jnp.bfloat16)
    f32 = jnp.float32
    perm_halos = (
        jnp.where(wide_at > 0, permeability(x_lo.astype(f32)), 0.0),
        jnp.where(wide_at < last_w, permeability(x_hi.astype(f32)), 0.0),
        jnp.where(narrow_at > 0, permeability(y_lo.astype(f32)), 0.0),
        jnp.where(narrow_at < last_n, permeability(y_hi.astype(f32)), 0.0),
    )

    pressure = pressure_start
    for step in range(STEPS):
        pressure_halos = halos(pressure, pressure.dtype)
        pressure = advance(log_perm, perm_halos, pressure, pressure_halos, flow)
    return (log_perm, pressure)


def solution(mesh):
    in_specs = (
        P("member", "wide", "narrow"),
        P(),
        P(),
        P(),
        P("member", "wide", "narrow"),
        P("member"),
        P("member"),
        P("member"),
        P("member"),
    )
    out_specs = (P("member", "wide", "narrow"), P("member", "wide", "narrow"))
    return jax.shard_map(body, mesh=mesh, in_specs=in_specs, out_specs=out_specs, check_vma=False)
```

profile of v0, /device:TPU:11, one launch (start us, length us, event | category | flops | bytes accessed | tf_op | source)
XLA Modules:
  0.0 395.1 jit_solution(5816348506879502145)
XLA Ops:
  0.6 7.1 %copy.64 = bf16[16,8,64,256]{3,1,2,0:T(8,128)(2,1)} copy(bf16[16,8,64,256]{3,2,1,0:T(8,128)(2,1)} %bitcast.38) | data formatting | bytes 8388608
  7.8 6.4 %copy.41 = bf16[16384,128]{1,0:T(8,128)(2,1)} copy(bf16[16384,128]{0,1:T(8,128)(2,1)} %bitcast.37) | data formatting | bytes 8388608 | tf_op jit(solution)/shard_map/dot_general | solution.py:102
  14.2 3.4 convert_bitcast_fusion
  20.0 99.4 %all_to_all.10 = bf16[16,8,64,256]{3,2,1,0:T(8,128)(2,1)S(1)} all-to-all(bf16[16,8,64,256]{3,2,1,0:T(8,128)(2,1)S(1)} %copy.42), channel_id=1, replica_groups=mesh['member'=2,'wide'=8,'narrow'=2] {'wide','narrow'}, dimensions={0} | all-to-all | bytes 8388608 | tf_op jit(solution)/shard_map/all_to_all | solution.py:110
  119.4 6.4 %copy.43 = bf16[8,8,64,2,256]{4,3,2,1,0:T(2,128)(2,1)} copy(bf16[8,8,64,2,256]{4,2,0,3,1:T(8,128)(2,1)S(1)} %bitcast.35) | data formatting | bytes 8388608 | tf_op jit(solution)/shard_map/transpose | solution.py:114
  125.8 7.6 %reshape.45 = bf16[8,512,512]{2,1,0:T(8,128)(2,1)} reshape(bf16[8,8,64,2,256]{4,3,2,1,0:T(2,128)(2,1)} %copy.43) | data formatting | bytes 8388608 | tf_op jit(solution)/shard_map/reshape | solution.py:114
  133.5 7.7 %fusion.8 = bf16[8,512,512]{2,1,0:T(8,128)(2,1)} fusion(bf16[8,512,512]{2,1,0:T(8,128)(2,1)} %reshape.45, bf16[512,512]{1,0:T(8,128)(2,1)S(1)} %copy-done, bf16[512,512]{1,0:T(8,128)(2,1)S(1)} %copy-done.11), kind=kOutput, calls=%fused_computation.12 | convolution fusion | flops 4299161600 | bytes 9437184 | tf_op jit(solution)/shard_map/zxb,jb->zxj/dot_general | solution.py:118
  141.2 6.9 %reshape.37 = bf16[8,8,64,2,256]{4,3,2,1,0:T(2,128)(2,1)} reshape(bf16[8,512,512]{2,1,0:T(8,128)(2,1)} %fusion.8) | data formatting | bytes 8388608 | tf_op jit(solution)/shard_map/reshape | solution.py:121
  148.1 5.1 %copy.46 = bf16[8,2,8,64,256]{4,3,2,1,0:T(8,128)(2,1)} copy(bf16[8,2,8,64,256]{4,1,3,0,2:T(2,128)(2,1)} %bitcast.36) | data formatting | bytes 8388608 | tf_op jit(solution)/shard_map/transpose | solution.py:121
  153.2 4.8 %all-to-all-start.1 = ((bf16[16,8,64,256]{3,2,1,0:T(8,128)(2,1)}), bf16[16,8,64,256]{3,2,1,0:T(8,128)(2,1)}, u32[]{:S(2)}, u32[]{:S(2)}) async-start(bf16[16,8,64,256]{3,2,1,0:T(8,128)(2,1)} %bitcast.33), calls=%async_computation.1 | async-start | bytes 8388608 | tf_op jit(solution)/shard_map/all_to_all | solution.py:122
  158.0 4.3 %fusion.21 = (bf16[128,64,1]{2,1,0:T(8,128)(2,1)S(1)}, bf16[128,64,1]{2,1,0:T(8,128)(2,1)}) fusion(bf16[128,64,256]{2,1,0:T(8,128)(2,1)} %pa_ref.1), kind=kLoop, calls=%fused_computation.29 | loop fusion | bytes 65536 | tf_op jit(solution)/shard_map/slice | solution.py:33
  162.3 3.7 copy.62
  177.1 3.3 collective-permute-start.5
  180.5 6.7 %fusion = f32[8192,256]{1,0:T(8,128)} fusion(f32[256]{0:T(256)S(1)} %get-tuple-element.2, s32[256]{0:T(256)S(1)} %multiply_add_fusion, s32[256]{0:T(256)S(1)} %get-tuple-element.3), kind=kOutput, calls=%fused_computation | convolution fusion | flops 6446710784 | bytes 8391680 | tf_op jit(solution)/shard_map/dot_general | solution.py:146
  187.2 3.9 copy.53.qyl_ref
  191.1 3.9 copy.54.qyh_ref
  195.0 53.3 %all-to-all-done.1 = bf16[16,8,64,256]{3,2,1,0:T(8,128)(2,1)} async-done(((bf16[16,8,64,256]{3,2,1,0:T(8,128)(2,1)}), bf16[16,8,64,256]{3,2,1,0:T(8,128)(2,1)}, u32[]{:S(2)}, u32[]{:S(2)}) %all-to-all-start.1) | async-done | bytes 4194336 | tf_op jit(solution)/shard_map/all_to_all | solution.py:122
  248.3 4.3 %fusion.23 = (bf16[128,64,1]{2,1,0:T(8,128)(2,1)S(1)}, bf16[128,64,1]{2,1,0:T(8,128)(2,1)}) fusion(bf16[128,64,256]{2,1,0:T(8,128)(2,1)} %bitcast.11.lpm_ref.lpb_ref.lpa_ref), kind=kLoop, calls=%fused_computation.31 | loop fusion | bytes 65536 | tf_op jit(solution)/shard_map/slice | solution.py:33
  252.6 3.7 copy.47
  266.2 6.1 %collective-permute-start = (bf16[128,1,256]{2,1,0:T(2,128)(2,1)S(1)}, bf16[128,1,256]{2,1,0:T(2,128)(2,1)S(1)}, u32[]{:S(2)}, u32[]{:S(2)}) collective-permute-start(bf16[128,1,256]{2,1,0:T(2,128)(2,1)S(1)} %get-tuple-element.15), channel_id=1, source_target_pairs={{0,2},{2,4},{4,6},{6,8},{8,10},{10,12},{12,14},{1,3},{3,5},{5,7},{... | collective-permute-start | bytes 196616 | tf_op jit(solution)/shard_map/ppermute | solution.py:30
  272.3 4.4 %copy.48 = f32[128,64,1]{2,1,0:T(8,128)} copy(f32[128,64,1]{0,1,2:T(8,128)S(1)} %convert_multiply_fusion.1) | data formatting | bytes 65536 | tf_op jit(solution)/shard_map/div | solution.py:17
  276.7 4.4 %copy.50 = f32[128,64,1]{2,1,0:T(8,128)} copy(f32[128,64,1]{0,1,2:T(8,128)S(1)} %convert_multiply_fusion) | data formatting | bytes 65536 | tf_op jit(solution)/shard_map/div | solution.py:17
  281.1 9.2 %exponential_select_fusion = (f32[128,64,1]{2,1,0:T(8,128)}, f32[128,64,1]{2,1,0:T(8,128)}) fusion(f32[128,64,1]{2,1,0:T(8,128)} %copy.50, pred[]{:T(512)S(6)} %lt.16, f32[128,64,1]{2,1,0:T(8,128)} %copy.48, pred[]{:T(512)S(6)} %gt.7), kind=kLoop, calls=%fused_computation.8 | loop fusion | flops 32768 | bytes 131074 | tf_op jit(solution)/shard_map/jit(_where)/select_n | solution.py:156
  292.9 29.1 %shard_map.104.pm_ref.pb_ref.pa_ref = f32[128,64,256]{2,1,0:T(8,128)} custom-call(bf16[128,64,256]{2,1,0:T(8,128)(2,1)} %bitcast.11.lpm_ref.lpb_ref.lpa_ref, bf16[128,64,256]{2,1,0:T(8,128)(2,1)} %bitcast.11.lpm_ref.lpb_ref.lpa_ref, bf16[128,64,256]{2,1,0:T(8,128)(2,1)} %bitcast.11.lpm_ref.lpb_ref.lpa_ref, f32[128,1,256]{2,1,0:T(1,128)} %broadcast_select_fusion.1.kxl_ref, ...), custom_call_target="tpu_custom_call" | custom-call | tf_op jit(solution)/shard_map/pallas_call | solution.py:90
  323.8 4.3 %collective-permute-start.8 = (f32[128,1,256]{2,1,0:T(1,128)S(1)}, f32[128,1,256]{2,1,0:T(1,128)S(1)}, u32[]{:S(2)}, u32[]{:S(2)}) collective-permute-start(f32[128,1,256]{2,1,0:T(1,128)S(1)} %get-tuple-element.7), channel_id=1, source_target_pairs={{0,2},{2,4},{4,6},{6,8},{8,10},{10,12},{12,14},{1,3},{3,5},{5,7},{... | collective-permute-start | bytes 393224 | tf_op jit(solution)/shard_map/ppermute | solution.py:30
  330.0 8.1 %fusion.19 = (f32[128,64,1]{2,1,0:T(8,128)}, f32[128,64,1]{2,1,0:T(8,128)}) fusion(f32[128,64,256]{2,1,0:T(8,128)} %shard_map.104.pm_ref.pb_ref.pa_ref), kind=kLoop, calls=%fused_computation.27 | loop fusion | bytes 131072 | tf_op jit(solution)/shard_map/slice | solution.py:33
  338.1 3.7 copy.55
  343.2 3.7 copy.56
  350.1 4.5 %copy.57.qyl_ref = f32[128,64,1]{2,1,0:T(8,128)} copy(f32[128,64,1]{0,1,2:T(8,128)S(1)} %collective-permute-done.10) | data formatting | bytes 65536 | tf_op jit(solution)/shard_map/ppermute | solution.py:32
  354.6 4.5 %copy.58.qyh_ref = f32[128,64,1]{2,1,0:T(8,128)} copy(f32[128,64,1]{0,1,2:T(8,128)S(1)} %collective-permute-done.11) | data formatting | bytes 65536 | tf_op jit(solution)/shard_map/ppermute | solution.py:33
  360.3 29.8 %shard_map.105 = f32[128,64,256]{2,1,0:T(8,128)} custom-call(bf16[128,64,256]{2,1,0:T(8,128)(2,1)} %bitcast.11.lpm_ref.lpb_ref.lpa_ref, bf16[128,64,256]{2,1,0:T(8,128)(2,1)} %bitcast.11.lpm_ref.lpb_ref.lpa_ref, bf16[128,64,256]{2,1,0:T(8,128)(2,1)} %bitcast.11.lpm_ref.lpb_ref.lpa_ref, f32[128,1,256]{2,1,0:T(1,128)} %broadcast_select_fusion.1.kxl_ref, ...), custom_call_target="tpu_custom_call" | custom-call | tf_op jit(solution)/shard_map/pallas_call | solution.py:90
  390.1 4.8 %copy.66 = bf16[128,64,256]{2,1,0:T(8,128)(2,1)} copy(bf16[128,64,256]{2,1,0:T(8,128)(2,1)} %bitcast.11.lpm_ref.lpb_ref.lpa_ref) | data formatting | bytes 8388608
  (57 shorter events, 35.3 us)
Async XLA Ops:
  0.6 132.9 %copy-start = (bf16[512,512]{1,0:T(8,128)(2,1)S(1)}, bf16[512,512]{1,0:T(8,128)(2,1)}, u32[]{:S(2)}) copy-start(bf16[512,512]{1,0:T(8,128)(2,1)} %param.12) | copy-start | bytes 1572868
  7.8 6.4 %copy-start.6 = (bf16[128,128]{1,0:T(8,128)(2,1)S(1)}, bf16[128,128]{1,0:T(8,128)(2,1)}, u32[]{:S(2)}) copy-start(bf16[128,128]{1,0:T(8,128)(2,1)} %param.10) | copy-start | bytes 98308
  125.8 7.6 %copy-start.11 = (bf16[512,512]{1,0:T(8,128)(2,1)S(1)}, bf16[512,512]{1,0:T(8,128)(2,1)}, u32[]{:S(2)}) copy-start(bf16[512,512]{1,0:T(8,128)(2,1)} %param.11) | copy-start | bytes 1572868
  153.2 95.1 %all-to-all-start.1 = ((bf16[16,8,64,256]{3,2,1,0:T(8,128)(2,1)}), bf16[16,8,64,256]{3,2,1,0:T(8,128)(2,1)}, u32[]{:S(2)}, u32[]{:S(2)}) async-start(bf16[16,8,64,256]{3,2,1,0:T(8,128)(2,1)} %bitcast.33), calls=%async_computation.1 | async-start | bytes 8388608 | tf_op jit(solution)/shard_map/all_to_all | solution.py:122
  162.3 18.1 %copy-start.7 = (s32[256]{0:T(256)S(1)}, s32[256]{0:T(256)}, u32[]{:S(2)}) copy-start(s32[256]{0:T(256)} %param.14) | copy-start | bytes 3076
  162.3 18.1 %copy-start.8 = (s32[256]{0:T(256)S(1)}, s32[256]{0:T(256)}, u32[]{:S(2)}) copy-start(s32[256]{0:T(256)} %param.16) | copy-start | bytes 3076
  162.3 18.1 %copy-start.9 = (f32[256]{0:T(256)S(1)}, f32[256]{0:T(256)}, u32[]{:S(2)}) copy-start(f32[256]{0:T(256)} %param.17) | copy-start | bytes 3076
  162.3 18.1 %copy-start.10 = (s32[256]{0:T(256)S(1)}, s32[256]{0:T(256)}, u32[]{:S(2)}) copy-start(s32[256]{0:T(256)} %param.15) | copy-start | bytes 3076
  166.0 21.2 %collective-permute-start.6 = (bf16[128,64,1]{0,1,2:T(8,128)(2,1)S(1)}, bf16[128,64,1]{0,1,2:T(8,128)(2,1)S(1)}, u32[]{:S(2)}, u32[]{:S(2)}) collective-permute-start(bf16[128,64,1]{0,1,2:T(8,128)(2,1)S(1)} %copy.62), channel_id=1, source_target_pairs={{0,1},{2,3},{4,5},{6,7},{8,9},{10,11},{12,13},{14,15},{16,17},{18,... | collective-permute-start | bytes 49160 | tf_op jit(solution)/shard_map/ppermute | solution.py:32
  169.5 21.6 %collective-permute-start.7 = (bf16[128,64,1]{0,1,2:T(8,128)(2,1)S(1)}, bf16[128,64,1]{0,1,2:T(8,128)(2,1)S(1)}, u32[]{:S(2)}, u32[]{:S(2)}) collective-permute-start(bf16[128,64,1]{0,1,2:T(8,128)(2,1)S(1)} %copy.63), channel_id=1, source_target_pairs={{1,0},{3,2},{5,4},{7,6},{9,8},{11,10},{13,12},{15,14},{17,16},{19,... | collective-permute-start | bytes 49160 | tf_op jit(solution)/shard_map/ppermute | solution.py:33
  174.0 118.3 %collective-permute-start.4 = (bf16[128,1,256]{2,1,0:T(2,128)(2,1)S(1)}, bf16[128,1,256]{2,1,0:T(2,128)(2,1)S(1)}, u32[]{:S(2)}, u32[]{:S(2)}) collective-permute-start(bf16[128,1,256]{2,1,0:T(2,128)(2,1)S(1)} %get-tuple-element.11), channel_id=1, source_target_pairs={{0,2},{2,4},{4,6},{6,8},{8,10},{10,12},{12,14},{1,3},{3,5},{5,7},{... | collective-permute-start | bytes 196616 | tf_op jit(solution)/shard_map/ppermute | solution.py:30
  177.1 115.2 %collective-permute-start.5 = (bf16[128,1,256]{2,1,0:T(2,128)(2,1)S(1)}, bf16[128,1,256]{2,1,0:T(2,128)(2,1)S(1)}, u32[]{:S(2)}, u32[]{:S(2)}) collective-permute-start(bf16[128,1,256]{2,1,0:T(2,128)(2,1)S(1)} %get-tuple-element.10), channel_id=1, source_target_pairs={{2,0},{4,2},{6,4},{8,6},{10,8},{12,10},{14,12},{3,1},{5,3},{7,5},{... | collective-permute-start | bytes 196616 | tf_op jit(solution)/shard_map/ppermute | solution.py:31
  256.3 9.9 %collective-permute-start.2 = (bf16[128,64,1]{0,1,2:T(8,128)(2,1)S(1)}, bf16[128,64,1]{0,1,2:T(8,128)(2,1)S(1)}, u32[]{:S(2)}, u32[]{:S(2)}) collective-permute-start(bf16[128,64,1]{0,1,2:T(8,128)(2,1)S(1)} %copy.47), channel_id=1, source_target_pairs={{0,1},{2,3},{4,5},{6,7},{8,9},{10,11},{12,13},{14,15},{16,17},{18,... | collective-permute-start | bytes 49160 | tf_op jit(solution)/shard_map/ppermute | solution.py:32
  261.2 15.5 %collective-permute-start.3 = (bf16[128,64,1]{0,1,2:T(8,128)(2,1)S(1)}, bf16[128,64,1]{0,1,2:T(8,128)(2,1)S(1)}, u32[]{:S(2)}, u32[]{:S(2)}) collective-permute-start(bf16[128,64,1]{0,1,2:T(8,128)(2,1)S(1)} %copy.49), channel_id=1, source_target_pairs={{1,0},{3,2},{5,4},{7,6},{9,8},{11,10},{13,12},{15,14},{17,16},{19,... | collective-permute-start | bytes 49160 | tf_op jit(solution)/shard_map/ppermute | solution.py:33
  264.3 26.1 %collective-permute-start.1 = (bf16[128,1,256]{2,1,0:T(2,128)(2,1)S(1)}, bf16[128,1,256]{2,1,0:T(2,128)(2,1)S(1)}, u32[]{:S(2)}, u32[]{:S(2)}) collective-permute-start(bf16[128,1,256]{2,1,0:T(2,128)(2,1)S(1)} %get-tuple-element.14), channel_id=1, source_target_pairs={{2,0},{4,2},{6,4},{8,6},{10,8},{12,10},{14,12},{3,1},{5,3},{7,5},{... | collective-permute-start | bytes 196616 | tf_op jit(solution)/shard_map/ppermute | solution.py:31
  266.2 25.1 %collective-permute-start = (bf16[128,1,256]{2,1,0:T(2,128)(2,1)S(1)}, bf16[128,1,256]{2,1,0:T(2,128)(2,1)S(1)}, u32[]{:S(2)}, u32[]{:S(2)}) collective-permute-start(bf16[128,1,256]{2,1,0:T(2,128)(2,1)S(1)} %get-tuple-element.15), channel_id=1, source_target_pairs={{0,2},{2,4},{4,6},{6,8},{8,10},{10,12},{12,14},{1,3},{3,5},{5,7},{... | collective-permute-start | bytes 196616 | tf_op jit(solution)/shard_map/ppermute | solution.py:30
  292.2 0.7 copy-start.2
  292.3 0.7 copy-start.3
  323.8 35.3 %collective-permute-start.8 = (f32[128,1,256]{2,1,0:T(1,128)S(1)}, f32[128,1,256]{2,1,0:T(1,128)S(1)}, u32[]{:S(2)}, u32[]{:S(2)}) collective-permute-start(f32[128,1,256]{2,1,0:T(1,128)S(1)} %get-tuple-element.7), channel_id=1, source_target_pairs={{0,2},{2,4},{4,6},{6,8},{8,10},{10,12},{12,14},{1,3},{3,5},{5,7},{... | collective-permute-start | bytes 393224 | tf_op jit(solution)/shard_map/ppermute | solution.py:30
  328.0 31.0 %collective-permute-start.9 = (f32[128,1,256]{2,1,0:T(1,128)S(1)}, f32[128,1,256]{2,1,0:T(1,128)S(1)}, u32[]{:S(2)}, u32[]{:S(2)}) collective-permute-start(f32[128,1,256]{2,1,0:T(1,128)S(1)} %get-tuple-element.6), channel_id=1, source_target_pairs={{2,0},{4,2},{6,4},{8,6},{10,8},{12,10},{14,12},{3,1},{5,3},{7,5},{... | collective-permute-start | bytes 393224 | tf_op jit(solution)/shard_map/ppermute | solution.py:31
  341.9 8.2 %collective-permute-start.10 = (f32[128,64,1]{0,1,2:T(8,128)S(1)}, f32[128,64,1]{0,1,2:T(8,128)S(1)}, u32[]{:S(2)}, u32[]{:S(2)}) collective-permute-start(f32[128,64,1]{0,1,2:T(8,128)S(1)} %copy.55), channel_id=1, source_target_pairs={{0,1},{2,3},{4,5},{6,7},{8,9},{10,11},{12,13},{14,15},{16,17},{18,... | collective-permute-start | bytes 98312 | tf_op jit(solution)/shard_map/ppermute | solution.py:32
  346.9 7.7 %collective-permute-start.11 = (f32[128,64,1]{0,1,2:T(8,128)S(1)}, f32[128,64,1]{0,1,2:T(8,128)S(1)}, u32[]{:S(2)}, u32[]{:S(2)}) collective-permute-start(f32[128,64,1]{0,1,2:T(8,128)S(1)} %copy.56), channel_id=1, source_target_pairs={{1,0},{3,2},{5,4},{7,6},{9,8},{11,10},{13,12},{15,14},{17,16},{19,... | collective-permute-start | bytes 98312 | tf_op jit(solution)/shard_map/ppermute | solution.py:33
  359.0 0.7 copy-start.4
  359.7 0.6 copy-start.5
  360.3 34.6 %copy-start.1 = (bf16[512,512]{1,0:T(8,128)(2,1)S(1)}, bf16[512,512]{1,0:T(8,128)(2,1)}, u32[]{:S(2)}) copy-start(bf16[512,512]{1,0:T(8,128)(2,1)} %param.12) | copy-start | bytes 1572868
where the time goes:
time: 403 us; the launch traced here: 395 us
  local copies, waits for them, and re-layouts  115 us (29%)
  blocking collectives  99.4 us (25%)
  Pallas kernels  58.9 us (15%)
  waiting for transfers between devices  53.3 us (13%)
  starting transfers between devices  38.4 us (10%)
  matrix products  17.9 us (4%)
  other arithmetic  11.1 us (3%)
    all_to_all x1, blocking collectives, body(): lax.all_to_all(first.reshape(groups, planes, rows_x, rows_y), ('wide', 'n...  99.4 us
    pallas_call x2, Pallas kernels, advance(): pl.pallas_call(step_kernel, out_shape=jax.ShapeDtypeStruct((depth, nx, ny...  58.9 us
    all_to_all x1, waiting for transfers between devices, body(): lax.all_to_all(outgoing.reshape(groups, planes, rows_x, rows_y), ('wide',...  53.3 us
    slice x5, local copies, waits for them, and re-layouts, halos(): y_hi = lax.ppermute(block[:, :, :1], 'narrow', backward_n)  22.8 us
    unnamed x28, local copies, waits for them, and re-layouts  19.9 us
    ppermute x3, starting transfers between devices, halos(): x_lo = lax.ppermute(block[:, -1:, :], 'wide', forward_w)  13.4 us
    ppermute x3, starting transfers between devices, halos(): y_hi = lax.ppermute(block[:, :, :1], 'narrow', backward_n)  9.23 us
    select_n x1, other arithmetic, body(): jnp.where(narrow_at < last_n, permeability(y_hi.astype(f32)), 0.0)  9.23 us
  transfers between devices with their start and end apart: 13, of which 1 were waited for; matrix products, arithmetic and copies ran while one was open for 21% of the time, Pallas kernels for 0%

commit v1 on v0

--- a/solution.py
+++ b/solution.py
@@ -21,27 +21,40 @@
     return 2.0 * a * b / (a + b)
 
 
-def halos(block, dtype):
+def block_edges(block):
+    return block[:, :1, :], block[:, -1:, :], block[:, :, :1], block[:, :, -1:]
+
+
+def halos(edges):
     forward_w = [(i, i + 1) for i in range(lax.axis_size("wide") - 1)]
     backward_w = [(j, i) for i, j in forward_w]
     forward_n = [(i, i + 1) for i in range(lax.axis_size("narrow") - 1)]
     backward_n = [(j, i) for i, j in forward_n]
-    block = block.astype(dtype)
-    x_lo = lax.ppermute(block[:, -1:, :], "wide", forward_w)
-    x_hi = lax.ppermute(block[:, :1, :], "wide", backward_w)
-    y_lo = lax.ppermute(block[:, :, -1:], "narrow", forward_n)
-    y_hi = lax.ppermute(block[:, :, :1], "narrow", backward_n)
+    first_x, last_x, first_y, last_y = edges
+    x_lo = lax.ppermute(last_x, "wide", forward_w)
+    x_hi = lax.ppermute(first_x, "wide", backward_w)
+    y_lo = lax.ppermute(last_y, "narrow", forward_n)
+    y_hi = lax.ppermute(first_y, "narrow", backward_n)
     return x_lo, x_hi, y_lo, y_hi
 
 
 def step_kernel(
-    lpm_ref, lpb_ref, lpa_ref, kxl_ref, kxh_ref, kyl_ref, kyh_ref,
-    pm_ref, pb_ref, pa_ref, qxl_ref, qxh_ref, qyl_ref, qyh_ref, f_ref, o_ref,
+    inside_ref, lpm_ref, lpb_ref, lpa_ref, lxl_ref, lxh_ref, lyl_ref, lyh_ref,
+    pm_ref, pb_ref, pa_ref, qxl_ref, qxh_ref, qyl_ref, qyh_ref, f_ref,
+    o_ref, exl_ref, exh_ref, eyl_ref, eyh_ref,
 ):
     c = pl.program_id(0)
     last = pl.num_programs(0) - 1
     tz, nx, ny = pm_ref.shape
     f32 = jnp.float32
+
+    def side_perm(ref, k):
+        return jnp.where(inside_ref[k] > 0, permeability(ref[...].astype(f32)), 0.0)
+
+    kxl = side_perm(lxl_ref, 0)
+    kxh = side_perm(lxh_ref, 1)
+    kyl = side_perm(lyl_ref, 2)
+    kyh = side_perm(lyh_ref, 3)
 
     below = jnp.where(c == 0, 0.0, permeability(lpb_ref[...].astype(f32)))
     above = jnp.where(c == last, 0.0, permeability(lpa_ref[...].astype(f32)))
@@ -55,11 +68,11 @@
     yi = lax.broadcasted_iota(jnp.int32, (tz, nx, ny), 2)
 
     fx = harmonic(centre, pltpu.roll(centre, nx - 1, 1))
-    t_xp = jnp.where(xi == nx - 1, harmonic(centre[:, nx - 1 :, :], kxh_ref[...]), fx)
-    t_xm = jnp.where(xi == 0, harmonic(centre[:, :1, :], kxl_ref[...]), pltpu.roll(fx, 1, 1))
+    t_xp = jnp.where(xi == nx - 1, harmonic(centre[:, nx - 1 :, :], kxh), fx)
+    t_xm = jnp.where(xi == 0, harmonic(centre[:, :1, :], kxl), pltpu.roll(fx, 1, 1))
     fy = harmonic(centre, pltpu.roll(centre, ny - 1, 2))
-    t_yp = jnp.where(yi == ny - 1, harmonic(centre[:, :, ny - 1 :], kyh_ref[...]), fy)
-    t_ym = jnp.where(yi == 0, harmonic(centre[:, :, :1], kyl_ref[...]), pltpu.roll(fy, 1, 2))
+    t_yp = jnp.where(yi == ny - 1, harmonic(centre[:, :, ny - 1 :], kyh), fy)
+    t_ym = jnp.where(yi == 0, harmonic(centre[:, :, :1], kyl), pltpu.roll(fy, 1, 2))
 
     p = pm_ref[...].astype(f32)
     pext = jnp.concatenate([pb_ref[...].astype(f32), p, pa_ref[...].astype(f32)], axis=0)
@@ -74,10 +87,15 @@
     flux = flux + t_xm * (n_xm - p)
     flux = flux + t_yp * (n_yp - p)
     flux = flux + t_ym * (n_ym - p)
-    o_ref[...] = p + STEP_SIZE * (flux + f_ref[...]) / (1.0 + 0.5 * p * p)
-
-
-def advance(log_perm, perm_halos, pressure, pressure_halos, flow):
+    new = p + STEP_SIZE * (flux + f_ref[...]) / (1.0 + 0.5 * p * p)
+    o_ref[...] = new
+    exl_ref[...] = new[:, :1, :]
+    exh_ref[...] = new[:, nx - 1 :, :]
+    eyl_ref[...] = new[:, :, :1]
+    eyh_ref[...] = new[:, :, ny - 1 :]
+
+
+def advance(inside, log_perm, perm_halos, pressure, pressure_halos, flow):
     depth, nx, ny = pressure.shape
     tz = CHUNK_Z
     grid = (depth // tz,)
@@ -87,14 +105,24 @@
     row = pl.BlockSpec((tz, 1, ny), lambda c: (c, 0, 0))
     col = pl.BlockSpec((tz, nx, 1), lambda c: (c, 0, 0))
     side = [row, row, col, col]
-    return pl.pallas_call(
+    smem = pl.BlockSpec(memory_space=pltpu.SMEM)
+    f32 = jnp.float32
+    out_shape = (
+        jax.ShapeDtypeStruct((depth, nx, ny), f32),
+        jax.ShapeDtypeStruct((depth, 1, ny), f32),
+        jax.ShapeDtypeStruct((depth, 1, ny), f32),
+        jax.ShapeDtypeStruct((depth, nx, 1), f32),
+        jax.ShapeDtypeStruct((depth, nx, 1), f32),
+    )
+    new, x_lo, x_hi, y_lo, y_hi = pl.pallas_call(
         step_kernel,
-        out_shape=jax.ShapeDtypeStruct((depth, nx, ny), jnp.float32),
+        out_shape=out_shape,
         grid=grid,
-        in_specs=[main, below, above] + side + [main, below, above] + side + [main],
-        out_specs=main,
+        in_specs=[smem, main, below, above] + side + [main, below, above] + side + [main],
+        out_specs=[main] + side,
         compiler_params=pltpu.CompilerParams(dimension_semantics=("arbitrary",)),
-    )(log_perm, log_perm, log_perm, *perm_halos, pressure, pressure, pressure, *pressure_halos, flow)
+    )(inside, log_perm, log_perm, log_perm, *perm_halos, pressure, pressure, pressure, *pressure_halos, flow)
+    return new, (x_lo, x_hi, y_lo, y_hi)
 
 
 def body(noise, root_z, root_x, root_y, pressure_start, well_x, well_y, well_z, well_rate):
@@ -147,19 +175,14 @@
         pick_rows, pick_cols, precision=lax.Precision.HIGHEST, preferred_element_type=jnp.float32
     ).reshape(depth, rows_x, rows_y)
 
-    x_lo, x_hi, y_lo, y_hi = halos(log_perm, jnp.bfloat16)
-    f32 = jnp.float32
-    perm_halos = (
-        jnp.where(wide_at > 0, permeability(x_lo.astype(f32)), 0.0),
-        jnp.where(wide_at < last_w, permeability(x_hi.astype(f32)), 0.0),
-        jnp.where(narrow_at > 0, permeability(y_lo.astype(f32)), 0.0),
-        jnp.where(narrow_at < last_n, permeability(y_hi.astype(f32)), 0.0),
-    )
-
+    inside = jnp.stack(
+        [wide_at > 0, wide_at < last_w, narrow_at > 0, narrow_at < last_n]
+    ).astype(jnp.int32)
+    perm_halos = halos(block_edges(log_perm))
     pressure = pressure_start
+    edges = block_edges(pressure_start)
     for step in range(STEPS):
-        pressure_halos = halos(pressure, pressure.dtype)
-        pressure = advance(log_perm, perm_halos, pressure, pressure_halos, flow)
+        pressure, edges = advance(inside, log_perm, perm_halos, pressure, halos(edges), flow)
     return (log_perm, pressure)
 
 

time: 403 us -> 394 us (0.978)
  local copies, waits for them, and re-layouts: 115 us -> 104 us
  other arithmetic: 11.1 us -> 0.58 us
  waiting for transfers between devices: 53.3 us -> 61.1 us
  Pallas kernels: 58.9 us -> 63.9 us
    slice x10 -> x6, local copies, waits for them, and re-layouts: 34.8 us -> 17.4 us  [the longest x3 10.9 us: block_edges(): block[:, :, :1]]
    select_n x3 -> x0, other arithmetic: 11.1 us -> none  [the longest x1 9.23 us: body(): jnp.where(narrow_at < last_n, permeability(y_hi.astype(f32)), 0.0)]
    div x2 -> x0, local copies, waits for them, and re-layouts: 8.83 us -> none  [permeability(): return jnp.exp(CAP_LOG * jnp.tanh(values / CAP_LOG))]
    ppermute x4 -> x6, local copies, waits for them, and re-layouts: 16.8 us -> 24.7 us  [the longest x3 12.4 us: halos(): y_hi = lax.ppermute(first_y, 'narrow', backward_n)]
    all_to_all x1, waiting for transfers between devices: 53.3 us -> 61.1 us  [body(): lax.all_to_all(outgoing.reshape(groups, planes, rows_x, rows_y), ('wide',...]
    pallas_call x0 -> x2, local copies, waits for them, and re-layouts: none -> 7.49 us  [advance(): pl.pallas_call(step_kernel, out_shape=out_shape, grid=grid, in_specs=[sme...]
    pallas_call x2, Pallas kernels: 58.9 us -> 63.9 us  [advance(): pl.pallas_call(step_kernel, out_shape=out_shape, grid=grid, in_specs=[sme...]
    unnamed x28 -> x32, local copies, waits for them, and re-layouts: 19.9 us -> 19.5 us
  transfers between devices with their start and end apart: 13 -> 13, of which waited for: 1 -> 1; matrix products, arithmetic and copies ran while one was open for 21% -> 16% of each run, Pallas kernels for 0% -> 0%
where the time goes in v1:
time: 394 us; the launch traced here: 386 us
  local copies, waits for them, and re-layouts  104 us (26%)
  blocking collectives  99.4 us (25%)
  Pallas kernels  63.9 us (16%)
  waiting for transfers between devices  61.1 us (16%)
  starting transfers between devices  38.1 us (10%)
  matrix products  17.9 us (5%)
    all_to_all x1, blocking collectives, body(): lax.all_to_all(first.reshape(groups, planes, rows_x, rows_y), ('wide', 'n...  99.4 us
    pallas_call x2, Pallas kernels, advance(): pl.pallas_call(step_kernel, out_shape=out_shape, grid=grid, in_specs=[sme...  63.9 us
    all_to_all x1, waiting for transfers between devices, body(): lax.all_to_all(outgoing.reshape(groups, planes, rows_x, rows_y), ('wide',...  61.1 us
    unnamed x32, local copies, waits for them, and re-layouts  19.5 us
    ppermute x3, local copies, waits for them, and re-layouts, halos(): y_hi = lax.ppermute(first_y, 'narrow', backward_n)  12.4 us
    ppermute x3, local copies, waits for them, and re-layouts, halos(): y_lo = lax.ppermute(last_y, 'narrow', forward_n)  12.3 us
    ppermute x3, starting transfers between devices, halos(): x_lo = lax.ppermute(last_x, 'wide', forward_w)  12.1 us
    slice x3, local copies, waits for them, and re-layouts, block_edges(): block[:, :, :1]  10.9 us
  transfers between devices with their start and end apart: 13, of which 1 were waited for; matrix products, arithmetic and copies ran while one was open for 16% of the time, Pallas kernels for 0%

profile of v1, /device:TPU:11, one launch (start us, length us, event | category | flops | bytes accessed | tf_op | source)
XLA Modules:
  0.0 386.2 jit_solution(12943225677221337263)
XLA Ops:
  0.6 7.1 %copy.46 = bf16[16,8,64,256]{3,1,2,0:T(8,128)(2,1)} copy(bf16[16,8,64,256]{3,2,1,0:T(8,128)(2,1)} %bitcast.42) | data formatting | bytes 8388608
  7.8 6.4 %copy.21 = bf16[16384,128]{1,0:T(8,128)(2,1)} copy(bf16[16384,128]{0,1:T(8,128)(2,1)} %bitcast.41) | data formatting | bytes 8388608 | tf_op jit(solution)/shard_map/dot_general | solution.py:130
  14.2 3.4 convert_bitcast_fusion
  20.0 99.4 %all_to_all.10 = bf16[16,8,64,256]{3,2,1,0:T(8,128)(2,1)S(1)} all-to-all(bf16[16,8,64,256]{3,2,1,0:T(8,128)(2,1)S(1)} %copy.22), channel_id=1, replica_groups=mesh['member'=2,'wide'=8,'narrow'=2] {'wide','narrow'}, dimensions={0} | all-to-all | bytes 8388608 | tf_op jit(solution)/shard_map/all_to_all | solution.py:138
  119.4 6.4 %copy.23 = bf16[8,8,64,2,256]{4,3,2,1,0:T(2,128)(2,1)} copy(bf16[8,8,64,2,256]{4,2,0,3,1:T(8,128)(2,1)S(1)} %bitcast.39) | data formatting | bytes 8388608 | tf_op jit(solution)/shard_map/transpose | solution.py:142
  125.8 7.6 %reshape.45 = bf16[8,512,512]{2,1,0:T(8,128)(2,1)} reshape(bf16[8,8,64,2,256]{4,3,2,1,0:T(2,128)(2,1)} %copy.23) | data formatting | bytes 8388608 | tf_op jit(solution)/shard_map/reshape | solution.py:142
  133.5 7.7 %fusion.8 = bf16[8,512,512]{2,1,0:T(8,128)(2,1)} fusion(bf16[8,512,512]{2,1,0:T(8,128)(2,1)} %reshape.45, bf16[512,512]{1,0:T(8,128)(2,1)S(1)} %copy-done, bf16[512,512]{1,0:T(8,128)(2,1)S(1)} %copy-done.13), kind=kOutput, calls=%fused_computation.10 | convolution fusion | flops 4299161600 | bytes 9437184 | tf_op jit(solution)/shard_map/zxb,jb->zxj/dot_general | solution.py:146
  141.2 6.9 %reshape.37 = bf16[8,8,64,2,256]{4,3,2,1,0:T(2,128)(2,1)} reshape(bf16[8,512,512]{2,1,0:T(8,128)(2,1)} %fusion.8) | data formatting | bytes 8388608 | tf_op jit(solution)/shard_map/reshape | solution.py:149
  148.1 5.1 %copy.26 = bf16[8,2,8,64,256]{4,3,2,1,0:T(8,128)(2,1)} copy(bf16[8,2,8,64,256]{4,1,3,0,2:T(2,128)(2,1)} %bitcast.40) | data formatting | bytes 8388608 | tf_op jit(solution)/shard_map/transpose | solution.py:149
  153.2 4.8 %all-to-all-start.1 = ((bf16[16,8,64,256]{3,2,1,0:T(8,128)(2,1)}), bf16[16,8,64,256]{3,2,1,0:T(8,128)(2,1)}, u32[]{:S(2)}, u32[]{:S(2)}) async-start(bf16[16,8,64,256]{3,2,1,0:T(8,128)(2,1)} %bitcast.37), calls=%async_computation.1 | async-start | bytes 8388608 | tf_op jit(solution)/shard_map/all_to_all | solution.py:150
  158.0 4.3 %fusion.19 = (bf16[128,64,1]{2,1,0:T(8,128)(2,1)S(1)}, bf16[128,64,1]{2,1,0:T(8,128)(2,1)}) fusion(bf16[128,64,256]{2,1,0:T(8,128)(2,1)} %pa_ref.1), kind=kLoop, calls=%fused_computation.22 | loop fusion | bytes 65536 | tf_op jit(solution)/shard_map/slice | solution.py:25
  162.3 3.7 copy.44
  174.0 3.1 collective-permute-start.4
  177.1 3.3 collective-permute-start.5
  180.5 6.7 %fusion = f32[8192,256]{1,0:T(8,128)} fusion(f32[256]{0:T(256)S(1)} %get-tuple-element.14, s32[256]{0:T(256)S(1)} %multiply_add_fusion, s32[256]{0:T(256)S(1)} %get-tuple-element.15), kind=kOutput, calls=%fused_computation | convolution fusion | flops 6446710784 | bytes 8391680 | tf_op jit(solution)/shard_map/dot_general | solution.py:174
  187.2 61.1 %all-to-all-done.1 = bf16[16,8,64,256]{3,2,1,0:T(8,128)(2,1)} async-done(((bf16[16,8,64,256]{3,2,1,0:T(8,128)(2,1)}), bf16[16,8,64,256]{3,2,1,0:T(8,128)(2,1)}, u32[]{:S(2)}, u32[]{:S(2)}) %all-to-all-start.1) | async-done | bytes 4194336 | tf_op jit(solution)/shard_map/all_to_all | solution.py:150
  248.3 4.3 %fusion.21 = (bf16[128,64,1]{2,1,0:T(8,128)(2,1)S(1)}, bf16[128,64,1]{2,1,0:T(8,128)(2,1)}) fusion(bf16[128,64,256]{2,1,0:T(8,128)(2,1)} %bitcast.11.lpm_ref.lpb_ref.lpa_ref), kind=kLoop, calls=%fused_computation.24 | loop fusion | bytes 65536 | tf_op jit(solution)/shard_map/slice | solution.py:25
  252.6 3.7 copy.27
  264.3 5.7 %collective-permute-start = (bf16[128,1,256]{2,1,0:T(2,128)(2,1)S(1)}, bf16[128,1,256]{2,1,0:T(2,128)(2,1)S(1)}, u32[]{:S(2)}, u32[]{:S(2)}) collective-permute-start(bf16[128,1,256]{2,1,0:T(2,128)(2,1)S(1)} %get-tuple-element.23), channel_id=1, source_target_pairs={{0,2},{2,4},{4,6},{6,8},{8,10},{10,12},{12,14},{1,3},{3,5},{5,7},{... | collective-permute-start | bytes 196616 | tf_op jit(solution)/shard_map/ppermute | solution.py:34
  272.5 4.0 %copy.33.qyl_ref = bf16[128,64,1]{2,1,0:T(8,128)(2,1)} copy(bf16[128,64,1]{0,1,2:T(8,128)(2,1)S(1)} %collective-permute-done.6) | data formatting | bytes 32768 | tf_op jit(solution)/shard_map/ppermute | solution.py:36
  276.4 3.9 %copy.34.qyh_ref = bf16[128,64,1]{2,1,0:T(8,128)(2,1)} copy(bf16[128,64,1]{0,1,2:T(8,128)(2,1)S(1)} %collective-permute-done.7) | data formatting | bytes 32768 | tf_op jit(solution)/shard_map/ppermute | solution.py:37
  280.4 3.9 %copy.37.lyl_ref = bf16[128,64,1]{2,1,0:T(8,128)(2,1)} copy(bf16[128,64,1]{0,1,2:T(8,128)(2,1)S(1)} %collective-permute-done.2) | data formatting | bytes 32768 | tf_op jit(solution)/shard_map/ppermute | solution.py:36
  284.3 4.0 %copy.38.lyh_ref = bf16[128,64,1]{2,1,0:T(8,128)(2,1)} copy(bf16[128,64,1]{0,1,2:T(8,128)(2,1)S(1)} %collective-permute-done.3) | data formatting | bytes 32768 | tf_op jit(solution)/shard_map/ppermute | solution.py:37
  289.1 32.0 %shard_map.104 = (f32[128,64,256]{2,1,0:T(8,128)}, f32[128,1,256]{2,1,0:T(1,128)}, f32[128,1,256]{2,1,0:T(1,128)}, f32[128,64,1]{2,1,0:T(8,128)}, f32[128,64,1]{2,1,0:T(8,128)}) custom-call(s32[4]{0:T(128)} %add_convert_fusion.inside_ref, bf16[128,64,256]{2,1,0:T(8,128)(2,1)} %bitcast.11.lpm_ref.lpb_ref.lpa_ref, ...), custom_call_target="tpu_custom_call" | custom-call | tf_op jit(solution)/shard_map/pallas_call | solution.py:117
  321.1 3.4 collective-permute-start.8
  327.3 3.7 copy.35
  332.4 3.7 copy.36
  336.1 3.3 collective-permute-start.11
  339.4 4.4 %copy.39.qyl_ref = f32[128,64,1]{2,1,0:T(8,128)} copy(f32[128,64,1]{0,1,2:T(8,128)S(1)} %collective-permute-done.10) | data formatting | bytes 65536 | tf_op jit(solution)/shard_map/ppermute | solution.py:36
  343.8 4.5 %copy.40.qyh_ref = f32[128,64,1]{2,1,0:T(8,128)} copy(f32[128,64,1]{0,1,2:T(8,128)S(1)} %collective-permute-done.11) | data formatting | bytes 65536 | tf_op jit(solution)/shard_map/ppermute | solution.py:37
  349.1 31.9 %shard_map.105 = (f32[128,64,256]{2,1,0:T(8,128)}, f32[128,1,256]{2,1,0:T(1,128)}, f32[128,1,256]{2,1,0:T(1,128)}, f32[128,64,1]{2,1,0:T(8,128)}, f32[128,64,1]{2,1,0:T(8,128)}) custom-call(s32[4]{0:T(128)} %add_convert_fusion.inside_ref, bf16[128,64,256]{2,1,0:T(8,128)(2,1)} %bitcast.11.lpm_ref.lpb_ref.lpa_ref, ...), custom_call_target="tpu_custom_call" | custom-call | tf_op jit(solution)/shard_map/pallas_call | solution.py:117
  381.0 4.8 %copy.48 = bf16[128,64,256]{2,1,0:T(8,128)(2,1)} copy(bf16[128,64,256]{2,1,0:T(8,128)(2,1)} %bitcast.11.lpm_ref.lpb_ref.lpa_ref) | data formatting | bytes 8388608
  (55 shorter events, 26.5 us)
Async XLA Ops:
  0.6 132.9 %copy-start = (bf16[512,512]{1,0:T(8,128)(2,1)S(1)}, bf16[512,512]{1,0:T(8,128)(2,1)}, u32[]{:S(2)}) copy-start(bf16[512,512]{1,0:T(8,128)(2,1)} %param.12) | copy-start | bytes 1572868
  7.8 6.4 %copy-start.8 = (bf16[128,128]{1,0:T(8,128)(2,1)S(1)}, bf16[128,128]{1,0:T(8,128)(2,1)}, u32[]{:S(2)}) copy-start(bf16[128,128]{1,0:T(8,128)(2,1)} %param.10) | copy-start | bytes 98308
  125.8 7.6 %copy-start.13 = (bf16[512,512]{1,0:T(8,128)(2,1)S(1)}, bf16[512,512]{1,0:T(8,128)(2,1)}, u32[]{:S(2)}) copy-start(bf16[512,512]{1,0:T(8,128)(2,1)} %param.11) | copy-start | bytes 1572868
  153.2 95.1 %all-to-all-start.1 = ((bf16[16,8,64,256]{3,2,1,0:T(8,128)(2,1)}), bf16[16,8,64,256]{3,2,1,0:T(8,128)(2,1)}, u32[]{:S(2)}, u32[]{:S(2)}) async-start(bf16[16,8,64,256]{3,2,1,0:T(8,128)(2,1)} %bitcast.37), calls=%async_computation.1 | async-start | bytes 8388608 | tf_op jit(solution)/shard_map/all_to_all | solution.py:150
  162.3 18.1 %copy-start.9 = (s32[256]{0:T(256)S(1)}, s32[256]{0:T(256)}, u32[]{:S(2)}) copy-start(s32[256]{0:T(256)} %param.14) | copy-start | bytes 3076
  162.3 18.1 %copy-start.10 = (s32[256]{0:T(256)S(1)}, s32[256]{0:T(256)}, u32[]{:S(2)}) copy-start(s32[256]{0:T(256)} %param.16) | copy-start | bytes 3076
  162.3 18.1 %copy-start.11 = (f32[256]{0:T(256)S(1)}, f32[256]{0:T(256)}, u32[]{:S(2)}) copy-start(f32[256]{0:T(256)} %param.17) | copy-start | bytes 3076
  162.3 18.1 %copy-start.12 = (s32[256]{0:T(256)S(1)}, s32[256]{0:T(256)}, u32[]{:S(2)}) copy-start(s32[256]{0:T(256)} %param.15) | copy-start | bytes 3076
  166.0 95.2 %collective-permute-start.6 = (bf16[128,64,1]{0,1,2:T(8,128)(2,1)S(1)}, bf16[128,64,1]{0,1,2:T(8,128)(2,1)S(1)}, u32[]{:S(2)}, u32[]{:S(2)}) collective-permute-start(bf16[128,64,1]{0,1,2:T(8,128)(2,1)S(1)} %copy.44), channel_id=1, source_target_pairs={{0,1},{2,3},{4,5},{6,7},{8,9},{10,11},{12,13},{14,15},{16,17},{18,... | collective-permute-start | bytes 49160 | tf_op jit(solution)/shard_map/ppermute | solution.py:36
  169.5 94.8 %collective-permute-start.7 = (bf16[128,64,1]{0,1,2:T(8,128)(2,1)S(1)}, bf16[128,64,1]{0,1,2:T(8,128)(2,1)S(1)}, u32[]{:S(2)}, u32[]{:S(2)}) collective-permute-start(bf16[128,64,1]{0,1,2:T(8,128)(2,1)S(1)} %copy.45), channel_id=1, source_target_pairs={{1,0},{3,2},{5,4},{7,6},{9,8},{11,10},{13,12},{15,14},{17,16},{19,... | collective-permute-start | bytes 49160 | tf_op jit(solution)/shard_map/ppermute | solution.py:37
  174.0 114.3 %collective-permute-start.4 = (bf16[128,1,256]{2,1,0:T(2,128)(2,1)S(1)}, bf16[128,1,256]{2,1,0:T(2,128)(2,1)S(1)}, u32[]{:S(2)}, u32[]{:S(2)}) collective-permute-start(bf16[128,1,256]{2,1,0:T(2,128)(2,1)S(1)} %get-tuple-element.19), channel_id=1, source_target_pairs={{0,2},{2,4},{4,6},{6,8},{8,10},{10,12},{12,14},{1,3},{3,5},{5,7},{... | collective-permute-start | bytes 196616 | tf_op jit(solution)/shard_map/ppermute | solution.py:34
  177.1 111.2 %collective-permute-start.5 = (bf16[128,1,256]{2,1,0:T(2,128)(2,1)S(1)}, bf16[128,1,256]{2,1,0:T(2,128)(2,1)S(1)}, u32[]{:S(2)}, u32[]{:S(2)}) collective-permute-start(bf16[128,1,256]{2,1,0:T(2,128)(2,1)S(1)} %get-tuple-element.18), channel_id=1, source_target_pairs={{2,0},{4,2},{6,4},{8,6},{10,8},{12,10},{14,12},{3,1},{5,3},{7,5},{... | collective-permute-start | bytes 196616 | tf_op jit(solution)/shard_map/ppermute | solution.py:35
  256.3 13.6 %collective-permute-start.2 = (bf16[128,64,1]{0,1,2:T(8,128)(2,1)S(1)}, bf16[128,64,1]{0,1,2:T(8,128)(2,1)S(1)}, u32[]{:S(2)}, u32[]{:S(2)}) collective-permute-start(bf16[128,64,1]{0,1,2:T(8,128)(2,1)S(1)} %copy.27), channel_id=1, source_target_pairs={{0,1},{2,3},{4,5},{6,7},{8,9},{10,11},{12,13},{14,15},{16,17},{18,... | collective-permute-start | bytes 49160 | tf_op jit(solution)/shard_map/ppermute | solution.py:36
  261.2 23.1 %collective-permute-start.3 = (bf16[128,64,1]{0,1,2:T(8,128)(2,1)S(1)}, bf16[128,64,1]{0,1,2:T(8,128)(2,1)S(1)}, u32[]{:S(2)}, u32[]{:S(2)}) collective-permute-start(bf16[128,64,1]{0,1,2:T(8,128)(2,1)S(1)} %copy.28), channel_id=1, source_target_pairs={{1,0},{3,2},{5,4},{7,6},{9,8},{11,10},{13,12},{15,14},{17,16},{19,... | collective-permute-start | bytes 49160 | tf_op jit(solution)/shard_map/ppermute | solution.py:37
  264.3 24.0 %collective-permute-start = (bf16[128,1,256]{2,1,0:T(2,128)(2,1)S(1)}, bf16[128,1,256]{2,1,0:T(2,128)(2,1)S(1)}, u32[]{:S(2)}, u32[]{:S(2)}) collective-permute-start(bf16[128,1,256]{2,1,0:T(2,128)(2,1)S(1)} %get-tuple-element.23), channel_id=1, source_target_pairs={{0,2},{2,4},{4,6},{6,8},{8,10},{10,12},{12,14},{1,3},{3,5},{5,7},{... | collective-permute-start | bytes 196616 | tf_op jit(solution)/shard_map/ppermute | solution.py:34
  270.0 18.4 %collective-permute-start.1 = (bf16[128,1,256]{2,1,0:T(2,128)(2,1)S(1)}, bf16[128,1,256]{2,1,0:T(2,128)(2,1)S(1)}, u32[]{:S(2)}, u32[]{:S(2)}) collective-permute-start(bf16[128,1,256]{2,1,0:T(2,128)(2,1)S(1)} %get-tuple-element.22), channel_id=1, source_target_pairs={{2,0},{4,2},{6,4},{8,6},{10,8},{12,10},{14,12},{3,1},{5,3},{7,5},{... | collective-permute-start | bytes 196616 | tf_op jit(solution)/shard_map/ppermute | solution.py:35
  288.3 0.6 copy-start.4
  288.3 0.7 copy-start.5
  288.3 0.8 copy-start.2
  288.3 0.8 copy-start.3
  321.1 27.2 %collective-permute-start.8 = (f32[128,1,256]{2,1,0:T(1,128)}, f32[128,1,256]{2,1,0:T(1,128)S(1)}, u32[]{:S(2)}, u32[]{:S(2)}) collective-permute-start(f32[128,1,256]{2,1,0:T(1,128)} %get-tuple-element.9), channel_id=1, source_target_pairs={{0,2},{2,4},{4,6},{6,8},{8,10},{10,12},{12,14},{1,3},{3,5},{5,7},{... | collective-permute-start | bytes 393224 | tf_op jit(solution)/shard_map/ppermute | solution.py:34
  324.5 23.8 %collective-permute-start.9 = (f32[128,1,256]{2,1,0:T(1,128)}, f32[128,1,256]{2,1,0:T(1,128)S(1)}, u32[]{:S(2)}, u32[]{:S(2)}) collective-permute-start(f32[128,1,256]{2,1,0:T(1,128)} %get-tuple-element.10), channel_id=1, source_target_pairs={{2,0},{4,2},{6,4},{8,6},{10,8},{12,10},{14,12},{3,1},{5,3},{7,5},{... | collective-permute-start | bytes 393224 | tf_op jit(solution)/shard_map/ppermute | solution.py:35
  331.1 8.3 %collective-permute-start.10 = (f32[128,64,1]{0,1,2:T(8,128)S(1)}, f32[128,64,1]{0,1,2:T(8,128)S(1)}, u32[]{:S(2)}, u32[]{:S(2)}) collective-permute-start(f32[128,64,1]{0,1,2:T(8,128)S(1)} %copy.35), channel_id=1, source_target_pairs={{0,1},{2,3},{4,5},{6,7},{8,9},{10,11},{12,13},{14,15},{16,17},{18,... | collective-permute-start | bytes 98312 | tf_op jit(solution)/shard_map/ppermute | solution.py:36
  336.1 7.7 %collective-permute-start.11 = (f32[128,64,1]{0,1,2:T(8,128)S(1)}, f32[128,64,1]{0,1,2:T(8,128)S(1)}, u32[]{:S(2)}, u32[]{:S(2)}) collective-permute-start(f32[128,64,1]{0,1,2:T(8,128)S(1)} %copy.36), channel_id=1, source_target_pairs={{1,0},{3,2},{5,4},{7,6},{9,8},{11,10},{13,12},{15,14},{17,16},{19,... | collective-permute-start | bytes 98312 | tf_op jit(solution)/shard_map/ppermute | solution.py:37
  348.3 0.7 copy-start.6
  348.3 0.7 copy-start.7
  380.9 4.9 %copy-start.1 = (bf16[512,512]{1,0:T(8,128)(2,1)S(1)}, bf16[512,512]{1,0:T(8,128)(2,1)}, u32[]{:S(2)}) copy-start(bf16[512,512]{1,0:T(8,128)(2,1)} %param.12) | copy-start | bytes 1572868

commit v2 on v1

--- a/solution.py
+++ b/solution.py
@@ -22,7 +22,8 @@
 
 
 def block_edges(block):
-    return block[:, :1, :], block[:, -1:, :], block[:, :, :1], block[:, :, -1:]
+    f32 = jnp.float32
+    return block[:, :1, :], block[:, -1:, :], block[:, :, 0].astype(f32), block[:, :, -1].astype(f32)
 
 
 def halos(edges):
@@ -38,6 +39,34 @@
     return x_lo, x_hi, y_lo, y_hi
 
 
+def to_columns(rows):
+    tz, nx = rows.shape
+    eye = lax.broadcasted_iota(jnp.int32, (nx, nx), 0) == lax.broadcasted_iota(jnp.int32, (nx, nx), 1)
+    ones = jnp.ones((nx, 128), jnp.float32)
+    cols = []
+    for k in range(tz):
+        diag = jnp.where(eye, jnp.broadcast_to(rows[k : k + 1, :], (nx, nx)), 0.0)
+        full = jnp.dot(diag, ones, precision=lax.Precision.HIGHEST, preferred_element_type=jnp.float32)
+        cols.append(full[:, :1][None])
+    return jnp.concatenate(cols, axis=0)
+
+
+def to_rows(block):
+    tz, nx, ny = block.shape
+    lane = lax.broadcasted_iota(jnp.int32, (8, ny), 1)
+    pick = lax.broadcasted_iota(jnp.int32, (8, ny), 0)
+    sel = jnp.where(((pick == 0) & (lane == 0)) | ((pick == 1) & (lane == ny - 1)), 1.0, 0.0)
+    first, last = [], []
+    for k in range(tz):
+        both = lax.dot_general(
+            sel, block[k], (((1,), (1,)), ((), ())),
+            precision=lax.Precision.HIGHEST, preferred_element_type=jnp.float32,
+        )
+        first.append(both[0:1])
+        last.append(both[1:2])
+    return jnp.concatenate(first, axis=0), jnp.concatenate(last, axis=0)
+
+
 def step_kernel(
     inside_ref, lpm_ref, lpb_ref, lpa_ref, lxl_ref, lxh_ref, lyl_ref, lyh_ref,
     pm_ref, pb_ref, pa_ref, qxl_ref, qxh_ref, qyl_ref, qyh_ref, f_ref,
@@ -53,8 +82,8 @@
 
     kxl = side_perm(lxl_ref, 0)
     kxh = side_perm(lxh_ref, 1)
-    kyl = side_perm(lyl_ref, 2)
-    kyh = side_perm(lyh_ref, 3)
+    kyl = to_columns(side_perm(lyl_ref, 2))
+    kyh = to_columns(side_perm(lyh_ref, 3))
 
     below = jnp.where(c == 0, 0.0, permeability(lpb_ref[...].astype(f32)))
     above = jnp.where(c == last, 0.0, permeability(lpa_ref[...].astype(f32)))
@@ -78,8 +107,8 @@
     pext = jnp.concatenate([pb_ref[...].astype(f32), p, pa_ref[...].astype(f32)], axis=0)
     n_xp = jnp.where(xi == nx - 1, qxh_ref[...].astype(f32), pltpu.roll(p, nx - 1, 1))
     n_xm = jnp.where(xi == 0, qxl_ref[...].astype(f32), pltpu.roll(p, 1, 1))
-    n_yp = jnp.where(yi == ny - 1, qyh_ref[...].astype(f32), pltpu.roll(p, ny - 1, 2))
-    n_ym = jnp.where(yi == 0, qyl_ref[...].astype(f32), pltpu.roll(p, 1, 2))
+    n_yp = jnp.where(yi == ny - 1, to_columns(qyh_ref[...]), pltpu.roll(p, ny - 1, 2))
+    n_ym = jnp.where(yi == 0, to_columns(qyl_ref[...]), pltpu.roll(p, 1, 2))
 
     flux = t_zp * (pext[2:] - p)
     flux = flux + t_zm * (pext[:-2] - p)
@@ -91,8 +120,7 @@
     o_ref[...] = new
     exl_ref[...] = new[:, :1, :]
     exh_ref[...] = new[:, nx - 1 :, :]
-    eyl_ref[...] = new[:, :, :1]
-    eyh_ref[...] = new[:, :, ny - 1 :]
+    eyl_ref[...], eyh_ref[...] = to_rows(new)
 
 
 def advance(inside, log_perm, perm_halos, pressure, pressure_halos, flow):
@@ -103,7 +131,7 @@
     below = pl.BlockSpec((1, nx, ny), lambda c: (jnp.maximum(c * tz - 1, 0), 0, 0))
     above = pl.BlockSpec((1, nx, ny), lambda c: (jnp.minimum(c * tz + tz, depth - 1), 0, 0))
     row = pl.BlockSpec((tz, 1, ny), lambda c: (c, 0, 0))
-    col = pl.BlockSpec((tz, nx, 1), lambda c: (c, 0, 0))
+    col = pl.BlockSpec((tz, nx), lambda c: (c, 0))
     side = [row, row, col, col]
     smem = pl.BlockSpec(memory_space=pltpu.SMEM)
     f32 = jnp.float32
@@ -111,8 +139,8 @@
         jax.ShapeDtypeStruct((depth, nx, ny), f32),
         jax.ShapeDtypeStruct((depth, 1, ny), f32),
         jax.ShapeDtypeStruct((depth, 1, ny), f32),
-        jax.ShapeDtypeStruct((depth, nx, 1), f32),
-        jax.ShapeDtypeStruct((depth, nx, 1), f32),
+        jax.ShapeDtypeStruct((depth, nx), f32),
+        jax.ShapeDtypeStruct((depth, nx), f32),
     )
     new, x_lo, x_hi, y_lo, y_hi = pl.pallas_call(
         step_kernel,

time: 394 us -> 409 us (1.038); the launches traced: 386 us -> 406 us
  Pallas kernels: 63.9 us -> 75.5 us
  waiting for transfers between devices: 61.1 us -> 68.4 us
    ppermute x6 -> x2, local copies, waits for them, and re-layouts: 24.7 us -> 1.5 us  [the longest x1 0.76 us: halos(): x_lo = lax.ppermute(last_x, 'wide', forward_w)]
    slice x2 -> x3, local copies, waits for them, and re-layouts: 2.83 us -> 25.3 us  [block_edges(): block[:, :1, :]]
    all_to_all x0 -> x1, local copies, waits for them, and re-layouts: none -> 12.9 us  [body(): lax.all_to_all(outgoing.reshape(groups, planes, rows_x, rows_y), ('wide',...]
    pallas_call x2, Pallas kernels: 63.9 us -> 75.5 us  [advance(): pl.pallas_call(step_kernel, out_shape=out_shape, grid=grid, in_specs=[sme...]
    pallas_call x2 -> x0, local copies, waits for them, and re-layouts: 7.49 us -> none  [advance(): pl.pallas_call(step_kernel, out_shape=out_shape, grid=grid, in_specs=[sme...]
    all_to_all x1, waiting for transfers between devices: 61.1 us -> 66.8 us  [body(): lax.all_to_all(outgoing.reshape(groups, planes, rows_x, rows_y), ('wide',...]
    unnamed x32 -> x40, local copies, waits for them, and re-layouts: 19.5 us -> 16.6 us
    slice x4 -> x2, local copies, waits for them, and re-layouts: 14.6 us -> 14.6 us  [the longest x1 10.2 us: block_edges(): block[:, -1:, :]]
  transfers between devices with their start and end apart: 13 -> 13, of which waited for: 1 -> 3; matrix products, arithmetic and copies ran while one was open for 16% -> 16% of each run, Pallas kernels for 0% -> 0%
where the time goes in v2:
time: 409 us; the launch traced here: 406 us
  local copies, waits for them, and re-layouts  106 us (26%)
  blocking collectives  99.2 us (24%)
  Pallas kernels  75.5 us (18%)
  waiting for transfers between devices  68.4 us (17%)
  starting transfers between devices  37.1 us (9%)
  matrix products  17.9 us (4%)
    all_to_all x1, blocking collectives, body(): lax.all_to_all(first.reshape(groups, planes, rows_x, rows_y), ('wide', 'n...  99.2 us
    pallas_call x2, Pallas kernels, advance(): pl.pallas_call(step_kernel, out_shape=out_shape, grid=grid, in_specs=[sme...  75.5 us
    all_to_all x1, waiting for transfers between devices, body(): lax.all_to_all(outgoing.reshape(groups, planes, rows_x, rows_y), ('wide',...  66.8 us
    slice x3, local copies, waits for them, and re-layouts, block_edges(): block[:, :1, :]  25.3 us
    unnamed x40, local copies, waits for them, and re-layouts  16.6 us
    all_to_all x1, local copies, waits for them, and re-layouts, body(): lax.all_to_all(outgoing.reshape(groups, planes, rows_x, rows_y), ('wide',...  12.9 us
    ppermute x3, starting transfers between devices, halos(): x_lo = lax.ppermute(last_x, 'wide', forward_w)  12.7 us
    slice x1, local copies, waits for them, and re-layouts, block_edges(): block[:, -1:, :]  10.2 us
  transfers between devices with their start and end apart: 13, of which 3 were waited for; matrix products, arithmetic and copies ran while one was open for 16% of the time, Pallas kernels for 0%

profile of v2, /device:TPU:11, one launch (start us, length us, event | category | flops | bytes accessed | tf_op | source)
XLA Modules:
  0.0 406.3 jit_solution(16374419908616323870)
XLA Ops:
  0.6 7.1 %copy.94 = bf16[16,8,64,256]{3,1,2,0:T(8,128)(2,1)} copy(bf16[16,8,64,256]{3,2,1,0:T(8,128)(2,1)} %bitcast.67) | data formatting | bytes 8388608
  7.8 6.4 %copy.60 = bf16[16384,128]{1,0:T(8,128)(2,1)} copy(bf16[16384,128]{0,1:T(8,128)(2,1)} %bitcast.66) | data formatting | bytes 8388608 | tf_op jit(solution)/shard_map/dot_general | solution.py:158
  14.2 3.4 convert_bitcast_fusion
  17.6 2.4 copy.61
  20.0 99.2 %all_to_all.10 = bf16[16,8,64,256]{3,2,1,0:T(8,128)(2,1)S(1)} all-to-all(bf16[16,8,64,256]{3,2,1,0:T(8,128)(2,1)S(1)} %copy.61), channel_id=1, replica_groups=mesh['member'=2,'wide'=8,'narrow'=2] {'wide','narrow'}, dimensions={0} | all-to-all | bytes 8388608 | tf_op jit(solution)/shard_map/all_to_all | solution.py:166
  119.2 6.4 %copy.62 = bf16[8,8,64,2,256]{4,3,2,1,0:T(2,128)(2,1)} copy(bf16[8,8,64,2,256]{4,2,0,3,1:T(8,128)(2,1)S(1)} %bitcast.64) | data formatting | bytes 8388608 | tf_op jit(solution)/shard_map/transpose | solution.py:170
  125.7 7.6 %reshape.57 = bf16[8,512,512]{2,1,0:T(8,128)(2,1)} reshape(bf16[8,8,64,2,256]{4,3,2,1,0:T(2,128)(2,1)} %copy.62) | data formatting | bytes 8388608 | tf_op jit(solution)/shard_map/reshape | solution.py:170
  133.3 7.7 %fusion.8 = bf16[8,512,512]{2,1,0:T(8,128)(2,1)} fusion(bf16[8,512,512]{2,1,0:T(8,128)(2,1)} %reshape.57, bf16[512,512]{1,0:T(8,128)(2,1)S(1)} %copy-done, bf16[512,512]{1,0:T(8,128)(2,1)S(1)} %copy-done.17), kind=kOutput, calls=%fused_computation.10 | convolution fusion | flops 4299161600 | bytes 9437184 | tf_op jit(solution)/shard_map/zxb,jb->zxj/dot_general | solution.py:174
  141.1 6.9 %reshape.45 = bf16[8,8,64,2,256]{4,3,2,1,0:T(2,128)(2,1)} reshape(bf16[8,512,512]{2,1,0:T(8,128)(2,1)} %fusion.8) | data formatting | bytes 8388608 | tf_op jit(solution)/shard_map/reshape | solution.py:177
  147.9 5.1 %copy.65 = bf16[8,2,8,64,256]{4,3,2,1,0:T(8,128)(2,1)} copy(bf16[8,2,8,64,256]{4,1,3,0,2:T(2,128)(2,1)} %bitcast.65) | data formatting | bytes 8388608 | tf_op jit(solution)/shard_map/transpose | solution.py:177
  153.0 4.8 %all-to-all-start.1 = ((bf16[16,8,64,256]{3,2,1,0:T(8,128)(2,1)}), bf16[16,8,64,256]{3,2,1,0:T(8,128)(2,1)}, u32[]{:S(2)}, u32[]{:S(2)}) async-start(bf16[16,8,64,256]{3,2,1,0:T(8,128)(2,1)} %bitcast.62), calls=%async_computation.1 | async-start | bytes 8388608 | tf_op jit(solution)/shard_map/all_to_all | solution.py:178
  159.2 3.1 collective-permute-start.4
  162.3 3.1 collective-permute-start.5
  165.4 4.3 %fusion.22 = (bf16[128,64,1]{2,1,0:T(8,128)(2,1)S(1)}, bf16[128,64,1]{2,1,0:T(8,128)(2,1)}) fusion(bf16[128,64,256]{2,1,0:T(8,128)(2,1)} %pa_ref.1), kind=kLoop, calls=%fused_computation.29 | loop fusion | bytes 65536 | tf_op jit(solution)/shard_map/slice | solution.py:26
  169.8 2.2 copy.92
  172.0 1.5 collective-permute-start.6
  174.6 6.7 %fusion = f32[8192,256]{1,0:T(8,128)} fusion(f32[256]{0:T(256)S(1)} %get-tuple-element.22, s32[256]{0:T(256)S(1)} %multiply_add_fusion, s32[256]{0:T(256)S(1)} %get-tuple-element.23), kind=kOutput, calls=%fused_computation | convolution fusion | flops 6446710784 | bytes 8391680 | tf_op jit(solution)/shard_map/dot_general | solution.py:202
  181.4 66.8 %all-to-all-done.1 = bf16[16,8,64,256]{3,2,1,0:T(8,128)(2,1)} async-done(((bf16[16,8,64,256]{3,2,1,0:T(8,128)(2,1)}), bf16[16,8,64,256]{3,2,1,0:T(8,128)(2,1)}, u32[]{:S(2)}, u32[]{:S(2)}) %all-to-all-start.1) | async-done | bytes 4194336 | tf_op jit(solution)/shard_map/all_to_all | solution.py:178
  248.2 12.9 %copy.66 = bf16[16,8,64,256]{2,1,0,3:T(8,128)(2,1)} copy(bf16[16,8,64,256]{3,2,1,0:T(8,128)(2,1)} %all-to-all-done.1) | data formatting | bytes 8388608 | tf_op jit(solution)/shard_map/all_to_all | solution.py:178
  261.1 13.6 %fusion.21 = (bf16[128,1,256]{1,0,2:T(8,128)(2,1)}, bf16[128,1,256]{1,0,2:T(8,128)(2,1)}) fusion(bf16[128,64,256]{1,0,2:T(8,128)(2,1)} %bitcast.60), kind=kLoop, calls=%fused_computation.28 | loop fusion | bytes 262144 | tf_op jit(solution)/shard_map/slice | solution.py:26
  274.7 10.2 %copy.67 = bf16[128,1,256]{2,0,1:T(8,128)(2,1)S(1)} copy(bf16[128,1,256]{1,0,2:T(8,128)(2,1)} %get-tuple-element.27) | data formatting | bytes 131072 | tf_op jit(solution)/shard_map/slice | solution.py:26
  284.9 5.7 %collective-permute-start = (bf16[128,1,256]{2,0,1:T(8,128)(2,1)S(1)}, bf16[128,1,256]{2,0,1:T(8,128)(2,1)S(1)}, u32[]{:S(2)}, u32[]{:S(2)}) collective-permute-start(bf16[128,1,256]{2,0,1:T(8,128)(2,1)S(1)} %copy.67), channel_id=1, source_target_pairs={{0,2},{2,4},{4,6},{6,8},{8,10},{10,12},{12,14},{1,3},{3,5},{5,7},{... | collective-permute-start | bytes 196616 | tf_op jit(solution)/shard_map/ppermute | solution.py:35
  290.6 10.3 %copy.68 = bf16[128,1,256]{2,0,1:T(8,128)(2,1)S(1)} copy(bf16[128,1,256]{1,0,2:T(8,128)(2,1)} %get-tuple-element.26) | data formatting | bytes 131072 | tf_op jit(solution)/shard_map/slice | solution.py:26
  300.9 1.9 collective-permute-start.1
  303.6 2.0 collective-permute-start.7
  306.9 3.0 collective-permute-start.3
  312.8 39.1 %shard_map.104 = (f32[128,64,256]{2,1,0:T(8,128)}, f32[128,1,256]{2,1,0:T(1,128)}, f32[128,1,256]{2,1,0:T(1,128)}, f32[128,64]{1,0:T(8,128)}, f32[128,64]{1,0:T(8,128)}) custom-call(s32[4]{0:T(128)} %add_convert_fusion.inside_ref, bf16[128,64,256]{2,1,0:T(8,128)(2,1)} %bitcast.12.lpm_ref.lpb_ref.lpa_ref, ...), custom_call_target="tpu_custom_call" | custom-call | tf_op jit(solution)/shard_map/pallas_call | solution.py:145
  351.9 3.9 collective-permute-start.8
  355.8 2.3 collective-permute-start.9
  359.4 3.3 collective-permute-start.11
  365.0 36.4 %shard_map.105 = (f32[128,64,256]{2,1,0:T(8,128)}, f32[128,1,256]{2,1,0:T(1,128)}, f32[128,1,256]{2,1,0:T(1,128)}, f32[128,64]{1,0:T(8,128)}, f32[128,64]{1,0:T(8,128)}) custom-call(s32[4]{0:T(128)} %add_convert_fusion.inside_ref, bf16[128,64,256]{2,1,0:T(8,128)(2,1)} %bitcast.12.lpm_ref.lpb_ref.lpa_ref, ...), custom_call_target="tpu_custom_call" | custom-call | tf_op jit(solution)/shard_map/pallas_call | solution.py:145
  401.4 4.8 %copy.96 = bf16[128,64,256]{2,1,0:T(8,128)(2,1)} copy(bf16[128,64,256]{2,1,0:T(8,128)(2,1)} %bitcast.12.lpm_ref.lpb_ref.lpa_ref) | data formatting | bytes 8388608
  (60 shorter events, 11.0 us)
Async XLA Ops:
  0.6 132.7 %copy-start = (bf16[512,512]{1,0:T(8,128)(2,1)S(1)}, bf16[512,512]{1,0:T(8,128)(2,1)}, u32[]{:S(2)}) copy-start(bf16[512,512]{1,0:T(8,128)(2,1)} %param.12) | copy-start | bytes 1572868
  7.8 6.4 %copy-start.12 = (bf16[128,128]{1,0:T(8,128)(2,1)S(1)}, bf16[128,128]{1,0:T(8,128)(2,1)}, u32[]{:S(2)}) copy-start(bf16[128,128]{1,0:T(8,128)(2,1)} %param.10) | copy-start | bytes 98308
  125.7 7.6 %copy-start.17 = (bf16[512,512]{1,0:T(8,128)(2,1)S(1)}, bf16[512,512]{1,0:T(8,128)(2,1)}, u32[]{:S(2)}) copy-start(bf16[512,512]{1,0:T(8,128)(2,1)} %param.11) | copy-start | bytes 1572868
  153.0 95.1 %all-to-all-start.1 = ((bf16[16,8,64,256]{3,2,1,0:T(8,128)(2,1)}), bf16[16,8,64,256]{3,2,1,0:T(8,128)(2,1)}, u32[]{:S(2)}, u32[]{:S(2)}) async-start(bf16[16,8,64,256]{3,2,1,0:T(8,128)(2,1)} %bitcast.62), calls=%async_computation.1 | async-start | bytes 8388608 | tf_op jit(solution)/shard_map/all_to_all | solution.py:178
  159.2 152.9 %collective-permute-start.4 = (bf16[128,1,256]{2,1,0:T(2,128)(2,1)S(1)}, bf16[128,1,256]{2,1,0:T(2,128)(2,1)S(1)}, u32[]{:S(2)}, u32[]{:S(2)}) collective-permute-start(bf16[128,1,256]{2,1,0:T(2,128)(2,1)S(1)} %get-tuple-element.31), channel_id=1, source_target_pairs={{0,2},{2,4},{4,6},{6,8},{8,10},{10,12},{12,14},{1,3},{3,5},{5,7},{... | collective-permute-start | bytes 196616 | tf_op jit(solution)/shard_map/ppermute | solution.py:35
  162.3 149.8 %collective-permute-start.5 = (bf16[128,1,256]{2,1,0:T(2,128)(2,1)S(1)}, bf16[128,1,256]{2,1,0:T(2,128)(2,1)S(1)}, u32[]{:S(2)}, u32[]{:S(2)}) collective-permute-start(bf16[128,1,256]{2,1,0:T(2,128)(2,1)S(1)} %get-tuple-element.30), channel_id=1, source_target_pairs={{2,0},{4,2},{6,4},{8,6},{10,8},{12,10},{14,12},{3,1},{5,3},{7,5},{... | collective-permute-start | bytes 196616 | tf_op jit(solution)/shard_map/ppermute | solution.py:36
  169.8 4.8 %copy-start.13 = (s32[256]{0:T(256)S(1)}, s32[256]{0:T(256)}, u32[]{:S(2)}) copy-start(s32[256]{0:T(256)} %param.14) | copy-start | bytes 3076
  169.8 4.8 %copy-start.14 = (s32[256]{0:T(256)S(1)}, s32[256]{0:T(256)}, u32[]{:S(2)}) copy-start(s32[256]{0:T(256)} %param.16) | copy-start | bytes 3076
  169.8 4.8 %copy-start.15 = (f32[256]{0:T(256)S(1)}, f32[256]{0:T(256)}, u32[]{:S(2)}) copy-start(f32[256]{0:T(256)} %param.17) | copy-start | bytes 3076
  169.8 4.8 %copy-start.16 = (s32[256]{0:T(256)S(1)}, s32[256]{0:T(256)}, u32[]{:S(2)}) copy-start(s32[256]{0:T(256)} %param.15) | copy-start | bytes 3076
  172.0 131.6 %collective-permute-start.6 = (f32[128,64]{1,0:T(8,128)S(1)}, f32[128,64]{1,0:T(8,128)S(1)}, u32[]{:S(2)}, u32[]{:S(2)}) collective-permute-start(f32[128,64]{1,0:T(8,128)S(1)} %bitcast_convert_fusion.1), channel_id=1, source_target_pairs={{0,1},{2,3},{4,5},{6,7},{8,9},{10,11},{12,13},{14,15},{16,17},{18,... | collective-permute-start | bytes 98312 | tf_op jit(solution)/shard_map/ppermute | solution.py:37
  284.9 20.7 %collective-permute-start = (bf16[128,1,256]{2,0,1:T(8,128)(2,1)S(1)}, bf16[128,1,256]{2,0,1:T(8,128)(2,1)S(1)}, u32[]{:S(2)}, u32[]{:S(2)}) collective-permute-start(bf16[128,1,256]{2,0,1:T(8,128)(2,1)S(1)} %copy.67), channel_id=1, source_target_pairs={{0,2},{2,4},{4,6},{6,8},{8,10},{10,12},{12,14},{1,3},{3,5},{5,7},{... | collective-permute-start | bytes 196616 | tf_op jit(solution)/shard_map/ppermute | solution.py:35
  300.9 6.0 %collective-permute-start.1 = (bf16[128,1,256]{2,0,1:T(8,128)(2,1)S(1)}, bf16[128,1,256]{2,0,1:T(8,128)(2,1)S(1)}, u32[]{:S(2)}, u32[]{:S(2)}) collective-permute-start(bf16[128,1,256]{2,0,1:T(8,128)(2,1)S(1)} %copy.68), channel_id=1, source_target_pairs={{2,0},{4,2},{6,4},{8,6},{10,8},{12,10},{14,12},{3,1},{5,3},{7,5},{... | collective-permute-start | bytes 196616 | tf_op jit(solution)/shard_map/ppermute | solution.py:36
  303.6 8.6 %copy-start.8 = (f32[128,64]{1,0:T(8,128)}, f32[128,64]{1,0:T(8,128)S(1)}, u32[]{:S(2)}) copy-start(f32[128,64]{1,0:T(8,128)S(1)} %collective-permute-done.6.qyl_ref) | copy-start | bytes 98308
  303.6 8.5 %collective-permute-start.7 = (f32[128,64]{1,0:T(8,128)S(1)}, f32[128,64]{1,0:T(8,128)S(1)}, u32[]{:S(2)}, u32[]{:S(2)}) collective-permute-start(f32[128,64]{1,0:T(8,128)S(1)} %bitcast_convert_fusion), channel_id=1, source_target_pairs={{1,0},{3,2},{5,4},{7,6},{9,8},{11,10},{13,12},{15,14},{17,16},{19,... | collective-permute-start | bytes 98312 | tf_op jit(solution)/shard_map/ppermute | solution.py:38
  305.6 6.5 %collective-permute-start.2 = (f32[128,64]{1,0:T(8,128)S(1)}, f32[128,64]{1,0:T(8,128)S(1)}, u32[]{:S(2)}, u32[]{:S(2)}) collective-permute-start(f32[128,64]{1,0:T(8,128)S(1)} %get-tuple-element.25), channel_id=1, source_target_pairs={{0,1},{2,3},{4,5},{6,7},{8,9},{10,11},{12,13},{14,15},{16,17},{18,... | collective-permute-start | bytes 98312 | tf_op jit(solution)/shard_map/ppermute | solution.py:37
  306.9 5.2 %collective-permute-start.3 = (f32[128,64]{1,0:T(8,128)S(1)}, f32[128,64]{1,0:T(8,128)S(1)}, u32[]{:S(2)}, u32[]{:S(2)}) collective-permute-start(f32[128,64]{1,0:T(8,128)S(1)} %get-tuple-element.24), channel_id=1, source_target_pairs={{1,0},{3,2},{5,4},{7,6},{9,8},{11,10},{13,12},{15,14},{17,16},{19,... | collective-permute-start | bytes 98312 | tf_op jit(solution)/shard_map/ppermute | solution.py:38
  312.1 0.6 copy-start.9
  312.1 0.7 copy-start.4
  312.1 0.7 copy-start.5
  312.1 0.7 copy-start.2
  312.1 0.7 copy-start.3
  351.9 11.6 %collective-permute-start.8 = (f32[128,1,256]{2,1,0:T(1,128)}, f32[128,1,256]{2,1,0:T(1,128)S(1)}, u32[]{:S(2)}, u32[]{:S(2)}) collective-permute-start(f32[128,1,256]{2,1,0:T(1,128)} %get-tuple-element.9), channel_id=1, source_target_pairs={{0,2},{2,4},{4,6},{6,8},{8,10},{10,12},{12,14},{1,3},{3,5},{5,7},{... | collective-permute-start | bytes 393224 | tf_op jit(solution)/shard_map/ppermute | solution.py:35
  355.8 8.5 %collective-permute-start.9 = (f32[128,1,256]{2,1,0:T(1,128)}, f32[128,1,256]{2,1,0:T(1,128)S(1)}, u32[]{:S(2)}, u32[]{:S(2)}) collective-permute-start(f32[128,1,256]{2,1,0:T(1,128)} %get-tuple-element.10), channel_id=1, source_target_pairs={{2,0},{4,2},{6,4},{8,6},{10,8},{12,10},{14,12},{3,1},{5,3},{7,5},{... | collective-permute-start | bytes 393224 | tf_op jit(solution)/shard_map/ppermute | solution.py:36
  358.1 4.6 %collective-permute-start.10 = (f32[128,64]{1,0:T(8,128)}, f32[128,64]{1,0:T(8,128)S(1)}, u32[]{:S(2)}, u32[]{:S(2)}) collective-permute-start(f32[128,64]{1,0:T(8,128)} %get-tuple-element.11), channel_id=1, source_target_pairs={{0,1},{2,3},{4,5},{6,7},{8,9},{10,11},{12,13},{14,15},{16,17},{18,... | collective-permute-start | bytes 98312 | tf_op jit(solution)/shard_map/ppermute | solution.py:37
  359.4 4.1 %collective-permute-start.11 = (f32[128,64]{1,0:T(8,128)}, f32[128,64]{1,0:T(8,128)S(1)}, u32[]{:S(2)}, u32[]{:S(2)}) collective-permute-start(f32[128,64]{1,0:T(8,128)} %get-tuple-element.12), channel_id=1, source_target_pairs={{1,0},{3,2},{5,4},{7,6},{9,8},{11,10},{13,12},{15,14},{17,16},{19,... | collective-permute-start | bytes 98312 | tf_op jit(solution)/shard_map/ppermute | solution.py:38
  362.7 1.6 copy-start.10
  363.6 0.8 copy-start.11
  363.6 0.8 copy-start.6
  364.3 0.7 copy-start.7
  401.4 4.9 %copy-start.1 = (bf16[512,512]{1,0:T(8,128)(2,1)S(1)}, bf16[512,512]{1,0:T(8,128)(2,1)}, u32[]{:S(2)}) copy-start(bf16[512,512]{1,0:T(8,128)(2,1)} %param.12) | copy-start | bytes 1572868

commit v3 on v2

--- a/solution.py
+++ b/solution.py
@@ -19,11 +19,6 @@
 
 def harmonic(a, b):
     return 2.0 * a * b / (a + b)
-
-
-def block_edges(block):
-    f32 = jnp.float32
-    return block[:, :1, :], block[:, -1:, :], block[:, :, 0].astype(f32), block[:, :, -1].astype(f32)
 
 
 def halos(edges):
@@ -41,30 +36,73 @@
 
 def to_columns(rows):
     tz, nx = rows.shape
-    eye = lax.broadcasted_iota(jnp.int32, (nx, nx), 0) == lax.broadcasted_iota(jnp.int32, (nx, nx), 1)
-    ones = jnp.ones((nx, 128), jnp.float32)
-    cols = []
-    for k in range(tz):
-        diag = jnp.where(eye, jnp.broadcast_to(rows[k : k + 1, :], (nx, nx)), 0.0)
-        full = jnp.dot(diag, ones, precision=lax.Precision.HIGHEST, preferred_element_type=jnp.float32)
-        cols.append(full[:, :1][None])
-    return jnp.concatenate(cols, axis=0)
+    eye = jnp.where(
+        lax.broadcasted_iota(jnp.int32, (nx, nx), 0) == lax.broadcasted_iota(jnp.int32, (nx, nx), 1),
+        1.0, 0.0,
+    )
+    cols = lax.dot_general(
+        eye, rows, (((1,), (1,)), ((), ())),
+        precision=lax.Precision.HIGHEST, preferred_element_type=jnp.float32,
+    )
+    return jnp.concatenate([cols[:, k : k + 1][None] for k in range(tz)], axis=0)
+
+
+def x_rows(ref):
+    return jnp.concatenate([ref[k : k + 1, :][None] for k in range(ref.shape[0])], axis=0)
+
+
+def store_x_rows(ref, rows):
+    for k in range(ref.shape[0]):
+        ref[k : k + 1, :] = rows[k]
 
 
 def to_rows(block):
     tz, nx, ny = block.shape
-    lane = lax.broadcasted_iota(jnp.int32, (8, ny), 1)
-    pick = lax.broadcasted_iota(jnp.int32, (8, ny), 0)
-    sel = jnp.where(((pick == 0) & (lane == 0)) | ((pick == 1) & (lane == ny - 1)), 1.0, 0.0)
-    first, last = [], []
-    for k in range(tz):
-        both = lax.dot_general(
-            sel, block[k], (((1,), (1,)), ((), ())),
-            precision=lax.Precision.HIGHEST, preferred_element_type=jnp.float32,
+    lane = lax.broadcasted_iota(jnp.int32, (nx, 128), 1)
+    pick = jnp.where(
+        lax.broadcasted_iota(jnp.int32, (tz, 128), 0) == lax.broadcasted_iota(jnp.int32, (tz, 128), 1),
+        1.0, 0.0,
+    )
+    result = []
+    for column in (0, ny - 1):
+        gathered = jnp.zeros((nx, 128), jnp.float32)
+        for k in range(tz):
+            gathered = jnp.where(lane == k, block[k, :, column : column + 1], gathered)
+        result.append(
+            lax.dot_general(
+                pick, gathered, (((1,), (1,)), ((), ())),
+                precision=lax.Precision.HIGHEST, preferred_element_type=jnp.float32,
+            )
         )
-        first.append(both[0:1])
-        last.append(both[1:2])
-    return jnp.concatenate(first, axis=0), jnp.concatenate(last, axis=0)
+    return result[0], result[1]
+
+
+def edge_kernel(block_ref, xl_ref, xh_ref, yl_ref, yh_ref):
+    block = block_ref[...].astype(jnp.float32)
+    store_x_rows(xl_ref, block[:, :1, :])
+    store_x_rows(xh_ref, block[:, -1:, :])
+    yl_ref[...], yh_ref[...] = to_rows(block)
+
+
+def block_edges(block):
+    depth, nx, ny = block.shape
+    tz = CHUNK_Z
+    f32 = jnp.float32
+    row = pl.BlockSpec((tz, ny), lambda c: (c, 0))
+    col = pl.BlockSpec((tz, nx), lambda c: (c, 0))
+    return pl.pallas_call(
+        edge_kernel,
+        out_shape=(
+            jax.ShapeDtypeStruct((depth, ny), f32),
+            jax.ShapeDtypeStruct((depth, ny), f32),
+            jax.ShapeDtypeStruct((depth, nx), f32),
+            jax.ShapeDtypeStruct((depth, nx), f32),
+        ),
+        grid=(depth // tz,),
+        in_specs=[pl.BlockSpec((tz, nx, ny), lambda c: (c, 0, 0))],
+        out_specs=[row, row, col, col],
+        compiler_params=pltpu.CompilerParams(dimension_semantics=("arbitrary",)),
+    )(block)
 
 
 def step_kernel(
@@ -80,8 +118,8 @@
     def side_perm(ref, k):
         return jnp.where(inside_ref[k] > 0, permeability(ref[...].astype(f32)), 0.0)
 
-    kxl = side_perm(lxl_ref, 0)
-    kxh = side_perm(lxh_ref, 1)
+    kxl = jnp.where(inside_ref[0] > 0, permeability(x_rows(lxl_ref)), 0.0)
+    kxh = jnp.where(inside_ref[1] > 0, permeability(x_rows(lxh_ref)), 0.0)
     kyl = to_columns(side_perm(lyl_ref, 2))
     kyh = to_columns(side_perm(lyh_ref, 3))
 
@@ -105,8 +143,8 @@
 
     p = pm_ref[...].astype(f32)
     pext = jnp.concatenate([pb_ref[...].astype(f32), p, pa_ref[...].astype(f32)], axis=0)
-    n_xp = jnp.where(xi == nx - 1, qxh_ref[...].astype(f32), pltpu.roll(p, nx - 1, 1))
-    n_xm = jnp.where(xi == 0, qxl_ref[...].astype(f32), pltpu.roll(p, 1, 1))
+    n_xp = jnp.where(xi == nx - 1, x_rows(qxh_ref), pltpu.roll(p, nx - 1, 1))
+    n_xm = jnp.where(xi == 0, x_rows(qxl_ref), pltpu.roll(p, 1, 1))
     n_yp = jnp.where(yi == ny - 1, to_columns(qyh_ref[...]), pltpu.roll(p, ny - 1, 2))
     n_ym = jnp.where(yi == 0, to_columns(qyl_ref[...]), pltpu.roll(p, 1, 2))
 
@@ -118,8 +156,8 @@
     flux = flux + t_ym * (n_ym - p)
     new = p + STEP_SIZE * (flux + f_ref[...]) / (1.0 + 0.5 * p * p)
     o_ref[...] = new
-    exl_ref[...] = new[:, :1, :]
-    exh_ref[...] = new[:, nx - 1 :, :]
+    store_x_rows(exl_ref, new[:, :1, :])
+    store_x_rows(exh_ref, new[:, nx - 1 :, :])
     eyl_ref[...], eyh_ref[...] = to_rows(new)
 
 
@@ -130,15 +168,15 @@
     main = pl.BlockSpec((tz, nx, ny), lambda c: (c, 0, 0))
     below = pl.BlockSpec((1, nx, ny), lambda c: (jnp.maximum(c * tz - 1, 0), 0, 0))
     above = pl.BlockSpec((1, nx, ny), lambda c: (jnp.minimum(c * tz + tz, depth - 1), 0, 0))
-    row = pl.BlockSpec((tz, 1, ny), lambda c: (c, 0, 0))
+    row = pl.BlockSpec((tz, ny), lambda c: (c, 0))
     col = pl.BlockSpec((tz, nx), lambda c: (c, 0))
     side = [row, row, col, col]
     smem = pl.BlockSpec(memory_space=pltpu.SMEM)
     f32 = jnp.float32
     out_shape = (
         jax.ShapeDtypeStruct((depth, nx, ny), f32),
-        jax.ShapeDtypeStruct((depth, 1, ny), f32),
-        jax.ShapeDtypeStruct((depth, 1, ny), f32),
+        jax.ShapeDtypeStruct((depth, ny), f32),
+        jax.ShapeDtypeStruct((depth, ny), f32),
         jax.ShapeDtypeStruct((depth, nx), f32),
         jax.ShapeDtypeStruct((depth, nx), f32),
     )

time: 409 us -> 377 us (0.922)
  local copies, waits for them, and re-layouts: 106 us -> 48.3 us
  Pallas kernels: 75.5 us -> 100 us
    slice x5 -> x0, local copies, waits for them, and re-layouts: 39.9 us -> none  [the longest x3 25.3 us: block_edges(): block[:, :1, :]]
    pallas_call x0 -> x2, Pallas kernels: none -> 23.6 us  [block_edges(): pl.pallas_call(edge_kernel, out_shape=(jax.ShapeDtypeStruct((depth, ny),...]
    all_to_all x1 -> x0, local copies, waits for them, and re-layouts: 12.9 us -> none  [body(): lax.all_to_all(outgoing.reshape(groups, planes, rows_x, rows_y), ('wide',...]
    unnamed x40 -> x46, local copies, waits for them, and re-layouts: 16.6 us -> 13.5 us
  transfers between devices with their start and end apart: 13 -> 13, of which waited for: 3 -> 2; matrix products, arithmetic and copies ran while one was open for 16% -> 2% of each run, Pallas kernels for 0% -> 6%
where the time goes in v3:
time: 377 us; the launch traced here: 374 us
  Pallas kernels  100 us (27%)
  blocking collectives  99.2 us (26%)
  waiting for transfers between devices  69 us (18%)
  local copies, waits for them, and re-layouts  48.3 us (13%)
  starting transfers between devices  37.9 us (10%)
  matrix products  17.9 us (5%)
    all_to_all x1, blocking collectives, body(): lax.all_to_all(first.reshape(groups, planes, rows_x, rows_y), ('wide', 'n...  99.2 us
    pallas_call x2, Pallas kernels, advance(): pl.pallas_call(step_kernel, out_shape=out_shape, grid=grid, in_specs=[sme...  76.6 us
    all_to_all x1, waiting for transfers between devices, body(): lax.all_to_all(outgoing.reshape(groups, planes, rows_x, rows_y), ('wide',...  67.9 us
    pallas_call x2, Pallas kernels, block_edges(): pl.pallas_call(edge_kernel, out_shape=(jax.ShapeDtypeStruct((depth, ny),...  23.6 us
    unnamed x46, local copies, waits for them, and re-layouts  13.5 us
    ppermute x3, starting transfers between devices, halos(): x_lo = lax.ppermute(last_x, 'wide', forward_w)  12.1 us
    ppermute x3, starting transfers between devices, halos(): y_hi = lax.ppermute(first_y, 'narrow', backward_n)  9.32 us
    ppermute x3, starting transfers between devices, halos(): x_hi = lax.ppermute(first_x, 'wide', backward_w)  7.83 us
  transfers between devices with their start and end apart: 13, of which 2 were waited for; matrix products, arithmetic and copies ran while one was open for 2% of the time, Pallas kernels for 6%

profile of v3, /device:TPU:11, one launch (start us, length us, event | category | flops | bytes accessed | tf_op | source)
XLA Modules:
  0.0 374.3 jit_solution(1917146514058251608)
XLA Ops:
  0.6 7.1 %copy.24 = bf16[16,8,64,256]{3,1,2,0:T(8,128)(2,1)} copy(bf16[16,8,64,256]{3,2,1,0:T(8,128)(2,1)} %bitcast.42) | data formatting | bytes 8388608
  7.8 6.4 %copy.15 = bf16[16384,128]{1,0:T(8,128)(2,1)} copy(bf16[16384,128]{0,1:T(8,128)(2,1)} %bitcast.41) | data formatting | bytes 8388608 | tf_op jit(solution)/shard_map/dot_general | solution.py:196
  14.2 3.4 convert_bitcast_fusion
  17.6 2.4 copy.16
  20.0 99.2 %all_to_all.10 = bf16[16,8,64,256]{3,2,1,0:T(8,128)(2,1)S(1)} all-to-all(bf16[16,8,64,256]{3,2,1,0:T(8,128)(2,1)S(1)} %copy.16), channel_id=1, replica_groups=mesh['member'=2,'wide'=8,'narrow'=2] {'wide','narrow'}, dimensions={0} | all-to-all | bytes 8388608 | tf_op jit(solution)/shard_map/all_to_all | solution.py:204
  119.2 6.4 %copy.17 = bf16[8,8,64,2,256]{4,3,2,1,0:T(2,128)(2,1)} copy(bf16[8,8,64,2,256]{4,2,0,3,1:T(8,128)(2,1)S(1)} %bitcast.39) | data formatting | bytes 8388608 | tf_op jit(solution)/shard_map/transpose | solution.py:208
  125.7 7.6 %reshape.45 = bf16[8,512,512]{2,1,0:T(8,128)(2,1)} reshape(bf16[8,8,64,2,256]{4,3,2,1,0:T(2,128)(2,1)} %copy.17) | data formatting | bytes 8388608 | tf_op jit(solution)/shard_map/reshape | solution.py:208
  133.3 7.7 %fusion.8 = bf16[8,512,512]{2,1,0:T(8,128)(2,1)} fusion(bf16[8,512,512]{2,1,0:T(8,128)(2,1)} %reshape.45, bf16[512,512]{1,0:T(8,128)(2,1)S(1)} %copy-done, bf16[512,512]{1,0:T(8,128)(2,1)S(1)} %copy-done.19), kind=kOutput, calls=%fused_computation.10 | convolution fusion | flops 4299161600 | bytes 9437184 | tf_op jit(solution)/shard_map/zxb,jb->zxj/dot_general | solution.py:212
  141.1 6.9 %reshape.37 = bf16[8,8,64,2,256]{4,3,2,1,0:T(2,128)(2,1)} reshape(bf16[8,512,512]{2,1,0:T(8,128)(2,1)} %fusion.8) | data formatting | bytes 8388608 | tf_op jit(solution)/shard_map/reshape | solution.py:215
  147.9 5.1 %copy.20 = bf16[8,2,8,64,256]{4,3,2,1,0:T(8,128)(2,1)} copy(bf16[8,2,8,64,256]{4,1,3,0,2:T(2,128)(2,1)} %bitcast.40) | data formatting | bytes 8388608 | tf_op jit(solution)/shard_map/transpose | solution.py:215
  153.0 4.8 %all-to-all-start.1 = ((bf16[16,8,64,256]{3,2,1,0:T(8,128)(2,1)}), bf16[16,8,64,256]{3,2,1,0:T(8,128)(2,1)}, u32[]{:S(2)}, u32[]{:S(2)}) async-start(bf16[16,8,64,256]{3,2,1,0:T(8,128)(2,1)} %bitcast.37), calls=%async_computation.1 | async-start | bytes 8388608 | tf_op jit(solution)/shard_map/all_to_all | solution.py:216
  157.8 11.8 %shard_map.105 = (f32[128,256]{1,0:T(8,128)}, f32[128,256]{1,0:T(8,128)}, f32[128,64]{1,0:T(8,128)}, f32[128,64]{1,0:T(8,128)}) custom-call(bf16[128,64,256]{2,1,0:T(8,128)(2,1)} %pa_ref.1), custom_call_target="tpu_custom_call" | custom-call | tf_op jit(solution)/shard_map/pallas_call | solution.py:93
  169.6 3.1 collective-permute-start.4
  172.7 3.1 collective-permute-start.5
  175.8 1.3 collective-permute-start.6
  177.1 3.0 collective-permute-start.7
  180.2 67.9 %all-to-all-done.1 = bf16[16,8,64,256]{3,2,1,0:T(8,128)(2,1)} async-done(((bf16[16,8,64,256]{3,2,1,0:T(8,128)(2,1)}), bf16[16,8,64,256]{3,2,1,0:T(8,128)(2,1)}, u32[]{:S(2)}, u32[]{:S(2)}) %all-to-all-start.1) | async-done | bytes 4194336 | tf_op jit(solution)/shard_map/all_to_all | solution.py:216
  248.2 11.8 %shard_map.104 = (f32[128,256]{1,0:T(8,128)}, f32[128,256]{1,0:T(8,128)}, f32[128,64]{1,0:T(8,128)}, f32[128,64]{1,0:T(8,128)}) custom-call(bf16[128,64,256]{2,1,0:T(8,128)(2,1)} %bitcast.11.block_ref.lpm_ref.lpb_ref.lpa_ref), custom_call_target="tpu_custom_call" | custom-call | tf_op jit(solution)/shard_map/pallas_call | solution.py:93
  259.9 5.7 %collective-permute-start = (f32[128,256]{1,0:T(8,128)}, f32[128,256]{1,0:T(8,128)S(1)}, u32[]{:S(2)}, u32[]{:S(2)}) collective-permute-start(f32[128,256]{1,0:T(8,128)} %get-tuple-element.16), channel_id=1, source_target_pairs={{0,2},{2,4},{4,6},{6,8},{8,10},{10,12},{12,14},{1,3},{3,5},{5,7},{... | collective-permute-start | bytes 393224 | tf_op jit(solution)/shard_map/ppermute | solution.py:30
  265.6 1.9 collective-permute-start.1
  267.6 6.7 %fusion = f32[8192,256]{1,0:T(8,128)} fusion(f32[256]{0:T(256)S(1)} %get-tuple-element.30, s32[256]{0:T(256)S(1)} %multiply_add_fusion, s32[256]{0:T(256)S(1)} %get-tuple-element.31), kind=kOutput, calls=%fused_computation | convolution fusion | flops 6446710784 | bytes 8391680 | tf_op jit(solution)/shard_map/dot_general | solution.py:240
  274.3 1.3 collective-permute-start.2
  275.7 3.3 collective-permute-start.3
  278.9 0.7 add_convert_fusion.inside_ref
  280.4 38.4 %shard_map.106 = (f32[128,64,256]{2,1,0:T(8,128)}, f32[128,256]{1,0:T(8,128)}, f32[128,256]{1,0:T(8,128)}, f32[128,64]{1,0:T(8,128)}, f32[128,64]{1,0:T(8,128)}) custom-call(s32[4]{0:T(128)} %add_convert_fusion.inside_ref, bf16[128,64,256]{2,1,0:T(8,128)(2,1)} %bitcast.11.block_ref.lpm_ref.lpb_ref.lpa_ref, ...), custom_call_target="tpu_custom_call" | custom-call | tf_op jit(solution)/shard_map/pallas_call | solution.py:183
  318.8 3.4 collective-permute-start.8
  322.2 2.8 collective-permute-start.9
  325.0 1.3 collective-permute-start.10
  326.3 3.0 collective-permute-start.11
  329.4 1.1 collective-permute-done.11.qyh_ref
  331.2 38.2 %shard_map.107 = (f32[128,64,256]{2,1,0:T(8,128)}, f32[128,256]{1,0:T(8,128)}, f32[128,256]{1,0:T(8,128)}, f32[128,64]{1,0:T(8,128)}, f32[128,64]{1,0:T(8,128)}) custom-call(s32[4]{0:T(128)} %add_convert_fusion.inside_ref, bf16[128,64,256]{2,1,0:T(8,128)(2,1)} %bitcast.11.block_ref.lpm_ref.lpb_ref.lpa_ref, ...), custom_call_target="tpu_custom_call" | custom-call | tf_op jit(solution)/shard_map/pallas_call | solution.py:183
  369.4 4.8 %copy.26 = bf16[128,64,256]{2,1,0:T(8,128)(2,1)} copy(bf16[128,64,256]{2,1,0:T(8,128)(2,1)} %bitcast.11.block_ref.lpm_ref.lpb_ref.lpa_ref) | data formatting | bytes 8388608
  (57 shorter events, 1.5 us)
Async XLA Ops:
  0.6 132.7 %copy-start = (bf16[512,512]{1,0:T(8,128)(2,1)S(1)}, bf16[512,512]{1,0:T(8,128)(2,1)}, u32[]{:S(2)}) copy-start(bf16[512,512]{1,0:T(8,128)(2,1)} %param.12) | copy-start | bytes 1572868
  7.8 6.4 %copy-start.14 = (bf16[128,128]{1,0:T(8,128)(2,1)S(1)}, bf16[128,128]{1,0:T(8,128)(2,1)}, u32[]{:S(2)}) copy-start(bf16[128,128]{1,0:T(8,128)(2,1)} %param.10) | copy-start | bytes 98308
  125.7 7.6 %copy-start.19 = (bf16[512,512]{1,0:T(8,128)(2,1)S(1)}, bf16[512,512]{1,0:T(8,128)(2,1)}, u32[]{:S(2)}) copy-start(bf16[512,512]{1,0:T(8,128)(2,1)} %param.11) | copy-start | bytes 1572868
  153.0 95.1 %all-to-all-start.1 = ((bf16[16,8,64,256]{3,2,1,0:T(8,128)(2,1)}), bf16[16,8,64,256]{3,2,1,0:T(8,128)(2,1)}, u32[]{:S(2)}, u32[]{:S(2)}) async-start(bf16[16,8,64,256]{3,2,1,0:T(8,128)(2,1)} %bitcast.37), calls=%async_computation.1 | async-start | bytes 8388608 | tf_op jit(solution)/shard_map/all_to_all | solution.py:216
  157.8 22.4 %copy-start.15 = (s32[256]{0:T(256)S(1)}, s32[256]{0:T(256)}, u32[]{:S(2)}) copy-start(s32[256]{0:T(256)} %param.14) | copy-start | bytes 3076
  157.8 22.4 %copy-start.17 = (f32[256]{0:T(256)S(1)}, f32[256]{0:T(256)}, u32[]{:S(2)}) copy-start(f32[256]{0:T(256)} %param.17) | copy-start | bytes 3076
  157.8 22.4 %copy-start.18 = (s32[256]{0:T(256)S(1)}, s32[256]{0:T(256)}, u32[]{:S(2)}) copy-start(s32[256]{0:T(256)} %param.15) | copy-start | bytes 3076
  157.8 22.4 %copy-start.16 = (s32[256]{0:T(256)S(1)}, s32[256]{0:T(256)}, u32[]{:S(2)}) copy-start(s32[256]{0:T(256)} %param.16) | copy-start | bytes 3076
  169.6 106.0 %collective-permute-start.4 = (f32[128,256]{1,0:T(8,128)}, f32[128,256]{1,0:T(8,128)S(1)}, u32[]{:S(2)}, u32[]{:S(2)}) collective-permute-start(f32[128,256]{1,0:T(8,128)} %get-tuple-element.20), channel_id=1, source_target_pairs={{0,2},{2,4},{4,6},{6,8},{8,10},{10,12},{12,14},{1,3},{3,5},{5,7},{... | collective-permute-start | bytes 393224 | tf_op jit(solution)/shard_map/ppermute | solution.py:30
  172.7 106.9 %collective-permute-start.5 = (f32[128,256]{1,0:T(8,128)}, f32[128,256]{1,0:T(8,128)S(1)}, u32[]{:S(2)}, u32[]{:S(2)}) collective-permute-start(f32[128,256]{1,0:T(8,128)} %get-tuple-element.21), channel_id=1, source_target_pairs={{2,0},{4,2},{6,4},{8,6},{10,8},{12,10},{14,12},{3,1},{5,3},{7,5},{... | collective-permute-start | bytes 393224 | tf_op jit(solution)/shard_map/ppermute | solution.py:31
  175.8 89.8 %collective-permute-start.6 = (f32[128,64]{1,0:T(8,128)}, f32[128,64]{1,0:T(8,128)S(1)}, u32[]{:S(2)}, u32[]{:S(2)}) collective-permute-start(f32[128,64]{1,0:T(8,128)} %get-tuple-element.22), channel_id=1, source_target_pairs={{0,1},{2,3},{4,5},{6,7},{8,9},{10,11},{12,13},{14,15},{16,17},{18,... | collective-permute-start | bytes 98312 | tf_op jit(solution)/shard_map/ppermute | solution.py:32
  177.1 97.2 %collective-permute-start.7 = (f32[128,64]{1,0:T(8,128)}, f32[128,64]{1,0:T(8,128)S(1)}, u32[]{:S(2)}, u32[]{:S(2)}) collective-permute-start(f32[128,64]{1,0:T(8,128)} %get-tuple-element.23), channel_id=1, source_target_pairs={{1,0},{3,2},{5,4},{7,6},{9,8},{11,10},{13,12},{15,14},{17,16},{19,... | collective-permute-start | bytes 98312 | tf_op jit(solution)/shard_map/ppermute | solution.py:33
  259.9 19.7 %collective-permute-start = (f32[128,256]{1,0:T(8,128)}, f32[128,256]{1,0:T(8,128)S(1)}, u32[]{:S(2)}, u32[]{:S(2)}) collective-permute-start(f32[128,256]{1,0:T(8,128)} %get-tuple-element.16), channel_id=1, source_target_pairs={{0,2},{2,4},{4,6},{6,8},{8,10},{10,12},{12,14},{1,3},{3,5},{5,7},{... | collective-permute-start | bytes 393224 | tf_op jit(solution)/shard_map/ppermute | solution.py:30
  265.6 8.7 %copy-start.10 = (f32[128,64]{1,0:T(8,128)}, f32[128,64]{1,0:T(8,128)S(1)}, u32[]{:S(2)}) copy-start(f32[128,64]{1,0:T(8,128)S(1)} %collective-permute-done.6.qyl_ref) | copy-start | bytes 98308
  265.6 14.0 %collective-permute-start.1 = (f32[128,256]{1,0:T(8,128)}, f32[128,256]{1,0:T(8,128)S(1)}, u32[]{:S(2)}, u32[]{:S(2)}) collective-permute-start(f32[128,256]{1,0:T(8,128)} %get-tuple-element.17), channel_id=1, source_target_pairs={{2,0},{4,2},{6,4},{8,6},{10,8},{12,10},{14,12},{3,1},{5,3},{7,5},{... | collective-permute-start | bytes 393224 | tf_op jit(solution)/shard_map/ppermute | solution.py:31
  267.6 6.8 %copy-start.21 = (f32[128,64]{1,0:T(8,128)S(1)}, f32[128,64]{1,0:T(8,128)}, u32[]{:S(2)}) copy-start(f32[128,64]{1,0:T(8,128)} %get-tuple-element.18) | copy-start | bytes 98308
  267.6 8.1 %copy-start.20 = (f32[128,64]{1,0:T(8,128)S(1)}, f32[128,64]{1,0:T(8,128)}, u32[]{:S(2)}) copy-start(f32[128,64]{1,0:T(8,128)} %get-tuple-element.19) | copy-start | bytes 98308
  274.3 5.4 %copy-start.11 = (f32[128,64]{1,0:T(8,128)}, f32[128,64]{1,0:T(8,128)S(1)}, u32[]{:S(2)}) copy-start(f32[128,64]{1,0:T(8,128)S(1)} %collective-permute-done.7.qyh_ref) | copy-start | bytes 98308
  274.3 5.3 %collective-permute-start.2 = (f32[128,64]{1,0:T(8,128)S(1)}, f32[128,64]{1,0:T(8,128)S(1)}, u32[]{:S(2)}, u32[]{:S(2)}) collective-permute-start(f32[128,64]{1,0:T(8,128)S(1)} %copy-done.21), channel_id=1, source_target_pairs={{0,1},{2,3},{4,5},{6,7},{8,9},{10,11},{12,13},{14,15},{16,17},{18,... | collective-permute-start | bytes 98312 | tf_op jit(solution)/shard_map/ppermute | solution.py:32
  275.6 4.0 %copy-start.6 = (f32[128,256]{1,0:T(8,128)}, f32[128,256]{1,0:T(8,128)S(1)}, u32[]{:S(2)}) copy-start(f32[128,256]{1,0:T(8,128)S(1)} %collective-permute-done.4.qxl_ref) | copy-start | bytes 393220
  275.7 4.0 %collective-permute-start.3 = (f32[128,64]{1,0:T(8,128)S(1)}, f32[128,64]{1,0:T(8,128)S(1)}, u32[]{:S(2)}, u32[]{:S(2)}) collective-permute-start(f32[128,64]{1,0:T(8,128)S(1)} %copy-done.20), channel_id=1, source_target_pairs={{1,0},{3,2},{5,4},{7,6},{9,8},{11,10},{13,12},{15,14},{17,16},{19,... | collective-permute-start | bytes 98312 | tf_op jit(solution)/shard_map/ppermute | solution.py:33
  279.6 0.7 copy-start.5
  279.7 0.7 copy-start.2
  279.7 0.7 copy-start.3
  318.8 11.6 %collective-permute-start.8 = (f32[128,256]{1,0:T(8,128)}, f32[128,256]{1,0:T(8,128)S(1)}, u32[]{:S(2)}, u32[]{:S(2)}) collective-permute-start(f32[128,256]{1,0:T(8,128)} %get-tuple-element.25), channel_id=1, source_target_pairs={{0,2},{2,4},{4,6},{6,8},{8,10},{10,12},{12,14},{1,3},{3,5},{5,7},{... | collective-permute-start | bytes 393224 | tf_op jit(solution)/shard_map/ppermute | solution.py:30
  322.2 8.3 %collective-permute-start.9 = (f32[128,256]{1,0:T(8,128)}, f32[128,256]{1,0:T(8,128)S(1)}, u32[]{:S(2)}, u32[]{:S(2)}) collective-permute-start(f32[128,256]{1,0:T(8,128)} %get-tuple-element.26), channel_id=1, source_target_pairs={{2,0},{4,2},{6,4},{8,6},{10,8},{12,10},{14,12},{3,1},{5,3},{7,5},{... | collective-permute-start | bytes 393224 | tf_op jit(solution)/shard_map/ppermute | solution.py:31
  325.0 4.3 %collective-permute-start.10 = (f32[128,64]{1,0:T(8,128)}, f32[128,64]{1,0:T(8,128)S(1)}, u32[]{:S(2)}, u32[]{:S(2)}) collective-permute-start(f32[128,64]{1,0:T(8,128)} %get-tuple-element.27), channel_id=1, source_target_pairs={{0,1},{2,3},{4,5},{6,7},{8,9},{10,11},{12,13},{14,15},{16,17},{18,... | collective-permute-start | bytes 98312 | tf_op jit(solution)/shard_map/ppermute | solution.py:32
  326.3 4.1 %collective-permute-start.11 = (f32[128,64]{1,0:T(8,128)}, f32[128,64]{1,0:T(8,128)S(1)}, u32[]{:S(2)}, u32[]{:S(2)}) collective-permute-start(f32[128,64]{1,0:T(8,128)} %get-tuple-element.28), channel_id=1, source_target_pairs={{1,0},{3,2},{5,4},{7,6},{9,8},{11,10},{13,12},{15,14},{17,16},{19,... | collective-permute-start | bytes 98312 | tf_op jit(solution)/shard_map/ppermute | solution.py:33
  329.3 1.1 copy-start.12
  330.4 0.7 copy-start.8
  330.4 0.7 copy-start.9
  369.4 4.9 %copy-start.1 = (bf16[512,512]{1,0:T(8,128)(2,1)S(1)}, bf16[512,512]{1,0:T(8,128)(2,1)}, u32[]{:S(2)}) copy-start(bf16[512,512]{1,0:T(8,128)(2,1)} %param.12) | copy-start | bytes 1572868
  (3 other events, 1.9 us)

commit v4 on v3

--- a/solution.py
+++ b/solution.py
@@ -1,3 +1,5 @@
+import functools
+
 import jax
 import jax.numpy as jnp
 from jax import lax
@@ -191,6 +193,39 @@
     return new, (x_lo, x_hi, y_lo, y_hi)
 
 
+def line_kernel(g_ref, rx_ref, ry_ref, o_ref, *, count_w, count_n):
+    f32 = jnp.float32
+    nx = g_ref.shape[2]
+    ny = g_ref.shape[3]
+    rx = rx_ref[...]
+    halves = []
+    for n in range(count_n):
+        lines = jnp.concatenate([g_ref[w * count_n + n, 0] for w in range(count_w)], axis=0)
+        halves.append(jnp.dot(rx, lines, preferred_element_type=f32).astype(jnp.bfloat16))
+    second = jnp.concatenate(halves, axis=1)
+    third = lax.dot_general(
+        second, ry_ref[...], (((1,), (1,)), ((), ())), preferred_element_type=f32
+    ).astype(jnp.bfloat16)
+    for w in range(count_w):
+        for n in range(count_n):
+            o_ref[w * count_n + n, 0] = third[w * nx : (w + 1) * nx, n * ny : (n + 1) * ny]
+
+
+def line_transforms(gathered, root_x, root_y, count_w, count_n):
+    groups, planes, nx, ny = gathered.shape
+    block = pl.BlockSpec((groups, 1, nx, ny), lambda z: (0, z, 0, 0))
+    whole_x = pl.BlockSpec(root_x.shape, lambda z: (0, 0))
+    whole_y = pl.BlockSpec(root_y.shape, lambda z: (0, 0))
+    return pl.pallas_call(
+        functools.partial(line_kernel, count_w=count_w, count_n=count_n),
+        out_shape=jax.ShapeDtypeStruct(gathered.shape, jnp.bfloat16),
+        grid=(planes,),
+        in_specs=[block, whole_x, whole_y],
+        out_specs=block,
+        compiler_params=pltpu.CompilerParams(dimension_semantics=("arbitrary",)),
+    )(gathered, root_x, root_y)
+
+
 def body(noise, root_z, root_x, root_y, pressure_start, well_x, well_y, well_z, well_rate):
     depth, rows_x, rows_y = noise.shape
     first = jnp.dot(
@@ -204,18 +239,10 @@
     gathered = lax.all_to_all(
         first.reshape(groups, planes, rows_x, rows_y),
         ("wide", "narrow"), split_axis=0, concat_axis=0, tiled=True,
-    ).reshape(count_w, count_n, planes, rows_x, rows_y)
-    gathered = gathered.transpose(2, 0, 3, 1, 4).reshape(planes, count_w * rows_x, count_n * rows_y)
-    second = jnp.einsum(
-        "ia,zay->ziy", root_x, gathered, preferred_element_type=jnp.float32
-    ).astype(jnp.bfloat16)
-    third = jnp.einsum(
-        "zxb,jb->zxj", second, root_y, preferred_element_type=jnp.float32
-    ).astype(jnp.bfloat16)
-    outgoing = third.reshape(planes, count_w, rows_x, count_n, rows_y).transpose(1, 3, 0, 2, 4)
+    )
+    outgoing = line_transforms(gathered, root_x, root_y, count_w, count_n)
     log_perm = lax.all_to_all(
-        outgoing.reshape(groups, planes, rows_x, rows_y),
-        ("wide", "narrow"), split_axis=0, concat_axis=0, tiled=True,
+        outgoing, ("wide", "narrow"), split_axis=0, concat_axis=0, tiled=True,
     ).reshape(depth, rows_x, rows_y)
 
     wide_at = lax.axis_index("wide")

time: 377 us -> 353 us (0.936)
  local copies, waits for them, and re-layouts: 48.3 us -> 22.1 us
  Pallas kernels: 100 us -> 110 us
  matrix products: 17.9 us -> 10.2 us
    reshape x3 -> x0, local copies, waits for them, and re-layouts: 16.9 us -> none  [the longest x1 7.64 us: body(): gathered.transpose(2, 0, 3, 1, 4)]
    transpose x2 -> x0, local copies, waits for them, and re-layouts: 11.5 us -> none  [the longest x1 6.43 us: body(): gathered.transpose(2, 0, 3, 1, 4)]
    pallas_call x0 -> x1, Pallas kernels: none -> 9.62 us  [line_transforms(): pl.pallas_call(functools.partial(line_kernel, count_w=count_w, count_n=co...]
    dot_general x1 -> x0, matrix products: 7.74 us -> none  [body(): jnp.einsum('zxb,jb->zxj', second, root_y, preferred_element_type=jnp.floa...]
    unnamed x46 -> x42, local copies, waits for them, and re-layouts: 13.5 us -> 13.4 us
  transfers between devices with their start and end apart: 13 -> 13, of which waited for: 2 -> 2; matrix products, arithmetic and copies ran while one was open for 2% -> 2% of each run, Pallas kernels for 6% -> 7%
where the time goes in v4:
time: 353 us; the launch traced here: 350 us
  Pallas kernels  110 us (31%)
  blocking collectives  99.3 us (28%)
  waiting for transfers between devices  69 us (20%)
  starting transfers between devices  37.9 us (11%)
  local copies, waits for them, and re-layouts  22.1 us (6%)
  matrix products  10.2 us (3%)
    all_to_all x1, blocking collectives, body(): lax.all_to_all(first.reshape(groups, planes, rows_x, rows_y), ('wide', 'n...  99.3 us
    pallas_call x2, Pallas kernels, advance(): pl.pallas_call(step_kernel, out_shape=out_shape, grid=grid, in_specs=[sme...  76.6 us
    all_to_all x1, waiting for transfers between devices, body(): lax.all_to_all(outgoing, ('wide', 'narrow'), split_axis=0, concat_axis=0,...  67.9 us
    pallas_call x2, Pallas kernels, block_edges(): pl.pallas_call(edge_kernel, out_shape=(jax.ShapeDtypeStruct((depth, ny),...  23.6 us
    unnamed x42, local copies, waits for them, and re-layouts  13.4 us
    ppermute x3, starting transfers between devices, halos(): x_lo = lax.ppermute(last_x, 'wide', forward_w)  12.1 us
    pallas_call x1, Pallas kernels, line_transforms(): pl.pallas_call(functools.partial(line_kernel, count_w=count_w, count_n=co...  9.62 us
    ppermute x3, starting transfers between devices, halos(): y_hi = lax.ppermute(first_y, 'narrow', backward_n)  9.28 us
  transfers between devices with their start and end apart: 13, of which 2 were waited for; matrix products, arithmetic and copies ran while one was open for 2% of the time, Pallas kernels for 7%

profile of v4, /device:TPU:11, one launch (start us, length us, event | category | flops | bytes accessed | tf_op | source)
XLA Modules:
  0.0 350.0 jit_solution(17247695096430654889)
XLA Ops:
  0.6 7.1 %copy.13 = bf16[16,8,64,256]{3,1,2,0:T(8,128)(2,1)} copy(bf16[16,8,64,256]{3,2,1,0:T(8,128)(2,1)} %bitcast.21) | data formatting | bytes 8388608
  7.7 6.4 %copy.11 = bf16[16384,128]{1,0:T(8,128)(2,1)} copy(bf16[16384,128]{0,1:T(8,128)(2,1)} %bitcast.20) | data formatting | bytes 8388608 | tf_op jit(solution)/shard_map/dot_general | solution.py:231
  14.1 3.4 convolution_convert_fusion
  17.5 2.4 copy.12
  20.0 99.3 %all_to_all.10.g_ref = bf16[16,8,64,256]{3,2,1,0:T(8,128)(2,1)} all-to-all(bf16[16,8,64,256]{3,2,1,0:T(8,128)(2,1)S(1)} %bitcast.19), channel_id=1, replica_groups=mesh['member'=2,'wide'=8,'narrow'=2] {'wide','narrow'}, dimensions={0} | all-to-all | bytes 8388608 | tf_op jit(solution)/shard_map/all_to_all | solution.py:239
  119.3 9.6 %shard_map.104 = bf16[16,8,64,256]{3,2,1,0:T(8,128)(2,1)} custom-call(bf16[16,8,64,256]{3,2,1,0:T(8,128)(2,1)} %all_to_all.10.g_ref, bf16[512,512]{1,0:T(8,128)(2,1)} %rx_ref.1, bf16[512,512]{1,0:T(8,128)(2,1)} %ry_ref.1), custom_call_target="tpu_custom_call" | custom-call | tf_op jit(solution)/shard_map/pallas_call | solution.py:219
  128.9 4.8 %all-to-all-start.1 = ((bf16[16,8,64,256]{3,2,1,0:T(8,128)(2,1)}), bf16[16,8,64,256]{3,2,1,0:T(8,128)(2,1)}, u32[]{:S(2)}, u32[]{:S(2)}) async-start(bf16[16,8,64,256]{3,2,1,0:T(8,128)(2,1)} %shard_map.104), calls=%async_computation.1 | async-start | bytes 8388608 | tf_op jit(solution)/shard_map/all_to_all | solution.py:244
  133.7 11.8 %shard_map.106 = (f32[128,256]{1,0:T(8,128)}, f32[128,256]{1,0:T(8,128)}, f32[128,64]{1,0:T(8,128)}, f32[128,64]{1,0:T(8,128)}) custom-call(bf16[128,64,256]{2,1,0:T(8,128)(2,1)} %pa_ref.1), custom_call_target="tpu_custom_call" | custom-call | tf_op jit(solution)/shard_map/pallas_call | solution.py:95
  145.5 3.1 collective-permute-start.4
  148.6 3.1 collective-permute-start.5
  151.7 1.3 collective-permute-start.6
  153.0 3.0 collective-permute-start.7
  156.1 67.9 %all-to-all-done.1 = bf16[16,8,64,256]{3,2,1,0:T(8,128)(2,1)} async-done(((bf16[16,8,64,256]{3,2,1,0:T(8,128)(2,1)}), bf16[16,8,64,256]{3,2,1,0:T(8,128)(2,1)}, u32[]{:S(2)}, u32[]{:S(2)}) %all-to-all-start.1) | async-done | bytes 4194336 | tf_op jit(solution)/shard_map/all_to_all | solution.py:244
  224.0 11.8 %shard_map.105 = (f32[128,256]{1,0:T(8,128)}, f32[128,256]{1,0:T(8,128)}, f32[128,64]{1,0:T(8,128)}, f32[128,64]{1,0:T(8,128)}) custom-call(bf16[128,64,256]{2,1,0:T(8,128)(2,1)} %bitcast.4.block_ref.lpm_ref.lpb_ref.lpa_ref), custom_call_target="tpu_custom_call" | custom-call | tf_op jit(solution)/shard_map/pallas_call | solution.py:95
  235.8 5.7 %collective-permute-start = (f32[128,256]{1,0:T(8,128)}, f32[128,256]{1,0:T(8,128)S(1)}, u32[]{:S(2)}, u32[]{:S(2)}) collective-permute-start(f32[128,256]{1,0:T(8,128)} %get-tuple-element.16), channel_id=1, source_target_pairs={{0,2},{2,4},{4,6},{6,8},{8,10},{10,12},{12,14},{1,3},{3,5},{5,7},{... | collective-permute-start | bytes 393224 | tf_op jit(solution)/shard_map/ppermute | solution.py:32
  241.5 1.9 collective-permute-start.1
  243.4 6.7 %fusion = f32[8192,256]{1,0:T(8,128)} fusion(f32[256]{0:T(256)S(1)} %get-tuple-element.30, s32[256]{0:T(256)S(1)} %multiply_add_fusion, s32[256]{0:T(256)S(1)} %get-tuple-element.31), kind=kOutput, calls=%fused_computation | convolution fusion | flops 6446710784 | bytes 8391680 | tf_op jit(solution)/shard_map/dot_general | solution.py:267
  250.2 1.3 collective-permute-start.2
  251.5 3.2 collective-permute-start.3
  254.7 0.7 add_convert_fusion.inside_ref
  255.5 0.6 copy-done.7
  256.2 38.4 %shard_map.107 = (f32[128,64,256]{2,1,0:T(8,128)}, f32[128,256]{1,0:T(8,128)}, f32[128,256]{1,0:T(8,128)}, f32[128,64]{1,0:T(8,128)}, f32[128,64]{1,0:T(8,128)}) custom-call(s32[4]{0:T(128)} %add_convert_fusion.inside_ref, bf16[128,64,256]{2,1,0:T(8,128)(2,1)} %bitcast.4.block_ref.lpm_ref.lpb_ref.lpa_ref, ...), custom_call_target="tpu_custom_call" | custom-call | tf_op jit(solution)/shard_map/pallas_call | solution.py:185
  294.6 3.4 collective-permute-start.8
  298.0 2.8 collective-permute-start.9
  300.8 1.3 collective-permute-start.10
  302.1 3.0 collective-permute-start.11
  305.1 1.1 collective-permute-done.11.qyh_ref
  306.2 0.6 copy-done.13
  306.8 0.1 copy-done.8
  306.9 0.1 copy-done.9
  307.0 38.2 %shard_map.108 = (f32[128,64,256]{2,1,0:T(8,128)}, f32[128,256]{1,0:T(8,128)}, f32[128,256]{1,0:T(8,128)}, f32[128,64]{1,0:T(8,128)}, f32[128,64]{1,0:T(8,128)}) custom-call(s32[4]{0:T(128)} %add_convert_fusion.inside_ref, bf16[128,64,256]{2,1,0:T(8,128)(2,1)} %bitcast.4.block_ref.lpm_ref.lpb_ref.lpa_ref, ...), custom_call_target="tpu_custom_call" | custom-call | tf_op jit(solution)/shard_map/pallas_call | solution.py:185
  345.2 4.8 %copy.15 = bf16[128,64,256]{2,1,0:T(8,128)(2,1)} copy(bf16[128,64,256]{2,1,0:T(8,128)(2,1)} %bitcast.4.block_ref.lpm_ref.lpb_ref.lpa_ref) | data formatting | bytes 8388608
  (49 shorter events, 0.3 us)
Async XLA Ops:
  0.6 13.5 %copy-start = (bf16[128,128]{1,0:T(8,128)(2,1)S(1)}, bf16[128,128]{1,0:T(8,128)(2,1)}, u32[]{:S(2)}) copy-start(bf16[128,128]{1,0:T(8,128)(2,1)} %param.10) | copy-start | bytes 98308
  128.9 95.1 %all-to-all-start.1 = ((bf16[16,8,64,256]{3,2,1,0:T(8,128)(2,1)}), bf16[16,8,64,256]{3,2,1,0:T(8,128)(2,1)}, u32[]{:S(2)}, u32[]{:S(2)}) async-start(bf16[16,8,64,256]{3,2,1,0:T(8,128)(2,1)} %shard_map.104), calls=%async_computation.1 | async-start | bytes 8388608 | tf_op jit(solution)/shard_map/all_to_all | solution.py:244
  133.7 22.4 %copy-start.14 = (s32[256]{0:T(256)S(1)}, s32[256]{0:T(256)}, u32[]{:S(2)}) copy-start(s32[256]{0:T(256)} %param.14) | copy-start | bytes 3076
  133.7 22.4 %copy-start.16 = (f32[256]{0:T(256)S(1)}, f32[256]{0:T(256)}, u32[]{:S(2)}) copy-start(f32[256]{0:T(256)} %param.17) | copy-start | bytes 3076
  133.7 22.4 %copy-start.17 = (s32[256]{0:T(256)S(1)}, s32[256]{0:T(256)}, u32[]{:S(2)}) copy-start(s32[256]{0:T(256)} %param.15) | copy-start | bytes 3076
  133.7 22.4 %copy-start.15 = (s32[256]{0:T(256)S(1)}, s32[256]{0:T(256)}, u32[]{:S(2)}) copy-start(s32[256]{0:T(256)} %param.16) | copy-start | bytes 3076
  145.5 106.0 %collective-permute-start.4 = (f32[128,256]{1,0:T(8,128)}, f32[128,256]{1,0:T(8,128)S(1)}, u32[]{:S(2)}, u32[]{:S(2)}) collective-permute-start(f32[128,256]{1,0:T(8,128)} %get-tuple-element.20), channel_id=1, source_target_pairs={{0,2},{2,4},{4,6},{6,8},{8,10},{10,12},{12,14},{1,3},{3,5},{5,7},{... | collective-permute-start | bytes 393224 | tf_op jit(solution)/shard_map/ppermute | solution.py:32
  148.6 106.8 %collective-permute-start.5 = (f32[128,256]{1,0:T(8,128)}, f32[128,256]{1,0:T(8,128)S(1)}, u32[]{:S(2)}, u32[]{:S(2)}) collective-permute-start(f32[128,256]{1,0:T(8,128)} %get-tuple-element.21), channel_id=1, source_target_pairs={{2,0},{4,2},{6,4},{8,6},{10,8},{12,10},{14,12},{3,1},{5,3},{7,5},{... | collective-permute-start | bytes 393224 | tf_op jit(solution)/shard_map/ppermute | solution.py:33
  151.7 89.8 %collective-permute-start.6 = (f32[128,64]{1,0:T(8,128)}, f32[128,64]{1,0:T(8,128)S(1)}, u32[]{:S(2)}, u32[]{:S(2)}) collective-permute-start(f32[128,64]{1,0:T(8,128)} %get-tuple-element.22), channel_id=1, source_target_pairs={{0,1},{2,3},{4,5},{6,7},{8,9},{10,11},{12,13},{14,15},{16,17},{18,... | collective-permute-start | bytes 98312 | tf_op jit(solution)/shard_map/ppermute | solution.py:34
  153.0 97.2 %collective-permute-start.7 = (f32[128,64]{1,0:T(8,128)}, f32[128,64]{1,0:T(8,128)S(1)}, u32[]{:S(2)}, u32[]{:S(2)}) collective-permute-start(f32[128,64]{1,0:T(8,128)} %get-tuple-element.23), channel_id=1, source_target_pairs={{1,0},{3,2},{5,4},{7,6},{9,8},{11,10},{13,12},{15,14},{17,16},{19,... | collective-permute-start | bytes 98312 | tf_op jit(solution)/shard_map/ppermute | solution.py:35
  235.8 19.6 %collective-permute-start = (f32[128,256]{1,0:T(8,128)}, f32[128,256]{1,0:T(8,128)S(1)}, u32[]{:S(2)}, u32[]{:S(2)}) collective-permute-start(f32[128,256]{1,0:T(8,128)} %get-tuple-element.16), channel_id=1, source_target_pairs={{0,2},{2,4},{4,6},{6,8},{8,10},{10,12},{12,14},{1,3},{3,5},{5,7},{... | collective-permute-start | bytes 393224 | tf_op jit(solution)/shard_map/ppermute | solution.py:32
  241.5 8.7 %copy-start.10 = (f32[128,64]{1,0:T(8,128)}, f32[128,64]{1,0:T(8,128)S(1)}, u32[]{:S(2)}) copy-start(f32[128,64]{1,0:T(8,128)S(1)} %collective-permute-done.6.qyl_ref) | copy-start | bytes 98308
  241.5 14.0 %collective-permute-start.1 = (f32[128,256]{1,0:T(8,128)}, f32[128,256]{1,0:T(8,128)S(1)}, u32[]{:S(2)}, u32[]{:S(2)}) collective-permute-start(f32[128,256]{1,0:T(8,128)} %get-tuple-element.17), channel_id=1, source_target_pairs={{2,0},{4,2},{6,4},{8,6},{10,8},{12,10},{14,12},{3,1},{5,3},{7,5},{... | collective-permute-start | bytes 393224 | tf_op jit(solution)/shard_map/ppermute | solution.py:33
  243.4 6.8 %copy-start.19 = (f32[128,64]{1,0:T(8,128)S(1)}, f32[128,64]{1,0:T(8,128)}, u32[]{:S(2)}) copy-start(f32[128,64]{1,0:T(8,128)} %get-tuple-element.18) | copy-start | bytes 98308
  243.4 8.1 %copy-start.18 = (f32[128,64]{1,0:T(8,128)S(1)}, f32[128,64]{1,0:T(8,128)}, u32[]{:S(2)}) copy-start(f32[128,64]{1,0:T(8,128)} %get-tuple-element.19) | copy-start | bytes 98308
  250.2 5.3 %copy-start.11 = (f32[128,64]{1,0:T(8,128)}, f32[128,64]{1,0:T(8,128)S(1)}, u32[]{:S(2)}) copy-start(f32[128,64]{1,0:T(8,128)S(1)} %collective-permute-done.7.qyh_ref) | copy-start | bytes 98308
  250.2 5.2 %collective-permute-start.2 = (f32[128,64]{1,0:T(8,128)S(1)}, f32[128,64]{1,0:T(8,128)S(1)}, u32[]{:S(2)}, u32[]{:S(2)}) collective-permute-start(f32[128,64]{1,0:T(8,128)S(1)} %copy-done.19), channel_id=1, source_target_pairs={{0,1},{2,3},{4,5},{6,7},{8,9},{10,11},{12,13},{14,15},{16,17},{18,... | collective-permute-start | bytes 98312 | tf_op jit(solution)/shard_map/ppermute | solution.py:34
  251.5 4.0 %copy-start.6 = (f32[128,256]{1,0:T(8,128)}, f32[128,256]{1,0:T(8,128)S(1)}, u32[]{:S(2)}) copy-start(f32[128,256]{1,0:T(8,128)S(1)} %collective-permute-done.4.qxl_ref) | copy-start | bytes 393220
  251.5 3.9 %collective-permute-start.3 = (f32[128,64]{1,0:T(8,128)S(1)}, f32[128,64]{1,0:T(8,128)S(1)}, u32[]{:S(2)}, u32[]{:S(2)}) collective-permute-start(f32[128,64]{1,0:T(8,128)S(1)} %copy-done.18), channel_id=1, source_target_pairs={{1,0},{3,2},{5,4},{7,6},{9,8},{11,10},{13,12},{15,14},{17,16},{19,... | collective-permute-start | bytes 98312 | tf_op jit(solution)/shard_map/ppermute | solution.py:35
  255.4 0.7 copy-start.7
  255.4 0.7 copy-start.4
  255.4 0.7 copy-start.5
  255.5 0.7 copy-start.2
  255.5 0.7 copy-start.3
  294.6 11.6 %collective-permute-start.8 = (f32[128,256]{1,0:T(8,128)}, f32[128,256]{1,0:T(8,128)S(1)}, u32[]{:S(2)}, u32[]{:S(2)}) collective-permute-start(f32[128,256]{1,0:T(8,128)} %get-tuple-element.25), channel_id=1, source_target_pairs={{0,2},{2,4},{4,6},{6,8},{8,10},{10,12},{12,14},{1,3},{3,5},{5,7},{... | collective-permute-start | bytes 393224 | tf_op jit(solution)/shard_map/ppermute | solution.py:32
  298.0 8.3 %collective-permute-start.9 = (f32[128,256]{1,0:T(8,128)}, f32[128,256]{1,0:T(8,128)S(1)}, u32[]{:S(2)}, u32[]{:S(2)}) collective-permute-start(f32[128,256]{1,0:T(8,128)} %get-tuple-element.26), channel_id=1, source_target_pairs={{2,0},{4,2},{6,4},{8,6},{10,8},{12,10},{14,12},{3,1},{5,3},{7,5},{... | collective-permute-start | bytes 393224 | tf_op jit(solution)/shard_map/ppermute | solution.py:33
  300.8 4.3 %collective-permute-start.10 = (f32[128,64]{1,0:T(8,128)}, f32[128,64]{1,0:T(8,128)S(1)}, u32[]{:S(2)}, u32[]{:S(2)}) collective-permute-start(f32[128,64]{1,0:T(8,128)} %get-tuple-element.27), channel_id=1, source_target_pairs={{0,1},{2,3},{4,5},{6,7},{8,9},{10,11},{12,13},{14,15},{16,17},{18,... | collective-permute-start | bytes 98312 | tf_op jit(solution)/shard_map/ppermute | solution.py:34
  302.1 4.1 %collective-permute-start.11 = (f32[128,64]{1,0:T(8,128)}, f32[128,64]{1,0:T(8,128)S(1)}, u32[]{:S(2)}, u32[]{:S(2)}) collective-permute-start(f32[128,64]{1,0:T(8,128)} %get-tuple-element.28), channel_id=1, source_target_pairs={{1,0},{3,2},{5,4},{7,6},{9,8},{11,10},{13,12},{15,14},{17,16},{19,... | collective-permute-start | bytes 98312 | tf_op jit(solution)/shard_map/ppermute | solution.py:35
  305.1 1.1 copy-start.12
  306.2 0.7 copy-start.8
  306.2 0.7 copy-start.9
  345.2 4.8 %copy-start.1 = (bf16[128,128]{1,0:T(8,128)(2,1)S(1)}, bf16[128,128]{1,0:T(8,128)(2,1)}, u32[]{:S(2)}) copy-start(bf16[128,128]{1,0:T(8,128)(2,1)} %param.10) | copy-start | bytes 98308
  (1 other events, 0.6 us)

commit v5 on v4

--- a/solution.py
+++ b/solution.py
@@ -120,47 +120,73 @@
     def side_perm(ref, k):
         return jnp.where(inside_ref[k] > 0, permeability(ref[...].astype(f32)), 0.0)
 
-    kxl = jnp.where(inside_ref[0] > 0, permeability(x_rows(lxl_ref)), 0.0)
-    kxh = jnp.where(inside_ref[1] > 0, permeability(x_rows(lxh_ref)), 0.0)
+    kxl = side_perm(lxl_ref, 0)
+    kxh = side_perm(lxh_ref, 1)
     kyl = to_columns(side_perm(lyl_ref, 2))
     kyh = to_columns(side_perm(lyh_ref, 3))
-
-    below = jnp.where(c == 0, 0.0, permeability(lpb_ref[...].astype(f32)))
-    above = jnp.where(c == last, 0.0, permeability(lpa_ref[...].astype(f32)))
-    centre = permeability(lpm_ref[...].astype(f32))
-    ext = jnp.concatenate([below, centre, above], axis=0)
-    faces = harmonic(ext[:-1], ext[1:])
-    t_zm = faces[:-1]
-    t_zp = faces[1:]
-
-    xi = lax.broadcasted_iota(jnp.int32, (tz, nx, ny), 1)
-    yi = lax.broadcasted_iota(jnp.int32, (tz, nx, ny), 2)
-
-    fx = harmonic(centre, pltpu.roll(centre, nx - 1, 1))
-    t_xp = jnp.where(xi == nx - 1, harmonic(centre[:, nx - 1 :, :], kxh), fx)
-    t_xm = jnp.where(xi == 0, harmonic(centre[:, :1, :], kxl), pltpu.roll(fx, 1, 1))
-    fy = harmonic(centre, pltpu.roll(centre, ny - 1, 2))
-    t_yp = jnp.where(yi == ny - 1, harmonic(centre[:, :, ny - 1 :], kyh), fy)
-    t_ym = jnp.where(yi == 0, harmonic(centre[:, :, :1], kyl), pltpu.roll(fy, 1, 2))
-
-    p = pm_ref[...].astype(f32)
-    pext = jnp.concatenate([pb_ref[...].astype(f32), p, pa_ref[...].astype(f32)], axis=0)
-    n_xp = jnp.where(xi == nx - 1, x_rows(qxh_ref), pltpu.roll(p, nx - 1, 1))
-    n_xm = jnp.where(xi == 0, x_rows(qxl_ref), pltpu.roll(p, 1, 1))
-    n_yp = jnp.where(yi == ny - 1, to_columns(qyh_ref[...]), pltpu.roll(p, ny - 1, 2))
-    n_ym = jnp.where(yi == 0, to_columns(qyl_ref[...]), pltpu.roll(p, 1, 2))
-
-    flux = t_zp * (pext[2:] - p)
-    flux = flux + t_zm * (pext[:-2] - p)
-    flux = flux + t_xp * (n_xp - p)
-    flux = flux + t_xm * (n_xm - p)
-    flux = flux + t_yp * (n_yp - p)
-    flux = flux + t_ym * (n_ym - p)
-    new = p + STEP_SIZE * (flux + f_ref[...]) / (1.0 + 0.5 * p * p)
-    o_ref[...] = new
-    store_x_rows(exl_ref, new[:, :1, :])
-    store_x_rows(exh_ref, new[:, nx - 1 :, :])
-    eyl_ref[...], eyh_ref[...] = to_rows(new)
+    qyl = to_columns(qyl_ref[...])
+    qyh = to_columns(qyh_ref[...])
+
+    xi = lax.broadcasted_iota(jnp.int32, (nx, ny), 0)
+    yi = lax.broadcasted_iota(jnp.int32, (nx, ny), 1)
+    lane = lax.broadcasted_iota(jnp.int32, (nx, 128), 1)
+
+    below = jnp.where(c == 0, 0.0, permeability(lpb_ref[0].astype(f32)))
+    above = jnp.where(c == last, 0.0, permeability(lpa_ref[0].astype(f32)))
+    p_below = pb_ref[0].astype(f32)
+    p_above = pa_ref[0].astype(f32)
+
+    centre = permeability(lpm_ref[0].astype(f32))
+    t_zm = harmonic(centre, below)
+    p = pm_ref[0].astype(f32)
+    p_prev = p_below
+    first_y = jnp.zeros((nx, 128), f32)
+    last_y = jnp.zeros((nx, 128), f32)
+    for k in range(tz):
+        if k + 1 < tz:
+            nxt = permeability(lpm_ref[k + 1].astype(f32))
+            p_next = pm_ref[k + 1].astype(f32)
+        else:
+            nxt = above
+            p_next = p_above
+        t_zp = harmonic(centre, nxt)
+
+        fx = harmonic(centre, pltpu.roll(centre, nx - 1, 0))
+        t_xp = jnp.where(xi == nx - 1, harmonic(centre[nx - 1 :, :], kxh[k : k + 1, :]), fx)
+        t_xm = jnp.where(xi == 0, harmonic(centre[:1, :], kxl[k : k + 1, :]), pltpu.roll(fx, 1, 0))
+        fy = harmonic(centre, pltpu.roll(centre, ny - 1, 1))
+        t_yp = jnp.where(yi == ny - 1, harmonic(centre[:, ny - 1 :], kyh[k]), fy)
+        t_ym = jnp.where(yi == 0, harmonic(centre[:, :1], kyl[k]), pltpu.roll(fy, 1, 1))
+
+        n_xp = jnp.where(xi == nx - 1, qxh_ref[k : k + 1, :], pltpu.roll(p, nx - 1, 0))
+        n_xm = jnp.where(xi == 0, qxl_ref[k : k + 1, :], pltpu.roll(p, 1, 0))
+        n_yp = jnp.where(yi == ny - 1, qyh[k], pltpu.roll(p, ny - 1, 1))
+        n_ym = jnp.where(yi == 0, qyl[k], pltpu.roll(p, 1, 1))
+
+        flux = t_zp * (p_next - p)
+        flux = flux + t_zm * (p_prev - p)
+        flux = flux + t_xp * (n_xp - p)
+        flux = flux + t_xm * (n_xm - p)
+        flux = flux + t_yp * (n_yp - p)
+        flux = flux + t_ym * (n_ym - p)
+        new = p + STEP_SIZE * (flux + f_ref[k]) / (1.0 + 0.5 * p * p)
+        o_ref[k] = new
+        exl_ref[k : k + 1, :] = new[:1, :]
+        exh_ref[k : k + 1, :] = new[nx - 1 :, :]
+        first_y = jnp.where(lane == k, new[:, :1], first_y)
+        last_y = jnp.where(lane == k, new[:, ny - 1 :], last_y)
+
+        centre, t_zm, p_prev, p = nxt, t_zp, p, p_next
+
+    pick = jnp.where(
+        lax.broadcasted_iota(jnp.int32, (tz, 128), 0) == lax.broadcasted_iota(jnp.int32, (tz, 128), 1),
+        1.0, 0.0,
+    )
+    for ref, gathered in ((eyl_ref, first_y), (eyh_ref, last_y)):
+        ref[...] = lax.dot_general(
+            pick, gathered, (((1,), (1,)), ((), ())),
+            precision=lax.Precision.HIGHEST, preferred_element_type=f32,
+        )
 
 
 def advance(inside, log_perm, perm_halos, pressure, pressure_halos, flow):

time: 353 us -> 379 us (1.074)
  Pallas kernels: 110 us -> 136 us
    pallas_call x2, Pallas kernels: 76.6 us -> 103 us  [advance(): pl.pallas_call(step_kernel, out_shape=out_shape, grid=grid, in_specs=[sme...]
  transfers between devices with their start and end apart: 13 -> 13, of which waited for: 2 -> 2; matrix products, arithmetic and copies ran while one was open for 2% -> 2% of each run, Pallas kernels for 7% -> 6%
where the time goes in v5:
time: 379 us; the launch traced here: 376 us
  Pallas kernels  136 us (36%)
  blocking collectives  99.3 us (26%)
  waiting for transfers between devices  69 us (18%)
  starting transfers between devices  37.9 us (10%)
  local copies, waits for them, and re-layouts  22.1 us (6%)
  matrix products  10.2 us (3%)
    pallas_call x2, Pallas kernels, advance(): pl.pallas_call(step_kernel, out_shape=out_shape, grid=grid, in_specs=[sme...  103 us
    all_to_all x1, blocking collectives, body(): lax.all_to_all(first.reshape(groups, planes, rows_x, rows_y), ('wide', 'n...  99.3 us
    all_to_all x1, waiting for transfers between devices, body(): lax.all_to_all(outgoing, ('wide', 'narrow'), split_axis=0, concat_axis=0,...  67.9 us
    pallas_call x2, Pallas kernels, block_edges(): pl.pallas_call(edge_kernel, out_shape=(jax.ShapeDtypeStruct((depth, ny),...  23.6 us
    unnamed x42, local copies, waits for them, and re-layouts  13.4 us
    ppermute x3, starting transfers between devices, halos(): x_lo = lax.ppermute(last_x, 'wide', forward_w)  12.1 us
    pallas_call x1, Pallas kernels, line_transforms(): pl.pallas_call(functools.partial(line_kernel, count_w=count_w, count_n=co...  9.62 us
    ppermute x3, starting transfers between devices, halos(): y_hi = lax.ppermute(first_y, 'narrow', backward_n)  9.28 us
  transfers between devices with their start and end apart: 13, of which 2 were waited for; matrix products, arithmetic and copies ran while one was open for 2% of the time, Pallas kernels for 6%

profile of v5, /device:TPU:11, one launch (start us, length us, event | category | flops | bytes accessed | tf_op | source)
XLA Modules:
  0.0 376.1 jit_solution(3091729649019704565)
XLA Ops:
  0.6 7.1 %copy.13 = bf16[16,8,64,256]{3,1,2,0:T(8,128)(2,1)} copy(bf16[16,8,64,256]{3,2,1,0:T(8,128)(2,1)} %bitcast.21) | data formatting | bytes 8388608
  7.7 6.4 %copy.11 = bf16[16384,128]{1,0:T(8,128)(2,1)} copy(bf16[16384,128]{0,1:T(8,128)(2,1)} %bitcast.20) | data formatting | bytes 8388608 | tf_op jit(solution)/shard_map/dot_general | solution.py:257
  14.1 3.4 convolution_convert_fusion
  17.5 2.4 copy.12
  20.0 99.3 %all_to_all.10.g_ref = bf16[16,8,64,256]{3,2,1,0:T(8,128)(2,1)} all-to-all(bf16[16,8,64,256]{3,2,1,0:T(8,128)(2,1)S(1)} %bitcast.19), channel_id=1, replica_groups=mesh['member'=2,'wide'=8,'narrow'=2] {'wide','narrow'}, dimensions={0} | all-to-all | bytes 8388608 | tf_op jit(solution)/shard_map/all_to_all | solution.py:265
  119.3 9.6 %shard_map.104 = bf16[16,8,64,256]{3,2,1,0:T(8,128)(2,1)} custom-call(bf16[16,8,64,256]{3,2,1,0:T(8,128)(2,1)} %all_to_all.10.g_ref, bf16[512,512]{1,0:T(8,128)(2,1)} %rx_ref.1, bf16[512,512]{1,0:T(8,128)(2,1)} %ry_ref.1), custom_call_target="tpu_custom_call" | custom-call | tf_op jit(solution)/shard_map/pallas_call | solution.py:245
  128.9 4.8 %all-to-all-start.1 = ((bf16[16,8,64,256]{3,2,1,0:T(8,128)(2,1)}), bf16[16,8,64,256]{3,2,1,0:T(8,128)(2,1)}, u32[]{:S(2)}, u32[]{:S(2)}) async-start(bf16[16,8,64,256]{3,2,1,0:T(8,128)(2,1)} %shard_map.104), calls=%async_computation.1 | async-start | bytes 8388608 | tf_op jit(solution)/shard_map/all_to_all | solution.py:270
  133.7 11.8 %shard_map.106 = (f32[128,256]{1,0:T(8,128)}, f32[128,256]{1,0:T(8,128)}, f32[128,64]{1,0:T(8,128)}, f32[128,64]{1,0:T(8,128)}) custom-call(bf16[128,64,256]{2,1,0:T(8,128)(2,1)} %pa_ref.1), custom_call_target="tpu_custom_call" | custom-call | tf_op jit(solution)/shard_map/pallas_call | solution.py:95
  145.5 3.1 collective-permute-start.4
  148.6 3.1 collective-permute-start.5
  151.7 1.3 collective-permute-start.6
  153.0 3.0 collective-permute-start.7
  156.1 67.9 %all-to-all-done.1 = bf16[16,8,64,256]{3,2,1,0:T(8,128)(2,1)} async-done(((bf16[16,8,64,256]{3,2,1,0:T(8,128)(2,1)}), bf16[16,8,64,256]{3,2,1,0:T(8,128)(2,1)}, u32[]{:S(2)}, u32[]{:S(2)}) %all-to-all-start.1) | async-done | bytes 4194336 | tf_op jit(solution)/shard_map/all_to_all | solution.py:270
  224.0 11.8 %shard_map.105 = (f32[128,256]{1,0:T(8,128)}, f32[128,256]{1,0:T(8,128)}, f32[128,64]{1,0:T(8,128)}, f32[128,64]{1,0:T(8,128)}) custom-call(bf16[128,64,256]{2,1,0:T(8,128)(2,1)} %bitcast.4.block_ref.lpm_ref.lpb_ref.lpa_ref), custom_call_target="tpu_custom_call" | custom-call | tf_op jit(solution)/shard_map/pallas_call | solution.py:95
  235.8 5.7 %collective-permute-start = (f32[128,256]{1,0:T(8,128)}, f32[128,256]{1,0:T(8,128)S(1)}, u32[]{:S(2)}, u32[]{:S(2)}) collective-permute-start(f32[128,256]{1,0:T(8,128)} %get-tuple-element.16), channel_id=1, source_target_pairs={{0,2},{2,4},{4,6},{6,8},{8,10},{10,12},{12,14},{1,3},{3,5},{5,7},{... | collective-permute-start | bytes 393224 | tf_op jit(solution)/shard_map/ppermute | solution.py:32
  241.5 1.9 collective-permute-start.1
  243.4 6.7 %fusion = f32[8192,256]{1,0:T(8,128)} fusion(f32[256]{0:T(256)S(1)} %get-tuple-element.30, s32[256]{0:T(256)S(1)} %multiply_add_fusion, s32[256]{0:T(256)S(1)} %get-tuple-element.31), kind=kOutput, calls=%fused_computation | convolution fusion | flops 6446710784 | bytes 8391680 | tf_op jit(solution)/shard_map/dot_general | solution.py:293
  250.2 1.3 collective-permute-start.2
  251.5 3.2 collective-permute-start.3
  254.7 0.7 add_convert_fusion.inside_ref
  255.5 0.6 copy-done.7
  256.2 51.1 %shard_map.107 = (f32[128,64,256]{2,1,0:T(8,128)}, f32[128,256]{1,0:T(8,128)}, f32[128,256]{1,0:T(8,128)}, f32[128,64]{1,0:T(8,128)}, f32[128,64]{1,0:T(8,128)}) custom-call(s32[4]{0:T(128)} %add_convert_fusion.inside_ref, bf16[128,64,256]{2,1,0:T(8,128)(2,1)} %bitcast.4.block_ref.lpm_ref.lpb_ref.lpa_ref, ...), custom_call_target="tpu_custom_call" | custom-call | tf_op jit(solution)/shard_map/pallas_call | solution.py:211
  307.3 3.4 collective-permute-start.8
  310.6 2.8 collective-permute-start.9
  313.5 1.3 collective-permute-start.10
  314.8 3.0 collective-permute-start.11
  317.8 1.1 collective-permute-done.11.qyh_ref
  318.9 0.6 copy-done.13
  319.5 0.1 copy-done.8
  319.6 0.1 copy-done.9
  319.7 51.6 %shard_map.108 = (f32[128,64,256]{2,1,0:T(8,128)}, f32[128,256]{1,0:T(8,128)}, f32[128,256]{1,0:T(8,128)}, f32[128,64]{1,0:T(8,128)}, f32[128,64]{1,0:T(8,128)}) custom-call(s32[4]{0:T(128)} %add_convert_fusion.inside_ref, bf16[128,64,256]{2,1,0:T(8,128)(2,1)} %bitcast.4.block_ref.lpm_ref.lpb_ref.lpa_ref, ...), custom_call_target="tpu_custom_call" | custom-call | tf_op jit(solution)/shard_map/pallas_call | solution.py:211
  371.3 4.8 %copy.15 = bf16[128,64,256]{2,1,0:T(8,128)(2,1)} copy(bf16[128,64,256]{2,1,0:T(8,128)(2,1)} %bitcast.4.block_ref.lpm_ref.lpb_ref.lpa_ref) | data formatting | bytes 8388608
  (49 shorter events, 0.3 us)
Async XLA Ops:
  0.6 13.5 %copy-start = (bf16[128,128]{1,0:T(8,128)(2,1)S(1)}, bf16[128,128]{1,0:T(8,128)(2,1)}, u32[]{:S(2)}) copy-start(bf16[128,128]{1,0:T(8,128)(2,1)} %param.10) | copy-start | bytes 98308
  128.9 95.1 %all-to-all-start.1 = ((bf16[16,8,64,256]{3,2,1,0:T(8,128)(2,1)}), bf16[16,8,64,256]{3,2,1,0:T(8,128)(2,1)}, u32[]{:S(2)}, u32[]{:S(2)}) async-start(bf16[16,8,64,256]{3,2,1,0:T(8,128)(2,1)} %shard_map.104), calls=%async_computation.1 | async-start | bytes 8388608 | tf_op jit(solution)/shard_map/all_to_all | solution.py:270
  133.7 22.4 %copy-start.14 = (s32[256]{0:T(256)S(1)}, s32[256]{0:T(256)}, u32[]{:S(2)}) copy-start(s32[256]{0:T(256)} %param.14) | copy-start | bytes 3076
  133.7 22.4 %copy-start.16 = (f32[256]{0:T(256)S(1)}, f32[256]{0:T(256)}, u32[]{:S(2)}) copy-start(f32[256]{0:T(256)} %param.17) | copy-start | bytes 3076
  133.7 22.4 %copy-start.17 = (s32[256]{0:T(256)S(1)}, s32[256]{0:T(256)}, u32[]{:S(2)}) copy-start(s32[256]{0:T(256)} %param.15) | copy-start | bytes 3076
  133.7 22.4 %copy-start.15 = (s32[256]{0:T(256)S(1)}, s32[256]{0:T(256)}, u32[]{:S(2)}) copy-start(s32[256]{0:T(256)} %param.16) | copy-start | bytes 3076
  145.5 106.0 %collective-permute-start.4 = (f32[128,256]{1,0:T(8,128)}, f32[128,256]{1,0:T(8,128)S(1)}, u32[]{:S(2)}, u32[]{:S(2)}) collective-permute-start(f32[128,256]{1,0:T(8,128)} %get-tuple-element.20), channel_id=1, source_target_pairs={{0,2},{2,4},{4,6},{6,8},{8,10},{10,12},{12,14},{1,3},{3,5},{5,7},{... | collective-permute-start | bytes 393224 | tf_op jit(solution)/shard_map/ppermute | solution.py:32
  148.6 106.8 %collective-permute-start.5 = (f32[128,256]{1,0:T(8,128)}, f32[128,256]{1,0:T(8,128)S(1)}, u32[]{:S(2)}, u32[]{:S(2)}) collective-permute-start(f32[128,256]{1,0:T(8,128)} %get-tuple-element.21), channel_id=1, source_target_pairs={{2,0},{4,2},{6,4},{8,6},{10,8},{12,10},{14,12},{3,1},{5,3},{7,5},{... | collective-permute-start | bytes 393224 | tf_op jit(solution)/shard_map/ppermute | solution.py:33
  151.7 89.8 %collective-permute-start.6 = (f32[128,64]{1,0:T(8,128)}, f32[128,64]{1,0:T(8,128)S(1)}, u32[]{:S(2)}, u32[]{:S(2)}) collective-permute-start(f32[128,64]{1,0:T(8,128)} %get-tuple-element.22), channel_id=1, source_target_pairs={{0,1},{2,3},{4,5},{6,7},{8,9},{10,11},{12,13},{14,15},{16,17},{18,... | collective-permute-start | bytes 98312 | tf_op jit(solution)/shard_map/ppermute | solution.py:34
  153.0 97.2 %collective-permute-start.7 = (f32[128,64]{1,0:T(8,128)}, f32[128,64]{1,0:T(8,128)S(1)}, u32[]{:S(2)}, u32[]{:S(2)}) collective-permute-start(f32[128,64]{1,0:T(8,128)} %get-tuple-element.23), channel_id=1, source_target_pairs={{1,0},{3,2},{5,4},{7,6},{9,8},{11,10},{13,12},{15,14},{17,16},{19,... | collective-permute-start | bytes 98312 | tf_op jit(solution)/shard_map/ppermute | solution.py:35
  235.8 19.6 %collective-permute-start = (f32[128,256]{1,0:T(8,128)}, f32[128,256]{1,0:T(8,128)S(1)}, u32[]{:S(2)}, u32[]{:S(2)}) collective-permute-start(f32[128,256]{1,0:T(8,128)} %get-tuple-element.16), channel_id=1, source_target_pairs={{0,2},{2,4},{4,6},{6,8},{8,10},{10,12},{12,14},{1,3},{3,5},{5,7},{... | collective-permute-start | bytes 393224 | tf_op jit(solution)/shard_map/ppermute | solution.py:32
  241.5 8.7 %copy-start.10 = (f32[128,64]{1,0:T(8,128)}, f32[128,64]{1,0:T(8,128)S(1)}, u32[]{:S(2)}) copy-start(f32[128,64]{1,0:T(8,128)S(1)} %collective-permute-done.6.qyl_ref) | copy-start | bytes 98308
  241.5 14.0 %collective-permute-start.1 = (f32[128,256]{1,0:T(8,128)}, f32[128,256]{1,0:T(8,128)S(1)}, u32[]{:S(2)}, u32[]{:S(2)}) collective-permute-start(f32[128,256]{1,0:T(8,128)} %get-tuple-element.17), channel_id=1, source_target_pairs={{2,0},{4,2},{6,4},{8,6},{10,8},{12,10},{14,12},{3,1},{5,3},{7,5},{... | collective-permute-start | bytes 393224 | tf_op jit(solution)/shard_map/ppermute | solution.py:33
  243.4 6.8 %copy-start.19 = (f32[128,64]{1,0:T(8,128)S(1)}, f32[128,64]{1,0:T(8,128)}, u32[]{:S(2)}) copy-start(f32[128,64]{1,0:T(8,128)} %get-tuple-element.18) | copy-start | bytes 98308
  243.4 8.1 %copy-start.18 = (f32[128,64]{1,0:T(8,128)S(1)}, f32[128,64]{1,0:T(8,128)}, u32[]{:S(2)}) copy-start(f32[128,64]{1,0:T(8,128)} %get-tuple-element.19) | copy-start | bytes 98308
  250.2 5.3 %copy-start.11 = (f32[128,64]{1,0:T(8,128)}, f32[128,64]{1,0:T(8,128)S(1)}, u32[]{:S(2)}) copy-start(f32[128,64]{1,0:T(8,128)S(1)} %collective-permute-done.7.qyh_ref) | copy-start | bytes 98308
  250.2 5.2 %collective-permute-start.2 = (f32[128,64]{1,0:T(8,128)S(1)}, f32[128,64]{1,0:T(8,128)S(1)}, u32[]{:S(2)}, u32[]{:S(2)}) collective-permute-start(f32[128,64]{1,0:T(8,128)S(1)} %copy-done.19), channel_id=1, source_target_pairs={{0,1},{2,3},{4,5},{6,7},{8,9},{10,11},{12,13},{14,15},{16,17},{18,... | collective-permute-start | bytes 98312 | tf_op jit(solution)/shard_map/ppermute | solution.py:34
  251.5 4.0 %copy-start.6 = (f32[128,256]{1,0:T(8,128)}, f32[128,256]{1,0:T(8,128)S(1)}, u32[]{:S(2)}) copy-start(f32[128,256]{1,0:T(8,128)S(1)} %collective-permute-done.4.qxl_ref) | copy-start | bytes 393220
  251.5 3.9 %collective-permute-start.3 = (f32[128,64]{1,0:T(8,128)S(1)}, f32[128,64]{1,0:T(8,128)S(1)}, u32[]{:S(2)}, u32[]{:S(2)}) collective-permute-start(f32[128,64]{1,0:T(8,128)S(1)} %copy-done.18), channel_id=1, source_target_pairs={{1,0},{3,2},{5,4},{7,6},{9,8},{11,10},{13,12},{15,14},{17,16},{19,... | collective-permute-start | bytes 98312 | tf_op jit(solution)/shard_map/ppermute | solution.py:35
  255.4 0.7 copy-start.7
  255.4 0.7 copy-start.4
  255.4 0.7 copy-start.5
  255.5 0.7 copy-start.2
  255.5 0.7 copy-start.3
  307.3 11.6 %collective-permute-start.8 = (f32[128,256]{1,0:T(8,128)}, f32[128,256]{1,0:T(8,128)S(1)}, u32[]{:S(2)}, u32[]{:S(2)}) collective-permute-start(f32[128,256]{1,0:T(8,128)} %get-tuple-element.25), channel_id=1, source_target_pairs={{0,2},{2,4},{4,6},{6,8},{8,10},{10,12},{12,14},{1,3},{3,5},{5,7},{... | collective-permute-start | bytes 393224 | tf_op jit(solution)/shard_map/ppermute | solution.py:32
  310.6 8.3 %collective-permute-start.9 = (f32[128,256]{1,0:T(8,128)}, f32[128,256]{1,0:T(8,128)S(1)}, u32[]{:S(2)}, u32[]{:S(2)}) collective-permute-start(f32[128,256]{1,0:T(8,128)} %get-tuple-element.26), channel_id=1, source_target_pairs={{2,0},{4,2},{6,4},{8,6},{10,8},{12,10},{14,12},{3,1},{5,3},{7,5},{... | collective-permute-start | bytes 393224 | tf_op jit(solution)/shard_map/ppermute | solution.py:33
  313.5 4.3 %collective-permute-start.10 = (f32[128,64]{1,0:T(8,128)}, f32[128,64]{1,0:T(8,128)S(1)}, u32[]{:S(2)}, u32[]{:S(2)}) collective-permute-start(f32[128,64]{1,0:T(8,128)} %get-tuple-element.27), channel_id=1, source_target_pairs={{0,1},{2,3},{4,5},{6,7},{8,9},{10,11},{12,13},{14,15},{16,17},{18,... | collective-permute-start | bytes 98312 | tf_op jit(solution)/shard_map/ppermute | solution.py:34
  314.8 4.1 %collective-permute-start.11 = (f32[128,64]{1,0:T(8,128)}, f32[128,64]{1,0:T(8,128)S(1)}, u32[]{:S(2)}, u32[]{:S(2)}) collective-permute-start(f32[128,64]{1,0:T(8,128)} %get-tuple-element.28), channel_id=1, source_target_pairs={{1,0},{3,2},{5,4},{7,6},{9,8},{11,10},{13,12},{15,14},{17,16},{19,... | collective-permute-start | bytes 98312 | tf_op jit(solution)/shard_map/ppermute | solution.py:35
  317.8 1.1 copy-start.12
  318.9 0.7 copy-start.8
  318.9 0.7 copy-start.9
  371.3 4.8 %copy-start.1 = (bf16[128,128]{1,0:T(8,128)(2,1)S(1)}, bf16[128,128]{1,0:T(8,128)(2,1)}, u32[]{:S(2)}) copy-start(bf16[128,128]{1,0:T(8,128)(2,1)} %param.10) | copy-start | bytes 98308
  (1 other events, 0.6 us)

commit v6 on v4

--- a/solution.py
+++ b/solution.py
@@ -13,6 +13,7 @@
 STEP_SIZE = 0.03
 CAP_LOG = 1.5
 CHUNK_Z = 8
+EDGE_Z = 32
 
 
 def permeability(values):
@@ -79,30 +80,39 @@
     return result[0], result[1]
 
 
-def edge_kernel(block_ref, xl_ref, xh_ref, yl_ref, yh_ref):
-    block = block_ref[...].astype(jnp.float32)
+def edge_kernel(block_ref, xl_ref, xh_ref, yl_ref, yh_ref, *copy_ref):
+    block = block_ref[...]
+    if copy_ref:
+        copy_ref[0][...] = block
+    block = block.astype(jnp.float32)
     store_x_rows(xl_ref, block[:, :1, :])
     store_x_rows(xh_ref, block[:, -1:, :])
     yl_ref[...], yh_ref[...] = to_rows(block)
 
 
-def block_edges(block):
+def block_edges(block, keep=False):
     depth, nx, ny = block.shape
-    tz = CHUNK_Z
+    tz = EDGE_Z
     f32 = jnp.float32
+    whole = pl.BlockSpec((tz, nx, ny), lambda c: (c, 0, 0))
     row = pl.BlockSpec((tz, ny), lambda c: (c, 0))
     col = pl.BlockSpec((tz, nx), lambda c: (c, 0))
+    out_shape = [
+        jax.ShapeDtypeStruct((depth, ny), f32),
+        jax.ShapeDtypeStruct((depth, ny), f32),
+        jax.ShapeDtypeStruct((depth, nx), f32),
+        jax.ShapeDtypeStruct((depth, nx), f32),
+    ]
+    out_specs = [row, row, col, col]
+    if keep:
+        out_shape.append(jax.ShapeDtypeStruct(block.shape, block.dtype))
+        out_specs.append(whole)
     return pl.pallas_call(
         edge_kernel,
-        out_shape=(
-            jax.ShapeDtypeStruct((depth, ny), f32),
-            jax.ShapeDtypeStruct((depth, ny), f32),
-            jax.ShapeDtypeStruct((depth, nx), f32),
-            jax.ShapeDtypeStruct((depth, nx), f32),
-        ),
+        out_shape=tuple(out_shape),
         grid=(depth // tz,),
-        in_specs=[pl.BlockSpec((tz, nx, ny), lambda c: (c, 0, 0))],
-        out_specs=[row, row, col, col],
+        in_specs=[whole],
+        out_specs=out_specs,
         compiler_params=pltpu.CompilerParams(dimension_semantics=("arbitrary",)),
     )(block)
 
@@ -271,9 +281,11 @@
     inside = jnp.stack(
         [wide_at > 0, wide_at < last_w, narrow_at > 0, narrow_at < last_n]
     ).astype(jnp.int32)
-    perm_halos = halos(block_edges(log_perm))
+    edges = block_edges(pressure_start)
+    flow, edges = lax.optimization_barrier((flow, edges))
+    *lp_edges, log_perm = block_edges(log_perm, keep=True)
+    perm_halos = halos(lp_edges)
     pressure = pressure_start
-    edges = block_edges(pressure_start)
     for step in range(STEPS):
         pressure, edges = advance(inside, log_perm, perm_halos, pressure, halos(edges), flow)
     return (log_perm, pressure)

time: 353 us -> 335 us (0.949)
  Pallas kernels: 110 us -> 97.1 us
  local copies, waits for them, and re-layouts: 22.1 us -> 17.3 us
    pallas_call x2, Pallas kernels: 23.6 us -> 10.9 us  [block_edges(): pl.pallas_call(edge_kernel, out_shape=tuple(out_shape), grid=(depth // tz...]
    unnamed x42 -> x45, local copies, waits for them, and re-layouts: 13.4 us -> 8.54 us
  transfers between devices with their start and end apart: 13 -> 13, of which waited for: 2 -> 3; matrix products, arithmetic and copies ran while one was open for 2% -> 2% of each run, Pallas kernels for 7% -> 3%
where the time goes in v6:
time: 335 us; the launch traced here: 333 us
  blocking collectives  99.3 us (30%)
  Pallas kernels  97.1 us (29%)
  waiting for transfers between devices  69.4 us (21%)
  starting transfers between devices  37.9 us (11%)
  local copies, waits for them, and re-layouts  17.3 us (5%)
  matrix products  10.2 us (3%)
    all_to_all x1, blocking collectives, body(): lax.all_to_all(first.reshape(groups, planes, rows_x, rows_y), ('wide', 'n...  99.3 us
    pallas_call x2, Pallas kernels, advance(): pl.pallas_call(step_kernel, out_shape=out_shape, grid=grid, in_specs=[sme...  76.6 us
    all_to_all x1, waiting for transfers between devices, body(): lax.all_to_all(outgoing, ('wide', 'narrow'), split_axis=0, concat_axis=0,...  67.8 us
    ppermute x3, starting transfers between devices, halos(): x_lo = lax.ppermute(last_x, 'wide', forward_w)  12.1 us
    pallas_call x2, Pallas kernels, block_edges(): pl.pallas_call(edge_kernel, out_shape=tuple(out_shape), grid=(depth // tz...  10.9 us
    pallas_call x1, Pallas kernels, line_transforms(): pl.pallas_call(functools.partial(line_kernel, count_w=count_w, count_n=co...  9.62 us
    ppermute x3, starting transfers between devices, halos(): y_hi = lax.ppermute(first_y, 'narrow', backward_n)  9.1 us
    unnamed x45, local copies, waits for them, and re-layouts  8.54 us
  transfers between devices with their start and end apart: 13, of which 3 were waited for; matrix products, arithmetic and copies ran while one was open for 2% of the time, Pallas kernels for 3%

profile of v6, /device:TPU:11, one launch (start us, length us, event | category | flops | bytes accessed | tf_op | source)
XLA Modules:
  0.0 332.9 jit_solution(761971684967328774)
XLA Ops:
  0.6 7.1 %copy.13 = bf16[16,8,64,256]{3,1,2,0:T(8,128)(2,1)} copy(bf16[16,8,64,256]{3,2,1,0:T(8,128)(2,1)} %bitcast.21) | data formatting | bytes 8388608
  7.7 6.4 %copy.11 = bf16[16384,128]{1,0:T(8,128)(2,1)} copy(bf16[16384,128]{0,1:T(8,128)(2,1)} %bitcast.20) | data formatting | bytes 8388608 | tf_op jit(solution)/shard_map/dot_general | solution.py:241
  14.1 3.4 %convolution_convert_fusion = bf16[128,64,256]{2,0,1:T(8,128)(2,1)S(1)} fusion(bf16[64,256,128]{2,1,0:T(8,128)(2,1)} %bitcast.18, bf16[128,128]{1,0:T(8,128)(2,1)S(1)} %copy-done), kind=kOutput, calls=%fused_computation.6 | convolution fusion | flops 538968064 | bytes 8421376 | tf_op jit(solution)/shard_map/dot_general | solution.py:241
  17.5 2.4 copy.12
  20.0 99.3 %all_to_all.10.g_ref = bf16[16,8,64,256]{3,2,1,0:T(8,128)(2,1)} all-to-all(bf16[16,8,64,256]{3,2,1,0:T(8,128)(2,1)S(1)} %bitcast.19), channel_id=1, replica_groups=mesh['member'=2,'wide'=8,'narrow'=2] {'wide','narrow'}, dimensions={0} | all-to-all | bytes 8388608 | tf_op jit(solution)/shard_map/all_to_all | solution.py:249
  119.3 9.6 %shard_map.104 = bf16[16,8,64,256]{3,2,1,0:T(8,128)(2,1)} custom-call(bf16[16,8,64,256]{3,2,1,0:T(8,128)(2,1)} %all_to_all.10.g_ref, bf16[512,512]{1,0:T(8,128)(2,1)} %rx_ref.1, bf16[512,512]{1,0:T(8,128)(2,1)} %ry_ref.1), custom_call_target="tpu_custom_call" | custom-call | tf_op jit(solution)/shard_map/pallas_call | solution.py:229
  128.9 4.8 %all-to-all-start.1 = ((bf16[16,8,64,256]{3,2,1,0:T(8,128)(2,1)}), bf16[16,8,64,256]{3,2,1,0:T(8,128)(2,1)}, u32[]{:S(2)}, u32[]{:S(2)}) async-start(bf16[16,8,64,256]{3,2,1,0:T(8,128)(2,1)} %shard_map.104), calls=%async_computation.1 | async-start | bytes 8388608 | tf_op jit(solution)/shard_map/all_to_all | solution.py:254
  133.7 4.9 %shard_map.106 = (f32[128,256]{1,0:T(8,128)}, f32[128,256]{1,0:T(8,128)}, f32[128,64]{1,0:T(8,128)}, f32[128,64]{1,0:T(8,128)}) custom-call(bf16[128,64,256]{2,1,0:T(8,128)(2,1)} %pa_ref.1), custom_call_target="tpu_custom_call" | custom-call | tf_op jit(solution)/shard_map/pallas_call | solution.py:110
  138.8 6.7 %fusion = f32[8192,256]{1,0:T(8,128)} fusion(f32[256]{0:T(256)S(1)} %get-tuple-element.42, s32[256]{0:T(256)S(1)} %multiply_add_fusion, s32[256]{0:T(256)S(1)} %get-tuple-element.43), kind=kOutput, calls=%fused_computation | convolution fusion | flops 6446710784 | bytes 8391680 | tf_op jit(solution)/shard_map/dot_general | solution.py:277
  145.5 3.1 collective-permute-start.4
  148.6 1.3 collective-permute-start.6
  149.9 3.0 collective-permute-start.7
  153.0 3.3 collective-permute-start.5
  156.2 67.8 %all-to-all-done.1 = bf16[16,8,64,256]{3,2,1,0:T(8,128)(2,1)} async-done(((bf16[16,8,64,256]{3,2,1,0:T(8,128)(2,1)}), bf16[16,8,64,256]{3,2,1,0:T(8,128)(2,1)}, u32[]{:S(2)}, u32[]{:S(2)}) %all-to-all-start.1) | async-done | bytes 4194336 | tf_op jit(solution)/shard_map/all_to_all | solution.py:254
  224.0 5.9 %shard_map.105 = (f32[128,256]{1,0:T(8,128)}, f32[128,256]{1,0:T(8,128)}, f32[128,64]{1,0:T(8,128)}, f32[128,64]{1,0:T(8,128)}, bf16[128,64,256]{2,1,0:T(8,128)(2,1)}) custom-call(bf16[128,64,256]{2,1,0:T(8,128)(2,1)} %bitcast.4.block_ref), custom_call_target="tpu_custom_call" | custom-call | tf_op jit(solution)/shard_map/pallas_call | solution.py:110
  229.9 5.7 %collective-permute-start = (f32[128,256]{1,0:T(8,128)}, f32[128,256]{1,0:T(8,128)S(1)}, u32[]{:S(2)}, u32[]{:S(2)}) collective-permute-start(f32[128,256]{1,0:T(8,128)} %get-tuple-element.23), channel_id=1, source_target_pairs={{0,2},{2,4},{4,6},{6,8},{8,10},{10,12},{12,14},{1,3},{3,5},{5,7},{... | collective-permute-start | bytes 393224 | tf_op jit(solution)/shard_map/ppermute | solution.py:33
  235.6 1.9 collective-permute-start.1
  237.6 1.3 collective-permute-start.2
  238.9 3.0 collective-permute-start.3
  242.0 0.6 add_convert_fusion.inside_ref
  242.6 0.5 collective-permute-done.3.lyh_ref
  243.1 0.1 copy-done.7
  243.2 0.4 copy-done.5
  243.8 38.4 %shard_map.107 = (f32[128,64,256]{2,1,0:T(8,128)}, f32[128,256]{1,0:T(8,128)}, f32[128,256]{1,0:T(8,128)}, f32[128,64]{1,0:T(8,128)}, f32[128,64]{1,0:T(8,128)}) custom-call(s32[4]{0:T(128)} %add_convert_fusion.inside_ref, bf16[128,64,256]{2,1,0:T(8,128)(2,1)} %get-tuple-element.20.lpm_ref.lpb_ref.lpa_ref, ...), custom_call_target="tpu_custom_call" | custom-call | tf_op jit(solution)/shard_map/pallas_call | solution.py:195
  282.2 3.4 %collective-permute-start.8 = (f32[128,256]{1,0:T(8,128)}, f32[128,256]{1,0:T(8,128)S(1)}, u32[]{:S(2)}, u32[]{:S(2)}) collective-permute-start(f32[128,256]{1,0:T(8,128)} %get-tuple-element.37), channel_id=1, source_target_pairs={{0,2},{2,4},{4,6},{6,8},{8,10},{10,12},{12,14},{1,3},{3,5},{5,7},{... | collective-permute-start | bytes 393224 | tf_op jit(solution)/shard_map/ppermute | solution.py:33
  285.5 2.8 collective-permute-start.9
  288.4 1.3 collective-permute-start.10
  289.7 3.0 collective-permute-start.11
  292.7 1.1 collective-permute-done.11.qyh_ref
  293.8 0.6 copy-done.13
  294.4 0.1 copy-done.8
  294.5 38.2 %shard_map.108 = (f32[128,64,256]{2,1,0:T(8,128)}, f32[128,256]{1,0:T(8,128)}, f32[128,256]{1,0:T(8,128)}, f32[128,64]{1,0:T(8,128)}, f32[128,64]{1,0:T(8,128)}) custom-call(s32[4]{0:T(128)} %add_convert_fusion.inside_ref, bf16[128,64,256]{2,1,0:T(8,128)(2,1)} %get-tuple-element.20.lpm_ref.lpb_ref.lpa_ref, ...), custom_call_target="tpu_custom_call" | custom-call | tf_op jit(solution)/shard_map/pallas_call | solution.py:195
  (52 shorter events, 0.3 us)
Async XLA Ops:
  0.6 13.5 %copy-start = (bf16[128,128]{1,0:T(8,128)(2,1)S(1)}, bf16[128,128]{1,0:T(8,128)(2,1)}, u32[]{:S(2)}) copy-start(bf16[128,128]{1,0:T(8,128)(2,1)} %param.10) | copy-start | bytes 98308
  128.9 95.1 %all-to-all-start.1 = ((bf16[16,8,64,256]{3,2,1,0:T(8,128)(2,1)}), bf16[16,8,64,256]{3,2,1,0:T(8,128)(2,1)}, u32[]{:S(2)}, u32[]{:S(2)}) async-start(bf16[16,8,64,256]{3,2,1,0:T(8,128)(2,1)} %shard_map.104), calls=%async_computation.1 | async-start | bytes 8388608 | tf_op jit(solution)/shard_map/all_to_all | solution.py:254
  133.7 5.0 %copy-start.14 = (s32[256]{0:T(256)S(1)}, s32[256]{0:T(256)}, u32[]{:S(2)}) copy-start(s32[256]{0:T(256)} %param.14) | copy-start | bytes 3076
  133.7 5.0 %copy-start.15 = (s32[256]{0:T(256)S(1)}, s32[256]{0:T(256)}, u32[]{:S(2)}) copy-start(s32[256]{0:T(256)} %param.16) | copy-start | bytes 3076
  133.7 5.0 %copy-start.16 = (f32[256]{0:T(256)S(1)}, f32[256]{0:T(256)}, u32[]{:S(2)}) copy-start(f32[256]{0:T(256)} %param.17) | copy-start | bytes 3076
  133.7 5.0 %copy-start.17 = (s32[256]{0:T(256)S(1)}, s32[256]{0:T(256)}, u32[]{:S(2)}) copy-start(s32[256]{0:T(256)} %param.15) | copy-start | bytes 3076
  138.7 6.8 %copy-start.19 = (f32[128,256]{1,0:T(8,128)S(1)}, f32[128,256]{1,0:T(8,128)}, u32[]{:S(2)}) copy-start(f32[128,256]{1,0:T(8,128)} %get-tuple-element.31) | copy-start | bytes 393220
  138.7 9.9 %copy-start.21 = (f32[128,64]{1,0:T(8,128)S(1)}, f32[128,64]{1,0:T(8,128)}, u32[]{:S(2)}) copy-start(f32[128,64]{1,0:T(8,128)} %get-tuple-element.33) | copy-start | bytes 98308
  138.7 11.2 %copy-start.20 = (f32[128,64]{1,0:T(8,128)S(1)}, f32[128,64]{1,0:T(8,128)}, u32[]{:S(2)}) copy-start(f32[128,64]{1,0:T(8,128)} %get-tuple-element.34) | copy-start | bytes 98308
  138.7 14.2 %copy-start.18 = (f32[128,256]{1,0:T(8,128)S(1)}, f32[128,256]{1,0:T(8,128)}, u32[]{:S(2)}) copy-start(f32[128,256]{1,0:T(8,128)} %get-tuple-element.32) | copy-start | bytes 393220
  145.5 93.4 %collective-permute-start.4 = (f32[128,256]{1,0:T(8,128)S(1)}, f32[128,256]{1,0:T(8,128)S(1)}, u32[]{:S(2)}, u32[]{:S(2)}) collective-permute-start(f32[128,256]{1,0:T(8,128)S(1)} %copy-done.19), channel_id=1, source_target_pairs={{0,2},{2,4},{4,6},{6,8},{8,10},{10,12},{12,14},{1,3},{3,5},{5,7},{... | collective-permute-start | bytes 393224 | tf_op jit(solution)/shard_map/ppermute | solution.py:33
  148.6 87.0 %collective-permute-start.6 = (f32[128,64]{1,0:T(8,128)S(1)}, f32[128,64]{1,0:T(8,128)S(1)}, u32[]{:S(2)}, u32[]{:S(2)}) collective-permute-start(f32[128,64]{1,0:T(8,128)S(1)} %copy-done.21), channel_id=1, source_target_pairs={{0,1},{2,3},{4,5},{6,7},{8,9},{10,11},{12,13},{14,15},{16,17},{18,... | collective-permute-start | bytes 98312 | tf_op jit(solution)/shard_map/ppermute | solution.py:35
  149.9 87.7 %collective-permute-start.7 = (f32[128,64]{1,0:T(8,128)S(1)}, f32[128,64]{1,0:T(8,128)S(1)}, u32[]{:S(2)}, u32[]{:S(2)}) collective-permute-start(f32[128,64]{1,0:T(8,128)S(1)} %copy-done.20), channel_id=1, source_target_pairs={{1,0},{3,2},{5,4},{7,6},{9,8},{11,10},{13,12},{15,14},{17,16},{19,... | collective-permute-start | bytes 98312 | tf_op jit(solution)/shard_map/ppermute | solution.py:36
  153.0 89.6 %collective-permute-start.5 = (f32[128,256]{1,0:T(8,128)S(1)}, f32[128,256]{1,0:T(8,128)S(1)}, u32[]{:S(2)}, u32[]{:S(2)}) collective-permute-start(f32[128,256]{1,0:T(8,128)S(1)} %copy-done.18), channel_id=1, source_target_pairs={{2,0},{4,2},{6,4},{8,6},{10,8},{12,10},{14,12},{3,1},{5,3},{7,5},{... | collective-permute-start | bytes 393224 | tf_op jit(solution)/shard_map/ppermute | solution.py:34
  229.9 13.1 %collective-permute-start = (f32[128,256]{1,0:T(8,128)}, f32[128,256]{1,0:T(8,128)S(1)}, u32[]{:S(2)}, u32[]{:S(2)}) collective-permute-start(f32[128,256]{1,0:T(8,128)} %get-tuple-element.23), channel_id=1, source_target_pairs={{0,2},{2,4},{4,6},{6,8},{8,10},{10,12},{12,14},{1,3},{3,5},{5,7},{... | collective-permute-start | bytes 393224 | tf_op jit(solution)/shard_map/ppermute | solution.py:33
  235.6 7.4 %copy-start.10 = (f32[128,64]{1,0:T(8,128)}, f32[128,64]{1,0:T(8,128)S(1)}, u32[]{:S(2)}) copy-start(f32[128,64]{1,0:T(8,128)S(1)} %collective-permute-done.6.qyl_ref) | copy-start | bytes 98308
  235.6 7.4 %collective-permute-start.1 = (f32[128,256]{1,0:T(8,128)}, f32[128,256]{1,0:T(8,128)S(1)}, u32[]{:S(2)}, u32[]{:S(2)}) collective-permute-start(f32[128,256]{1,0:T(8,128)} %get-tuple-element.24), channel_id=1, source_target_pairs={{2,0},{4,2},{6,4},{8,6},{10,8},{12,10},{14,12},{3,1},{5,3},{7,5},{... | collective-permute-start | bytes 393224 | tf_op jit(solution)/shard_map/ppermute | solution.py:34
  237.6 5.5 %copy-start.11 = (f32[128,64]{1,0:T(8,128)}, f32[128,64]{1,0:T(8,128)S(1)}, u32[]{:S(2)}) copy-start(f32[128,64]{1,0:T(8,128)S(1)} %collective-permute-done.7.qyh_ref) | copy-start | bytes 98308
  237.6 5.0 %collective-permute-start.2 = (f32[128,64]{1,0:T(8,128)}, f32[128,64]{1,0:T(8,128)S(1)}, u32[]{:S(2)}, u32[]{:S(2)}) collective-permute-start(f32[128,64]{1,0:T(8,128)} %get-tuple-element.25), channel_id=1, source_target_pairs={{0,1},{2,3},{4,5},{6,7},{8,9},{10,11},{12,13},{14,15},{16,17},{18,... | collective-permute-start | bytes 98312 | tf_op jit(solution)/shard_map/ppermute | solution.py:35
  238.9 4.2 %copy-start.6 = (f32[128,256]{1,0:T(8,128)}, f32[128,256]{1,0:T(8,128)S(1)}, u32[]{:S(2)}) copy-start(f32[128,256]{1,0:T(8,128)S(1)} %collective-permute-done.4.qxl_ref) | copy-start | bytes 393220
  238.9 4.1 %collective-permute-start.3 = (f32[128,64]{1,0:T(8,128)}, f32[128,64]{1,0:T(8,128)S(1)}, u32[]{:S(2)}, u32[]{:S(2)}) collective-permute-start(f32[128,64]{1,0:T(8,128)} %get-tuple-element.26), channel_id=1, source_target_pairs={{1,0},{3,2},{5,4},{7,6},{9,8},{11,10},{13,12},{15,14},{17,16},{19,... | collective-permute-start | bytes 98312 | tf_op jit(solution)/shard_map/ppermute | solution.py:36
  242.6 0.7 copy-start.4
  243.1 0.7 copy-start.2
  243.1 0.7 copy-start.3
  282.2 11.6 %collective-permute-start.8 = (f32[128,256]{1,0:T(8,128)}, f32[128,256]{1,0:T(8,128)S(1)}, u32[]{:S(2)}, u32[]{:S(2)}) collective-permute-start(f32[128,256]{1,0:T(8,128)} %get-tuple-element.37), channel_id=1, source_target_pairs={{0,2},{2,4},{4,6},{6,8},{8,10},{10,12},{12,14},{1,3},{3,5},{5,7},{... | collective-permute-start | bytes 393224 | tf_op jit(solution)/shard_map/ppermute | solution.py:33
  285.5 8.3 %collective-permute-start.9 = (f32[128,256]{1,0:T(8,128)}, f32[128,256]{1,0:T(8,128)S(1)}, u32[]{:S(2)}, u32[]{:S(2)}) collective-permute-start(f32[128,256]{1,0:T(8,128)} %get-tuple-element.38), channel_id=1, source_target_pairs={{2,0},{4,2},{6,4},{8,6},{10,8},{12,10},{14,12},{3,1},{5,3},{7,5},{... | collective-permute-start | bytes 393224 | tf_op jit(solution)/shard_map/ppermute | solution.py:34
  288.4 4.3 %collective-permute-start.10 = (f32[128,64]{1,0:T(8,128)}, f32[128,64]{1,0:T(8,128)S(1)}, u32[]{:S(2)}, u32[]{:S(2)}) collective-permute-start(f32[128,64]{1,0:T(8,128)} %get-tuple-element.39), channel_id=1, source_target_pairs={{0,1},{2,3},{4,5},{6,7},{8,9},{10,11},{12,13},{14,15},{16,17},{18,... | collective-permute-start | bytes 98312 | tf_op jit(solution)/shard_map/ppermute | solution.py:35
  289.7 4.1 %collective-permute-start.11 = (f32[128,64]{1,0:T(8,128)}, f32[128,64]{1,0:T(8,128)S(1)}, u32[]{:S(2)}, u32[]{:S(2)}) collective-permute-start(f32[128,64]{1,0:T(8,128)} %get-tuple-element.40), channel_id=1, source_target_pairs={{1,0},{3,2},{5,4},{7,6},{9,8},{11,10},{13,12},{15,14},{17,16},{19,... | collective-permute-start | bytes 98312 | tf_op jit(solution)/shard_map/ppermute | solution.py:36
  292.7 1.1 copy-start.12
  293.8 0.7 copy-start.8
  293.8 0.7 copy-start.9
  294.5 38.2 %copy-start.1 = (bf16[128,128]{1,0:T(8,128)(2,1)S(1)}, bf16[128,128]{1,0:T(8,128)(2,1)}, u32[]{:S(2)}) copy-start(bf16[128,128]{1,0:T(8,128)(2,1)} %param.10) | copy-start | bytes 98308
  (3 other events, 1.9 us)

commit v7 on v6

--- a/solution.py
+++ b/solution.py
@@ -14,6 +14,7 @@
 CAP_LOG = 1.5
 CHUNK_Z = 8
 EDGE_Z = 32
+DEPTH_X = 16
 
 
 def permeability(values):
@@ -203,6 +204,28 @@
     return new, (x_lo, x_hi, y_lo, y_hi)
 
 
+def depth_kernel(rz_ref, n_ref, o_ref):
+    rz = rz_ref[...]
+    for i in range(n_ref.shape[1]):
+        o_ref[:, i, :] = jnp.dot(rz, n_ref[:, i, :], preferred_element_type=jnp.float32).astype(
+            jnp.bfloat16
+        )
+
+
+def depth_transform(root_z, noise):
+    depth, nx, ny = noise.shape
+    bx = min(nx, DEPTH_X)
+    block = pl.BlockSpec((depth, bx, ny), lambda i: (0, i, 0))
+    return pl.pallas_call(
+        depth_kernel,
+        out_shape=jax.ShapeDtypeStruct(noise.shape, jnp.bfloat16),
+        grid=(nx // bx,),
+        in_specs=[pl.BlockSpec(root_z.shape, lambda i: (0, 0)), block],
+        out_specs=block,
+        compiler_params=pltpu.CompilerParams(dimension_semantics=("arbitrary",)),
+    )(root_z, noise)
+
+
 def line_kernel(g_ref, rx_ref, ry_ref, o_ref, *, count_w, count_n):
     f32 = jnp.float32
     nx = g_ref.shape[2]
@@ -238,10 +261,7 @@
 
 def body(noise, root_z, root_x, root_y, pressure_start, well_x, well_y, well_z, well_rate):
     depth, rows_x, rows_y = noise.shape
-    first = jnp.dot(
-        root_z, noise.reshape(depth, rows_x * rows_y), preferred_element_type=jnp.float32
-    )
-    first = first.reshape(depth, rows_x, rows_y).astype(jnp.bfloat16)
+    first = depth_transform(root_z, noise)
     count_w = lax.axis_size("wide")
     count_n = lax.axis_size("narrow")
     groups = count_w * count_n

time: 335 us -> 329 us (0.982)
  local copies, waits for them, and re-layouts: 17.3 us -> 1.41 us
  Pallas kernels: 97.1 us -> 111 us
  matrix products: 10.2 us -> 6.73 us
    pallas_call x0 -> x1, Pallas kernels: none -> 13.6 us  [depth_transform(): pl.pallas_call(depth_kernel, out_shape=jax.ShapeDtypeStruct(noise.shape,...]
    unnamed x45 -> x40, local copies, waits for them, and re-layouts: 8.54 us -> 1.41 us
    dot_general x1 -> x0, local copies, waits for them, and re-layouts: 6.35 us -> none  [body(): jnp.dot(root_z, noise.reshape(depth, rows_x * rows_y), preferred_element_...]
    dot_general x1 -> x0, matrix products: 3.44 us -> none  [body(): jnp.dot(root_z, noise.reshape(depth, rows_x * rows_y), preferred_element_...]
where the time goes in v7:
time: 329 us; the launch traced here: 327 us
  Pallas kernels  111 us (34%)
  blocking collectives  99.5 us (30%)
  waiting for transfers between devices  69.5 us (21%)
  starting transfers between devices  37.8 us (11%)
  matrix products  6.73 us (2%)
    all_to_all x1, blocking collectives, body(): lax.all_to_all(first.reshape(groups, planes, rows_x, rows_y), ('wide', 'n...  99.5 us
    pallas_call x2, Pallas kernels, advance(): pl.pallas_call(step_kernel, out_shape=out_shape, grid=grid, in_specs=[sme...  76.7 us
    all_to_all x1, waiting for transfers between devices, body(): lax.all_to_all(outgoing, ('wide', 'narrow'), split_axis=0, concat_axis=0,...  68 us
    pallas_call x1, Pallas kernels, depth_transform(): pl.pallas_call(depth_kernel, out_shape=jax.ShapeDtypeStruct(noise.shape,...  13.6 us
    ppermute x3, starting transfers between devices, halos(): x_lo = lax.ppermute(last_x, 'wide', forward_w)  12.1 us
    pallas_call x2, Pallas kernels, block_edges(): pl.pallas_call(edge_kernel, out_shape=tuple(out_shape), grid=(depth // tz...  10.9 us
    pallas_call x1, Pallas kernels, line_transforms(): pl.pallas_call(functools.partial(line_kernel, count_w=count_w, count_n=co...  9.62 us
    ppermute x3, starting transfers between devices, halos(): y_hi = lax.ppermute(first_y, 'narrow', backward_n)  9.1 us
  transfers between devices with their start and end apart: 13, of which 3 were waited for; matrix products, arithmetic and copies ran while one was open for 2% of the time, Pallas kernels for 3%

profile of v7, /device:TPU:11, one launch (start us, length us, event | category | flops | bytes accessed | tf_op | source)
XLA Modules:
  0.0 327.4 jit_solution(5381724682573422775)
XLA Ops:
  0.6 13.6 %shard_map.104 = bf16[128,64,256]{2,1,0:T(8,128)(2,1)} custom-call(bf16[128,128]{1,0:T(8,128)(2,1)} %rz_ref.1, bf16[128,64,256]{2,1,0:T(8,128)(2,1)} %n_ref.1), custom_call_target="tpu_custom_call" | custom-call | tf_op jit(solution)/shard_map/pallas_call | solution.py:219
  14.2 99.5 %all_to_all.10.g_ref = bf16[16,8,64,256]{3,2,1,0:T(8,128)(2,1)} all-to-all(bf16[16,8,64,256]{3,2,1,0:T(8,128)(2,1)} %bitcast.9), channel_id=1, replica_groups=mesh['member'=2,'wide'=8,'narrow'=2] {'wide','narrow'}, dimensions={0} | all-to-all | bytes 8388608 | tf_op jit(solution)/shard_map/all_to_all | solution.py:269
  113.7 9.6 %shard_map.105 = bf16[16,8,64,256]{3,2,1,0:T(8,128)(2,1)} custom-call(bf16[16,8,64,256]{3,2,1,0:T(8,128)(2,1)} %all_to_all.10.g_ref, bf16[512,512]{1,0:T(8,128)(2,1)} %rx_ref.1, bf16[512,512]{1,0:T(8,128)(2,1)} %ry_ref.1), custom_call_target="tpu_custom_call" | custom-call | tf_op jit(solution)/shard_map/pallas_call | solution.py:252
  123.4 4.9 %all-to-all-start.1 = ((bf16[16,8,64,256]{3,2,1,0:T(8,128)(2,1)}), bf16[16,8,64,256]{3,2,1,0:T(8,128)(2,1)}, u32[]{:S(2)}, u32[]{:S(2)}) async-start(bf16[16,8,64,256]{3,2,1,0:T(8,128)(2,1)} %shard_map.105), calls=%async_computation.1 | async-start | bytes 8388608 | tf_op jit(solution)/shard_map/all_to_all | solution.py:274
  128.3 4.9 %shard_map.107 = (f32[128,256]{1,0:T(8,128)}, f32[128,256]{1,0:T(8,128)}, f32[128,64]{1,0:T(8,128)}, f32[128,64]{1,0:T(8,128)}) custom-call(bf16[128,64,256]{2,1,0:T(8,128)(2,1)} %pa_ref.1), custom_call_target="tpu_custom_call" | custom-call | tf_op jit(solution)/shard_map/pallas_call | solution.py:111
  133.3 6.7 %fusion = f32[8192,256]{1,0:T(8,128)} fusion(f32[256]{0:T(256)S(1)} %get-tuple-element.42, s32[256]{0:T(256)S(1)} %multiply_add_fusion, s32[256]{0:T(256)S(1)} %get-tuple-element.43), kind=kOutput, calls=%fused_computation | convolution fusion | flops 6446710784 | bytes 8391680 | tf_op jit(solution)/shard_map/dot_general | solution.py:297
  140.0 3.1 collective-permute-start.4
  143.1 1.3 collective-permute-start.6
  144.4 3.0 collective-permute-start.7
  147.5 3.1 collective-permute-start.5
  150.6 68.0 %all-to-all-done.1 = bf16[16,8,64,256]{3,2,1,0:T(8,128)(2,1)} async-done(((bf16[16,8,64,256]{3,2,1,0:T(8,128)(2,1)}), bf16[16,8,64,256]{3,2,1,0:T(8,128)(2,1)}, u32[]{:S(2)}, u32[]{:S(2)}) %all-to-all-start.1) | async-done | bytes 4194336 | tf_op jit(solution)/shard_map/all_to_all | solution.py:274
  218.6 5.9 %shard_map.106 = (f32[128,256]{1,0:T(8,128)}, f32[128,256]{1,0:T(8,128)}, f32[128,64]{1,0:T(8,128)}, f32[128,64]{1,0:T(8,128)}, bf16[128,64,256]{2,1,0:T(8,128)(2,1)}) custom-call(bf16[128,64,256]{2,1,0:T(8,128)(2,1)} %bitcast.1.block_ref), custom_call_target="tpu_custom_call" | custom-call | tf_op jit(solution)/shard_map/pallas_call | solution.py:111
  224.6 5.7 %collective-permute-start = (f32[128,256]{1,0:T(8,128)}, f32[128,256]{1,0:T(8,128)S(1)}, u32[]{:S(2)}, u32[]{:S(2)}) collective-permute-start(f32[128,256]{1,0:T(8,128)} %get-tuple-element.23), channel_id=1, source_target_pairs={{0,2},{2,4},{4,6},{6,8},{8,10},{10,12},{12,14},{1,3},{3,5},{5,7},{... | collective-permute-start | bytes 393224 | tf_op jit(solution)/shard_map/ppermute | solution.py:34
  230.2 1.9 collective-permute-start.1
  232.2 1.3 collective-permute-start.2
  233.5 3.0 collective-permute-start.3
  236.6 0.7 add_convert_fusion.inside_ref
  237.3 0.4 collective-permute-done.3.lyh_ref
  237.7 0.2 copy-done.5
  237.9 0.0 copy-done.2
  237.9 0.4 copy-done.3
  238.3 0.1 copy-done
  238.4 38.4 %shard_map.108 = (f32[128,64,256]{2,1,0:T(8,128)}, f32[128,256]{1,0:T(8,128)}, f32[128,256]{1,0:T(8,128)}, f32[128,64]{1,0:T(8,128)}, f32[128,64]{1,0:T(8,128)}) custom-call(s32[4]{0:T(128)} %add_convert_fusion.inside_ref, bf16[128,64,256]{2,1,0:T(8,128)(2,1)} %get-tuple-element.20.lpm_ref.lpb_ref.lpa_ref, ...), custom_call_target="tpu_custom_call" | custom-call | tf_op jit(solution)/shard_map/pallas_call | solution.py:196
  276.8 3.4 %collective-permute-start.8 = (f32[128,256]{1,0:T(8,128)}, f32[128,256]{1,0:T(8,128)S(1)}, u32[]{:S(2)}, u32[]{:S(2)}) collective-permute-start(f32[128,256]{1,0:T(8,128)} %get-tuple-element.37), channel_id=1, source_target_pairs={{0,2},{2,4},{4,6},{6,8},{8,10},{10,12},{12,14},{1,3},{3,5},{5,7},{... | collective-permute-start | bytes 393224 | tf_op jit(solution)/shard_map/ppermute | solution.py:34
  280.2 2.8 collective-permute-start.9
  283.0 1.3 collective-permute-start.10
  284.3 3.0 collective-permute-start.11
  287.4 1.1 collective-permute-done.11.qyh_ref
  288.5 0.6 copy-done.11
  289.1 0.1 copy-done.6
  289.1 0.0 copy-done.7
  289.2 38.2 %shard_map.109 = (f32[128,64,256]{2,1,0:T(8,128)}, f32[128,256]{1,0:T(8,128)}, f32[128,256]{1,0:T(8,128)}, f32[128,64]{1,0:T(8,128)}, f32[128,64]{1,0:T(8,128)}) custom-call(s32[4]{0:T(128)} %add_convert_fusion.inside_ref, bf16[128,64,256]{2,1,0:T(8,128)(2,1)} %get-tuple-element.20.lpm_ref.lpb_ref.lpa_ref, ...), custom_call_target="tpu_custom_call" | custom-call | tf_op jit(solution)/shard_map/pallas_call | solution.py:196
  (45 shorter events, 0.1 us)
Async XLA Ops:
  123.3 9.9 %copy-start.12 = (s32[256]{0:T(256)S(1)}, s32[256]{0:T(256)}, u32[]{:S(2)}) copy-start(s32[256]{0:T(256)} %param.14) | copy-start | bytes 3076
  123.3 9.9 %copy-start.13 = (s32[256]{0:T(256)S(1)}, s32[256]{0:T(256)}, u32[]{:S(2)}) copy-start(s32[256]{0:T(256)} %param.16) | copy-start | bytes 3076
  123.3 9.9 %copy-start.14 = (f32[256]{0:T(256)S(1)}, f32[256]{0:T(256)}, u32[]{:S(2)}) copy-start(f32[256]{0:T(256)} %param.17) | copy-start | bytes 3076
  123.3 9.9 %copy-start.15 = (s32[256]{0:T(256)S(1)}, s32[256]{0:T(256)}, u32[]{:S(2)}) copy-start(s32[256]{0:T(256)} %param.15) | copy-start | bytes 3076
  123.4 95.3 %all-to-all-start.1 = ((bf16[16,8,64,256]{3,2,1,0:T(8,128)(2,1)}), bf16[16,8,64,256]{3,2,1,0:T(8,128)(2,1)}, u32[]{:S(2)}, u32[]{:S(2)}) async-start(bf16[16,8,64,256]{3,2,1,0:T(8,128)(2,1)} %shard_map.105), calls=%async_computation.1 | async-start | bytes 8388608 | tf_op jit(solution)/shard_map/all_to_all | solution.py:274
  133.2 6.8 %copy-start.17 = (f32[128,256]{1,0:T(8,128)S(1)}, f32[128,256]{1,0:T(8,128)}, u32[]{:S(2)}) copy-start(f32[128,256]{1,0:T(8,128)} %get-tuple-element.31) | copy-start | bytes 393220
  133.2 9.9 %copy-start.19 = (f32[128,64]{1,0:T(8,128)S(1)}, f32[128,64]{1,0:T(8,128)}, u32[]{:S(2)}) copy-start(f32[128,64]{1,0:T(8,128)} %get-tuple-element.33) | copy-start | bytes 98308
  133.2 11.2 %copy-start.18 = (f32[128,64]{1,0:T(8,128)S(1)}, f32[128,64]{1,0:T(8,128)}, u32[]{:S(2)}) copy-start(f32[128,64]{1,0:T(8,128)} %get-tuple-element.34) | copy-start | bytes 98308
  133.2 14.3 %copy-start.16 = (f32[128,256]{1,0:T(8,128)S(1)}, f32[128,256]{1,0:T(8,128)}, u32[]{:S(2)}) copy-start(f32[128,256]{1,0:T(8,128)} %get-tuple-element.32) | copy-start | bytes 393220
  140.0 93.5 %collective-permute-start.4 = (f32[128,256]{1,0:T(8,128)S(1)}, f32[128,256]{1,0:T(8,128)S(1)}, u32[]{:S(2)}, u32[]{:S(2)}) collective-permute-start(f32[128,256]{1,0:T(8,128)S(1)} %copy-done.17), channel_id=1, source_target_pairs={{0,2},{2,4},{4,6},{6,8},{8,10},{10,12},{12,14},{1,3},{3,5},{5,7},{... | collective-permute-start | bytes 393224 | tf_op jit(solution)/shard_map/ppermute | solution.py:34
  143.1 87.1 %collective-permute-start.6 = (f32[128,64]{1,0:T(8,128)S(1)}, f32[128,64]{1,0:T(8,128)S(1)}, u32[]{:S(2)}, u32[]{:S(2)}) collective-permute-start(f32[128,64]{1,0:T(8,128)S(1)} %copy-done.19), channel_id=1, source_target_pairs={{0,1},{2,3},{4,5},{6,7},{8,9},{10,11},{12,13},{14,15},{16,17},{18,... | collective-permute-start | bytes 98312 | tf_op jit(solution)/shard_map/ppermute | solution.py:36
  144.4 87.8 %collective-permute-start.7 = (f32[128,64]{1,0:T(8,128)S(1)}, f32[128,64]{1,0:T(8,128)S(1)}, u32[]{:S(2)}, u32[]{:S(2)}) collective-permute-start(f32[128,64]{1,0:T(8,128)S(1)} %copy-done.18), channel_id=1, source_target_pairs={{1,0},{3,2},{5,4},{7,6},{9,8},{11,10},{13,12},{15,14},{17,16},{19,... | collective-permute-start | bytes 98312 | tf_op jit(solution)/shard_map/ppermute | solution.py:37
  147.5 89.8 %collective-permute-start.5 = (f32[128,256]{1,0:T(8,128)S(1)}, f32[128,256]{1,0:T(8,128)S(1)}, u32[]{:S(2)}, u32[]{:S(2)}) collective-permute-start(f32[128,256]{1,0:T(8,128)S(1)} %copy-done.16), channel_id=1, source_target_pairs={{2,0},{4,2},{6,4},{8,6},{10,8},{12,10},{14,12},{3,1},{5,3},{7,5},{... | collective-permute-start | bytes 393224 | tf_op jit(solution)/shard_map/ppermute | solution.py:35
  224.6 13.1 %collective-permute-start = (f32[128,256]{1,0:T(8,128)}, f32[128,256]{1,0:T(8,128)S(1)}, u32[]{:S(2)}, u32[]{:S(2)}) collective-permute-start(f32[128,256]{1,0:T(8,128)} %get-tuple-element.23), channel_id=1, source_target_pairs={{0,2},{2,4},{4,6},{6,8},{8,10},{10,12},{12,14},{1,3},{3,5},{5,7},{... | collective-permute-start | bytes 393224 | tf_op jit(solution)/shard_map/ppermute | solution.py:34
  230.2 7.4 %copy-start.8 = (f32[128,64]{1,0:T(8,128)}, f32[128,64]{1,0:T(8,128)S(1)}, u32[]{:S(2)}) copy-start(f32[128,64]{1,0:T(8,128)S(1)} %collective-permute-done.6.qyl_ref) | copy-start | bytes 98308
  230.2 7.4 %collective-permute-start.1 = (f32[128,256]{1,0:T(8,128)}, f32[128,256]{1,0:T(8,128)S(1)}, u32[]{:S(2)}, u32[]{:S(2)}) collective-permute-start(f32[128,256]{1,0:T(8,128)} %get-tuple-element.24), channel_id=1, source_target_pairs={{2,0},{4,2},{6,4},{8,6},{10,8},{12,10},{14,12},{3,1},{5,3},{7,5},{... | collective-permute-start | bytes 393224 | tf_op jit(solution)/shard_map/ppermute | solution.py:35
  232.2 5.5 %copy-start.9 = (f32[128,64]{1,0:T(8,128)}, f32[128,64]{1,0:T(8,128)S(1)}, u32[]{:S(2)}) copy-start(f32[128,64]{1,0:T(8,128)S(1)} %collective-permute-done.7.qyh_ref) | copy-start | bytes 98308
  232.2 5.0 %collective-permute-start.2 = (f32[128,64]{1,0:T(8,128)}, f32[128,64]{1,0:T(8,128)S(1)}, u32[]{:S(2)}, u32[]{:S(2)}) collective-permute-start(f32[128,64]{1,0:T(8,128)} %get-tuple-element.25), channel_id=1, source_target_pairs={{0,1},{2,3},{4,5},{6,7},{8,9},{10,11},{12,13},{14,15},{16,17},{18,... | collective-permute-start | bytes 98312 | tf_op jit(solution)/shard_map/ppermute | solution.py:36
  233.5 4.2 %copy-start.4 = (f32[128,256]{1,0:T(8,128)}, f32[128,256]{1,0:T(8,128)S(1)}, u32[]{:S(2)}) copy-start(f32[128,256]{1,0:T(8,128)S(1)} %collective-permute-done.4.qxl_ref) | copy-start | bytes 393220
  233.5 4.1 %collective-permute-start.3 = (f32[128,64]{1,0:T(8,128)}, f32[128,64]{1,0:T(8,128)S(1)}, u32[]{:S(2)}, u32[]{:S(2)}) collective-permute-start(f32[128,64]{1,0:T(8,128)} %get-tuple-element.26), channel_id=1, source_target_pairs={{1,0},{3,2},{5,4},{7,6},{9,8},{11,10},{13,12},{15,14},{17,16},{19,... | collective-permute-start | bytes 98312 | tf_op jit(solution)/shard_map/ppermute | solution.py:37
  237.2 0.7 copy-start.5
  237.2 0.7 copy-start.2
  237.7 0.6 copy-start.3
  237.7 0.7 copy-start
  237.7 0.7 copy-start.1
  276.8 11.6 %collective-permute-start.8 = (f32[128,256]{1,0:T(8,128)}, f32[128,256]{1,0:T(8,128)S(1)}, u32[]{:S(2)}, u32[]{:S(2)}) collective-permute-start(f32[128,256]{1,0:T(8,128)} %get-tuple-element.37), channel_id=1, source_target_pairs={{0,2},{2,4},{4,6},{6,8},{8,10},{10,12},{12,14},{1,3},{3,5},{5,7},{... | collective-permute-start | bytes 393224 | tf_op jit(solution)/shard_map/ppermute | solution.py:34
  280.2 8.3 %collective-permute-start.9 = (f32[128,256]{1,0:T(8,128)}, f32[128,256]{1,0:T(8,128)S(1)}, u32[]{:S(2)}, u32[]{:S(2)}) collective-permute-start(f32[128,256]{1,0:T(8,128)} %get-tuple-element.38), channel_id=1, source_target_pairs={{2,0},{4,2},{6,4},{8,6},{10,8},{12,10},{14,12},{3,1},{5,3},{7,5},{... | collective-permute-start | bytes 393224 | tf_op jit(solution)/shard_map/ppermute | solution.py:35
  283.0 4.3 %collective-permute-start.10 = (f32[128,64]{1,0:T(8,128)}, f32[128,64]{1,0:T(8,128)S(1)}, u32[]{:S(2)}, u32[]{:S(2)}) collective-permute-start(f32[128,64]{1,0:T(8,128)} %get-tuple-element.39), channel_id=1, source_target_pairs={{0,1},{2,3},{4,5},{6,7},{8,9},{10,11},{12,13},{14,15},{16,17},{18,... | collective-permute-start | bytes 98312 | tf_op jit(solution)/shard_map/ppermute | solution.py:36
  284.3 4.1 %collective-permute-start.11 = (f32[128,64]{1,0:T(8,128)}, f32[128,64]{1,0:T(8,128)S(1)}, u32[]{:S(2)}, u32[]{:S(2)}) collective-permute-start(f32[128,64]{1,0:T(8,128)} %get-tuple-element.40), channel_id=1, source_target_pairs={{1,0},{3,2},{5,4},{7,6},{9,8},{11,10},{13,12},{15,14},{17,16},{19,... | collective-permute-start | bytes 98312 | tf_op jit(solution)/shard_map/ppermute | solution.py:37
  287.4 1.1 copy-start.10
  288.4 0.7 copy-start.6
  288.5 0.7 copy-start.7
  (1 other events, 0.6 us)

commit v8 on v7

--- a/solution.py
+++ b/solution.py
@@ -118,42 +118,13 @@
     )(block)
 
 
-def step_kernel(
-    inside_ref, lpm_ref, lpb_ref, lpa_ref, lxl_ref, lxh_ref, lyl_ref, lyh_ref,
-    pm_ref, pb_ref, pa_ref, qxl_ref, qxh_ref, qyl_ref, qyh_ref, f_ref,
-    o_ref, exl_ref, exh_ref, eyl_ref, eyh_ref,
-):
-    c = pl.program_id(0)
-    last = pl.num_programs(0) - 1
+def update(trans, pm_ref, pb_ref, pa_ref, qxl_ref, qxh_ref, qyl_ref, qyh_ref, f_ref, outs):
+    o_ref, exl_ref, exh_ref, eyl_ref, eyh_ref = outs
+    t_zp, t_zm, t_xp, t_xm, t_yp, t_ym = trans
     tz, nx, ny = pm_ref.shape
     f32 = jnp.float32
-
-    def side_perm(ref, k):
-        return jnp.where(inside_ref[k] > 0, permeability(ref[...].astype(f32)), 0.0)
-
-    kxl = jnp.where(inside_ref[0] > 0, permeability(x_rows(lxl_ref)), 0.0)
-    kxh = jnp.where(inside_ref[1] > 0, permeability(x_rows(lxh_ref)), 0.0)
-    kyl = to_columns(side_perm(lyl_ref, 2))
-    kyh = to_columns(side_perm(lyh_ref, 3))
-
-    below = jnp.where(c == 0, 0.0, permeability(lpb_ref[...].astype(f32)))
-    above = jnp.where(c == last, 0.0, permeability(lpa_ref[...].astype(f32)))
-    centre = permeability(lpm_ref[...].astype(f32))
-    ext = jnp.concatenate([below, centre, above], axis=0)
-    faces = harmonic(ext[:-1], ext[1:])
-    t_zm = faces[:-1]
-    t_zp = faces[1:]
-
     xi = lax.broadcasted_iota(jnp.int32, (tz, nx, ny), 1)
     yi = lax.broadcasted_iota(jnp.int32, (tz, nx, ny), 2)
-
-    fx = harmonic(centre, pltpu.roll(centre, nx - 1, 1))
-    t_xp = jnp.where(xi == nx - 1, harmonic(centre[:, nx - 1 :, :], kxh), fx)
-    t_xm = jnp.where(xi == 0, harmonic(centre[:, :1, :], kxl), pltpu.roll(fx, 1, 1))
-    fy = harmonic(centre, pltpu.roll(centre, ny - 1, 2))
-    t_yp = jnp.where(yi == ny - 1, harmonic(centre[:, :, ny - 1 :], kyh), fy)
-    t_ym = jnp.where(yi == 0, harmonic(centre[:, :, :1], kyl), pltpu.roll(fy, 1, 2))
-
     p = pm_ref[...].astype(f32)
     pext = jnp.concatenate([pb_ref[...].astype(f32), p, pa_ref[...].astype(f32)], axis=0)
     n_xp = jnp.where(xi == nx - 1, x_rows(qxh_ref), pltpu.roll(p, nx - 1, 1))
@@ -174,7 +145,78 @@
     eyl_ref[...], eyh_ref[...] = to_rows(new)
 
 
-def advance(inside, log_perm, perm_halos, pressure, pressure_halos, flow):
+def first_step_kernel(
+    inside_ref, lpm_ref, lpb_ref, lpa_ref, lxl_ref, lxh_ref, lyl_ref, lyh_ref,
+    pm_ref, pb_ref, pa_ref, qxl_ref, qxh_ref, qyl_ref, qyh_ref, f_ref,
+    o_ref, exl_ref, exh_ref, eyl_ref, eyh_ref, tzm_ref, txm_ref, tym_ref, txp_ref, typ_ref,
+):
+    c = pl.program_id(0)
+    last = pl.num_programs(0) - 1
+    tz, nx, ny = pm_ref.shape
+    f32 = jnp.float32
+
+    def side_perm(ref, k):
+        return jnp.where(inside_ref[k] > 0, permeability(ref[...].astype(f32)), 0.0)
+
+    kxl = jnp.where(inside_ref[0] > 0, permeability(x_rows(lxl_ref)), 0.0)
+    kxh = jnp.where(inside_ref[1] > 0, permeability(x_rows(lxh_ref)), 0.0)
+    kyl = to_columns(side_perm(lyl_ref, 2))
+    kyh = to_columns(side_perm(lyh_ref, 3))
+
+    below = jnp.where(c == 0, 0.0, permeability(lpb_ref[...].astype(f32)))
+    above = jnp.where(c == last, 0.0, permeability(lpa_ref[...].astype(f32)))
+    centre = permeability(lpm_ref[...].astype(f32))
+    ext = jnp.concatenate([below, centre, above], axis=0)
+    faces = harmonic(ext[:-1], ext[1:])
+    t_zm = faces[:-1]
+    t_zp = faces[1:]
+
+    xi = lax.broadcasted_iota(jnp.int32, (tz, nx, ny), 1)
+    yi = lax.broadcasted_iota(jnp.int32, (tz, nx, ny), 2)
+
+    fx = harmonic(centre, pltpu.roll(centre, nx - 1, 1))
+    t_xp = jnp.where(xi == nx - 1, harmonic(centre[:, nx - 1 :, :], kxh), fx)
+    t_xm = jnp.where(xi == 0, harmonic(centre[:, :1, :], kxl), pltpu.roll(fx, 1, 1))
+    fy = harmonic(centre, pltpu.roll(centre, ny - 1, 2))
+    t_yp = jnp.where(yi == ny - 1, harmonic(centre[:, :, ny - 1 :], kyh), fy)
+    t_ym = jnp.where(yi == 0, harmonic(centre[:, :, :1], kyl), pltpu.roll(fy, 1, 2))
+
+    tzm_ref[...] = t_zm
+    txm_ref[...] = t_xm
+    tym_ref[...] = t_ym
+    store_x_rows(txp_ref, t_xp[:, nx - 1 :, :])
+    typ_ref[...] = to_rows(t_yp)[1]
+    update(
+        (t_zp, t_zm, t_xp, t_xm, t_yp, t_ym),
+        pm_ref, pb_ref, pa_ref, qxl_ref, qxh_ref, qyl_ref, qyh_ref, f_ref,
+        (o_ref, exl_ref, exh_ref, eyl_ref, eyh_ref),
+    )
+
+
+def later_step_kernel(
+    tzm_ref, tza_ref, txm_ref, tym_ref, txp_ref, typ_ref,
+    pm_ref, pb_ref, pa_ref, qxl_ref, qxh_ref, qyl_ref, qyh_ref, f_ref,
+    o_ref, exl_ref, exh_ref, eyl_ref, eyh_ref,
+):
+    c = pl.program_id(0)
+    last = pl.num_programs(0) - 1
+    tz, nx, ny = pm_ref.shape
+    xi = lax.broadcasted_iota(jnp.int32, (tz, nx, ny), 1)
+    yi = lax.broadcasted_iota(jnp.int32, (tz, nx, ny), 2)
+    t_zm = tzm_ref[...]
+    t_zp = jnp.concatenate([t_zm[1:], jnp.where(c == last, 0.0, tza_ref[...])], axis=0)
+    t_xm = txm_ref[...]
+    t_xp = jnp.where(xi == nx - 1, x_rows(txp_ref), pltpu.roll(t_xm, nx - 1, 1))
+    t_ym = tym_ref[...]
+    t_yp = jnp.where(yi == ny - 1, to_columns(typ_ref[...]), pltpu.roll(t_ym, ny - 1, 2))
+    update(
+        (t_zp, t_zm, t_xp, t_xm, t_yp, t_ym),
+        pm_ref, pb_ref, pa_ref, qxl_ref, qxh_ref, qyl_ref, qyh_ref, f_ref,
+        (o_ref, exl_ref, exh_ref, eyl_ref, eyh_ref),
+    )
+
+
+def advance(stored, pressure, pressure_halos, flow, inside=None, log_perm=None, perm_halos=None):
     depth, nx, ny = pressure.shape
     tz = CHUNK_Z
     grid = (depth // tz,)
@@ -186,22 +228,34 @@
     side = [row, row, col, col]
     smem = pl.BlockSpec(memory_space=pltpu.SMEM)
     f32 = jnp.float32
-    out_shape = (
-        jax.ShapeDtypeStruct((depth, nx, ny), f32),
-        jax.ShapeDtypeStruct((depth, ny), f32),
-        jax.ShapeDtypeStruct((depth, ny), f32),
-        jax.ShapeDtypeStruct((depth, nx), f32),
-        jax.ShapeDtypeStruct((depth, nx), f32),
-    )
-    new, x_lo, x_hi, y_lo, y_hi = pl.pallas_call(
-        step_kernel,
-        out_shape=out_shape,
+    full = jax.ShapeDtypeStruct((depth, nx, ny), f32)
+    rows = jax.ShapeDtypeStruct((depth, ny), f32)
+    cols = jax.ShapeDtypeStruct((depth, nx), f32)
+    out_shape = [full, rows, rows, cols, cols]
+    out_specs = [main] + side
+    pressure_args = [pressure, pressure, pressure, *pressure_halos, flow]
+    pressure_specs = [main, below, above] + side + [main]
+    params = pltpu.CompilerParams(dimension_semantics=("arbitrary",))
+    if stored is None:
+        outs = pl.pallas_call(
+            first_step_kernel,
+            out_shape=tuple(out_shape + [full, full, full, rows, cols]),
+            grid=grid,
+            in_specs=[smem, main, below, above] + side + pressure_specs,
+            out_specs=out_specs + [main, main, main, row, col],
+            compiler_params=params,
+        )(inside, log_perm, log_perm, log_perm, *perm_halos, *pressure_args)
+        return outs[0], outs[1:5], outs[5:]
+    t_zm, t_xm, t_ym, t_xp, t_yp = stored
+    outs = pl.pallas_call(
+        later_step_kernel,
+        out_shape=tuple(out_shape),
         grid=grid,
-        in_specs=[smem, main, below, above] + side + [main, below, above] + side + [main],
-        out_specs=[main] + side,
-        compiler_params=pltpu.CompilerParams(dimension_semantics=("arbitrary",)),
-    )(inside, log_perm, log_perm, log_perm, *perm_halos, pressure, pressure, pressure, *pressure_halos, flow)
-    return new, (x_lo, x_hi, y_lo, y_hi)
+        in_specs=[main, above, main, main, row, col] + pressure_specs,
+        out_specs=out_specs,
+        compiler_params=params,
+    )(t_zm, t_zm, t_xm, t_ym, t_xp, t_yp, *pressure_args)
+    return outs[0], outs[1:5], stored
 
 
 def depth_kernel(rz_ref, n_ref, o_ref):
@@ -306,8 +360,11 @@
     *lp_edges, log_perm = block_edges(log_perm, keep=True)
     perm_halos = halos(lp_edges)
     pressure = pressure_start
+    stored = None
     for step in range(STEPS):
-        pressure, edges = advance(inside, log_perm, perm_halos, pressure, halos(edges), flow)
+        pressure, edges, stored = advance(
+            stored, pressure, halos(edges), flow, inside, log_perm, perm_halos
+        )
     return (log_perm, pressure)
 
 

time: 329 us -> 323 us (0.982)
  Pallas kernels: 111 us -> 103 us
    pallas_call x2, Pallas kernels: 76.7 us -> 69.3 us  [the longest x1 40.5 us: advance(): pl.pallas_call(first_step_kernel, out_shape=tuple(out_shape + [full, full...]
where the time goes in v8:
time: 323 us; the launch traced here: 320 us
  Pallas kernels  103 us (32%)
  blocking collectives  99.5 us (31%)
  waiting for transfers between devices  69.6 us (22%)
  starting transfers between devices  37.8 us (12%)
  matrix products  6.73 us (2%)
    all_to_all x1, blocking collectives, body(): lax.all_to_all(first.reshape(groups, planes, rows_x, rows_y), ('wide', 'n...  99.5 us
    all_to_all x1, waiting for transfers between devices, body(): lax.all_to_all(outgoing, ('wide', 'narrow'), split_axis=0, concat_axis=0,...  68 us
    pallas_call x1, Pallas kernels, advance(): pl.pallas_call(first_step_kernel, out_shape=tuple(out_shape + [full, full...  40.5 us
    pallas_call x1, Pallas kernels, advance(): pl.pallas_call(later_step_kernel, out_shape=tuple(out_shape), grid=grid,...  28.7 us
    pallas_call x1, Pallas kernels, depth_transform(): pl.pallas_call(depth_kernel, out_shape=jax.ShapeDtypeStruct(noise.shape,...  13.6 us
    ppermute x3, starting transfers between devices, halos(): x_lo = lax.ppermute(last_x, 'wide', forward_w)  12.1 us
    pallas_call x2, Pallas kernels, block_edges(): pl.pallas_call(edge_kernel, out_shape=tuple(out_shape), grid=(depth // tz...  10.9 us
    pallas_call x1, Pallas kernels, line_transforms(): pl.pallas_call(functools.partial(line_kernel, count_w=count_w, count_n=co...  9.62 us
  transfers between devices with their start and end apart: 13, of which 3 were waited for; matrix products, arithmetic and copies ran while one was open for 2% of the time, Pallas kernels for 3%

profile of v8, /device:TPU:11, one launch (start us, length us, event | category | flops | bytes accessed | tf_op | source)
XLA Modules:
  0.0 320.0 jit_solution(11521632982809793248)
XLA Ops:
  0.6 13.6 %shard_map.104 = bf16[128,64,256]{2,1,0:T(8,128)(2,1)} custom-call(bf16[128,128]{1,0:T(8,128)(2,1)} %rz_ref.1, bf16[128,64,256]{2,1,0:T(8,128)(2,1)} %n_ref.1), custom_call_target="tpu_custom_call" | custom-call | tf_op jit(solution)/shard_map/pallas_call | solution.py:273
  14.2 99.5 %all_to_all.10.g_ref = bf16[16,8,64,256]{3,2,1,0:T(8,128)(2,1)} all-to-all(bf16[16,8,64,256]{3,2,1,0:T(8,128)(2,1)} %bitcast.9), channel_id=1, replica_groups=mesh['member'=2,'wide'=8,'narrow'=2] {'wide','narrow'}, dimensions={0} | all-to-all | bytes 8388608 | tf_op jit(solution)/shard_map/all_to_all | solution.py:323
  113.7 9.6 %shard_map.105 = bf16[16,8,64,256]{3,2,1,0:T(8,128)(2,1)} custom-call(bf16[16,8,64,256]{3,2,1,0:T(8,128)(2,1)} %all_to_all.10.g_ref, bf16[512,512]{1,0:T(8,128)(2,1)} %rx_ref.1, bf16[512,512]{1,0:T(8,128)(2,1)} %ry_ref.1), custom_call_target="tpu_custom_call" | custom-call | tf_op jit(solution)/shard_map/pallas_call | solution.py:306
  123.3 4.9 %all-to-all-start.1 = ((bf16[16,8,64,256]{3,2,1,0:T(8,128)(2,1)}), bf16[16,8,64,256]{3,2,1,0:T(8,128)(2,1)}, u32[]{:S(2)}, u32[]{:S(2)}) async-start(bf16[16,8,64,256]{3,2,1,0:T(8,128)(2,1)} %shard_map.105), calls=%async_computation.1 | async-start | bytes 8388608 | tf_op jit(solution)/shard_map/all_to_all | solution.py:328
  128.3 4.9 %shard_map.107 = (f32[128,256]{1,0:T(8,128)}, f32[128,256]{1,0:T(8,128)}, f32[128,64]{1,0:T(8,128)}, f32[128,64]{1,0:T(8,128)}) custom-call(bf16[128,64,256]{2,1,0:T(8,128)(2,1)} %pa_ref.1), custom_call_target="tpu_custom_call" | custom-call | tf_op jit(solution)/shard_map/pallas_call | solution.py:111
  133.3 6.7 %fusion = f32[8192,256]{1,0:T(8,128)} fusion(f32[256]{0:T(256)S(1)} %get-tuple-element.52, s32[256]{0:T(256)S(1)} %multiply_add_fusion, s32[256]{0:T(256)S(1)} %get-tuple-element.53), kind=kOutput, calls=%fused_computation | convolution fusion | flops 6446710784 | bytes 8391680 | tf_op jit(solution)/shard_map/dot_general | solution.py:351
  140.0 3.1 collective-permute-start.4
  143.1 1.3 collective-permute-start.6
  144.4 3.0 collective-permute-start.7
  147.5 3.1 collective-permute-start.5
  150.6 68.0 %all-to-all-done.1 = bf16[16,8,64,256]{3,2,1,0:T(8,128)(2,1)} async-done(((bf16[16,8,64,256]{3,2,1,0:T(8,128)(2,1)}), bf16[16,8,64,256]{3,2,1,0:T(8,128)(2,1)}, u32[]{:S(2)}, u32[]{:S(2)}) %all-to-all-start.1) | async-done | bytes 4194336 | tf_op jit(solution)/shard_map/all_to_all | solution.py:328
  218.6 5.9 %shard_map.106 = (f32[128,256]{1,0:T(8,128)}, f32[128,256]{1,0:T(8,128)}, f32[128,64]{1,0:T(8,128)}, f32[128,64]{1,0:T(8,128)}, bf16[128,64,256]{2,1,0:T(8,128)(2,1)}) custom-call(bf16[128,64,256]{2,1,0:T(8,128)(2,1)} %bitcast.1.block_ref), custom_call_target="tpu_custom_call" | custom-call | tf_op jit(solution)/shard_map/pallas_call | solution.py:111
  224.5 5.7 %collective-permute-start = (f32[128,256]{1,0:T(8,128)}, f32[128,256]{1,0:T(8,128)S(1)}, u32[]{:S(2)}, u32[]{:S(2)}) collective-permute-start(f32[128,256]{1,0:T(8,128)} %get-tuple-element.28), channel_id=1, source_target_pairs={{0,2},{2,4},{4,6},{6,8},{8,10},{10,12},{12,14},{1,3},{3,5},{5,7},{... | collective-permute-start | bytes 393224 | tf_op jit(solution)/shard_map/ppermute | solution.py:34
  230.2 1.9 collective-permute-start.1
  232.2 1.3 collective-permute-start.2
  233.5 3.0 collective-permute-start.3
  236.5 0.6 add_convert_fusion.inside_ref
  237.2 0.5 collective-permute-done.3.lyh_ref
  237.7 0.1 copy-done.1
  237.8 0.4 copy-done.9
  238.3 0.1 copy-done.2
  238.3 0.0 copy-done.3
  238.4 40.5 %shard_map.108 = (f32[128,64,256]{2,1,0:T(8,128)}, f32[128,256]{1,0:T(8,128)}, f32[128,256]{1,0:T(8,128)}, f32[128,64]{1,0:T(8,128)}, f32[128,64]{1,0:T(8,128)},...) custom-call(s32[4]{0:T(128)} %add_convert_fusion.inside_ref, ...), custom_call_target="tpu_custom_call" | custom-call | tf_op jit(solution)/shard_map/pallas_call | solution.py:240
  278.9 3.4 %collective-permute-start.8 = (f32[128,256]{1,0:T(8,128)}, f32[128,256]{1,0:T(8,128)S(1)}, u32[]{:S(2)}, u32[]{:S(2)}) collective-permute-start(f32[128,256]{1,0:T(8,128)} %get-tuple-element.47), channel_id=1, source_target_pairs={{0,2},{2,4},{4,6},{6,8},{8,10},{10,12},{12,14},{1,3},{3,5},{5,7},{... | collective-permute-start | bytes 393224 | tf_op jit(solution)/shard_map/ppermute | solution.py:34
  282.2 2.8 collective-permute-start.9
  285.1 1.3 collective-permute-start.10
  286.4 3.0 collective-permute-start.11
  289.4 1.1 collective-permute-done.11.qyh_ref
  290.5 0.6 copy-done.11
  291.1 0.0 copy-done.4
  291.2 0.1 copy-done.5
  291.3 28.7 %shard_map.109 = (f32[128,64,256]{2,1,0:T(8,128)}, f32[128,256]{1,0:T(8,128)}, f32[128,256]{1,0:T(8,128)}, f32[128,64]{1,0:T(8,128)}, f32[128,64]{1,0:T(8,128)}) custom-call(f32[128,64,256]{2,1,0:T(8,128)} %get-tuple-element.41.tzm_ref.tza_ref, f32[128,64,256]{2,1,0:T(8,128)} %get-tuple-element.41.tzm_ref.tza_ref, ...), custom_call_target="tpu_custom_call" | custom-call | tf_op jit(solution)/shard_map/pallas_call | solution.py:250
  (45 shorter events, 0.1 us)
Async XLA Ops:
  123.3 9.9 %copy-start.12 = (s32[256]{0:T(256)S(1)}, s32[256]{0:T(256)}, u32[]{:S(2)}) copy-start(s32[256]{0:T(256)} %param.14) | copy-start | bytes 3076
  123.3 9.9 %copy-start.13 = (s32[256]{0:T(256)S(1)}, s32[256]{0:T(256)}, u32[]{:S(2)}) copy-start(s32[256]{0:T(256)} %param.16) | copy-start | bytes 3076
  123.3 9.9 %copy-start.14 = (f32[256]{0:T(256)S(1)}, f32[256]{0:T(256)}, u32[]{:S(2)}) copy-start(f32[256]{0:T(256)} %param.17) | copy-start | bytes 3076
  123.3 9.9 %copy-start.15 = (s32[256]{0:T(256)S(1)}, s32[256]{0:T(256)}, u32[]{:S(2)}) copy-start(s32[256]{0:T(256)} %param.15) | copy-start | bytes 3076
  123.3 95.3 %all-to-all-start.1 = ((bf16[16,8,64,256]{3,2,1,0:T(8,128)(2,1)}), bf16[16,8,64,256]{3,2,1,0:T(8,128)(2,1)}, u32[]{:S(2)}, u32[]{:S(2)}) async-start(bf16[16,8,64,256]{3,2,1,0:T(8,128)(2,1)} %shard_map.105), calls=%async_computation.1 | async-start | bytes 8388608 | tf_op jit(solution)/shard_map/all_to_all | solution.py:328
  133.2 6.8 %copy-start.17 = (f32[128,256]{1,0:T(8,128)S(1)}, f32[128,256]{1,0:T(8,128)}, u32[]{:S(2)}) copy-start(f32[128,256]{1,0:T(8,128)} %get-tuple-element.36) | copy-start | bytes 393220
  133.2 9.9 %copy-start.19 = (f32[128,64]{1,0:T(8,128)S(1)}, f32[128,64]{1,0:T(8,128)}, u32[]{:S(2)}) copy-start(f32[128,64]{1,0:T(8,128)} %get-tuple-element.38) | copy-start | bytes 98308
  133.2 11.2 %copy-start.18 = (f32[128,64]{1,0:T(8,128)S(1)}, f32[128,64]{1,0:T(8,128)}, u32[]{:S(2)}) copy-start(f32[128,64]{1,0:T(8,128)} %get-tuple-element.39) | copy-start | bytes 98308
  133.2 14.3 %copy-start.16 = (f32[128,256]{1,0:T(8,128)S(1)}, f32[128,256]{1,0:T(8,128)}, u32[]{:S(2)}) copy-start(f32[128,256]{1,0:T(8,128)} %get-tuple-element.37) | copy-start | bytes 393220
  140.0 93.5 %collective-permute-start.4 = (f32[128,256]{1,0:T(8,128)S(1)}, f32[128,256]{1,0:T(8,128)S(1)}, u32[]{:S(2)}, u32[]{:S(2)}) collective-permute-start(f32[128,256]{1,0:T(8,128)S(1)} %copy-done.17), channel_id=1, source_target_pairs={{0,2},{2,4},{4,6},{6,8},{8,10},{10,12},{12,14},{1,3},{3,5},{5,7},{... | collective-permute-start | bytes 393224 | tf_op jit(solution)/shard_map/ppermute | solution.py:34
  143.1 87.1 %collective-permute-start.6 = (f32[128,64]{1,0:T(8,128)S(1)}, f32[128,64]{1,0:T(8,128)S(1)}, u32[]{:S(2)}, u32[]{:S(2)}) collective-permute-start(f32[128,64]{1,0:T(8,128)S(1)} %copy-done.19), channel_id=1, source_target_pairs={{0,1},{2,3},{4,5},{6,7},{8,9},{10,11},{12,13},{14,15},{16,17},{18,... | collective-permute-start | bytes 98312 | tf_op jit(solution)/shard_map/ppermute | solution.py:36
  144.4 87.8 %collective-permute-start.7 = (f32[128,64]{1,0:T(8,128)S(1)}, f32[128,64]{1,0:T(8,128)S(1)}, u32[]{:S(2)}, u32[]{:S(2)}) collective-permute-start(f32[128,64]{1,0:T(8,128)S(1)} %copy-done.18), channel_id=1, source_target_pairs={{1,0},{3,2},{5,4},{7,6},{9,8},{11,10},{13,12},{15,14},{17,16},{19,... | collective-permute-start | bytes 98312 | tf_op jit(solution)/shard_map/ppermute | solution.py:37
  147.5 89.7 %collective-permute-start.5 = (f32[128,256]{1,0:T(8,128)S(1)}, f32[128,256]{1,0:T(8,128)S(1)}, u32[]{:S(2)}, u32[]{:S(2)}) collective-permute-start(f32[128,256]{1,0:T(8,128)S(1)} %copy-done.16), channel_id=1, source_target_pairs={{2,0},{4,2},{6,4},{8,6},{10,8},{12,10},{14,12},{3,1},{5,3},{7,5},{... | collective-permute-start | bytes 393224 | tf_op jit(solution)/shard_map/ppermute | solution.py:35
  224.5 13.1 %collective-permute-start = (f32[128,256]{1,0:T(8,128)}, f32[128,256]{1,0:T(8,128)S(1)}, u32[]{:S(2)}, u32[]{:S(2)}) collective-permute-start(f32[128,256]{1,0:T(8,128)} %get-tuple-element.28), channel_id=1, source_target_pairs={{0,2},{2,4},{4,6},{6,8},{8,10},{10,12},{12,14},{1,3},{3,5},{5,7},{... | collective-permute-start | bytes 393224 | tf_op jit(solution)/shard_map/ppermute | solution.py:34
  230.2 7.5 %copy-start.6 = (f32[128,64]{1,0:T(8,128)}, f32[128,64]{1,0:T(8,128)S(1)}, u32[]{:S(2)}) copy-start(f32[128,64]{1,0:T(8,128)S(1)} %collective-permute-done.6.qyl_ref) | copy-start | bytes 98308
  230.2 7.4 %collective-permute-start.1 = (f32[128,256]{1,0:T(8,128)}, f32[128,256]{1,0:T(8,128)S(1)}, u32[]{:S(2)}, u32[]{:S(2)}) collective-permute-start(f32[128,256]{1,0:T(8,128)} %get-tuple-element.29), channel_id=1, source_target_pairs={{2,0},{4,2},{6,4},{8,6},{10,8},{12,10},{14,12},{3,1},{5,3},{7,5},{... | collective-permute-start | bytes 393224 | tf_op jit(solution)/shard_map/ppermute | solution.py:35
  232.2 5.5 %copy-start.7 = (f32[128,64]{1,0:T(8,128)}, f32[128,64]{1,0:T(8,128)S(1)}, u32[]{:S(2)}) copy-start(f32[128,64]{1,0:T(8,128)S(1)} %collective-permute-done.7.qyh_ref) | copy-start | bytes 98308
  232.2 5.0 %collective-permute-start.2 = (f32[128,64]{1,0:T(8,128)}, f32[128,64]{1,0:T(8,128)S(1)}, u32[]{:S(2)}, u32[]{:S(2)}) collective-permute-start(f32[128,64]{1,0:T(8,128)} %get-tuple-element.30), channel_id=1, source_target_pairs={{0,1},{2,3},{4,5},{6,7},{8,9},{10,11},{12,13},{14,15},{16,17},{18,... | collective-permute-start | bytes 98312 | tf_op jit(solution)/shard_map/ppermute | solution.py:36
  233.5 4.2 %copy-start = (f32[128,256]{1,0:T(8,128)}, f32[128,256]{1,0:T(8,128)S(1)}, u32[]{:S(2)}) copy-start(f32[128,256]{1,0:T(8,128)S(1)} %collective-permute-done.4.qxl_ref) | copy-start | bytes 393220
  233.5 4.1 %collective-permute-start.3 = (f32[128,64]{1,0:T(8,128)}, f32[128,64]{1,0:T(8,128)S(1)}, u32[]{:S(2)}, u32[]{:S(2)}) collective-permute-start(f32[128,64]{1,0:T(8,128)} %get-tuple-element.31), channel_id=1, source_target_pairs={{1,0},{3,2},{5,4},{7,6},{9,8},{11,10},{13,12},{15,14},{17,16},{19,... | collective-permute-start | bytes 98312 | tf_op jit(solution)/shard_map/ppermute | solution.py:37
  237.2 0.7 copy-start.1
  237.2 0.7 copy-start.8
  237.6 0.7 copy-start.2
  237.7 0.7 copy-start.3
  278.9 11.6 %collective-permute-start.8 = (f32[128,256]{1,0:T(8,128)}, f32[128,256]{1,0:T(8,128)S(1)}, u32[]{:S(2)}, u32[]{:S(2)}) collective-permute-start(f32[128,256]{1,0:T(8,128)} %get-tuple-element.47), channel_id=1, source_target_pairs={{0,2},{2,4},{4,6},{6,8},{8,10},{10,12},{12,14},{1,3},{3,5},{5,7},{... | collective-permute-start | bytes 393224 | tf_op jit(solution)/shard_map/ppermute | solution.py:34
  282.2 8.3 %collective-permute-start.9 = (f32[128,256]{1,0:T(8,128)}, f32[128,256]{1,0:T(8,128)S(1)}, u32[]{:S(2)}, u32[]{:S(2)}) collective-permute-start(f32[128,256]{1,0:T(8,128)} %get-tuple-element.48), channel_id=1, source_target_pairs={{2,0},{4,2},{6,4},{8,6},{10,8},{12,10},{14,12},{3,1},{5,3},{7,5},{... | collective-permute-start | bytes 393224 | tf_op jit(solution)/shard_map/ppermute | solution.py:35
  285.1 4.3 %collective-permute-start.10 = (f32[128,64]{1,0:T(8,128)}, f32[128,64]{1,0:T(8,128)S(1)}, u32[]{:S(2)}, u32[]{:S(2)}) collective-permute-start(f32[128,64]{1,0:T(8,128)} %get-tuple-element.49), channel_id=1, source_target_pairs={{0,1},{2,3},{4,5},{6,7},{8,9},{10,11},{12,13},{14,15},{16,17},{18,... | collective-permute-start | bytes 98312 | tf_op jit(solution)/shard_map/ppermute | solution.py:36
  286.4 4.1 %collective-permute-start.11 = (f32[128,64]{1,0:T(8,128)}, f32[128,64]{1,0:T(8,128)S(1)}, u32[]{:S(2)}, u32[]{:S(2)}) collective-permute-start(f32[128,64]{1,0:T(8,128)} %get-tuple-element.50), channel_id=1, source_target_pairs={{1,0},{3,2},{5,4},{7,6},{9,8},{11,10},{13,12},{15,14},{17,16},{19,... | collective-permute-start | bytes 98312 | tf_op jit(solution)/shard_map/ppermute | solution.py:37
  289.4 1.1 copy-start.10
  290.5 0.6 copy-start.11
  290.5 0.7 copy-start.4
  290.5 0.7 copy-start.5
  (1 other events, 0.6 us)

commit v9 on v8

--- a/solution.py
+++ b/solution.py
@@ -12,9 +12,9 @@
 
 STEP_SIZE = 0.03
 CAP_LOG = 1.5
-CHUNK_Z = 8
+CHUNK_Z = 16
 EDGE_Z = 32
-DEPTH_X = 16
+DEPTH_X = 32
 
 
 def permeability(values):

time: 323 us -> 318 us (0.985)
  Pallas kernels: 103 us -> 99.3 us
    pallas_call x1, Pallas kernels: 40.5 us -> 36.3 us  [advance(): pl.pallas_call(first_step_kernel, out_shape=tuple(out_shape + [full, full...]
where the time goes in v9:
time: 318 us; the launch traced here: 316 us
  blocking collectives  99.5 us (31%)
  Pallas kernels  99.3 us (31%)
  waiting for transfers between devices  69.4 us (22%)
  starting transfers between devices  38 us (12%)
  matrix products  6.73 us (2%)
    all_to_all x1, blocking collectives, body(): lax.all_to_all(first.reshape(groups, planes, rows_x, rows_y), ('wide', 'n...  99.5 us
    all_to_all x1, waiting for transfers between devices, body(): lax.all_to_all(outgoing, ('wide', 'narrow'), split_axis=0, concat_axis=0,...  68 us
    pallas_call x1, Pallas kernels, advance(): pl.pallas_call(first_step_kernel, out_shape=tuple(out_shape + [full, full...  36.3 us
    pallas_call x1, Pallas kernels, advance(): pl.pallas_call(later_step_kernel, out_shape=tuple(out_shape), grid=grid,...  27 us
    pallas_call x1, Pallas kernels, depth_transform(): pl.pallas_call(depth_kernel, out_shape=jax.ShapeDtypeStruct(noise.shape,...  15.5 us
    ppermute x3, starting transfers between devices, halos(): x_lo = lax.ppermute(last_x, 'wide', forward_w)  12.1 us
    pallas_call x2, Pallas kernels, block_edges(): pl.pallas_call(edge_kernel, out_shape=tuple(out_shape), grid=(depth // tz...  10.9 us
    pallas_call x1, Pallas kernels, line_transforms(): pl.pallas_call(functools.partial(line_kernel, count_w=count_w, count_n=co...  9.62 us
  transfers between devices with their start and end apart: 13, of which 3 were waited for; matrix products, arithmetic and copies ran while one was open for 2% of the time, Pallas kernels for 3%

profile of v9, /device:TPU:11, one launch (start us, length us, event | category | flops | bytes accessed | tf_op | source)
XLA Modules:
  0.0 316.1 jit_solution(12761812228031062372)
XLA Ops:
  0.6 15.5 %shard_map.104 = bf16[128,64,256]{2,1,0:T(8,128)(2,1)} custom-call(bf16[128,128]{1,0:T(8,128)(2,1)} %rz_ref.1, bf16[128,64,256]{2,1,0:T(8,128)(2,1)} %n_ref.1), custom_call_target="tpu_custom_call" | custom-call | tf_op jit(solution)/shard_map/pallas_call | solution.py:273
  16.2 99.5 %all_to_all.10.g_ref = bf16[16,8,64,256]{3,2,1,0:T(8,128)(2,1)} all-to-all(bf16[16,8,64,256]{3,2,1,0:T(8,128)(2,1)} %bitcast.9), channel_id=1, replica_groups=mesh['member'=2,'wide'=8,'narrow'=2] {'wide','narrow'}, dimensions={0} | all-to-all | bytes 8388608 | tf_op jit(solution)/shard_map/all_to_all | solution.py:323
  115.7 9.6 %shard_map.105 = bf16[16,8,64,256]{3,2,1,0:T(8,128)(2,1)} custom-call(bf16[16,8,64,256]{3,2,1,0:T(8,128)(2,1)} %all_to_all.10.g_ref, bf16[512,512]{1,0:T(8,128)(2,1)} %rx_ref.1, bf16[512,512]{1,0:T(8,128)(2,1)} %ry_ref.1), custom_call_target="tpu_custom_call" | custom-call | tf_op jit(solution)/shard_map/pallas_call | solution.py:306
  125.3 4.9 %all-to-all-start.1 = ((bf16[16,8,64,256]{3,2,1,0:T(8,128)(2,1)}), bf16[16,8,64,256]{3,2,1,0:T(8,128)(2,1)}, u32[]{:S(2)}, u32[]{:S(2)}) async-start(bf16[16,8,64,256]{3,2,1,0:T(8,128)(2,1)} %shard_map.105), calls=%async_computation.1 | async-start | bytes 8388608 | tf_op jit(solution)/shard_map/all_to_all | solution.py:328
  130.2 4.9 %shard_map.107 = (f32[128,256]{1,0:T(8,128)}, f32[128,256]{1,0:T(8,128)}, f32[128,64]{1,0:T(8,128)}, f32[128,64]{1,0:T(8,128)}) custom-call(bf16[128,64,256]{2,1,0:T(8,128)(2,1)} %pa_ref.1), custom_call_target="tpu_custom_call" | custom-call | tf_op jit(solution)/shard_map/pallas_call | solution.py:111
  135.3 6.7 %fusion = f32[8192,256]{1,0:T(8,128)} fusion(f32[256]{0:T(256)S(1)} %get-tuple-element.52, s32[256]{0:T(256)S(1)} %multiply_add_fusion, s32[256]{0:T(256)S(1)} %get-tuple-element.53), kind=kOutput, calls=%fused_computation | convolution fusion | flops 6446710784 | bytes 8391680 | tf_op jit(solution)/shard_map/dot_general | solution.py:351
  142.0 3.1 collective-permute-start.4
  145.1 1.3 collective-permute-start.6
  146.4 3.0 collective-permute-start.7
  149.4 3.1 collective-permute-start.5
  152.5 68.0 %all-to-all-done.1 = bf16[16,8,64,256]{3,2,1,0:T(8,128)(2,1)} async-done(((bf16[16,8,64,256]{3,2,1,0:T(8,128)(2,1)}), bf16[16,8,64,256]{3,2,1,0:T(8,128)(2,1)}, u32[]{:S(2)}, u32[]{:S(2)}) %all-to-all-start.1) | async-done | bytes 4194336 | tf_op jit(solution)/shard_map/all_to_all | solution.py:328
  220.6 5.9 %shard_map.106 = (f32[128,256]{1,0:T(8,128)}, f32[128,256]{1,0:T(8,128)}, f32[128,64]{1,0:T(8,128)}, f32[128,64]{1,0:T(8,128)}, bf16[128,64,256]{2,1,0:T(8,128)(2,1)}) custom-call(bf16[128,64,256]{2,1,0:T(8,128)(2,1)} %bitcast.1.block_ref), custom_call_target="tpu_custom_call" | custom-call | tf_op jit(solution)/shard_map/pallas_call | solution.py:111
  226.5 5.7 %collective-permute-start = (f32[128,256]{1,0:T(8,128)}, f32[128,256]{1,0:T(8,128)S(1)}, u32[]{:S(2)}, u32[]{:S(2)}) collective-permute-start(f32[128,256]{1,0:T(8,128)} %get-tuple-element.28), channel_id=1, source_target_pairs={{0,2},{2,4},{4,6},{6,8},{8,10},{10,12},{12,14},{1,3},{3,5},{5,7},{... | collective-permute-start | bytes 393224 | tf_op jit(solution)/shard_map/ppermute | solution.py:34
  232.2 1.9 collective-permute-start.1
  234.2 1.3 collective-permute-start.2
  235.5 3.2 %collective-permute-start.3 = (f32[128,64]{1,0:T(8,128)}, f32[128,64]{1,0:T(8,128)S(1)}, u32[]{:S(2)}, u32[]{:S(2)}) collective-permute-start(f32[128,64]{1,0:T(8,128)} %get-tuple-element.31), channel_id=1, source_target_pairs={{1,0},{3,2},{5,4},{7,6},{9,8},{11,10},{13,12},{15,14},{17,16},{19,... | collective-permute-start | bytes 98312 | tf_op jit(solution)/shard_map/ppermute | solution.py:37
  238.7 0.6 add_convert_fusion.inside_ref
  239.3 0.3 collective-permute-done.3.lyh_ref
  239.7 0.3 copy-done.1
  240.0 0.2 copy-done.9
  240.2 0.1 copy-done.2
  240.3 0.0 copy-done.3
  240.3 36.3 %shard_map.108 = (f32[128,64,256]{2,1,0:T(8,128)}, f32[128,256]{1,0:T(8,128)}, f32[128,256]{1,0:T(8,128)}, f32[128,64]{1,0:T(8,128)}, f32[128,64]{1,0:T(8,128)},...) custom-call(s32[4]{0:T(128)} %add_convert_fusion.inside_ref, ...), custom_call_target="tpu_custom_call" | custom-call | tf_op jit(solution)/shard_map/pallas_call | solution.py:240
  276.6 3.4 %collective-permute-start.8 = (f32[128,256]{1,0:T(8,128)}, f32[128,256]{1,0:T(8,128)S(1)}, u32[]{:S(2)}, u32[]{:S(2)}) collective-permute-start(f32[128,256]{1,0:T(8,128)} %get-tuple-element.47), channel_id=1, source_target_pairs={{0,2},{2,4},{4,6},{6,8},{8,10},{10,12},{12,14},{1,3},{3,5},{5,7},{... | collective-permute-start | bytes 393224 | tf_op jit(solution)/shard_map/ppermute | solution.py:34
  280.0 2.8 collective-permute-start.9
  282.8 1.3 collective-permute-start.10
  284.1 3.0 collective-permute-start.11
  287.2 1.1 collective-permute-done.11.qyh_ref
  288.3 0.6 copy-done.11
  288.9 0.0 copy-done.4
  288.9 0.1 copy-done.5
  289.0 27.0 %shard_map.109 = (f32[128,64,256]{2,1,0:T(8,128)}, f32[128,256]{1,0:T(8,128)}, f32[128,256]{1,0:T(8,128)}, f32[128,64]{1,0:T(8,128)}, f32[128,64]{1,0:T(8,128)}) custom-call(f32[128,64,256]{2,1,0:T(8,128)} %get-tuple-element.41.tzm_ref.tza_ref, f32[128,64,256]{2,1,0:T(8,128)} %get-tuple-element.41.tzm_ref.tza_ref, ...), custom_call_target="tpu_custom_call" | custom-call | tf_op jit(solution)/shard_map/pallas_call | solution.py:250
  (45 shorter events, 0.1 us)
Async XLA Ops:
  125.3 9.9 %copy-start.12 = (s32[256]{0:T(256)S(1)}, s32[256]{0:T(256)}, u32[]{:S(2)}) copy-start(s32[256]{0:T(256)} %param.14) | copy-start | bytes 3076
  125.3 9.9 %copy-start.13 = (s32[256]{0:T(256)S(1)}, s32[256]{0:T(256)}, u32[]{:S(2)}) copy-start(s32[256]{0:T(256)} %param.16) | copy-start | bytes 3076
  125.3 9.9 %copy-start.14 = (f32[256]{0:T(256)S(1)}, f32[256]{0:T(256)}, u32[]{:S(2)}) copy-start(f32[256]{0:T(256)} %param.17) | copy-start | bytes 3076
  125.3 9.9 %copy-start.15 = (s32[256]{0:T(256)S(1)}, s32[256]{0:T(256)}, u32[]{:S(2)}) copy-start(s32[256]{0:T(256)} %param.15) | copy-start | bytes 3076
  125.3 95.3 %all-to-all-start.1 = ((bf16[16,8,64,256]{3,2,1,0:T(8,128)(2,1)}), bf16[16,8,64,256]{3,2,1,0:T(8,128)(2,1)}, u32[]{:S(2)}, u32[]{:S(2)}) async-start(bf16[16,8,64,256]{3,2,1,0:T(8,128)(2,1)} %shard_map.105), calls=%async_computation.1 | async-start | bytes 8388608 | tf_op jit(solution)/shard_map/all_to_all | solution.py:328
  135.2 6.8 %copy-start.17 = (f32[128,256]{1,0:T(8,128)S(1)}, f32[128,256]{1,0:T(8,128)}, u32[]{:S(2)}) copy-start(f32[128,256]{1,0:T(8,128)} %get-tuple-element.36) | copy-start | bytes 393220
  135.2 9.9 %copy-start.19 = (f32[128,64]{1,0:T(8,128)S(1)}, f32[128,64]{1,0:T(8,128)}, u32[]{:S(2)}) copy-start(f32[128,64]{1,0:T(8,128)} %get-tuple-element.38) | copy-start | bytes 98308
  135.2 11.2 %copy-start.18 = (f32[128,64]{1,0:T(8,128)S(1)}, f32[128,64]{1,0:T(8,128)}, u32[]{:S(2)}) copy-start(f32[128,64]{1,0:T(8,128)} %get-tuple-element.39) | copy-start | bytes 98308
  135.2 14.3 %copy-start.16 = (f32[128,256]{1,0:T(8,128)S(1)}, f32[128,256]{1,0:T(8,128)}, u32[]{:S(2)}) copy-start(f32[128,256]{1,0:T(8,128)} %get-tuple-element.37) | copy-start | bytes 393220
  142.0 93.5 %collective-permute-start.4 = (f32[128,256]{1,0:T(8,128)S(1)}, f32[128,256]{1,0:T(8,128)S(1)}, u32[]{:S(2)}, u32[]{:S(2)}) collective-permute-start(f32[128,256]{1,0:T(8,128)S(1)} %copy-done.17), channel_id=1, source_target_pairs={{0,2},{2,4},{4,6},{6,8},{8,10},{10,12},{12,14},{1,3},{3,5},{5,7},{... | collective-permute-start | bytes 393224 | tf_op jit(solution)/shard_map/ppermute | solution.py:34
  145.1 87.1 %collective-permute-start.6 = (f32[128,64]{1,0:T(8,128)S(1)}, f32[128,64]{1,0:T(8,128)S(1)}, u32[]{:S(2)}, u32[]{:S(2)}) collective-permute-start(f32[128,64]{1,0:T(8,128)S(1)} %copy-done.19), channel_id=1, source_target_pairs={{0,1},{2,3},{4,5},{6,7},{8,9},{10,11},{12,13},{14,15},{16,17},{18,... | collective-permute-start | bytes 98312 | tf_op jit(solution)/shard_map/ppermute | solution.py:36
  146.4 87.8 %collective-permute-start.7 = (f32[128,64]{1,0:T(8,128)S(1)}, f32[128,64]{1,0:T(8,128)S(1)}, u32[]{:S(2)}, u32[]{:S(2)}) collective-permute-start(f32[128,64]{1,0:T(8,128)S(1)} %copy-done.18), channel_id=1, source_target_pairs={{1,0},{3,2},{5,4},{7,6},{9,8},{11,10},{13,12},{15,14},{17,16},{19,... | collective-permute-start | bytes 98312 | tf_op jit(solution)/shard_map/ppermute | solution.py:37
  149.4 89.9 %collective-permute-start.5 = (f32[128,256]{1,0:T(8,128)S(1)}, f32[128,256]{1,0:T(8,128)S(1)}, u32[]{:S(2)}, u32[]{:S(2)}) collective-permute-start(f32[128,256]{1,0:T(8,128)S(1)} %copy-done.16), channel_id=1, source_target_pairs={{2,0},{4,2},{6,4},{8,6},{10,8},{12,10},{14,12},{3,1},{5,3},{7,5},{... | collective-permute-start | bytes 393224 | tf_op jit(solution)/shard_map/ppermute | solution.py:35
  226.5 13.1 %collective-permute-start = (f32[128,256]{1,0:T(8,128)}, f32[128,256]{1,0:T(8,128)S(1)}, u32[]{:S(2)}, u32[]{:S(2)}) collective-permute-start(f32[128,256]{1,0:T(8,128)} %get-tuple-element.28), channel_id=1, source_target_pairs={{0,2},{2,4},{4,6},{6,8},{8,10},{10,12},{12,14},{1,3},{3,5},{5,7},{... | collective-permute-start | bytes 393224 | tf_op jit(solution)/shard_map/ppermute | solution.py:34
  232.2 7.5 %copy-start.6 = (f32[128,64]{1,0:T(8,128)}, f32[128,64]{1,0:T(8,128)S(1)}, u32[]{:S(2)}) copy-start(f32[128,64]{1,0:T(8,128)S(1)} %collective-permute-done.6.qyl_ref) | copy-start | bytes 98308
  232.2 7.4 %collective-permute-start.1 = (f32[128,256]{1,0:T(8,128)}, f32[128,256]{1,0:T(8,128)S(1)}, u32[]{:S(2)}, u32[]{:S(2)}) collective-permute-start(f32[128,256]{1,0:T(8,128)} %get-tuple-element.29), channel_id=1, source_target_pairs={{2,0},{4,2},{6,4},{8,6},{10,8},{12,10},{14,12},{3,1},{5,3},{7,5},{... | collective-permute-start | bytes 393224 | tf_op jit(solution)/shard_map/ppermute | solution.py:35
  234.2 5.5 %copy-start.7 = (f32[128,64]{1,0:T(8,128)}, f32[128,64]{1,0:T(8,128)S(1)}, u32[]{:S(2)}) copy-start(f32[128,64]{1,0:T(8,128)S(1)} %collective-permute-done.7.qyh_ref) | copy-start | bytes 98308
  234.2 5.2 %collective-permute-start.2 = (f32[128,64]{1,0:T(8,128)}, f32[128,64]{1,0:T(8,128)S(1)}, u32[]{:S(2)}, u32[]{:S(2)}) collective-permute-start(f32[128,64]{1,0:T(8,128)} %get-tuple-element.30), channel_id=1, source_target_pairs={{0,1},{2,3},{4,5},{6,7},{8,9},{10,11},{12,13},{14,15},{16,17},{18,... | collective-permute-start | bytes 98312 | tf_op jit(solution)/shard_map/ppermute | solution.py:36
  235.5 4.2 %copy-start = (f32[128,256]{1,0:T(8,128)}, f32[128,256]{1,0:T(8,128)S(1)}, u32[]{:S(2)}) copy-start(f32[128,256]{1,0:T(8,128)S(1)} %collective-permute-done.4.qxl_ref) | copy-start | bytes 393220
  235.5 4.1 %collective-permute-start.3 = (f32[128,64]{1,0:T(8,128)}, f32[128,64]{1,0:T(8,128)S(1)}, u32[]{:S(2)}, u32[]{:S(2)}) collective-permute-start(f32[128,64]{1,0:T(8,128)} %get-tuple-element.31), channel_id=1, source_target_pairs={{1,0},{3,2},{5,4},{7,6},{9,8},{11,10},{13,12},{15,14},{17,16},{19,... | collective-permute-start | bytes 98312 | tf_op jit(solution)/shard_map/ppermute | solution.py:37
  239.3 0.7 copy-start.1
  239.3 0.7 copy-start.8
  239.6 0.7 copy-start.2
  239.6 0.7 copy-start.3
  276.6 11.6 %collective-permute-start.8 = (f32[128,256]{1,0:T(8,128)}, f32[128,256]{1,0:T(8,128)S(1)}, u32[]{:S(2)}, u32[]{:S(2)}) collective-permute-start(f32[128,256]{1,0:T(8,128)} %get-tuple-element.47), channel_id=1, source_target_pairs={{0,2},{2,4},{4,6},{6,8},{8,10},{10,12},{12,14},{1,3},{3,5},{5,7},{... | collective-permute-start | bytes 393224 | tf_op jit(solution)/shard_map/ppermute | solution.py:34
  280.0 8.3 %collective-permute-start.9 = (f32[128,256]{1,0:T(8,128)}, f32[128,256]{1,0:T(8,128)S(1)}, u32[]{:S(2)}, u32[]{:S(2)}) collective-permute-start(f32[128,256]{1,0:T(8,128)} %get-tuple-element.48), channel_id=1, source_target_pairs={{2,0},{4,2},{6,4},{8,6},{10,8},{12,10},{14,12},{3,1},{5,3},{7,5},{... | collective-permute-start | bytes 393224 | tf_op jit(solution)/shard_map/ppermute | solution.py:35
  282.8 4.3 %collective-permute-start.10 = (f32[128,64]{1,0:T(8,128)}, f32[128,64]{1,0:T(8,128)S(1)}, u32[]{:S(2)}, u32[]{:S(2)}) collective-permute-start(f32[128,64]{1,0:T(8,128)} %get-tuple-element.49), channel_id=1, source_target_pairs={{0,1},{2,3},{4,5},{6,7},{8,9},{10,11},{12,13},{14,15},{16,17},{18,... | collective-permute-start | bytes 98312 | tf_op jit(solution)/shard_map/ppermute | solution.py:36
  284.1 4.1 %collective-permute-start.11 = (f32[128,64]{1,0:T(8,128)}, f32[128,64]{1,0:T(8,128)S(1)}, u32[]{:S(2)}, u32[]{:S(2)}) collective-permute-start(f32[128,64]{1,0:T(8,128)} %get-tuple-element.50), channel_id=1, source_target_pairs={{1,0},{3,2},{5,4},{7,6},{9,8},{11,10},{13,12},{15,14},{17,16},{19,... | collective-permute-start | bytes 98312 | tf_op jit(solution)/shard_map/ppermute | solution.py:37
  287.1 1.1 copy-start.10
  288.2 0.6 copy-start.11
  288.2 0.7 copy-start.4
  288.2 0.7 copy-start.5
  (1 other events, 0.6 us)

commit v10 on v9

--- a/solution.py
+++ b/solution.py
@@ -14,7 +14,7 @@
 CAP_LOG = 1.5
 CHUNK_Z = 16
 EDGE_Z = 32
-DEPTH_X = 32
+DEPTH_X = 16
 
 
 def permeability(values):
@@ -146,7 +146,7 @@
 
 
 def first_step_kernel(
-    inside_ref, lpm_ref, lpb_ref, lpa_ref, lxl_ref, lxh_ref, lyl_ref, lyh_ref,
+    inside_ref, lpm_ref, lpb_ref, lpa_ref, rim_ref,
     pm_ref, pb_ref, pa_ref, qxl_ref, qxh_ref, qyl_ref, qyh_ref, f_ref,
     o_ref, exl_ref, exh_ref, eyl_ref, eyh_ref, tzm_ref, txm_ref, tym_ref, txp_ref, typ_ref,
 ):
@@ -155,13 +155,13 @@
     tz, nx, ny = pm_ref.shape
     f32 = jnp.float32
 
-    def side_perm(ref, k):
-        return jnp.where(inside_ref[k] > 0, permeability(ref[...].astype(f32)), 0.0)
-
-    kxl = jnp.where(inside_ref[0] > 0, permeability(x_rows(lxl_ref)), 0.0)
-    kxh = jnp.where(inside_ref[1] > 0, permeability(x_rows(lxh_ref)), 0.0)
-    kyl = to_columns(side_perm(lyl_ref, 2))
-    kyh = to_columns(side_perm(lyh_ref, 3))
+    def side_perm(values, k):
+        return jnp.where(inside_ref[k] > 0, permeability(values), 0.0)
+
+    kxl = side_perm(rim_ref[:, 0:1, :], 0)
+    kxh = side_perm(rim_ref[:, 1:2, :], 1)
+    kyl = to_columns(side_perm(rim_ref[:, 2, 0:nx], 2))
+    kyh = to_columns(side_perm(rim_ref[:, 3, 0:nx], 3))
 
     below = jnp.where(c == 0, 0.0, permeability(lpb_ref[...].astype(f32)))
     above = jnp.where(c == last, 0.0, permeability(lpa_ref[...].astype(f32)))
@@ -216,7 +216,7 @@
     )
 
 
-def advance(stored, pressure, pressure_halos, flow, inside=None, log_perm=None, perm_halos=None):
+def advance(stored, pressure, pressure_halos, flow, inside=None, log_perm=None, rims=None):
     depth, nx, ny = pressure.shape
     tz = CHUNK_Z
     grid = (depth // tz,)
@@ -241,10 +241,11 @@
             first_step_kernel,
             out_shape=tuple(out_shape + [full, full, full, rows, cols]),
             grid=grid,
-            in_specs=[smem, main, below, above] + side + pressure_specs,
+            in_specs=[smem, main, below, above, pl.BlockSpec((tz, 4, ny), lambda c: (c, 0, 0))]
+            + pressure_specs,
             out_specs=out_specs + [main, main, main, row, col],
             compiler_params=params,
-        )(inside, log_perm, log_perm, log_perm, *perm_halos, *pressure_args)
+        )(inside, log_perm, log_perm, log_perm, rims, *pressure_args)
         return outs[0], outs[1:5], outs[5:]
     t_zm, t_xm, t_ym, t_xp, t_yp = stored
     outs = pl.pallas_call(
@@ -280,7 +281,7 @@
     )(root_z, noise)
 
 
-def line_kernel(g_ref, rx_ref, ry_ref, o_ref, *, count_w, count_n):
+def line_kernel(g_ref, rx_ref, ry_ref, o_ref, h_ref, *, count_w, count_n):
     f32 = jnp.float32
     nx = g_ref.shape[2]
     ny = g_ref.shape[3]
@@ -297,18 +298,49 @@
         for n in range(count_n):
             o_ref[w * count_n + n, 0] = third[w * nx : (w + 1) * nx, n * ny : (n + 1) * ny]
 
+    total_y = count_n * ny
+    wanted = [n * ny - 1 if n > 0 else 0 for n in range(count_n)]
+    wanted += [(n + 1) * ny if n < count_n - 1 else 0 for n in range(count_n)]
+    picks = max(8, len(wanted))
+    row = lax.broadcasted_iota(jnp.int32, (picks, total_y), 0)
+    lane = lax.broadcasted_iota(jnp.int32, (picks, total_y), 1)
+    sel = jnp.zeros((picks, total_y), jnp.bool_)
+    for r, y in enumerate(wanted):
+        sel = sel | ((row == r) & (lane == y))
+    columns = lax.dot_general(
+        jnp.where(sel, 1.0, 0.0).astype(jnp.bfloat16), third, (((1,), (1,)), ((), ())),
+        preferred_element_type=f32,
+    )
+    h_ref[...] = jnp.zeros(h_ref.shape, f32)
+    for w in range(count_w):
+        for n in range(count_n):
+            d = w * count_n + n
+            ys = slice(n * ny, (n + 1) * ny)
+            if w > 0:
+                h_ref[d, 0, 0:1, :] = third[w * nx - 1 : w * nx, ys].astype(f32)
+            if w < count_w - 1:
+                h_ref[d, 0, 1:2, :] = third[(w + 1) * nx : (w + 1) * nx + 1, ys].astype(f32)
+            if n > 0:
+                h_ref[d, 0, 2:3, 0:nx] = columns[n : n + 1, w * nx : (w + 1) * nx]
+            if n < count_n - 1:
+                h_ref[d, 0, 3:4, 0:nx] = columns[count_n + n : count_n + n + 1, w * nx : (w + 1) * nx]
+
 
 def line_transforms(gathered, root_x, root_y, count_w, count_n):
     groups, planes, nx, ny = gathered.shape
     block = pl.BlockSpec((groups, 1, nx, ny), lambda z: (0, z, 0, 0))
     whole_x = pl.BlockSpec(root_x.shape, lambda z: (0, 0))
     whole_y = pl.BlockSpec(root_y.shape, lambda z: (0, 0))
+    rims = pl.BlockSpec((groups, 1, 4, ny), lambda z: (0, z, 0, 0))
     return pl.pallas_call(
         functools.partial(line_kernel, count_w=count_w, count_n=count_n),
-        out_shape=jax.ShapeDtypeStruct(gathered.shape, jnp.bfloat16),
+        out_shape=(
+            jax.ShapeDtypeStruct(gathered.shape, jnp.bfloat16),
+            jax.ShapeDtypeStruct((groups, planes, 4, ny), jnp.float32),
+        ),
         grid=(planes,),
         in_specs=[block, whole_x, whole_y],
-        out_specs=block,
+        out_specs=(block, rims),
         compiler_params=pltpu.CompilerParams(dimension_semantics=("arbitrary",)),
     )(gathered, root_x, root_y)
 
@@ -324,7 +356,7 @@
         first.reshape(groups, planes, rows_x, rows_y),
         ("wide", "narrow"), split_axis=0, concat_axis=0, tiled=True,
     )
-    outgoing = line_transforms(gathered, root_x, root_y, count_w, count_n)
+    outgoing, rims = line_transforms(gathered, root_x, root_y, count_w, count_n)
     log_perm = lax.all_to_all(
         outgoing, ("wide", "narrow"), split_axis=0, concat_axis=0, tiled=True,
     ).reshape(depth, rows_x, rows_y)
@@ -357,13 +389,14 @@
     ).astype(jnp.int32)
     edges = block_edges(pressure_start)
     flow, edges = lax.optimization_barrier((flow, edges))
-    *lp_edges, log_perm = block_edges(log_perm, keep=True)
-    perm_halos = halos(lp_edges)
+    rims = lax.all_to_all(
+        rims, ("wide", "narrow"), split_axis=0, concat_axis=0, tiled=True,
+    ).reshape(depth, 4, rows_y)
     pressure = pressure_start
     stored = None
     for step in range(STEPS):
         pressure, edges, stored = advance(
-            stored, pressure, halos(edges), flow, inside, log_perm, perm_halos
+            stored, pressure, halos(edges), flow, inside, log_perm, rims
         )
     return (log_perm, pressure)
 

time: 318 us -> 325 us (1.022)
  blocking collectives: 99.5 us -> 119 us
  starting transfers between devices: 38 us -> 30.1 us
  Pallas kernels: 99.3 us -> 92.8 us
  local copies, waits for them, and re-layouts: 1.45 us -> 5.53 us
    all_to_all x1, waiting for transfers between devices: 68 us -> 16.8 us  [body(): lax.all_to_all(outgoing, ('wide', 'narrow'), split_axis=0, concat_axis=0,...]
    ppermute x3 -> x2, waiting for transfers between devices: 0.01 us -> 50.3 us  [halos(): x_lo = lax.ppermute(last_x, 'wide', forward_w)]
    all_to_all x0 -> x1, blocking collectives: none -> 19 us  [body(): lax.all_to_all(rims, ('wide', 'narrow'), split_axis=0, concat_axis=0, til...]
    pallas_call x2 -> x1, Pallas kernels: 10.9 us -> 4.93 us  [block_edges(): pl.pallas_call(edge_kernel, out_shape=tuple(out_shape), grid=(depth // tz...]
    unnamed x40 -> x33, local copies, waits for them, and re-layouts: 1.45 us -> 5.53 us
    ppermute x3 -> x2, starting transfers between devices: 9.28 us -> 6.27 us  [halos(): y_hi = lax.ppermute(first_y, 'narrow', backward_n)]
    ppermute x3 -> x2, starting transfers between devices: 7.83 us -> 5 us  [halos(): x_hi = lax.ppermute(first_x, 'wide', backward_w)]
    ppermute x3 -> x2, starting transfers between devices: 12.1 us -> 11.5 us  [halos(): x_lo = lax.ppermute(last_x, 'wide', forward_w)]
  transfers between devices with their start and end apart: 13 -> 9, of which waited for: 3 -> 4; matrix products, arithmetic and copies ran while one was open for 2% -> 2% of each run, Pallas kernels for 3% -> 2%
where the time goes in v10:
time: 325 us; the launch traced here: 323 us
  blocking collectives  119 us (37%)
  Pallas kernels  92.8 us (29%)
  waiting for transfers between devices  68.3 us (21%)
  starting transfers between devices  30.1 us (9%)
  matrix products  6.73 us (2%)
  local copies, waits for them, and re-layouts  5.53 us (2%)
    all_to_all x1, blocking collectives, body(): lax.all_to_all(first.reshape(groups, planes, rows_x, rows_y), ('wide', 'n...  99.5 us
    ppermute x2, waiting for transfers between devices, halos(): x_lo = lax.ppermute(last_x, 'wide', forward_w)  50.3 us
    pallas_call x1, Pallas kernels, advance(): pl.pallas_call(first_step_kernel, out_shape=tuple(out_shape + [full, full...  36.2 us
    pallas_call x1, Pallas kernels, advance(): pl.pallas_call(later_step_kernel, out_shape=tuple(out_shape), grid=grid,...  27.1 us
    all_to_all x1, blocking collectives, body(): lax.all_to_all(rims, ('wide', 'narrow'), split_axis=0, concat_axis=0, til...  19 us
    all_to_all x1, waiting for transfers between devices, body(): lax.all_to_all(outgoing, ('wide', 'narrow'), split_axis=0, concat_axis=0,...  16.8 us
    pallas_call x1, Pallas kernels, depth_transform(): pl.pallas_call(depth_kernel, out_shape=jax.ShapeDtypeStruct(noise.shape,...  13.6 us
    ppermute x2, starting transfers between devices, halos(): x_lo = lax.ppermute(last_x, 'wide', forward_w)  11.5 us
  transfers between devices with their start and end apart: 9, of which 4 were waited for; matrix products, arithmetic and copies ran while one was open for 2% of the time, Pallas kernels for 2%

profile of v10, /device:TPU:11, one launch (start us, length us, event | category | flops | bytes accessed | tf_op | source)
XLA Modules:
  0.0 323.4 jit_solution(5506247246030486241)
XLA Ops:
  0.6 13.6 %shard_map.104 = bf16[128,64,256]{2,1,0:T(8,128)(2,1)} custom-call(bf16[128,128]{1,0:T(8,128)(2,1)} %rz_ref.1, bf16[128,64,256]{2,1,0:T(8,128)(2,1)} %n_ref.1), custom_call_target="tpu_custom_call" | custom-call | tf_op jit(solution)/shard_map/pallas_call | solution.py:274
  14.2 99.5 %all_to_all.15.g_ref = bf16[16,8,64,256]{3,2,1,0:T(8,128)(2,1)} all-to-all(bf16[16,8,64,256]{3,2,1,0:T(8,128)(2,1)} %bitcast.10), channel_id=1, replica_groups=mesh['member'=2,'wide'=8,'narrow'=2] {'wide','narrow'}, dimensions={0} | all-to-all | bytes 8388608 | tf_op jit(solution)/shard_map/all_to_all | solution.py:355
  113.7 10.9 %shard_map.105 = (bf16[16,8,64,256]{3,2,1,0:T(8,128)(2,1)}, f32[16,8,4,256]{3,2,1,0:T(4,128)}) custom-call(bf16[16,8,64,256]{3,2,1,0:T(8,128)(2,1)} %all_to_all.15.g_ref, bf16[512,512]{1,0:T(8,128)(2,1)} %rx_ref.1, bf16[512,512]{1,0:T(8,128)(2,1)} %ry_ref.1), custom_call_target="tpu_custom_call" | custom-call | tf_op jit(solution)/shard_map/pallas_call | solution.py:335
  124.7 19.0 %all_to_all.16 = f32[16,8,4,256]{3,2,1,0:T(4,128)} all-to-all(f32[16,8,4,256]{3,2,1,0:T(4,128)} %get-tuple-element.25), channel_id=1, replica_groups=mesh['member'=2,'wide'=8,'narrow'=2] {'wide','narrow'}, dimensions={0} | all-to-all | bytes 1048576 | tf_op jit(solution)/shard_map/all_to_all | solution.py:392
  143.7 4.7 %all-to-all-start.1 = ((bf16[16,8,64,256]{3,2,1,0:T(8,128)(2,1)}), bf16[16,8,64,256]{3,2,1,0:T(8,128)(2,1)}, u32[]{:S(2)}, u32[]{:S(2)}) async-start(bf16[16,8,64,256]{3,2,1,0:T(8,128)(2,1)} %get-tuple-element.24), calls=%async_computation.1 | async-start | bytes 8388608 | tf_op jit(solution)/shard_map/all_to_all | solution.py:360
  148.4 4.9 %shard_map.106 = (f32[128,256]{1,0:T(8,128)}, f32[128,256]{1,0:T(8,128)}, f32[128,64]{1,0:T(8,128)}, f32[128,64]{1,0:T(8,128)}) custom-call(bf16[128,64,256]{2,1,0:T(8,128)(2,1)} %pa_ref.1), custom_call_target="tpu_custom_call" | custom-call | tf_op jit(solution)/shard_map/pallas_call | solution.py:111
  153.4 6.7 %fusion = f32[8192,256]{1,0:T(8,128)} fusion(f32[256]{0:T(256)S(1)} %get-tuple-element.46, s32[256]{0:T(256)S(1)} %multiply_add_fusion, s32[256]{0:T(256)S(1)} %get-tuple-element.47), kind=kOutput, calls=%fused_computation | convolution fusion | flops 6446710784 | bytes 8391680 | tf_op jit(solution)/shard_map/dot_general | solution.py:383
  160.1 3.1 collective-permute-start
  163.2 3.1 collective-permute-start.1
  166.3 1.3 collective-permute-start.2
  167.7 3.0 collective-permute-start.3
  170.7 0.6 add_convert_fusion.inside_ref
  171.4 0.0 collective-permute-done.2.qyl_ref
  171.4 0.2 collective-permute-done.3.qyh_ref
  171.6 50.3 %collective-permute-done.qxl_ref = f32[128,256]{1,0:T(8,128)S(1)} collective-permute-done((f32[128,256]{1,0:T(8,128)S(1)}, f32[128,256]{1,0:T(8,128)S(1)}, u32[]{:S(2)}, u32[]{:S(2)}) %collective-permute-start) | collective-permute-done | bytes 131104 | tf_op jit(solution)/shard_map/ppermute | solution.py:34
  221.9 0.0 collective-permute-done.1.qxh_ref
  221.9 16.8 %all-to-all-done.1 = bf16[16,8,64,256]{3,2,1,0:T(8,128)(2,1)} async-done(((bf16[16,8,64,256]{3,2,1,0:T(8,128)(2,1)}), bf16[16,8,64,256]{3,2,1,0:T(8,128)(2,1)}, u32[]{:S(2)}, u32[]{:S(2)}) %all-to-all-start.1) | async-done | bytes 4194336 | tf_op jit(solution)/shard_map/all_to_all | solution.py:360
  238.7 36.2 %shard_map.107 = (f32[128,64,256]{2,1,0:T(8,128)}, f32[128,256]{1,0:T(8,128)}, f32[128,256]{1,0:T(8,128)}, f32[128,64]{1,0:T(8,128)}, f32[128,64]{1,0:T(8,128)},...) custom-call(s32[4]{0:T(128)} %add_convert_fusion.inside_ref, ...), custom_call_target="tpu_custom_call" | custom-call | tf_op jit(solution)/shard_map/pallas_call | solution.py:240
  274.9 8.4 %collective-permute-start.4 = (f32[128,256]{1,0:T(8,128)}, f32[128,256]{1,0:T(8,128)S(1)}, u32[]{:S(2)}, u32[]{:S(2)}) collective-permute-start(f32[128,256]{1,0:T(8,128)} %get-tuple-element.41), channel_id=1, source_target_pairs={{0,2},{2,4},{4,6},{6,8},{8,10},{10,12},{12,14},{1,3},{3,5},{5,7},{... | collective-permute-start | bytes 393224 | tf_op jit(solution)/shard_map/ppermute | solution.py:34
  283.3 1.9 collective-permute-start.5
  285.3 1.3 collective-permute-start.6
  286.6 3.2 %collective-permute-start.7 = (f32[128,64]{1,0:T(8,128)}, f32[128,64]{1,0:T(8,128)S(1)}, u32[]{:S(2)}, u32[]{:S(2)}) collective-permute-start(f32[128,64]{1,0:T(8,128)} %get-tuple-element.44), channel_id=1, source_target_pairs={{1,0},{3,2},{5,4},{7,6},{9,8},{11,10},{13,12},{15,14},{17,16},{19,... | collective-permute-start | bytes 98312 | tf_op jit(solution)/shard_map/ppermute | solution.py:37
  289.8 0.0 collective-permute-done.6.qyl_ref
  289.8 0.9 collective-permute-done.7.qyh_ref
  290.7 0.0 collective-permute-done.4.qxl_ref
  290.7 0.0 collective-permute-done.5.qxh_ref
  290.7 0.0 copy-start.3
  290.8 0.6 copy-done.7
  291.4 0.0 copy-done.2
  291.4 0.0 copy-done.3
  291.4 27.1 %shard_map.108 = (f32[128,64,256]{2,1,0:T(8,128)}, f32[128,256]{1,0:T(8,128)}, f32[128,256]{1,0:T(8,128)}, f32[128,64]{1,0:T(8,128)}, f32[128,64]{1,0:T(8,128)}) custom-call(f32[128,64,256]{2,1,0:T(8,128)} %get-tuple-element.35.tzm_ref.tza_ref, f32[128,64,256]{2,1,0:T(8,128)} %get-tuple-element.35.tzm_ref.tza_ref, ...), custom_call_target="tpu_custom_call" | custom-call | tf_op jit(solution)/shard_map/pallas_call | solution.py:251
  318.6 4.8 %copy.12 = bf16[128,64,256]{2,1,0:T(8,128)(2,1)} copy(bf16[128,64,256]{2,1,0:T(8,128)(2,1)} %bitcast.1.lpm_ref.lpb_ref.lpa_ref) | data formatting | bytes 8388608
  (30 shorter events, 0.1 us)
Async XLA Ops:
  113.7 39.6 %copy-start.8 = (s32[256]{0:T(256)S(1)}, s32[256]{0:T(256)}, u32[]{:S(2)}) copy-start(s32[256]{0:T(256)} %param.14) | copy-start | bytes 3076
  113.7 39.6 %copy-start.9 = (s32[256]{0:T(256)S(1)}, s32[256]{0:T(256)}, u32[]{:S(2)}) copy-start(s32[256]{0:T(256)} %param.16) | copy-start | bytes 3076
  113.7 39.7 %copy-start.10 = (f32[256]{0:T(256)S(1)}, f32[256]{0:T(256)}, u32[]{:S(2)}) copy-start(f32[256]{0:T(256)} %param.17) | copy-start | bytes 3076
  113.7 39.7 %copy-start.11 = (s32[256]{0:T(256)S(1)}, s32[256]{0:T(256)}, u32[]{:S(2)}) copy-start(s32[256]{0:T(256)} %param.15) | copy-start | bytes 3076
  143.7 95.1 %all-to-all-start.1 = ((bf16[16,8,64,256]{3,2,1,0:T(8,128)(2,1)}), bf16[16,8,64,256]{3,2,1,0:T(8,128)(2,1)}, u32[]{:S(2)}, u32[]{:S(2)}) async-start(bf16[16,8,64,256]{3,2,1,0:T(8,128)(2,1)} %get-tuple-element.24), calls=%async_computation.1 | async-start | bytes 8388608 | tf_op jit(solution)/shard_map/all_to_all | solution.py:360
  153.3 6.8 %copy-start.13 = (f32[128,256]{1,0:T(8,128)S(1)}, f32[128,256]{1,0:T(8,128)}, u32[]{:S(2)}) copy-start(f32[128,256]{1,0:T(8,128)} %get-tuple-element.30) | copy-start | bytes 393220
  153.3 9.9 %copy-start.12 = (f32[128,256]{1,0:T(8,128)S(1)}, f32[128,256]{1,0:T(8,128)}, u32[]{:S(2)}) copy-start(f32[128,256]{1,0:T(8,128)} %get-tuple-element.31) | copy-start | bytes 393220
  153.3 13.0 %copy-start.15 = (f32[128,64]{1,0:T(8,128)S(1)}, f32[128,64]{1,0:T(8,128)}, u32[]{:S(2)}) copy-start(f32[128,64]{1,0:T(8,128)} %get-tuple-element.32) | copy-start | bytes 98308
  153.3 14.3 %copy-start.14 = (f32[128,64]{1,0:T(8,128)S(1)}, f32[128,64]{1,0:T(8,128)}, u32[]{:S(2)}) copy-start(f32[128,64]{1,0:T(8,128)} %get-tuple-element.33) | copy-start | bytes 98308
  160.1 61.8 %collective-permute-start = (f32[128,256]{1,0:T(8,128)S(1)}, f32[128,256]{1,0:T(8,128)S(1)}, u32[]{:S(2)}, u32[]{:S(2)}) collective-permute-start(f32[128,256]{1,0:T(8,128)S(1)} %copy-done.13), channel_id=1, source_target_pairs={{0,2},{2,4},{4,6},{6,8},{8,10},{10,12},{12,14},{1,3},{3,5},{5,7},{... | collective-permute-start | bytes 393224 | tf_op jit(solution)/shard_map/ppermute | solution.py:34
  163.2 58.7 %collective-permute-start.1 = (f32[128,256]{1,0:T(8,128)S(1)}, f32[128,256]{1,0:T(8,128)S(1)}, u32[]{:S(2)}, u32[]{:S(2)}) collective-permute-start(f32[128,256]{1,0:T(8,128)S(1)} %copy-done.12), channel_id=1, source_target_pairs={{2,0},{4,2},{6,4},{8,6},{10,8},{12,10},{14,12},{3,1},{5,3},{7,5},{... | collective-permute-start | bytes 393224 | tf_op jit(solution)/shard_map/ppermute | solution.py:35
  166.3 5.0 %collective-permute-start.2 = (f32[128,64]{1,0:T(8,128)S(1)}, f32[128,64]{1,0:T(8,128)S(1)}, u32[]{:S(2)}, u32[]{:S(2)}) collective-permute-start(f32[128,64]{1,0:T(8,128)S(1)} %copy-done.15), channel_id=1, source_target_pairs={{0,1},{2,3},{4,5},{6,7},{8,9},{10,11},{12,13},{14,15},{16,17},{18,... | collective-permute-start | bytes 98312 | tf_op jit(solution)/shard_map/ppermute | solution.py:36
  167.7 3.9 %collective-permute-start.3 = (f32[128,64]{1,0:T(8,128)S(1)}, f32[128,64]{1,0:T(8,128)S(1)}, u32[]{:S(2)}, u32[]{:S(2)}) collective-permute-start(f32[128,64]{1,0:T(8,128)S(1)} %copy-done.14), channel_id=1, source_target_pairs={{1,0},{3,2},{5,4},{7,6},{9,8},{11,10},{13,12},{15,14},{17,16},{19,... | collective-permute-start | bytes 98312 | tf_op jit(solution)/shard_map/ppermute | solution.py:37
  171.4 67.4 %copy-start.4 = (f32[128,64]{1,0:T(8,128)}, f32[128,64]{1,0:T(8,128)S(1)}, u32[]{:S(2)}) copy-start(f32[128,64]{1,0:T(8,128)S(1)} %collective-permute-done.2.qyl_ref) | copy-start | bytes 98308
  171.6 67.2 %copy-start.5 = (f32[128,64]{1,0:T(8,128)}, f32[128,64]{1,0:T(8,128)S(1)}, u32[]{:S(2)}) copy-start(f32[128,64]{1,0:T(8,128)S(1)} %collective-permute-done.3.qyh_ref) | copy-start | bytes 98308
  221.9 16.8 %copy-start = (f32[128,256]{1,0:T(8,128)}, f32[128,256]{1,0:T(8,128)S(1)}, u32[]{:S(2)}) copy-start(f32[128,256]{1,0:T(8,128)S(1)} %collective-permute-done.qxl_ref) | copy-start | bytes 393220
  221.9 16.8 %copy-start.1 = (f32[128,256]{1,0:T(8,128)}, f32[128,256]{1,0:T(8,128)S(1)}, u32[]{:S(2)}) copy-start(f32[128,256]{1,0:T(8,128)S(1)} %collective-permute-done.1.qxh_ref) | copy-start | bytes 393220
  274.9 15.8 %collective-permute-start.4 = (f32[128,256]{1,0:T(8,128)}, f32[128,256]{1,0:T(8,128)S(1)}, u32[]{:S(2)}, u32[]{:S(2)}) collective-permute-start(f32[128,256]{1,0:T(8,128)} %get-tuple-element.41), channel_id=1, source_target_pairs={{0,2},{2,4},{4,6},{6,8},{8,10},{10,12},{12,14},{1,3},{3,5},{5,7},{... | collective-permute-start | bytes 393224 | tf_op jit(solution)/shard_map/ppermute | solution.py:34
  283.3 7.4 %collective-permute-start.5 = (f32[128,256]{1,0:T(8,128)}, f32[128,256]{1,0:T(8,128)S(1)}, u32[]{:S(2)}, u32[]{:S(2)}) collective-permute-start(f32[128,256]{1,0:T(8,128)} %get-tuple-element.42), channel_id=1, source_target_pairs={{2,0},{4,2},{6,4},{8,6},{10,8},{12,10},{14,12},{3,1},{5,3},{7,5},{... | collective-permute-start | bytes 393224 | tf_op jit(solution)/shard_map/ppermute | solution.py:35
  285.3 4.5 %collective-permute-start.6 = (f32[128,64]{1,0:T(8,128)}, f32[128,64]{1,0:T(8,128)S(1)}, u32[]{:S(2)}, u32[]{:S(2)}) collective-permute-start(f32[128,64]{1,0:T(8,128)} %get-tuple-element.43), channel_id=1, source_target_pairs={{0,1},{2,3},{4,5},{6,7},{8,9},{10,11},{12,13},{14,15},{16,17},{18,... | collective-permute-start | bytes 98312 | tf_op jit(solution)/shard_map/ppermute | solution.py:36
  286.6 4.2 %collective-permute-start.7 = (f32[128,64]{1,0:T(8,128)}, f32[128,64]{1,0:T(8,128)S(1)}, u32[]{:S(2)}, u32[]{:S(2)}) collective-permute-start(f32[128,64]{1,0:T(8,128)} %get-tuple-element.44), channel_id=1, source_target_pairs={{1,0},{3,2},{5,4},{7,6},{9,8},{11,10},{13,12},{15,14},{17,16},{19,... | collective-permute-start | bytes 98312 | tf_op jit(solution)/shard_map/ppermute | solution.py:37
  289.8 0.9 copy-start.6
  290.7 0.6 copy-start.7
  290.7 0.7 copy-start.2
  290.7 0.7 copy-start.3

commit v11 on v10

--- a/solution.py
+++ b/solution.py
@@ -158,10 +158,10 @@
     def side_perm(values, k):
         return jnp.where(inside_ref[k] > 0, permeability(values), 0.0)
 
-    kxl = side_perm(rim_ref[:, 0:1, :], 0)
-    kxh = side_perm(rim_ref[:, 1:2, :], 1)
-    kyl = to_columns(side_perm(rim_ref[:, 2, 0:nx], 2))
-    kyh = to_columns(side_perm(rim_ref[:, 3, 0:nx], 3))
+    kxl = side_perm(rim_ref[:, 0:1, :].astype(f32), 0)
+    kxh = side_perm(rim_ref[:, 1:2, :].astype(f32), 1)
+    kyl = to_columns(side_perm(rim_ref[:, 2, 0:nx].astype(f32), 2))
+    kyh = to_columns(side_perm(rim_ref[:, 3, 0:nx].astype(f32), 3))
 
     below = jnp.where(c == 0, 0.0, permeability(lpb_ref[...].astype(f32)))
     above = jnp.where(c == last, 0.0, permeability(lpa_ref[...].astype(f32)))
@@ -389,8 +389,9 @@
     ).astype(jnp.int32)
     edges = block_edges(pressure_start)
     flow, edges = lax.optimization_barrier((flow, edges))
+    rims, flow = lax.optimization_barrier((rims, flow))
     rims = lax.all_to_all(
-        rims, ("wide", "narrow"), split_axis=0, concat_axis=0, tiled=True,
+        rims.astype(jnp.bfloat16), ("wide", "narrow"), split_axis=0, concat_axis=0, tiled=True,
     ).reshape(depth, 4, rows_y)
     pressure = pressure_start
     stored = None

time: 325 us -> 322 us (level)
  blocking collectives: 119 us -> 15.6 us
  waiting for transfers between devices: 68.3 us -> 159 us
  starting transfers between devices: 30.1 us -> 37.8 us
    all_to_all x2 -> x1, blocking collectives: 119 us -> 15.6 us  [body(): lax.all_to_all(rims.astype(jnp.bfloat16), ('wide', 'narrow'), split_axis=...]
    all_to_all x0 -> x1, waiting for transfers between devices: none -> 78.6 us  [body(): lax.all_to_all(first.reshape(groups, planes, rows_x, rows_y), ('wide', 'n...]
    ppermute x2, waiting for transfers between devices: 50.3 us -> 62.1 us  [halos(): x_lo = lax.ppermute(last_x, 'wide', forward_w)]
    all_to_all x0 -> x1, starting transfers between devices: none -> 6.75 us  [body(): lax.all_to_all(first.reshape(groups, planes, rows_x, rows_y), ('wide', 'n...]
  transfers between devices with their start and end apart: 9 -> 10, of which waited for: 4 -> 5; matrix products, arithmetic and copies ran while one was open for 2% -> 2% of each run, Pallas kernels for 2% -> 2%
where the time goes in v11:
time: 322 us; the launch traced here: 320 us
  waiting for transfers between devices  159 us (49%)
  Pallas kernels  92.5 us (29%)
  starting transfers between devices  37.8 us (12%)
  blocking collectives  15.6 us (5%)
  matrix products  6.72 us (2%)
  local copies, waits for them, and re-layouts  5.53 us (2%)
    all_to_all x1, waiting for transfers between devices, body(): lax.all_to_all(first.reshape(groups, planes, rows_x, rows_y), ('wide', 'n...  78.6 us
    ppermute x2, waiting for transfers between devices, halos(): x_lo = lax.ppermute(last_x, 'wide', forward_w)  62.1 us
    pallas_call x1, Pallas kernels, advance(): pl.pallas_call(first_step_kernel, out_shape=tuple(out_shape + [full, full...  36 us
    pallas_call x1, Pallas kernels, advance(): pl.pallas_call(later_step_kernel, out_shape=tuple(out_shape), grid=grid,...  27.1 us
    all_to_all x1, waiting for transfers between devices, body(): lax.all_to_all(outgoing, ('wide', 'narrow'), split_axis=0, concat_axis=0,...  16.8 us
    all_to_all x1, blocking collectives, body(): lax.all_to_all(rims.astype(jnp.bfloat16), ('wide', 'narrow'), split_axis=...  15.6 us
    pallas_call x1, Pallas kernels, depth_transform(): pl.pallas_call(depth_kernel, out_shape=jax.ShapeDtypeStruct(noise.shape,...  13.6 us
    ppermute x2, starting transfers between devices, halos(): x_lo = lax.ppermute(last_x, 'wide', forward_w)  11.5 us
  transfers between devices with their start and end apart: 10, of which 5 were waited for; matrix products, arithmetic and copies ran while one was open for 2% of the time, Pallas kernels for 2%

profile of v11, /device:TPU:11, one launch (start us, length us, event | category | flops | bytes accessed | tf_op | source)
XLA Modules:
  0.0 319.7 jit_solution(3884366107155887890)
XLA Ops:
  0.6 13.6 %shard_map.104 = bf16[128,64,256]{2,1,0:T(8,128)(2,1)} custom-call(bf16[128,128]{1,0:T(8,128)(2,1)} %rz_ref.1, bf16[128,64,256]{2,1,0:T(8,128)(2,1)} %n_ref.1), custom_call_target="tpu_custom_call" | custom-call | tf_op jit(solution)/shard_map/pallas_call | solution.py:274
  14.2 0.0 copy-start.11
  14.2 6.8 %all-to-all-start = ((bf16[16,8,64,256]{3,2,1,0:T(8,128)(2,1)}), bf16[16,8,64,256]{3,2,1,0:T(8,128)(2,1)}, u32[]{:S(2)}, u32[]{:S(2)}) async-start(bf16[16,8,64,256]{3,2,1,0:T(8,128)(2,1)} %bitcast.10), calls=%async_computation | async-start | bytes 8388608 | tf_op jit(solution)/shard_map/all_to_all | solution.py:355
  21.0 4.9 %shard_map.106 = (f32[128,256]{1,0:T(8,128)}, f32[128,256]{1,0:T(8,128)}, f32[128,64]{1,0:T(8,128)}, f32[128,64]{1,0:T(8,128)}) custom-call(bf16[128,64,256]{2,1,0:T(8,128)(2,1)} %pa_ref.1), custom_call_target="tpu_custom_call" | custom-call | tf_op jit(solution)/shard_map/pallas_call | solution.py:111
  26.0 6.7 %fusion = f32[8192,256]{1,0:T(8,128)} fusion(f32[256]{0:T(256)S(1)} %get-tuple-element.50, s32[256]{0:T(256)S(1)} %multiply_add_fusion, s32[256]{0:T(256)S(1)} %get-tuple-element.51), kind=kOutput, calls=%fused_computation | convolution fusion | flops 6446710784 | bytes 8391680 | tf_op jit(solution)/shard_map/dot_general | solution.py:383
  32.7 78.6 %all-to-all-done.g_ref = bf16[16,8,64,256]{3,2,1,0:T(8,128)(2,1)} async-done(((bf16[16,8,64,256]{3,2,1,0:T(8,128)(2,1)}), bf16[16,8,64,256]{3,2,1,0:T(8,128)(2,1)}, u32[]{:S(2)}, u32[]{:S(2)}) %all-to-all-start) | async-done | bytes 4194336 | tf_op jit(solution)/shard_map/all_to_all | solution.py:355
  111.3 10.9 %shard_map.105 = (bf16[16,8,64,256]{3,2,1,0:T(8,128)(2,1)}, f32[16,8,4,256]{3,2,1,0:T(4,128)}) custom-call(bf16[16,8,64,256]{3,2,1,0:T(8,128)(2,1)} %all-to-all-done.g_ref, bf16[512,512]{1,0:T(8,128)(2,1)} %rx_ref.1, bf16[512,512]{1,0:T(8,128)(2,1)} %ry_ref.1), custom_call_target="tpu_custom_call" | custom-call | tf_op jit(solution)/shard_map/pallas_call | solution.py:335
  122.2 1.1 convert_element_type.8
  123.3 15.6 %all_to_all.15 = bf16[16,8,4,256]{3,2,1,0:T(4,128)(2,1)} all-to-all(bf16[16,8,4,256]{3,2,1,0:T(4,128)(2,1)S(1)} %convert_element_type.8), channel_id=1, replica_groups=mesh['member'=2,'wide'=8,'narrow'=2] {'wide','narrow'}, dimensions={0} | all-to-all | bytes 524288 | tf_op jit(solution)/shard_map/all_to_all | solution.py:393
  139.0 5.8 %all-to-all-start.1 = ((bf16[16,8,64,256]{3,2,1,0:T(8,128)(2,1)}), bf16[16,8,64,256]{3,2,1,0:T(8,128)(2,1)}, u32[]{:S(2)}, u32[]{:S(2)}) async-start(bf16[16,8,64,256]{3,2,1,0:T(8,128)(2,1)} %get-tuple-element.26), calls=%async_computation.1 | async-start | bytes 8388608 | tf_op jit(solution)/shard_map/all_to_all | solution.py:360
  144.7 3.1 collective-permute-start
  147.9 3.1 collective-permute-start.1
  151.0 1.3 collective-permute-start.2
  152.3 3.0 collective-permute-start.3
  155.3 0.7 add_convert_fusion.inside_ref
  156.0 0.2 collective-permute-done.3.qyh_ref
  156.2 62.1 %collective-permute-done.qxl_ref = f32[128,256]{1,0:T(8,128)S(1)} collective-permute-done((f32[128,256]{1,0:T(8,128)S(1)}, f32[128,256]{1,0:T(8,128)S(1)}, u32[]{:S(2)}, u32[]{:S(2)}) %collective-permute-start) | collective-permute-done | bytes 131104 | tf_op jit(solution)/shard_map/ppermute | solution.py:34
  218.2 0.0 collective-permute-done.1.qxh_ref
  218.3 16.8 %all-to-all-done.1 = bf16[16,8,64,256]{3,2,1,0:T(8,128)(2,1)} async-done(((bf16[16,8,64,256]{3,2,1,0:T(8,128)(2,1)}), bf16[16,8,64,256]{3,2,1,0:T(8,128)(2,1)}, u32[]{:S(2)}, u32[]{:S(2)}) %all-to-all-start.1) | async-done | bytes 4194336 | tf_op jit(solution)/shard_map/all_to_all | solution.py:360
  235.1 36.0 %shard_map.107 = (f32[128,64,256]{2,1,0:T(8,128)}, f32[128,256]{1,0:T(8,128)}, f32[128,256]{1,0:T(8,128)}, f32[128,64]{1,0:T(8,128)}, f32[128,64]{1,0:T(8,128)},...) custom-call(s32[4]{0:T(128)} %add_convert_fusion.inside_ref, ...), custom_call_target="tpu_custom_call" | custom-call | tf_op jit(solution)/shard_map/pallas_call | solution.py:240
  271.1 8.4 %collective-permute-start.4 = (f32[128,256]{1,0:T(8,128)}, f32[128,256]{1,0:T(8,128)S(1)}, u32[]{:S(2)}, u32[]{:S(2)}) collective-permute-start(f32[128,256]{1,0:T(8,128)} %get-tuple-element.45), channel_id=1, source_target_pairs={{0,2},{2,4},{4,6},{6,8},{8,10},{10,12},{12,14},{1,3},{3,5},{5,7},{... | collective-permute-start | bytes 393224 | tf_op jit(solution)/shard_map/ppermute | solution.py:34
  279.5 1.9 collective-permute-start.5
  281.4 1.5 collective-permute-start.6
  282.9 3.1 collective-permute-start.7
  286.0 1.1 collective-permute-done.7.qyh_ref
  287.1 0.0 collective-permute-done.4.qxl_ref
  287.1 0.0 copy-start.3
  287.1 0.6 copy-done.7
  287.7 0.0 copy-done.2
  287.7 0.0 copy-done.3
  287.8 27.1 %shard_map.108 = (f32[128,64,256]{2,1,0:T(8,128)}, f32[128,256]{1,0:T(8,128)}, f32[128,256]{1,0:T(8,128)}, f32[128,64]{1,0:T(8,128)}, f32[128,64]{1,0:T(8,128)}) custom-call(f32[128,64,256]{2,1,0:T(8,128)} %get-tuple-element.39.tzm_ref.tza_ref, f32[128,64,256]{2,1,0:T(8,128)} %get-tuple-element.39.tzm_ref.tza_ref, ...), custom_call_target="tpu_custom_call" | custom-call | tf_op jit(solution)/shard_map/pallas_call | solution.py:251
  314.9 4.8 %copy.12 = bf16[128,64,256]{2,1,0:T(8,128)(2,1)} copy(bf16[128,64,256]{2,1,0:T(8,128)(2,1)} %bitcast.1.lpm_ref.lpb_ref.lpa_ref) | data formatting | bytes 8388608
  (32 shorter events, 0.1 us)
Async XLA Ops:
  14.2 11.7 %copy-start.8 = (s32[256]{0:T(256)S(1)}, s32[256]{0:T(256)}, u32[]{:S(2)}) copy-start(s32[256]{0:T(256)} %param.14) | copy-start | bytes 3076
  14.2 11.7 %copy-start.9 = (s32[256]{0:T(256)S(1)}, s32[256]{0:T(256)}, u32[]{:S(2)}) copy-start(s32[256]{0:T(256)} %param.16) | copy-start | bytes 3076
  14.2 11.7 %copy-start.10 = (f32[256]{0:T(256)S(1)}, f32[256]{0:T(256)}, u32[]{:S(2)}) copy-start(f32[256]{0:T(256)} %param.17) | copy-start | bytes 3076
  14.2 11.7 %copy-start.11 = (s32[256]{0:T(256)S(1)}, s32[256]{0:T(256)}, u32[]{:S(2)}) copy-start(s32[256]{0:T(256)} %param.15) | copy-start | bytes 3076
  14.2 97.1 %all-to-all-start = ((bf16[16,8,64,256]{3,2,1,0:T(8,128)(2,1)}), bf16[16,8,64,256]{3,2,1,0:T(8,128)(2,1)}, u32[]{:S(2)}, u32[]{:S(2)}) async-start(bf16[16,8,64,256]{3,2,1,0:T(8,128)(2,1)} %bitcast.10), calls=%async_computation | async-start | bytes 8388608 | tf_op jit(solution)/shard_map/all_to_all | solution.py:355
  32.7 112.1 %copy-start.13 = (f32[128,256]{1,0:T(8,128)S(1)}, f32[128,256]{1,0:T(8,128)}, u32[]{:S(2)}) copy-start(f32[128,256]{1,0:T(8,128)} %get-tuple-element.34) | copy-start | bytes 393220
  32.7 115.2 %copy-start.12 = (f32[128,256]{1,0:T(8,128)S(1)}, f32[128,256]{1,0:T(8,128)}, u32[]{:S(2)}) copy-start(f32[128,256]{1,0:T(8,128)} %get-tuple-element.35) | copy-start | bytes 393220
  32.7 118.3 %copy-start.15 = (f32[128,64]{1,0:T(8,128)S(1)}, f32[128,64]{1,0:T(8,128)}, u32[]{:S(2)}) copy-start(f32[128,64]{1,0:T(8,128)} %get-tuple-element.36) | copy-start | bytes 98308
  32.7 119.6 %copy-start.14 = (f32[128,64]{1,0:T(8,128)S(1)}, f32[128,64]{1,0:T(8,128)}, u32[]{:S(2)}) copy-start(f32[128,64]{1,0:T(8,128)} %get-tuple-element.37) | copy-start | bytes 98308
  139.0 96.1 %all-to-all-start.1 = ((bf16[16,8,64,256]{3,2,1,0:T(8,128)(2,1)}), bf16[16,8,64,256]{3,2,1,0:T(8,128)(2,1)}, u32[]{:S(2)}, u32[]{:S(2)}) async-start(bf16[16,8,64,256]{3,2,1,0:T(8,128)(2,1)} %get-tuple-element.26), calls=%async_computation.1 | async-start | bytes 8388608 | tf_op jit(solution)/shard_map/all_to_all | solution.py:360
  144.7 73.5 %collective-permute-start = (f32[128,256]{1,0:T(8,128)S(1)}, f32[128,256]{1,0:T(8,128)S(1)}, u32[]{:S(2)}, u32[]{:S(2)}) collective-permute-start(f32[128,256]{1,0:T(8,128)S(1)} %copy-done.13), channel_id=1, source_target_pairs={{0,2},{2,4},{4,6},{6,8},{8,10},{10,12},{12,14},{1,3},{3,5},{5,7},{... | collective-permute-start | bytes 393224 | tf_op jit(solution)/shard_map/ppermute | solution.py:34
  147.9 70.4 %collective-permute-start.1 = (f32[128,256]{1,0:T(8,128)S(1)}, f32[128,256]{1,0:T(8,128)S(1)}, u32[]{:S(2)}, u32[]{:S(2)}) collective-permute-start(f32[128,256]{1,0:T(8,128)S(1)} %copy-done.12), channel_id=1, source_target_pairs={{2,0},{4,2},{6,4},{8,6},{10,8},{12,10},{14,12},{3,1},{5,3},{7,5},{... | collective-permute-start | bytes 393224 | tf_op jit(solution)/shard_map/ppermute | solution.py:35
  151.0 5.0 %collective-permute-start.2 = (f32[128,64]{1,0:T(8,128)S(1)}, f32[128,64]{1,0:T(8,128)S(1)}, u32[]{:S(2)}, u32[]{:S(2)}) collective-permute-start(f32[128,64]{1,0:T(8,128)S(1)} %copy-done.15), channel_id=1, source_target_pairs={{0,1},{2,3},{4,5},{6,7},{8,9},{10,11},{12,13},{14,15},{16,17},{18,... | collective-permute-start | bytes 98312 | tf_op jit(solution)/shard_map/ppermute | solution.py:36
  152.3 3.9 %collective-permute-start.3 = (f32[128,64]{1,0:T(8,128)S(1)}, f32[128,64]{1,0:T(8,128)S(1)}, u32[]{:S(2)}, u32[]{:S(2)}) collective-permute-start(f32[128,64]{1,0:T(8,128)S(1)} %copy-done.14), channel_id=1, source_target_pairs={{1,0},{3,2},{5,4},{7,6},{9,8},{11,10},{13,12},{15,14},{17,16},{19,... | collective-permute-start | bytes 98312 | tf_op jit(solution)/shard_map/ppermute | solution.py:37
  156.0 79.1 %copy-start.4 = (f32[128,64]{1,0:T(8,128)}, f32[128,64]{1,0:T(8,128)S(1)}, u32[]{:S(2)}) copy-start(f32[128,64]{1,0:T(8,128)S(1)} %collective-permute-done.2.qyl_ref) | copy-start | bytes 98308
  156.2 78.9 %copy-start.5 = (f32[128,64]{1,0:T(8,128)}, f32[128,64]{1,0:T(8,128)S(1)}, u32[]{:S(2)}) copy-start(f32[128,64]{1,0:T(8,128)S(1)} %collective-permute-done.3.qyh_ref) | copy-start | bytes 98308
  218.2 16.8 %copy-start = (f32[128,256]{1,0:T(8,128)}, f32[128,256]{1,0:T(8,128)S(1)}, u32[]{:S(2)}) copy-start(f32[128,256]{1,0:T(8,128)S(1)} %collective-permute-done.qxl_ref) | copy-start | bytes 393220
  218.3 16.8 %copy-start.1 = (f32[128,256]{1,0:T(8,128)}, f32[128,256]{1,0:T(8,128)S(1)}, u32[]{:S(2)}) copy-start(f32[128,256]{1,0:T(8,128)S(1)} %collective-permute-done.1.qxh_ref) | copy-start | bytes 393220
  271.1 15.9 %collective-permute-start.4 = (f32[128,256]{1,0:T(8,128)}, f32[128,256]{1,0:T(8,128)S(1)}, u32[]{:S(2)}, u32[]{:S(2)}) collective-permute-start(f32[128,256]{1,0:T(8,128)} %get-tuple-element.45), channel_id=1, source_target_pairs={{0,2},{2,4},{4,6},{6,8},{8,10},{10,12},{12,14},{1,3},{3,5},{5,7},{... | collective-permute-start | bytes 393224 | tf_op jit(solution)/shard_map/ppermute | solution.py:34
  279.5 7.6 %collective-permute-start.5 = (f32[128,256]{1,0:T(8,128)}, f32[128,256]{1,0:T(8,128)S(1)}, u32[]{:S(2)}, u32[]{:S(2)}) collective-permute-start(f32[128,256]{1,0:T(8,128)} %get-tuple-element.46), channel_id=1, source_target_pairs={{2,0},{4,2},{6,4},{8,6},{10,8},{12,10},{14,12},{3,1},{5,3},{7,5},{... | collective-permute-start | bytes 393224 | tf_op jit(solution)/shard_map/ppermute | solution.py:35
  281.4 4.5 %collective-permute-start.6 = (f32[128,64]{1,0:T(8,128)}, f32[128,64]{1,0:T(8,128)S(1)}, u32[]{:S(2)}, u32[]{:S(2)}) collective-permute-start(f32[128,64]{1,0:T(8,128)} %get-tuple-element.47), channel_id=1, source_target_pairs={{0,1},{2,3},{4,5},{6,7},{8,9},{10,11},{12,13},{14,15},{16,17},{18,... | collective-permute-start | bytes 98312 | tf_op jit(solution)/shard_map/ppermute | solution.py:36
  282.9 4.2 %collective-permute-start.7 = (f32[128,64]{1,0:T(8,128)}, f32[128,64]{1,0:T(8,128)S(1)}, u32[]{:S(2)}, u32[]{:S(2)}) collective-permute-start(f32[128,64]{1,0:T(8,128)} %get-tuple-element.48), channel_id=1, source_target_pairs={{1,0},{3,2},{5,4},{7,6},{9,8},{11,10},{13,12},{15,14},{17,16},{19,... | collective-permute-start | bytes 98312 | tf_op jit(solution)/shard_map/ppermute | solution.py:37
  286.0 1.1 copy-start.6
  287.1 0.6 copy-start.7
  287.1 0.7 copy-start.2
  287.1 0.7 copy-start.3

commit v12 on v9

--- a/solution.py
+++ b/solution.py
@@ -14,7 +14,7 @@
 CAP_LOG = 1.5
 CHUNK_Z = 16
 EDGE_Z = 32
-DEPTH_X = 32
+DEPTH_X = 16
 
 
 def permeability(values):
@@ -324,11 +324,6 @@
         first.reshape(groups, planes, rows_x, rows_y),
         ("wide", "narrow"), split_axis=0, concat_axis=0, tiled=True,
     )
-    outgoing = line_transforms(gathered, root_x, root_y, count_w, count_n)
-    log_perm = lax.all_to_all(
-        outgoing, ("wide", "narrow"), split_axis=0, concat_axis=0, tiled=True,
-    ).reshape(depth, rows_x, rows_y)
-
     wide_at = lax.axis_index("wide")
     narrow_at = lax.axis_index("narrow")
     last_w = lax.axis_size("wide") - 1
@@ -356,7 +351,12 @@
         [wide_at > 0, wide_at < last_w, narrow_at > 0, narrow_at < last_n]
     ).astype(jnp.int32)
     edges = block_edges(pressure_start)
-    flow, edges = lax.optimization_barrier((flow, edges))
+    gathered, flow, edges = lax.optimization_barrier((gathered, flow, edges))
+    outgoing = line_transforms(gathered, root_x, root_y, count_w, count_n)
+    log_perm = lax.all_to_all(
+        outgoing, ("wide", "narrow"), split_axis=0, concat_axis=0, tiled=True,
+    ).reshape(depth, rows_x, rows_y)
+
     *lp_edges, log_perm = block_edges(log_perm, keep=True)
     perm_halos = halos(lp_edges)
     pressure = pressure_start

time: 318 us -> 316 us (level)
  blocking collectives: 99.5 us -> 0 us
  waiting for transfers between devices: 69.4 us -> 160 us
  starting transfers between devices: 38 us -> 46.9 us
    all_to_all x1 -> x0, blocking collectives: 99.5 us -> none  [body(): lax.all_to_all(first.reshape(groups, planes, rows_x, rows_y), ('wide', 'n...]
    all_to_all x0 -> x1, waiting for transfers between devices: none -> 78.6 us  [body(): lax.all_to_all(first.reshape(groups, planes, rows_x, rows_y), ('wide', 'n...]
    all_to_all x1, waiting for transfers between devices: 68 us -> 79.8 us  [body(): lax.all_to_all(outgoing, ('wide', 'narrow'), split_axis=0, concat_axis=0,...]
    all_to_all x0 -> x1, starting transfers between devices: none -> 6.75 us  [body(): lax.all_to_all(first.reshape(groups, planes, rows_x, rows_y), ('wide', 'n...]
  transfers between devices with their start and end apart: 13 -> 14, of which waited for: 3 -> 4; matrix products, arithmetic and copies ran while one was open for 2% -> 2% of each run, Pallas kernels for 3% -> 3%
where the time goes in v12:
time: 316 us; the launch traced here: 314 us
  waiting for transfers between devices  160 us (51%)
  Pallas kernels  97.4 us (31%)
  starting transfers between devices  46.9 us (15%)
  matrix products  6.74 us (2%)
    all_to_all x1, waiting for transfers between devices, body(): lax.all_to_all(outgoing, ('wide', 'narrow'), split_axis=0, concat_axis=0,...  79.8 us
    all_to_all x1, waiting for transfers between devices, body(): lax.all_to_all(first.reshape(groups, planes, rows_x, rows_y), ('wide', 'n...  78.6 us
    pallas_call x1, Pallas kernels, advance(): pl.pallas_call(first_step_kernel, out_shape=tuple(out_shape + [full, full...  36.3 us
    pallas_call x1, Pallas kernels, advance(): pl.pallas_call(later_step_kernel, out_shape=tuple(out_shape), grid=grid,...  27 us
    pallas_call x1, Pallas kernels, depth_transform(): pl.pallas_call(depth_kernel, out_shape=jax.ShapeDtypeStruct(noise.shape,...  13.6 us
    ppermute x3, starting transfers between devices, halos(): x_lo = lax.ppermute(last_x, 'wide', forward_w)  12.1 us
    pallas_call x2, Pallas kernels, block_edges(): pl.pallas_call(edge_kernel, out_shape=tuple(out_shape), grid=(depth // tz...  10.9 us
    pallas_call x1, Pallas kernels, line_transforms(): pl.pallas_call(functools.partial(line_kernel, count_w=count_w, count_n=co...  9.68 us
  transfers between devices with their start and end apart: 14, of which 4 were waited for; matrix products, arithmetic and copies ran while one was open for 2% of the time, Pallas kernels for 3%

profile of v12, /device:TPU:11, one launch (start us, length us, event | category | flops | bytes accessed | tf_op | source)
XLA Modules:
  0.0 314.0 jit_solution(9036925528117627114)
XLA Ops:
  0.6 13.6 %shard_map.104 = bf16[128,64,256]{2,1,0:T(8,128)(2,1)} custom-call(bf16[128,128]{1,0:T(8,128)(2,1)} %rz_ref.1, bf16[128,64,256]{2,1,0:T(8,128)(2,1)} %n_ref.1), custom_call_target="tpu_custom_call" | custom-call | tf_op jit(solution)/shard_map/pallas_call | solution.py:273
  14.2 6.8 %all-to-all-start = ((bf16[16,8,64,256]{3,2,1,0:T(8,128)(2,1)}), bf16[16,8,64,256]{3,2,1,0:T(8,128)(2,1)}, u32[]{:S(2)}, u32[]{:S(2)}) async-start(bf16[16,8,64,256]{3,2,1,0:T(8,128)(2,1)} %bitcast.9), calls=%async_computation | async-start | bytes 8388608 | tf_op jit(solution)/shard_map/all_to_all | solution.py:323
  21.0 4.9 %shard_map.105 = (f32[128,256]{1,0:T(8,128)}, f32[128,256]{1,0:T(8,128)}, f32[128,64]{1,0:T(8,128)}, f32[128,64]{1,0:T(8,128)}) custom-call(bf16[128,64,256]{2,1,0:T(8,128)(2,1)} %pa_ref.1), custom_call_target="tpu_custom_call" | custom-call | tf_op jit(solution)/shard_map/pallas_call | solution.py:111
  26.0 6.7 %fusion = f32[8192,256]{1,0:T(8,128)} fusion(f32[256]{0:T(256)S(1)} %get-tuple-element.54, s32[256]{0:T(256)S(1)} %multiply_add_fusion, s32[256]{0:T(256)S(1)} %get-tuple-element.55), kind=kOutput, calls=%fused_computation | convolution fusion | flops 6446710784 | bytes 8391680 | tf_op jit(solution)/shard_map/dot_general | solution.py:346
  32.7 78.6 %all-to-all-done.g_ref = bf16[16,8,64,256]{3,2,1,0:T(8,128)(2,1)} async-done(((bf16[16,8,64,256]{3,2,1,0:T(8,128)(2,1)}), bf16[16,8,64,256]{3,2,1,0:T(8,128)(2,1)}, u32[]{:S(2)}, u32[]{:S(2)}) %all-to-all-start) | async-done | bytes 4194336 | tf_op jit(solution)/shard_map/all_to_all | solution.py:323
  111.3 9.7 %shard_map.106 = bf16[16,8,64,256]{3,2,1,0:T(8,128)(2,1)} custom-call(bf16[16,8,64,256]{3,2,1,0:T(8,128)(2,1)} %all-to-all-done.g_ref, bf16[512,512]{1,0:T(8,128)(2,1)} %rx_ref.1, bf16[512,512]{1,0:T(8,128)(2,1)} %ry_ref.1), custom_call_target="tpu_custom_call" | custom-call | tf_op jit(solution)/shard_map/pallas_call | solution.py:306
  121.0 7.1 %all-to-all-start.1 = ((bf16[16,8,64,256]{3,2,1,0:T(8,128)(2,1)}), bf16[16,8,64,256]{3,2,1,0:T(8,128)(2,1)}, u32[]{:S(2)}, u32[]{:S(2)}) async-start(bf16[16,8,64,256]{3,2,1,0:T(8,128)(2,1)} %shard_map.106), calls=%async_computation.1 | async-start | bytes 8388608 | tf_op jit(solution)/shard_map/all_to_all | solution.py:356
  128.0 3.1 collective-permute-start.4
  131.2 1.3 collective-permute-start.6
  132.5 3.0 collective-permute-start.7
  135.5 3.1 collective-permute-start.5
  138.6 79.8 %all-to-all-done.1 = bf16[16,8,64,256]{3,2,1,0:T(8,128)(2,1)} async-done(((bf16[16,8,64,256]{3,2,1,0:T(8,128)(2,1)}), bf16[16,8,64,256]{3,2,1,0:T(8,128)(2,1)}, u32[]{:S(2)}, u32[]{:S(2)}) %all-to-all-start.1) | async-done | bytes 4194336 | tf_op jit(solution)/shard_map/all_to_all | solution.py:356
  218.4 5.9 %shard_map.107 = (f32[128,256]{1,0:T(8,128)}, f32[128,256]{1,0:T(8,128)}, f32[128,64]{1,0:T(8,128)}, f32[128,64]{1,0:T(8,128)}, bf16[128,64,256]{2,1,0:T(8,128)(2,1)}) custom-call(bf16[128,64,256]{2,1,0:T(8,128)(2,1)} %bitcast.2.block_ref), custom_call_target="tpu_custom_call" | custom-call | tf_op jit(solution)/shard_map/pallas_call | solution.py:111
  224.3 5.7 %collective-permute-start = (f32[128,256]{1,0:T(8,128)}, f32[128,256]{1,0:T(8,128)S(1)}, u32[]{:S(2)}, u32[]{:S(2)}) collective-permute-start(f32[128,256]{1,0:T(8,128)} %get-tuple-element.34), channel_id=1, source_target_pairs={{0,2},{2,4},{4,6},{6,8},{8,10},{10,12},{12,14},{1,3},{3,5},{5,7},{... | collective-permute-start | bytes 393224 | tf_op jit(solution)/shard_map/ppermute | solution.py:34
  230.0 1.9 collective-permute-start.1
  232.0 1.3 collective-permute-start.2
  233.3 3.2 %collective-permute-start.3 = (f32[128,64]{1,0:T(8,128)}, f32[128,64]{1,0:T(8,128)S(1)}, u32[]{:S(2)}, u32[]{:S(2)}) collective-permute-start(f32[128,64]{1,0:T(8,128)} %get-tuple-element.37), channel_id=1, source_target_pairs={{1,0},{3,2},{5,4},{7,6},{9,8},{11,10},{13,12},{15,14},{17,16},{19,... | collective-permute-start | bytes 98312 | tf_op jit(solution)/shard_map/ppermute | solution.py:37
  236.5 0.7 add_convert_fusion.inside_ref
  237.2 0.2 collective-permute-done.3.lyh_ref
  237.5 0.4 copy-done.1
  237.9 0.2 copy-done.9
  238.1 0.1 copy-done.2
  238.1 36.3 %shard_map.108 = (f32[128,64,256]{2,1,0:T(8,128)}, f32[128,256]{1,0:T(8,128)}, f32[128,256]{1,0:T(8,128)}, f32[128,64]{1,0:T(8,128)}, f32[128,64]{1,0:T(8,128)},...) custom-call(s32[4]{0:T(128)} %add_convert_fusion.inside_ref, ...), custom_call_target="tpu_custom_call" | custom-call | tf_op jit(solution)/shard_map/pallas_call | solution.py:240
  274.4 3.4 %collective-permute-start.8 = (f32[128,256]{1,0:T(8,128)}, f32[128,256]{1,0:T(8,128)S(1)}, u32[]{:S(2)}, u32[]{:S(2)}) collective-permute-start(f32[128,256]{1,0:T(8,128)} %get-tuple-element.49), channel_id=1, source_target_pairs={{0,2},{2,4},{4,6},{6,8},{8,10},{10,12},{12,14},{1,3},{3,5},{5,7},{... | collective-permute-start | bytes 393224 | tf_op jit(solution)/shard_map/ppermute | solution.py:34
  277.8 2.8 collective-permute-start.9
  280.6 1.3 collective-permute-start.10
  281.9 3.0 collective-permute-start.11
  285.0 1.1 collective-permute-done.11.qyh_ref
  286.1 0.6 copy-done.11
  286.7 0.1 copy-done.4
  286.8 0.1 copy-done.5
  286.8 27.0 %shard_map.109 = (f32[128,64,256]{2,1,0:T(8,128)}, f32[128,256]{1,0:T(8,128)}, f32[128,256]{1,0:T(8,128)}, f32[128,64]{1,0:T(8,128)}, f32[128,64]{1,0:T(8,128)}) custom-call(f32[128,64,256]{2,1,0:T(8,128)} %get-tuple-element.43.tzm_ref.tza_ref, f32[128,64,256]{2,1,0:T(8,128)} %get-tuple-element.43.tzm_ref.tza_ref, ...), custom_call_target="tpu_custom_call" | custom-call | tf_op jit(solution)/shard_map/pallas_call | solution.py:250
  (46 shorter events, 0.2 us)
Async XLA Ops:
  14.2 11.7 %copy-start.12 = (s32[256]{0:T(256)S(1)}, s32[256]{0:T(256)}, u32[]{:S(2)}) copy-start(s32[256]{0:T(256)} %param.14) | copy-start | bytes 3076
  14.2 11.7 %copy-start.13 = (s32[256]{0:T(256)S(1)}, s32[256]{0:T(256)}, u32[]{:S(2)}) copy-start(s32[256]{0:T(256)} %param.16) | copy-start | bytes 3076
  14.2 11.7 %copy-start.14 = (f32[256]{0:T(256)S(1)}, f32[256]{0:T(256)}, u32[]{:S(2)}) copy-start(f32[256]{0:T(256)} %param.17) | copy-start | bytes 3076
  14.2 11.7 %copy-start.15 = (s32[256]{0:T(256)S(1)}, s32[256]{0:T(256)}, u32[]{:S(2)}) copy-start(s32[256]{0:T(256)} %param.15) | copy-start | bytes 3076
  14.2 97.1 %all-to-all-start = ((bf16[16,8,64,256]{3,2,1,0:T(8,128)(2,1)}), bf16[16,8,64,256]{3,2,1,0:T(8,128)(2,1)}, u32[]{:S(2)}, u32[]{:S(2)}) async-start(bf16[16,8,64,256]{3,2,1,0:T(8,128)(2,1)} %bitcast.9), calls=%async_computation | async-start | bytes 8388608 | tf_op jit(solution)/shard_map/all_to_all | solution.py:323
  111.3 16.8 %copy-start.17 = (f32[128,256]{1,0:T(8,128)S(1)}, f32[128,256]{1,0:T(8,128)}, u32[]{:S(2)}) copy-start(f32[128,256]{1,0:T(8,128)} %get-tuple-element.38) | copy-start | bytes 393220
  111.3 19.9 %copy-start.19 = (f32[128,64]{1,0:T(8,128)S(1)}, f32[128,64]{1,0:T(8,128)}, u32[]{:S(2)}) copy-start(f32[128,64]{1,0:T(8,128)} %get-tuple-element.40) | copy-start | bytes 98308
  111.3 21.2 %copy-start.18 = (f32[128,64]{1,0:T(8,128)S(1)}, f32[128,64]{1,0:T(8,128)}, u32[]{:S(2)}) copy-start(f32[128,64]{1,0:T(8,128)} %get-tuple-element.41) | copy-start | bytes 98308
  111.3 24.2 %copy-start.16 = (f32[128,256]{1,0:T(8,128)S(1)}, f32[128,256]{1,0:T(8,128)}, u32[]{:S(2)}) copy-start(f32[128,256]{1,0:T(8,128)} %get-tuple-element.39) | copy-start | bytes 393220
  121.0 97.4 %all-to-all-start.1 = ((bf16[16,8,64,256]{3,2,1,0:T(8,128)(2,1)}), bf16[16,8,64,256]{3,2,1,0:T(8,128)(2,1)}, u32[]{:S(2)}, u32[]{:S(2)}) async-start(bf16[16,8,64,256]{3,2,1,0:T(8,128)(2,1)} %shard_map.106), calls=%async_computation.1 | async-start | bytes 8388608 | tf_op jit(solution)/shard_map/all_to_all | solution.py:356
  128.0 105.2 %collective-permute-start.4 = (f32[128,256]{1,0:T(8,128)S(1)}, f32[128,256]{1,0:T(8,128)S(1)}, u32[]{:S(2)}, u32[]{:S(2)}) collective-permute-start(f32[128,256]{1,0:T(8,128)S(1)} %copy-done.17), channel_id=1, source_target_pairs={{0,2},{2,4},{4,6},{6,8},{8,10},{10,12},{12,14},{1,3},{3,5},{5,7},{... | collective-permute-start | bytes 393224 | tf_op jit(solution)/shard_map/ppermute | solution.py:34
  131.2 98.8 %collective-permute-start.6 = (f32[128,64]{1,0:T(8,128)S(1)}, f32[128,64]{1,0:T(8,128)S(1)}, u32[]{:S(2)}, u32[]{:S(2)}) collective-permute-start(f32[128,64]{1,0:T(8,128)S(1)} %copy-done.19), channel_id=1, source_target_pairs={{0,1},{2,3},{4,5},{6,7},{8,9},{10,11},{12,13},{14,15},{16,17},{18,... | collective-permute-start | bytes 98312 | tf_op jit(solution)/shard_map/ppermute | solution.py:36
  132.5 99.5 %collective-permute-start.7 = (f32[128,64]{1,0:T(8,128)S(1)}, f32[128,64]{1,0:T(8,128)S(1)}, u32[]{:S(2)}, u32[]{:S(2)}) collective-permute-start(f32[128,64]{1,0:T(8,128)S(1)} %copy-done.18), channel_id=1, source_target_pairs={{1,0},{3,2},{5,4},{7,6},{9,8},{11,10},{13,12},{15,14},{17,16},{19,... | collective-permute-start | bytes 98312 | tf_op jit(solution)/shard_map/ppermute | solution.py:37
  135.5 101.7 %collective-permute-start.5 = (f32[128,256]{1,0:T(8,128)S(1)}, f32[128,256]{1,0:T(8,128)S(1)}, u32[]{:S(2)}, u32[]{:S(2)}) collective-permute-start(f32[128,256]{1,0:T(8,128)S(1)} %copy-done.16), channel_id=1, source_target_pairs={{2,0},{4,2},{6,4},{8,6},{10,8},{12,10},{14,12},{3,1},{5,3},{7,5},{... | collective-permute-start | bytes 393224 | tf_op jit(solution)/shard_map/ppermute | solution.py:35
  224.3 13.1 %collective-permute-start = (f32[128,256]{1,0:T(8,128)}, f32[128,256]{1,0:T(8,128)S(1)}, u32[]{:S(2)}, u32[]{:S(2)}) collective-permute-start(f32[128,256]{1,0:T(8,128)} %get-tuple-element.34), channel_id=1, source_target_pairs={{0,2},{2,4},{4,6},{6,8},{8,10},{10,12},{12,14},{1,3},{3,5},{5,7},{... | collective-permute-start | bytes 393224 | tf_op jit(solution)/shard_map/ppermute | solution.py:34
  230.0 7.5 %copy-start.6 = (f32[128,64]{1,0:T(8,128)}, f32[128,64]{1,0:T(8,128)S(1)}, u32[]{:S(2)}) copy-start(f32[128,64]{1,0:T(8,128)S(1)} %collective-permute-done.6.qyl_ref) | copy-start | bytes 98308
  230.0 7.4 %collective-permute-start.1 = (f32[128,256]{1,0:T(8,128)}, f32[128,256]{1,0:T(8,128)S(1)}, u32[]{:S(2)}, u32[]{:S(2)}) collective-permute-start(f32[128,256]{1,0:T(8,128)} %get-tuple-element.35), channel_id=1, source_target_pairs={{2,0},{4,2},{6,4},{8,6},{10,8},{12,10},{14,12},{3,1},{5,3},{7,5},{... | collective-permute-start | bytes 393224 | tf_op jit(solution)/shard_map/ppermute | solution.py:35
  232.0 5.5 %copy-start.7 = (f32[128,64]{1,0:T(8,128)}, f32[128,64]{1,0:T(8,128)S(1)}, u32[]{:S(2)}) copy-start(f32[128,64]{1,0:T(8,128)S(1)} %collective-permute-done.7.qyh_ref) | copy-start | bytes 98308
  232.0 5.2 %collective-permute-start.2 = (f32[128,64]{1,0:T(8,128)}, f32[128,64]{1,0:T(8,128)S(1)}, u32[]{:S(2)}, u32[]{:S(2)}) collective-permute-start(f32[128,64]{1,0:T(8,128)} %get-tuple-element.36), channel_id=1, source_target_pairs={{0,1},{2,3},{4,5},{6,7},{8,9},{10,11},{12,13},{14,15},{16,17},{18,... | collective-permute-start | bytes 98312 | tf_op jit(solution)/shard_map/ppermute | solution.py:36
  233.3 4.2 %copy-start = (f32[128,256]{1,0:T(8,128)}, f32[128,256]{1,0:T(8,128)S(1)}, u32[]{:S(2)}) copy-start(f32[128,256]{1,0:T(8,128)S(1)} %collective-permute-done.4.qxl_ref) | copy-start | bytes 393220
  233.3 4.1 %collective-permute-start.3 = (f32[128,64]{1,0:T(8,128)}, f32[128,64]{1,0:T(8,128)S(1)}, u32[]{:S(2)}, u32[]{:S(2)}) collective-permute-start(f32[128,64]{1,0:T(8,128)} %get-tuple-element.37), channel_id=1, source_target_pairs={{1,0},{3,2},{5,4},{7,6},{9,8},{11,10},{13,12},{15,14},{17,16},{19,... | collective-permute-start | bytes 98312 | tf_op jit(solution)/shard_map/ppermute | solution.py:37
  237.2 0.7 copy-start.1
  237.2 0.7 copy-start.8
  237.4 0.7 copy-start.2
  237.4 0.7 copy-start.3
  274.4 11.6 %collective-permute-start.8 = (f32[128,256]{1,0:T(8,128)}, f32[128,256]{1,0:T(8,128)S(1)}, u32[]{:S(2)}, u32[]{:S(2)}) collective-permute-start(f32[128,256]{1,0:T(8,128)} %get-tuple-element.49), channel_id=1, source_target_pairs={{0,2},{2,4},{4,6},{6,8},{8,10},{10,12},{12,14},{1,3},{3,5},{5,7},{... | collective-permute-start | bytes 393224 | tf_op jit(solution)/shard_map/ppermute | solution.py:34
  277.8 8.3 %collective-permute-start.9 = (f32[128,256]{1,0:T(8,128)}, f32[128,256]{1,0:T(8,128)S(1)}, u32[]{:S(2)}, u32[]{:S(2)}) collective-permute-start(f32[128,256]{1,0:T(8,128)} %get-tuple-element.50), channel_id=1, source_target_pairs={{2,0},{4,2},{6,4},{8,6},{10,8},{12,10},{14,12},{3,1},{5,3},{7,5},{... | collective-permute-start | bytes 393224 | tf_op jit(solution)/shard_map/ppermute | solution.py:35
  280.6 4.3 %collective-permute-start.10 = (f32[128,64]{1,0:T(8,128)}, f32[128,64]{1,0:T(8,128)S(1)}, u32[]{:S(2)}, u32[]{:S(2)}) collective-permute-start(f32[128,64]{1,0:T(8,128)} %get-tuple-element.51), channel_id=1, source_target_pairs={{0,1},{2,3},{4,5},{6,7},{8,9},{10,11},{12,13},{14,15},{16,17},{18,... | collective-permute-start | bytes 98312 | tf_op jit(solution)/shard_map/ppermute | solution.py:36
  281.9 4.1 %collective-permute-start.11 = (f32[128,64]{1,0:T(8,128)}, f32[128,64]{1,0:T(8,128)S(1)}, u32[]{:S(2)}, u32[]{:S(2)}) collective-permute-start(f32[128,64]{1,0:T(8,128)} %get-tuple-element.52), channel_id=1, source_target_pairs={{1,0},{3,2},{5,4},{7,6},{9,8},{11,10},{13,12},{15,14},{17,16},{19,... | collective-permute-start | bytes 98312 | tf_op jit(solution)/shard_map/ppermute | solution.py:37
  285.0 1.1 copy-start.10
  286.1 0.7 copy-start.4
  286.1 0.7 copy-start.5
  (2 other events, 1.2 us)

commit v13 on v12

--- a/solution.py
+++ b/solution.py
@@ -12,7 +12,7 @@
 
 STEP_SIZE = 0.03
 CAP_LOG = 1.5
-CHUNK_Z = 16
+CHUNK_Z = 32
 EDGE_Z = 32
 DEPTH_X = 16
 

time: 316 us -> 317 us (level)
  no operation moved by 1% of the time
where the time goes in v13:
time: 317 us; the launch traced here: 315 us
  waiting for transfers between devices  159 us (50%)
  Pallas kernels  98.2 us (31%)
  starting transfers between devices  47.1 us (15%)
  matrix products  6.74 us (2%)
    all_to_all x1, waiting for transfers between devices, body(): lax.all_to_all(outgoing, ('wide', 'narrow'), split_axis=0, concat_axis=0,...  79.8 us
    all_to_all x1, waiting for transfers between devices, body(): lax.all_to_all(first.reshape(groups, planes, rows_x, rows_y), ('wide', 'n...  78.6 us
    pallas_call x1, Pallas kernels, advance(): pl.pallas_call(first_step_kernel, out_shape=tuple(out_shape + [full, full...  36.1 us
    pallas_call x1, Pallas kernels, advance(): pl.pallas_call(later_step_kernel, out_shape=tuple(out_shape), grid=grid,...  28 us
    pallas_call x1, Pallas kernels, depth_transform(): pl.pallas_call(depth_kernel, out_shape=jax.ShapeDtypeStruct(noise.shape,...  13.6 us
    ppermute x3, starting transfers between devices, halos(): x_lo = lax.ppermute(last_x, 'wide', forward_w)  12.1 us
    pallas_call x2, Pallas kernels, block_edges(): pl.pallas_call(edge_kernel, out_shape=tuple(out_shape), grid=(depth // tz...  10.9 us
    pallas_call x1, Pallas kernels, line_transforms(): pl.pallas_call(functools.partial(line_kernel, count_w=count_w, count_n=co...  9.68 us
  transfers between devices with their start and end apart: 14, of which 4 were waited for; matrix products, arithmetic and copies ran while one was open for 2% of the time, Pallas kernels for 3%

profile of v13, /device:TPU:11, one launch (start us, length us, event | category | flops | bytes accessed | tf_op | source)
XLA Modules:
  0.0 314.9 jit_solution(16505411624410542023)
XLA Ops:
  0.6 13.6 %shard_map.104 = bf16[128,64,256]{2,1,0:T(8,128)(2,1)} custom-call(bf16[128,128]{1,0:T(8,128)(2,1)} %rz_ref.1, bf16[128,64,256]{2,1,0:T(8,128)(2,1)} %n_ref.1), custom_call_target="tpu_custom_call" | custom-call | tf_op jit(solution)/shard_map/pallas_call | solution.py:273
  14.2 6.8 %all-to-all-start = ((bf16[16,8,64,256]{3,2,1,0:T(8,128)(2,1)}), bf16[16,8,64,256]{3,2,1,0:T(8,128)(2,1)}, u32[]{:S(2)}, u32[]{:S(2)}) async-start(bf16[16,8,64,256]{3,2,1,0:T(8,128)(2,1)} %bitcast.9), calls=%async_computation | async-start | bytes 8388608 | tf_op jit(solution)/shard_map/all_to_all | solution.py:323
  21.0 4.9 %shard_map.105 = (f32[128,256]{1,0:T(8,128)}, f32[128,256]{1,0:T(8,128)}, f32[128,64]{1,0:T(8,128)}, f32[128,64]{1,0:T(8,128)}) custom-call(bf16[128,64,256]{2,1,0:T(8,128)(2,1)} %pa_ref.1), custom_call_target="tpu_custom_call" | custom-call | tf_op jit(solution)/shard_map/pallas_call | solution.py:111
  26.0 6.7 %fusion = f32[8192,256]{1,0:T(8,128)} fusion(f32[256]{0:T(256)S(1)} %get-tuple-element.54, s32[256]{0:T(256)S(1)} %multiply_add_fusion, s32[256]{0:T(256)S(1)} %get-tuple-element.55), kind=kOutput, calls=%fused_computation | convolution fusion | flops 6446710784 | bytes 8391680 | tf_op jit(solution)/shard_map/dot_general | solution.py:346
  32.7 78.6 %all-to-all-done.g_ref = bf16[16,8,64,256]{3,2,1,0:T(8,128)(2,1)} async-done(((bf16[16,8,64,256]{3,2,1,0:T(8,128)(2,1)}), bf16[16,8,64,256]{3,2,1,0:T(8,128)(2,1)}, u32[]{:S(2)}, u32[]{:S(2)}) %all-to-all-start) | async-done | bytes 4194336 | tf_op jit(solution)/shard_map/all_to_all | solution.py:323
  111.3 9.7 %shard_map.106 = bf16[16,8,64,256]{3,2,1,0:T(8,128)(2,1)} custom-call(bf16[16,8,64,256]{3,2,1,0:T(8,128)(2,1)} %all-to-all-done.g_ref, bf16[512,512]{1,0:T(8,128)(2,1)} %rx_ref.1, bf16[512,512]{1,0:T(8,128)(2,1)} %ry_ref.1), custom_call_target="tpu_custom_call" | custom-call | tf_op jit(solution)/shard_map/pallas_call | solution.py:306
  121.0 7.1 %all-to-all-start.1 = ((bf16[16,8,64,256]{3,2,1,0:T(8,128)(2,1)}), bf16[16,8,64,256]{3,2,1,0:T(8,128)(2,1)}, u32[]{:S(2)}, u32[]{:S(2)}) async-start(bf16[16,8,64,256]{3,2,1,0:T(8,128)(2,1)} %shard_map.106), calls=%async_computation.1 | async-start | bytes 8388608 | tf_op jit(solution)/shard_map/all_to_all | solution.py:356
  128.0 3.1 collective-permute-start.4
  131.2 1.3 collective-permute-start.6
  132.5 3.0 collective-permute-start.7
  135.5 3.1 collective-permute-start.5
  138.6 79.8 %all-to-all-done.1 = bf16[16,8,64,256]{3,2,1,0:T(8,128)(2,1)} async-done(((bf16[16,8,64,256]{3,2,1,0:T(8,128)(2,1)}), bf16[16,8,64,256]{3,2,1,0:T(8,128)(2,1)}, u32[]{:S(2)}, u32[]{:S(2)}) %all-to-all-start.1) | async-done | bytes 4194336 | tf_op jit(solution)/shard_map/all_to_all | solution.py:356
  218.4 5.9 %shard_map.107 = (f32[128,256]{1,0:T(8,128)}, f32[128,256]{1,0:T(8,128)}, f32[128,64]{1,0:T(8,128)}, f32[128,64]{1,0:T(8,128)}, bf16[128,64,256]{2,1,0:T(8,128)(2,1)}) custom-call(bf16[128,64,256]{2,1,0:T(8,128)(2,1)} %bitcast.2.block_ref), custom_call_target="tpu_custom_call" | custom-call | tf_op jit(solution)/shard_map/pallas_call | solution.py:111
  224.3 5.7 %collective-permute-start = (f32[128,256]{1,0:T(8,128)}, f32[128,256]{1,0:T(8,128)S(1)}, u32[]{:S(2)}, u32[]{:S(2)}) collective-permute-start(f32[128,256]{1,0:T(8,128)} %get-tuple-element.34), channel_id=1, source_target_pairs={{0,2},{2,4},{4,6},{6,8},{8,10},{10,12},{12,14},{1,3},{3,5},{5,7},{... | collective-permute-start | bytes 393224 | tf_op jit(solution)/shard_map/ppermute | solution.py:34
  230.0 1.9 collective-permute-start.1
  232.0 1.3 collective-permute-start.2
  233.3 3.2 %collective-permute-start.3 = (f32[128,64]{1,0:T(8,128)}, f32[128,64]{1,0:T(8,128)S(1)}, u32[]{:S(2)}, u32[]{:S(2)}) collective-permute-start(f32[128,64]{1,0:T(8,128)} %get-tuple-element.37), channel_id=1, source_target_pairs={{1,0},{3,2},{5,4},{7,6},{9,8},{11,10},{13,12},{15,14},{17,16},{19,... | collective-permute-start | bytes 98312 | tf_op jit(solution)/shard_map/ppermute | solution.py:37
  236.5 0.7 add_convert_fusion.inside_ref
  237.2 0.2 collective-permute-done.3.lyh_ref
  237.5 0.4 copy-done.1
  237.9 0.2 copy-done.9
  238.1 0.1 copy-done.2
  238.1 36.1 %shard_map.108 = (f32[128,64,256]{2,1,0:T(8,128)}, f32[128,256]{1,0:T(8,128)}, f32[128,256]{1,0:T(8,128)}, f32[128,64]{1,0:T(8,128)}, f32[128,64]{1,0:T(8,128)},...) custom-call(s32[4]{0:T(128)} %add_convert_fusion.inside_ref, ...), custom_call_target="tpu_custom_call" | custom-call | tf_op jit(solution)/shard_map/pallas_call | solution.py:240
  274.3 3.4 %collective-permute-start.8 = (f32[128,256]{1,0:T(8,128)}, f32[128,256]{1,0:T(8,128)S(1)}, u32[]{:S(2)}, u32[]{:S(2)}) collective-permute-start(f32[128,256]{1,0:T(8,128)} %get-tuple-element.49), channel_id=1, source_target_pairs={{0,2},{2,4},{4,6},{6,8},{8,10},{10,12},{12,14},{1,3},{3,5},{5,7},{... | collective-permute-start | bytes 393224 | tf_op jit(solution)/shard_map/ppermute | solution.py:34
  277.6 2.8 collective-permute-start.9
  280.5 1.3 collective-permute-start.10
  281.8 3.3 %collective-permute-start.11 = (f32[128,64]{1,0:T(8,128)}, f32[128,64]{1,0:T(8,128)S(1)}, u32[]{:S(2)}, u32[]{:S(2)}) collective-permute-start(f32[128,64]{1,0:T(8,128)} %get-tuple-element.52), channel_id=1, source_target_pairs={{1,0},{3,2},{5,4},{7,6},{9,8},{11,10},{13,12},{15,14},{17,16},{19,... | collective-permute-start | bytes 98312 | tf_op jit(solution)/shard_map/ppermute | solution.py:37
  285.0 0.9 collective-permute-done.11.qyh_ref
  285.9 0.6 copy-done.11
  286.5 0.1 copy-done.4
  286.6 0.1 copy-done.5
  286.7 28.0 %shard_map.109 = (f32[128,64,256]{2,1,0:T(8,128)}, f32[128,256]{1,0:T(8,128)}, f32[128,256]{1,0:T(8,128)}, f32[128,64]{1,0:T(8,128)}, f32[128,64]{1,0:T(8,128)}) custom-call(f32[128,64,256]{2,1,0:T(8,128)} %get-tuple-element.43.tzm_ref.tza_ref, f32[128,64,256]{2,1,0:T(8,128)} %get-tuple-element.43.tzm_ref.tza_ref, ...), custom_call_target="tpu_custom_call" | custom-call | tf_op jit(solution)/shard_map/pallas_call | solution.py:250
  (46 shorter events, 0.2 us)
Async XLA Ops:
  14.2 11.7 %copy-start.12 = (s32[256]{0:T(256)S(1)}, s32[256]{0:T(256)}, u32[]{:S(2)}) copy-start(s32[256]{0:T(256)} %param.14) | copy-start | bytes 3076
  14.2 11.7 %copy-start.13 = (s32[256]{0:T(256)S(1)}, s32[256]{0:T(256)}, u32[]{:S(2)}) copy-start(s32[256]{0:T(256)} %param.16) | copy-start | bytes 3076
  14.2 11.7 %copy-start.14 = (f32[256]{0:T(256)S(1)}, f32[256]{0:T(256)}, u32[]{:S(2)}) copy-start(f32[256]{0:T(256)} %param.17) | copy-start | bytes 3076
  14.2 11.7 %copy-start.15 = (s32[256]{0:T(256)S(1)}, s32[256]{0:T(256)}, u32[]{:S(2)}) copy-start(s32[256]{0:T(256)} %param.15) | copy-start | bytes 3076
  14.2 97.1 %all-to-all-start = ((bf16[16,8,64,256]{3,2,1,0:T(8,128)(2,1)}), bf16[16,8,64,256]{3,2,1,0:T(8,128)(2,1)}, u32[]{:S(2)}, u32[]{:S(2)}) async-start(bf16[16,8,64,256]{3,2,1,0:T(8,128)(2,1)} %bitcast.9), calls=%async_computation | async-start | bytes 8388608 | tf_op jit(solution)/shard_map/all_to_all | solution.py:323
  111.3 16.8 %copy-start.17 = (f32[128,256]{1,0:T(8,128)S(1)}, f32[128,256]{1,0:T(8,128)}, u32[]{:S(2)}) copy-start(f32[128,256]{1,0:T(8,128)} %get-tuple-element.38) | copy-start | bytes 393220
  111.3 19.9 %copy-start.19 = (f32[128,64]{1,0:T(8,128)S(1)}, f32[128,64]{1,0:T(8,128)}, u32[]{:S(2)}) copy-start(f32[128,64]{1,0:T(8,128)} %get-tuple-element.40) | copy-start | bytes 98308
  111.3 21.2 %copy-start.18 = (f32[128,64]{1,0:T(8,128)S(1)}, f32[128,64]{1,0:T(8,128)}, u32[]{:S(2)}) copy-start(f32[128,64]{1,0:T(8,128)} %get-tuple-element.41) | copy-start | bytes 98308
  111.3 24.2 %copy-start.16 = (f32[128,256]{1,0:T(8,128)S(1)}, f32[128,256]{1,0:T(8,128)}, u32[]{:S(2)}) copy-start(f32[128,256]{1,0:T(8,128)} %get-tuple-element.39) | copy-start | bytes 393220
  121.0 97.4 %all-to-all-start.1 = ((bf16[16,8,64,256]{3,2,1,0:T(8,128)(2,1)}), bf16[16,8,64,256]{3,2,1,0:T(8,128)(2,1)}, u32[]{:S(2)}, u32[]{:S(2)}) async-start(bf16[16,8,64,256]{3,2,1,0:T(8,128)(2,1)} %shard_map.106), calls=%async_computation.1 | async-start | bytes 8388608 | tf_op jit(solution)/shard_map/all_to_all | solution.py:356
  128.0 105.2 %collective-permute-start.4 = (f32[128,256]{1,0:T(8,128)S(1)}, f32[128,256]{1,0:T(8,128)S(1)}, u32[]{:S(2)}, u32[]{:S(2)}) collective-permute-start(f32[128,256]{1,0:T(8,128)S(1)} %copy-done.17), channel_id=1, source_target_pairs={{0,2},{2,4},{4,6},{6,8},{8,10},{10,12},{12,14},{1,3},{3,5},{5,7},{... | collective-permute-start | bytes 393224 | tf_op jit(solution)/shard_map/ppermute | solution.py:34
  131.2 98.8 %collective-permute-start.6 = (f32[128,64]{1,0:T(8,128)S(1)}, f32[128,64]{1,0:T(8,128)S(1)}, u32[]{:S(2)}, u32[]{:S(2)}) collective-permute-start(f32[128,64]{1,0:T(8,128)S(1)} %copy-done.19), channel_id=1, source_target_pairs={{0,1},{2,3},{4,5},{6,7},{8,9},{10,11},{12,13},{14,15},{16,17},{18,... | collective-permute-start | bytes 98312 | tf_op jit(solution)/shard_map/ppermute | solution.py:36
  132.5 99.5 %collective-permute-start.7 = (f32[128,64]{1,0:T(8,128)S(1)}, f32[128,64]{1,0:T(8,128)S(1)}, u32[]{:S(2)}, u32[]{:S(2)}) collective-permute-start(f32[128,64]{1,0:T(8,128)S(1)} %copy-done.18), channel_id=1, source_target_pairs={{1,0},{3,2},{5,4},{7,6},{9,8},{11,10},{13,12},{15,14},{17,16},{19,... | collective-permute-start | bytes 98312 | tf_op jit(solution)/shard_map/ppermute | solution.py:37
  135.5 101.7 %collective-permute-start.5 = (f32[128,256]{1,0:T(8,128)S(1)}, f32[128,256]{1,0:T(8,128)S(1)}, u32[]{:S(2)}, u32[]{:S(2)}) collective-permute-start(f32[128,256]{1,0:T(8,128)S(1)} %copy-done.16), channel_id=1, source_target_pairs={{2,0},{4,2},{6,4},{8,6},{10,8},{12,10},{14,12},{3,1},{5,3},{7,5},{... | collective-permute-start | bytes 393224 | tf_op jit(solution)/shard_map/ppermute | solution.py:35
  224.3 13.1 %collective-permute-start = (f32[128,256]{1,0:T(8,128)}, f32[128,256]{1,0:T(8,128)S(1)}, u32[]{:S(2)}, u32[]{:S(2)}) collective-permute-start(f32[128,256]{1,0:T(8,128)} %get-tuple-element.34), channel_id=1, source_target_pairs={{0,2},{2,4},{4,6},{6,8},{8,10},{10,12},{12,14},{1,3},{3,5},{5,7},{... | collective-permute-start | bytes 393224 | tf_op jit(solution)/shard_map/ppermute | solution.py:34
  230.0 7.5 %copy-start.6 = (f32[128,64]{1,0:T(8,128)}, f32[128,64]{1,0:T(8,128)S(1)}, u32[]{:S(2)}) copy-start(f32[128,64]{1,0:T(8,128)S(1)} %collective-permute-done.6.qyl_ref) | copy-start | bytes 98308
  230.0 7.4 %collective-permute-start.1 = (f32[128,256]{1,0:T(8,128)}, f32[128,256]{1,0:T(8,128)S(1)}, u32[]{:S(2)}, u32[]{:S(2)}) collective-permute-start(f32[128,256]{1,0:T(8,128)} %get-tuple-element.35), channel_id=1, source_target_pairs={{2,0},{4,2},{6,4},{8,6},{10,8},{12,10},{14,12},{3,1},{5,3},{7,5},{... | collective-permute-start | bytes 393224 | tf_op jit(solution)/shard_map/ppermute | solution.py:35
  232.0 5.5 %copy-start.7 = (f32[128,64]{1,0:T(8,128)}, f32[128,64]{1,0:T(8,128)S(1)}, u32[]{:S(2)}) copy-start(f32[128,64]{1,0:T(8,128)S(1)} %collective-permute-done.7.qyh_ref) | copy-start | bytes 98308
  232.0 5.2 %collective-permute-start.2 = (f32[128,64]{1,0:T(8,128)}, f32[128,64]{1,0:T(8,128)S(1)}, u32[]{:S(2)}, u32[]{:S(2)}) collective-permute-start(f32[128,64]{1,0:T(8,128)} %get-tuple-element.36), channel_id=1, source_target_pairs={{0,1},{2,3},{4,5},{6,7},{8,9},{10,11},{12,13},{14,15},{16,17},{18,... | collective-permute-start | bytes 98312 | tf_op jit(solution)/shard_map/ppermute | solution.py:36
  233.3 4.2 %copy-start = (f32[128,256]{1,0:T(8,128)}, f32[128,256]{1,0:T(8,128)S(1)}, u32[]{:S(2)}) copy-start(f32[128,256]{1,0:T(8,128)S(1)} %collective-permute-done.4.qxl_ref) | copy-start | bytes 393220
  233.3 4.1 %collective-permute-start.3 = (f32[128,64]{1,0:T(8,128)}, f32[128,64]{1,0:T(8,128)S(1)}, u32[]{:S(2)}, u32[]{:S(2)}) collective-permute-start(f32[128,64]{1,0:T(8,128)} %get-tuple-element.37), channel_id=1, source_target_pairs={{1,0},{3,2},{5,4},{7,6},{9,8},{11,10},{13,12},{15,14},{17,16},{19,... | collective-permute-start | bytes 98312 | tf_op jit(solution)/shard_map/ppermute | solution.py:37
  237.2 0.7 copy-start.1
  237.2 0.7 copy-start.8
  237.4 0.7 copy-start.2
  237.4 0.7 copy-start.3
  274.3 11.6 %collective-permute-start.8 = (f32[128,256]{1,0:T(8,128)}, f32[128,256]{1,0:T(8,128)S(1)}, u32[]{:S(2)}, u32[]{:S(2)}) collective-permute-start(f32[128,256]{1,0:T(8,128)} %get-tuple-element.49), channel_id=1, source_target_pairs={{0,2},{2,4},{4,6},{6,8},{8,10},{10,12},{12,14},{1,3},{3,5},{5,7},{... | collective-permute-start | bytes 393224 | tf_op jit(solution)/shard_map/ppermute | solution.py:34
  277.6 8.3 %collective-permute-start.9 = (f32[128,256]{1,0:T(8,128)}, f32[128,256]{1,0:T(8,128)S(1)}, u32[]{:S(2)}, u32[]{:S(2)}) collective-permute-start(f32[128,256]{1,0:T(8,128)} %get-tuple-element.50), channel_id=1, source_target_pairs={{2,0},{4,2},{6,4},{8,6},{10,8},{12,10},{14,12},{3,1},{5,3},{7,5},{... | collective-permute-start | bytes 393224 | tf_op jit(solution)/shard_map/ppermute | solution.py:35
  280.5 4.6 %collective-permute-start.10 = (f32[128,64]{1,0:T(8,128)}, f32[128,64]{1,0:T(8,128)S(1)}, u32[]{:S(2)}, u32[]{:S(2)}) collective-permute-start(f32[128,64]{1,0:T(8,128)} %get-tuple-element.51), channel_id=1, source_target_pairs={{0,1},{2,3},{4,5},{6,7},{8,9},{10,11},{12,13},{14,15},{16,17},{18,... | collective-permute-start | bytes 98312 | tf_op jit(solution)/shard_map/ppermute | solution.py:36
  281.8 4.1 %collective-permute-start.11 = (f32[128,64]{1,0:T(8,128)}, f32[128,64]{1,0:T(8,128)S(1)}, u32[]{:S(2)}, u32[]{:S(2)}) collective-permute-start(f32[128,64]{1,0:T(8,128)} %get-tuple-element.52), channel_id=1, source_target_pairs={{1,0},{3,2},{5,4},{7,6},{9,8},{11,10},{13,12},{15,14},{17,16},{19,... | collective-permute-start | bytes 98312 | tf_op jit(solution)/shard_map/ppermute | solution.py:37
  285.0 0.9 copy-start.10
  285.9 0.7 copy-start.4
  285.9 0.7 copy-start.5
  (2 other events, 1.2 us)

commit v14 on v12

--- a/solution.py
+++ b/solution.py
@@ -13,7 +13,7 @@
 STEP_SIZE = 0.03
 CAP_LOG = 1.5
 CHUNK_Z = 16
-EDGE_Z = 32
+EDGE_Z = 64
 DEPTH_X = 16
 
 

time: 316 us -> 315 us (level)
  no operation moved by 1% of the time
where the time goes in v14:
time: 315 us; the launch traced here: 313 us
  waiting for transfers between devices  161 us (51%)
  Pallas kernels  95.3 us (30%)
  starting transfers between devices  46.9 us (15%)
  matrix products  6.74 us (2%)
    all_to_all x1, waiting for transfers between devices, body(): lax.all_to_all(outgoing, ('wide', 'narrow'), split_axis=0, concat_axis=0,...  79.8 us
    all_to_all x1, waiting for transfers between devices, body(): lax.all_to_all(first.reshape(groups, planes, rows_x, rows_y), ('wide', 'n...  79.5 us
    pallas_call x1, Pallas kernels, advance(): pl.pallas_call(first_step_kernel, out_shape=tuple(out_shape + [full, full...  36.3 us
    pallas_call x1, Pallas kernels, advance(): pl.pallas_call(later_step_kernel, out_shape=tuple(out_shape), grid=grid,...  27 us
    pallas_call x1, Pallas kernels, depth_transform(): pl.pallas_call(depth_kernel, out_shape=jax.ShapeDtypeStruct(noise.shape,...  13.6 us
    ppermute x3, starting transfers between devices, halos(): x_lo = lax.ppermute(last_x, 'wide', forward_w)  12.1 us
    pallas_call x1, Pallas kernels, line_transforms(): pl.pallas_call(functools.partial(line_kernel, count_w=count_w, count_n=co...  9.68 us
    ppermute x3, starting transfers between devices, halos(): y_hi = lax.ppermute(first_y, 'narrow', backward_n)  9.28 us
  transfers between devices with their start and end apart: 14, of which 4 were waited for; matrix products, arithmetic and copies ran while one was open for 2% of the time, Pallas kernels for 3%

profile of v14, /device:TPU:11, one launch (start us, length us, event | category | flops | bytes accessed | tf_op | source)
XLA Modules:
  0.0 312.8 jit_solution(13054475650408781063)
XLA Ops:
  0.6 13.6 %shard_map.104 = bf16[128,64,256]{2,1,0:T(8,128)(2,1)} custom-call(bf16[128,128]{1,0:T(8,128)(2,1)} %rz_ref.1, bf16[128,64,256]{2,1,0:T(8,128)(2,1)} %n_ref.1), custom_call_target="tpu_custom_call" | custom-call | tf_op jit(solution)/shard_map/pallas_call | solution.py:273
  14.2 6.8 %all-to-all-start = ((bf16[16,8,64,256]{3,2,1,0:T(8,128)(2,1)}), bf16[16,8,64,256]{3,2,1,0:T(8,128)(2,1)}, u32[]{:S(2)}, u32[]{:S(2)}) async-start(bf16[16,8,64,256]{3,2,1,0:T(8,128)(2,1)} %bitcast.9), calls=%async_computation | async-start | bytes 8388608 | tf_op jit(solution)/shard_map/all_to_all | solution.py:323
  21.0 4.0 %shard_map.105 = (f32[128,256]{1,0:T(8,128)}, f32[128,256]{1,0:T(8,128)}, f32[128,64]{1,0:T(8,128)}, f32[128,64]{1,0:T(8,128)}) custom-call(bf16[128,64,256]{2,1,0:T(8,128)(2,1)} %pa_ref.1), custom_call_target="tpu_custom_call" | custom-call | tf_op jit(solution)/shard_map/pallas_call | solution.py:111
  25.0 6.7 %fusion = f32[8192,256]{1,0:T(8,128)} fusion(f32[256]{0:T(256)S(1)} %get-tuple-element.54, s32[256]{0:T(256)S(1)} %multiply_add_fusion, s32[256]{0:T(256)S(1)} %get-tuple-element.55), kind=kOutput, calls=%fused_computation | convolution fusion | flops 6446710784 | bytes 8391680 | tf_op jit(solution)/shard_map/dot_general | solution.py:346
  31.8 79.5 %all-to-all-done.g_ref = bf16[16,8,64,256]{3,2,1,0:T(8,128)(2,1)} async-done(((bf16[16,8,64,256]{3,2,1,0:T(8,128)(2,1)}), bf16[16,8,64,256]{3,2,1,0:T(8,128)(2,1)}, u32[]{:S(2)}, u32[]{:S(2)}) %all-to-all-start) | async-done | bytes 4194336 | tf_op jit(solution)/shard_map/all_to_all | solution.py:323
  111.3 9.7 %shard_map.106 = bf16[16,8,64,256]{3,2,1,0:T(8,128)(2,1)} custom-call(bf16[16,8,64,256]{3,2,1,0:T(8,128)(2,1)} %all-to-all-done.g_ref, bf16[512,512]{1,0:T(8,128)(2,1)} %rx_ref.1, bf16[512,512]{1,0:T(8,128)(2,1)} %ry_ref.1), custom_call_target="tpu_custom_call" | custom-call | tf_op jit(solution)/shard_map/pallas_call | solution.py:306
  121.0 7.1 %all-to-all-start.1 = ((bf16[16,8,64,256]{3,2,1,0:T(8,128)(2,1)}), bf16[16,8,64,256]{3,2,1,0:T(8,128)(2,1)}, u32[]{:S(2)}, u32[]{:S(2)}) async-start(bf16[16,8,64,256]{3,2,1,0:T(8,128)(2,1)} %shard_map.106), calls=%async_computation.1 | async-start | bytes 8388608 | tf_op jit(solution)/shard_map/all_to_all | solution.py:356
  128.0 3.1 collective-permute-start.4
  131.2 1.3 collective-permute-start.6
  132.5 3.0 collective-permute-start.7
  135.5 3.1 collective-permute-start.5
  138.6 79.8 %all-to-all-done.1 = bf16[16,8,64,256]{3,2,1,0:T(8,128)(2,1)} async-done(((bf16[16,8,64,256]{3,2,1,0:T(8,128)(2,1)}), bf16[16,8,64,256]{3,2,1,0:T(8,128)(2,1)}, u32[]{:S(2)}, u32[]{:S(2)}) %all-to-all-start.1) | async-done | bytes 4194336 | tf_op jit(solution)/shard_map/all_to_all | solution.py:356
  218.4 4.7 %shard_map.107 = (f32[128,256]{1,0:T(8,128)}, f32[128,256]{1,0:T(8,128)}, f32[128,64]{1,0:T(8,128)}, f32[128,64]{1,0:T(8,128)}, bf16[128,64,256]{2,1,0:T(8,128)(2,1)}) custom-call(bf16[128,64,256]{2,1,0:T(8,128)(2,1)} %bitcast.2.block_ref), custom_call_target="tpu_custom_call" | custom-call | tf_op jit(solution)/shard_map/pallas_call | solution.py:111
  223.1 5.7 %collective-permute-start = (f32[128,256]{1,0:T(8,128)}, f32[128,256]{1,0:T(8,128)S(1)}, u32[]{:S(2)}, u32[]{:S(2)}) collective-permute-start(f32[128,256]{1,0:T(8,128)} %get-tuple-element.34), channel_id=1, source_target_pairs={{0,2},{2,4},{4,6},{6,8},{8,10},{10,12},{12,14},{1,3},{3,5},{5,7},{... | collective-permute-start | bytes 393224 | tf_op jit(solution)/shard_map/ppermute | solution.py:34
  228.8 1.9 collective-permute-start.1
  230.8 1.3 collective-permute-start.2
  232.1 3.2 %collective-permute-start.3 = (f32[128,64]{1,0:T(8,128)}, f32[128,64]{1,0:T(8,128)S(1)}, u32[]{:S(2)}, u32[]{:S(2)}) collective-permute-start(f32[128,64]{1,0:T(8,128)} %get-tuple-element.37), channel_id=1, source_target_pairs={{1,0},{3,2},{5,4},{7,6},{9,8},{11,10},{13,12},{15,14},{17,16},{19,... | collective-permute-start | bytes 98312 | tf_op jit(solution)/shard_map/ppermute | solution.py:37
  235.3 0.7 add_convert_fusion.inside_ref
  236.0 0.2 collective-permute-done.3.lyh_ref
  236.3 0.4 copy-done.1
  236.7 0.2 copy-done.9
  236.9 0.1 copy-done.2
  237.0 36.3 %shard_map.108 = (f32[128,64,256]{2,1,0:T(8,128)}, f32[128,256]{1,0:T(8,128)}, f32[128,256]{1,0:T(8,128)}, f32[128,64]{1,0:T(8,128)}, f32[128,64]{1,0:T(8,128)},...) custom-call(s32[4]{0:T(128)} %add_convert_fusion.inside_ref, ...), custom_call_target="tpu_custom_call" | custom-call | tf_op jit(solution)/shard_map/pallas_call | solution.py:240
  273.3 3.4 %collective-permute-start.8 = (f32[128,256]{1,0:T(8,128)}, f32[128,256]{1,0:T(8,128)S(1)}, u32[]{:S(2)}, u32[]{:S(2)}) collective-permute-start(f32[128,256]{1,0:T(8,128)} %get-tuple-element.49), channel_id=1, source_target_pairs={{0,2},{2,4},{4,6},{6,8},{8,10},{10,12},{12,14},{1,3},{3,5},{5,7},{... | collective-permute-start | bytes 393224 | tf_op jit(solution)/shard_map/ppermute | solution.py:34
  276.6 2.8 collective-permute-start.9
  279.4 1.3 collective-permute-start.10
  280.7 3.0 collective-permute-start.11
  283.8 1.1 collective-permute-done.11.qyh_ref
  284.9 0.6 copy-done.11
  285.5 0.1 copy-done.4
  285.6 0.1 copy-done.5
  285.6 27.0 %shard_map.109 = (f32[128,64,256]{2,1,0:T(8,128)}, f32[128,256]{1,0:T(8,128)}, f32[128,256]{1,0:T(8,128)}, f32[128,64]{1,0:T(8,128)}, f32[128,64]{1,0:T(8,128)}) custom-call(f32[128,64,256]{2,1,0:T(8,128)} %get-tuple-element.43.tzm_ref.tza_ref, f32[128,64,256]{2,1,0:T(8,128)} %get-tuple-element.43.tzm_ref.tza_ref, ...), custom_call_target="tpu_custom_call" | custom-call | tf_op jit(solution)/shard_map/pallas_call | solution.py:250
  (46 shorter events, 0.2 us)
Async XLA Ops:
  14.2 10.8 %copy-start.12 = (s32[256]{0:T(256)S(1)}, s32[256]{0:T(256)}, u32[]{:S(2)}) copy-start(s32[256]{0:T(256)} %param.14) | copy-start | bytes 3076
  14.2 10.8 %copy-start.13 = (s32[256]{0:T(256)S(1)}, s32[256]{0:T(256)}, u32[]{:S(2)}) copy-start(s32[256]{0:T(256)} %param.16) | copy-start | bytes 3076
  14.2 10.8 %copy-start.14 = (f32[256]{0:T(256)S(1)}, f32[256]{0:T(256)}, u32[]{:S(2)}) copy-start(f32[256]{0:T(256)} %param.17) | copy-start | bytes 3076
  14.2 10.8 %copy-start.15 = (s32[256]{0:T(256)S(1)}, s32[256]{0:T(256)}, u32[]{:S(2)}) copy-start(s32[256]{0:T(256)} %param.15) | copy-start | bytes 3076
  14.2 97.1 %all-to-all-start = ((bf16[16,8,64,256]{3,2,1,0:T(8,128)(2,1)}), bf16[16,8,64,256]{3,2,1,0:T(8,128)(2,1)}, u32[]{:S(2)}, u32[]{:S(2)}) async-start(bf16[16,8,64,256]{3,2,1,0:T(8,128)(2,1)} %bitcast.9), calls=%async_computation | async-start | bytes 8388608 | tf_op jit(solution)/shard_map/all_to_all | solution.py:323
  111.3 16.8 %copy-start.17 = (f32[128,256]{1,0:T(8,128)S(1)}, f32[128,256]{1,0:T(8,128)}, u32[]{:S(2)}) copy-start(f32[128,256]{1,0:T(8,128)} %get-tuple-element.38) | copy-start | bytes 393220
  111.3 19.9 %copy-start.19 = (f32[128,64]{1,0:T(8,128)S(1)}, f32[128,64]{1,0:T(8,128)}, u32[]{:S(2)}) copy-start(f32[128,64]{1,0:T(8,128)} %get-tuple-element.40) | copy-start | bytes 98308
  111.3 21.2 %copy-start.18 = (f32[128,64]{1,0:T(8,128)S(1)}, f32[128,64]{1,0:T(8,128)}, u32[]{:S(2)}) copy-start(f32[128,64]{1,0:T(8,128)} %get-tuple-element.41) | copy-start | bytes 98308
  111.3 24.2 %copy-start.16 = (f32[128,256]{1,0:T(8,128)S(1)}, f32[128,256]{1,0:T(8,128)}, u32[]{:S(2)}) copy-start(f32[128,256]{1,0:T(8,128)} %get-tuple-element.39) | copy-start | bytes 393220
  121.0 97.4 %all-to-all-start.1 = ((bf16[16,8,64,256]{3,2,1,0:T(8,128)(2,1)}), bf16[16,8,64,256]{3,2,1,0:T(8,128)(2,1)}, u32[]{:S(2)}, u32[]{:S(2)}) async-start(bf16[16,8,64,256]{3,2,1,0:T(8,128)(2,1)} %shard_map.106), calls=%async_computation.1 | async-start | bytes 8388608 | tf_op jit(solution)/shard_map/all_to_all | solution.py:356
  128.0 104.0 %collective-permute-start.4 = (f32[128,256]{1,0:T(8,128)S(1)}, f32[128,256]{1,0:T(8,128)S(1)}, u32[]{:S(2)}, u32[]{:S(2)}) collective-permute-start(f32[128,256]{1,0:T(8,128)S(1)} %copy-done.17), channel_id=1, source_target_pairs={{0,2},{2,4},{4,6},{6,8},{8,10},{10,12},{12,14},{1,3},{3,5},{5,7},{... | collective-permute-start | bytes 393224 | tf_op jit(solution)/shard_map/ppermute | solution.py:34
  131.2 97.6 %collective-permute-start.6 = (f32[128,64]{1,0:T(8,128)S(1)}, f32[128,64]{1,0:T(8,128)S(1)}, u32[]{:S(2)}, u32[]{:S(2)}) collective-permute-start(f32[128,64]{1,0:T(8,128)S(1)} %copy-done.19), channel_id=1, source_target_pairs={{0,1},{2,3},{4,5},{6,7},{8,9},{10,11},{12,13},{14,15},{16,17},{18,... | collective-permute-start | bytes 98312 | tf_op jit(solution)/shard_map/ppermute | solution.py:36
  132.5 98.3 %collective-permute-start.7 = (f32[128,64]{1,0:T(8,128)S(1)}, f32[128,64]{1,0:T(8,128)S(1)}, u32[]{:S(2)}, u32[]{:S(2)}) collective-permute-start(f32[128,64]{1,0:T(8,128)S(1)} %copy-done.18), channel_id=1, source_target_pairs={{1,0},{3,2},{5,4},{7,6},{9,8},{11,10},{13,12},{15,14},{17,16},{19,... | collective-permute-start | bytes 98312 | tf_op jit(solution)/shard_map/ppermute | solution.py:37
  135.5 100.5 %collective-permute-start.5 = (f32[128,256]{1,0:T(8,128)S(1)}, f32[128,256]{1,0:T(8,128)S(1)}, u32[]{:S(2)}, u32[]{:S(2)}) collective-permute-start(f32[128,256]{1,0:T(8,128)S(1)} %copy-done.16), channel_id=1, source_target_pairs={{2,0},{4,2},{6,4},{8,6},{10,8},{12,10},{14,12},{3,1},{5,3},{7,5},{... | collective-permute-start | bytes 393224 | tf_op jit(solution)/shard_map/ppermute | solution.py:35
  223.1 13.1 %collective-permute-start = (f32[128,256]{1,0:T(8,128)}, f32[128,256]{1,0:T(8,128)S(1)}, u32[]{:S(2)}, u32[]{:S(2)}) collective-permute-start(f32[128,256]{1,0:T(8,128)} %get-tuple-element.34), channel_id=1, source_target_pairs={{0,2},{2,4},{4,6},{6,8},{8,10},{10,12},{12,14},{1,3},{3,5},{5,7},{... | collective-permute-start | bytes 393224 | tf_op jit(solution)/shard_map/ppermute | solution.py:34
  228.8 7.5 %copy-start.6 = (f32[128,64]{1,0:T(8,128)}, f32[128,64]{1,0:T(8,128)S(1)}, u32[]{:S(2)}) copy-start(f32[128,64]{1,0:T(8,128)S(1)} %collective-permute-done.6.qyl_ref) | copy-start | bytes 98308
  228.8 7.4 %collective-permute-start.1 = (f32[128,256]{1,0:T(8,128)}, f32[128,256]{1,0:T(8,128)S(1)}, u32[]{:S(2)}, u32[]{:S(2)}) collective-permute-start(f32[128,256]{1,0:T(8,128)} %get-tuple-element.35), channel_id=1, source_target_pairs={{2,0},{4,2},{6,4},{8,6},{10,8},{12,10},{14,12},{3,1},{5,3},{7,5},{... | collective-permute-start | bytes 393224 | tf_op jit(solution)/shard_map/ppermute | solution.py:35
  230.8 5.5 %copy-start.7 = (f32[128,64]{1,0:T(8,128)}, f32[128,64]{1,0:T(8,128)S(1)}, u32[]{:S(2)}) copy-start(f32[128,64]{1,0:T(8,128)S(1)} %collective-permute-done.7.qyh_ref) | copy-start | bytes 98308
  230.8 5.2 %collective-permute-start.2 = (f32[128,64]{1,0:T(8,128)}, f32[128,64]{1,0:T(8,128)S(1)}, u32[]{:S(2)}, u32[]{:S(2)}) collective-permute-start(f32[128,64]{1,0:T(8,128)} %get-tuple-element.36), channel_id=1, source_target_pairs={{0,1},{2,3},{4,5},{6,7},{8,9},{10,11},{12,13},{14,15},{16,17},{18,... | collective-permute-start | bytes 98312 | tf_op jit(solution)/shard_map/ppermute | solution.py:36
  232.1 4.2 %copy-start = (f32[128,256]{1,0:T(8,128)}, f32[128,256]{1,0:T(8,128)S(1)}, u32[]{:S(2)}) copy-start(f32[128,256]{1,0:T(8,128)S(1)} %collective-permute-done.4.qxl_ref) | copy-start | bytes 393220
  232.1 4.1 %collective-permute-start.3 = (f32[128,64]{1,0:T(8,128)}, f32[128,64]{1,0:T(8,128)S(1)}, u32[]{:S(2)}, u32[]{:S(2)}) collective-permute-start(f32[128,64]{1,0:T(8,128)} %get-tuple-element.37), channel_id=1, source_target_pairs={{1,0},{3,2},{5,4},{7,6},{9,8},{11,10},{13,12},{15,14},{17,16},{19,... | collective-permute-start | bytes 98312 | tf_op jit(solution)/shard_map/ppermute | solution.py:37
  236.0 0.7 copy-start.1
  236.0 0.7 copy-start.8
  236.2 0.7 copy-start.2
  236.3 0.7 copy-start.3
  273.3 11.6 %collective-permute-start.8 = (f32[128,256]{1,0:T(8,128)}, f32[128,256]{1,0:T(8,128)S(1)}, u32[]{:S(2)}, u32[]{:S(2)}) collective-permute-start(f32[128,256]{1,0:T(8,128)} %get-tuple-element.49), channel_id=1, source_target_pairs={{0,2},{2,4},{4,6},{6,8},{8,10},{10,12},{12,14},{1,3},{3,5},{5,7},{... | collective-permute-start | bytes 393224 | tf_op jit(solution)/shard_map/ppermute | solution.py:34
  276.6 8.3 %collective-permute-start.9 = (f32[128,256]{1,0:T(8,128)}, f32[128,256]{1,0:T(8,128)S(1)}, u32[]{:S(2)}, u32[]{:S(2)}) collective-permute-start(f32[128,256]{1,0:T(8,128)} %get-tuple-element.50), channel_id=1, source_target_pairs={{2,0},{4,2},{6,4},{8,6},{10,8},{12,10},{14,12},{3,1},{5,3},{7,5},{... | collective-permute-start | bytes 393224 | tf_op jit(solution)/shard_map/ppermute | solution.py:35
  279.4 4.3 %collective-permute-start.10 = (f32[128,64]{1,0:T(8,128)}, f32[128,64]{1,0:T(8,128)S(1)}, u32[]{:S(2)}, u32[]{:S(2)}) collective-permute-start(f32[128,64]{1,0:T(8,128)} %get-tuple-element.51), channel_id=1, source_target_pairs={{0,1},{2,3},{4,5},{6,7},{8,9},{10,11},{12,13},{14,15},{16,17},{18,... | collective-permute-start | bytes 98312 | tf_op jit(solution)/shard_map/ppermute | solution.py:36
  280.7 4.1 %collective-permute-start.11 = (f32[128,64]{1,0:T(8,128)}, f32[128,64]{1,0:T(8,128)S(1)}, u32[]{:S(2)}, u32[]{:S(2)}) collective-permute-start(f32[128,64]{1,0:T(8,128)} %get-tuple-element.52), channel_id=1, source_target_pairs={{1,0},{3,2},{5,4},{7,6},{9,8},{11,10},{13,12},{15,14},{17,16},{19,... | collective-permute-start | bytes 98312 | tf_op jit(solution)/shard_map/ppermute | solution.py:37
  283.8 1.1 copy-start.10
  284.9 0.7 copy-start.4
  284.9 0.7 copy-start.5
  (2 other events, 1.2 us)

commit v15 on v14

--- a/solution.py
+++ b/solution.py
@@ -13,7 +13,7 @@
 STEP_SIZE = 0.03
 CAP_LOG = 1.5
 CHUNK_Z = 16
-EDGE_Z = 64
+EDGE_Z = 128
 DEPTH_X = 16
 
 

time: 315 us -> 316 us (level)
  no operation moved by 1% of the time
where the time goes in v15:
time: 316 us; the launch traced here: 314 us
  waiting for transfers between devices  160 us (51%)
  Pallas kernels  96.7 us (31%)
  starting transfers between devices  46.9 us (15%)
  matrix products  6.74 us (2%)
    all_to_all x1, waiting for transfers between devices, body(): lax.all_to_all(outgoing, ('wide', 'narrow'), split_axis=0, concat_axis=0,...  79.8 us
    all_to_all x1, waiting for transfers between devices, body(): lax.all_to_all(first.reshape(groups, planes, rows_x, rows_y), ('wide', 'n...  79.2 us
    pallas_call x1, Pallas kernels, advance(): pl.pallas_call(first_step_kernel, out_shape=tuple(out_shape + [full, full...  36.3 us
    pallas_call x1, Pallas kernels, advance(): pl.pallas_call(later_step_kernel, out_shape=tuple(out_shape), grid=grid,...  27 us
    pallas_call x1, Pallas kernels, depth_transform(): pl.pallas_call(depth_kernel, out_shape=jax.ShapeDtypeStruct(noise.shape,...  13.6 us
    ppermute x3, starting transfers between devices, halos(): x_lo = lax.ppermute(last_x, 'wide', forward_w)  12.1 us
    pallas_call x2, Pallas kernels, block_edges(): pl.pallas_call(edge_kernel, out_shape=tuple(out_shape), grid=(depth // tz...  10.1 us
    pallas_call x1, Pallas kernels, line_transforms(): pl.pallas_call(functools.partial(line_kernel, count_w=count_w, count_n=co...  9.68 us
  transfers between devices with their start and end apart: 14, of which 4 were waited for; matrix products, arithmetic and copies ran while one was open for 2% of the time, Pallas kernels for 3%

profile of v15, /device:TPU:11, one launch (start us, length us, event | category | flops | bytes accessed | tf_op | source)
XLA Modules:
  0.0 313.9 jit_solution(10311015502929749230)
XLA Ops:
  0.6 13.6 %shard_map.104 = bf16[128,64,256]{2,1,0:T(8,128)(2,1)} custom-call(bf16[128,128]{1,0:T(8,128)(2,1)} %rz_ref.1, bf16[128,64,256]{2,1,0:T(8,128)(2,1)} %n_ref.1), custom_call_target="tpu_custom_call" | custom-call | tf_op jit(solution)/shard_map/pallas_call | solution.py:273
  14.2 6.8 %all-to-all-start = ((bf16[16,8,64,256]{3,2,1,0:T(8,128)(2,1)}), bf16[16,8,64,256]{3,2,1,0:T(8,128)(2,1)}, u32[]{:S(2)}, u32[]{:S(2)}) async-start(bf16[16,8,64,256]{3,2,1,0:T(8,128)(2,1)} %bitcast.9), calls=%async_computation | async-start | bytes 8388608 | tf_op jit(solution)/shard_map/all_to_all | solution.py:323
  21.0 4.3 %shard_map.105 = (f32[128,256]{1,0:T(8,128)}, f32[128,256]{1,0:T(8,128)}, f32[128,64]{1,0:T(8,128)}, f32[128,64]{1,0:T(8,128)}) custom-call(bf16[128,64,256]{2,1,0:T(8,128)(2,1)} %pa_ref.1), custom_call_target="tpu_custom_call" | custom-call | tf_op jit(solution)/shard_map/pallas_call | solution.py:111
  25.3 6.7 %fusion = f32[8192,256]{1,0:T(8,128)} fusion(f32[256]{0:T(256)S(1)} %get-tuple-element.54, s32[256]{0:T(256)S(1)} %multiply_add_fusion, s32[256]{0:T(256)S(1)} %get-tuple-element.55), kind=kOutput, calls=%fused_computation | convolution fusion | flops 6446710784 | bytes 8391680 | tf_op jit(solution)/shard_map/dot_general | solution.py:346
  32.1 79.2 %all-to-all-done.g_ref = bf16[16,8,64,256]{3,2,1,0:T(8,128)(2,1)} async-done(((bf16[16,8,64,256]{3,2,1,0:T(8,128)(2,1)}), bf16[16,8,64,256]{3,2,1,0:T(8,128)(2,1)}, u32[]{:S(2)}, u32[]{:S(2)}) %all-to-all-start) | async-done | bytes 4194336 | tf_op jit(solution)/shard_map/all_to_all | solution.py:323
  111.3 9.7 %shard_map.106 = bf16[16,8,64,256]{3,2,1,0:T(8,128)(2,1)} custom-call(bf16[16,8,64,256]{3,2,1,0:T(8,128)(2,1)} %all-to-all-done.g_ref, bf16[512,512]{1,0:T(8,128)(2,1)} %rx_ref.1, bf16[512,512]{1,0:T(8,128)(2,1)} %ry_ref.1), custom_call_target="tpu_custom_call" | custom-call | tf_op jit(solution)/shard_map/pallas_call | solution.py:306
  121.0 7.1 %all-to-all-start.1 = ((bf16[16,8,64,256]{3,2,1,0:T(8,128)(2,1)}), bf16[16,8,64,256]{3,2,1,0:T(8,128)(2,1)}, u32[]{:S(2)}, u32[]{:S(2)}) async-start(bf16[16,8,64,256]{3,2,1,0:T(8,128)(2,1)} %shard_map.106), calls=%async_computation.1 | async-start | bytes 8388608 | tf_op jit(solution)/shard_map/all_to_all | solution.py:356
  128.0 3.1 collective-permute-start.4
  131.2 1.3 collective-permute-start.6
  132.5 3.0 collective-permute-start.7
  135.5 3.1 collective-permute-start.5
  138.6 79.8 %all-to-all-done.1 = bf16[16,8,64,256]{3,2,1,0:T(8,128)(2,1)} async-done(((bf16[16,8,64,256]{3,2,1,0:T(8,128)(2,1)}), bf16[16,8,64,256]{3,2,1,0:T(8,128)(2,1)}, u32[]{:S(2)}, u32[]{:S(2)}) %all-to-all-start.1) | async-done | bytes 4194336 | tf_op jit(solution)/shard_map/all_to_all | solution.py:356
  218.4 5.8 %shard_map.107 = (f32[128,256]{1,0:T(8,128)}, f32[128,256]{1,0:T(8,128)}, f32[128,64]{1,0:T(8,128)}, f32[128,64]{1,0:T(8,128)}, bf16[128,64,256]{2,1,0:T(8,128)(2,1)}) custom-call(bf16[128,64,256]{2,1,0:T(8,128)(2,1)} %bitcast.2.block_ref), custom_call_target="tpu_custom_call" | custom-call | tf_op jit(solution)/shard_map/pallas_call | solution.py:111
  224.2 5.7 %collective-permute-start = (f32[128,256]{1,0:T(8,128)}, f32[128,256]{1,0:T(8,128)S(1)}, u32[]{:S(2)}, u32[]{:S(2)}) collective-permute-start(f32[128,256]{1,0:T(8,128)} %get-tuple-element.34), channel_id=1, source_target_pairs={{0,2},{2,4},{4,6},{6,8},{8,10},{10,12},{12,14},{1,3},{3,5},{5,7},{... | collective-permute-start | bytes 393224 | tf_op jit(solution)/shard_map/ppermute | solution.py:34
  229.9 1.9 collective-permute-start.1
  231.9 1.3 collective-permute-start.2
  233.2 3.2 %collective-permute-start.3 = (f32[128,64]{1,0:T(8,128)}, f32[128,64]{1,0:T(8,128)S(1)}, u32[]{:S(2)}, u32[]{:S(2)}) collective-permute-start(f32[128,64]{1,0:T(8,128)} %get-tuple-element.37), channel_id=1, source_target_pairs={{1,0},{3,2},{5,4},{7,6},{9,8},{11,10},{13,12},{15,14},{17,16},{19,... | collective-permute-start | bytes 98312 | tf_op jit(solution)/shard_map/ppermute | solution.py:37
  236.4 0.7 add_convert_fusion.inside_ref
  237.1 0.2 collective-permute-done.3.lyh_ref
  237.4 0.4 copy-done.1
  237.8 0.2 copy-done.9
  237.9 0.1 copy-done.2
  238.0 36.3 %shard_map.108 = (f32[128,64,256]{2,1,0:T(8,128)}, f32[128,256]{1,0:T(8,128)}, f32[128,256]{1,0:T(8,128)}, f32[128,64]{1,0:T(8,128)}, f32[128,64]{1,0:T(8,128)},...) custom-call(s32[4]{0:T(128)} %add_convert_fusion.inside_ref, ...), custom_call_target="tpu_custom_call" | custom-call | tf_op jit(solution)/shard_map/pallas_call | solution.py:240
  274.3 3.4 %collective-permute-start.8 = (f32[128,256]{1,0:T(8,128)}, f32[128,256]{1,0:T(8,128)S(1)}, u32[]{:S(2)}, u32[]{:S(2)}) collective-permute-start(f32[128,256]{1,0:T(8,128)} %get-tuple-element.49), channel_id=1, source_target_pairs={{0,2},{2,4},{4,6},{6,8},{8,10},{10,12},{12,14},{1,3},{3,5},{5,7},{... | collective-permute-start | bytes 393224 | tf_op jit(solution)/shard_map/ppermute | solution.py:34
  277.7 2.8 collective-permute-start.9
  280.5 1.3 collective-permute-start.10
  281.8 3.0 collective-permute-start.11
  284.9 1.1 collective-permute-done.11.qyh_ref
  286.0 0.6 copy-done.11
  286.6 0.1 copy-done.4
  286.6 0.1 copy-done.5
  286.7 27.0 %shard_map.109 = (f32[128,64,256]{2,1,0:T(8,128)}, f32[128,256]{1,0:T(8,128)}, f32[128,256]{1,0:T(8,128)}, f32[128,64]{1,0:T(8,128)}, f32[128,64]{1,0:T(8,128)}) custom-call(f32[128,64,256]{2,1,0:T(8,128)} %get-tuple-element.43.tzm_ref.tza_ref, f32[128,64,256]{2,1,0:T(8,128)} %get-tuple-element.43.tzm_ref.tza_ref, ...), custom_call_target="tpu_custom_call" | custom-call | tf_op jit(solution)/shard_map/pallas_call | solution.py:250
  (46 shorter events, 0.2 us)
Async XLA Ops:
  14.2 11.1 %copy-start.12 = (s32[256]{0:T(256)S(1)}, s32[256]{0:T(256)}, u32[]{:S(2)}) copy-start(s32[256]{0:T(256)} %param.14) | copy-start | bytes 3076
  14.2 11.1 %copy-start.13 = (s32[256]{0:T(256)S(1)}, s32[256]{0:T(256)}, u32[]{:S(2)}) copy-start(s32[256]{0:T(256)} %param.16) | copy-start | bytes 3076
  14.2 11.1 %copy-start.14 = (f32[256]{0:T(256)S(1)}, f32[256]{0:T(256)}, u32[]{:S(2)}) copy-start(f32[256]{0:T(256)} %param.17) | copy-start | bytes 3076
  14.2 11.1 %copy-start.15 = (s32[256]{0:T(256)S(1)}, s32[256]{0:T(256)}, u32[]{:S(2)}) copy-start(s32[256]{0:T(256)} %param.15) | copy-start | bytes 3076
  14.2 97.1 %all-to-all-start = ((bf16[16,8,64,256]{3,2,1,0:T(8,128)(2,1)}), bf16[16,8,64,256]{3,2,1,0:T(8,128)(2,1)}, u32[]{:S(2)}, u32[]{:S(2)}) async-start(bf16[16,8,64,256]{3,2,1,0:T(8,128)(2,1)} %bitcast.9), calls=%async_computation | async-start | bytes 8388608 | tf_op jit(solution)/shard_map/all_to_all | solution.py:323
  111.3 16.8 %copy-start.17 = (f32[128,256]{1,0:T(8,128)S(1)}, f32[128,256]{1,0:T(8,128)}, u32[]{:S(2)}) copy-start(f32[128,256]{1,0:T(8,128)} %get-tuple-element.38) | copy-start | bytes 393220
  111.3 19.9 %copy-start.19 = (f32[128,64]{1,0:T(8,128)S(1)}, f32[128,64]{1,0:T(8,128)}, u32[]{:S(2)}) copy-start(f32[128,64]{1,0:T(8,128)} %get-tuple-element.40) | copy-start | bytes 98308
  111.3 21.2 %copy-start.18 = (f32[128,64]{1,0:T(8,128)S(1)}, f32[128,64]{1,0:T(8,128)}, u32[]{:S(2)}) copy-start(f32[128,64]{1,0:T(8,128)} %get-tuple-element.41) | copy-start | bytes 98308
  111.3 24.2 %copy-start.16 = (f32[128,256]{1,0:T(8,128)S(1)}, f32[128,256]{1,0:T(8,128)}, u32[]{:S(2)}) copy-start(f32[128,256]{1,0:T(8,128)} %get-tuple-element.39) | copy-start | bytes 393220
  121.0 97.4 %all-to-all-start.1 = ((bf16[16,8,64,256]{3,2,1,0:T(8,128)(2,1)}), bf16[16,8,64,256]{3,2,1,0:T(8,128)(2,1)}, u32[]{:S(2)}, u32[]{:S(2)}) async-start(bf16[16,8,64,256]{3,2,1,0:T(8,128)(2,1)} %shard_map.106), calls=%async_computation.1 | async-start | bytes 8388608 | tf_op jit(solution)/shard_map/all_to_all | solution.py:356
  128.0 105.1 %collective-permute-start.4 = (f32[128,256]{1,0:T(8,128)S(1)}, f32[128,256]{1,0:T(8,128)S(1)}, u32[]{:S(2)}, u32[]{:S(2)}) collective-permute-start(f32[128,256]{1,0:T(8,128)S(1)} %copy-done.17), channel_id=1, source_target_pairs={{0,2},{2,4},{4,6},{6,8},{8,10},{10,12},{12,14},{1,3},{3,5},{5,7},{... | collective-permute-start | bytes 393224 | tf_op jit(solution)/shard_map/ppermute | solution.py:34
  131.2 98.7 %collective-permute-start.6 = (f32[128,64]{1,0:T(8,128)S(1)}, f32[128,64]{1,0:T(8,128)S(1)}, u32[]{:S(2)}, u32[]{:S(2)}) collective-permute-start(f32[128,64]{1,0:T(8,128)S(1)} %copy-done.19), channel_id=1, source_target_pairs={{0,1},{2,3},{4,5},{6,7},{8,9},{10,11},{12,13},{14,15},{16,17},{18,... | collective-permute-start | bytes 98312 | tf_op jit(solution)/shard_map/ppermute | solution.py:36
  132.5 99.4 %collective-permute-start.7 = (f32[128,64]{1,0:T(8,128)S(1)}, f32[128,64]{1,0:T(8,128)S(1)}, u32[]{:S(2)}, u32[]{:S(2)}) collective-permute-start(f32[128,64]{1,0:T(8,128)S(1)} %copy-done.18), channel_id=1, source_target_pairs={{1,0},{3,2},{5,4},{7,6},{9,8},{11,10},{13,12},{15,14},{17,16},{19,... | collective-permute-start | bytes 98312 | tf_op jit(solution)/shard_map/ppermute | solution.py:37
  135.5 101.5 %collective-permute-start.5 = (f32[128,256]{1,0:T(8,128)S(1)}, f32[128,256]{1,0:T(8,128)S(1)}, u32[]{:S(2)}, u32[]{:S(2)}) collective-permute-start(f32[128,256]{1,0:T(8,128)S(1)} %copy-done.16), channel_id=1, source_target_pairs={{2,0},{4,2},{6,4},{8,6},{10,8},{12,10},{14,12},{3,1},{5,3},{7,5},{... | collective-permute-start | bytes 393224 | tf_op jit(solution)/shard_map/ppermute | solution.py:35
  224.2 13.1 %collective-permute-start = (f32[128,256]{1,0:T(8,128)}, f32[128,256]{1,0:T(8,128)S(1)}, u32[]{:S(2)}, u32[]{:S(2)}) collective-permute-start(f32[128,256]{1,0:T(8,128)} %get-tuple-element.34), channel_id=1, source_target_pairs={{0,2},{2,4},{4,6},{6,8},{8,10},{10,12},{12,14},{1,3},{3,5},{5,7},{... | collective-permute-start | bytes 393224 | tf_op jit(solution)/shard_map/ppermute | solution.py:34
  229.9 7.5 %copy-start.6 = (f32[128,64]{1,0:T(8,128)}, f32[128,64]{1,0:T(8,128)S(1)}, u32[]{:S(2)}) copy-start(f32[128,64]{1,0:T(8,128)S(1)} %collective-permute-done.6.qyl_ref) | copy-start | bytes 98308
  229.9 7.4 %collective-permute-start.1 = (f32[128,256]{1,0:T(8,128)}, f32[128,256]{1,0:T(8,128)S(1)}, u32[]{:S(2)}, u32[]{:S(2)}) collective-permute-start(f32[128,256]{1,0:T(8,128)} %get-tuple-element.35), channel_id=1, source_target_pairs={{2,0},{4,2},{6,4},{8,6},{10,8},{12,10},{14,12},{3,1},{5,3},{7,5},{... | collective-permute-start | bytes 393224 | tf_op jit(solution)/shard_map/ppermute | solution.py:35
  231.8 5.5 %copy-start.7 = (f32[128,64]{1,0:T(8,128)}, f32[128,64]{1,0:T(8,128)S(1)}, u32[]{:S(2)}) copy-start(f32[128,64]{1,0:T(8,128)S(1)} %collective-permute-done.7.qyh_ref) | copy-start | bytes 98308
  231.9 5.2 %collective-permute-start.2 = (f32[128,64]{1,0:T(8,128)}, f32[128,64]{1,0:T(8,128)S(1)}, u32[]{:S(2)}, u32[]{:S(2)}) collective-permute-start(f32[128,64]{1,0:T(8,128)} %get-tuple-element.36), channel_id=1, source_target_pairs={{0,1},{2,3},{4,5},{6,7},{8,9},{10,11},{12,13},{14,15},{16,17},{18,... | collective-permute-start | bytes 98312 | tf_op jit(solution)/shard_map/ppermute | solution.py:36
  233.2 4.2 %copy-start = (f32[128,256]{1,0:T(8,128)}, f32[128,256]{1,0:T(8,128)S(1)}, u32[]{:S(2)}) copy-start(f32[128,256]{1,0:T(8,128)S(1)} %collective-permute-done.4.qxl_ref) | copy-start | bytes 393220
  233.2 4.1 %collective-permute-start.3 = (f32[128,64]{1,0:T(8,128)}, f32[128,64]{1,0:T(8,128)S(1)}, u32[]{:S(2)}, u32[]{:S(2)}) collective-permute-start(f32[128,64]{1,0:T(8,128)} %get-tuple-element.37), channel_id=1, source_target_pairs={{1,0},{3,2},{5,4},{7,6},{9,8},{11,10},{13,12},{15,14},{17,16},{19,... | collective-permute-start | bytes 98312 | tf_op jit(solution)/shard_map/ppermute | solution.py:37
  237.1 0.7 copy-start.1
  237.1 0.7 copy-start.8
  237.3 0.7 copy-start.2
  237.3 0.7 copy-start.3
  274.3 11.6 %collective-permute-start.8 = (f32[128,256]{1,0:T(8,128)}, f32[128,256]{1,0:T(8,128)S(1)}, u32[]{:S(2)}, u32[]{:S(2)}) collective-permute-start(f32[128,256]{1,0:T(8,128)} %get-tuple-element.49), channel_id=1, source_target_pairs={{0,2},{2,4},{4,6},{6,8},{8,10},{10,12},{12,14},{1,3},{3,5},{5,7},{... | collective-permute-start | bytes 393224 | tf_op jit(solution)/shard_map/ppermute | solution.py:34
  277.7 8.3 %collective-permute-start.9 = (f32[128,256]{1,0:T(8,128)}, f32[128,256]{1,0:T(8,128)S(1)}, u32[]{:S(2)}, u32[]{:S(2)}) collective-permute-start(f32[128,256]{1,0:T(8,128)} %get-tuple-element.50), channel_id=1, source_target_pairs={{2,0},{4,2},{6,4},{8,6},{10,8},{12,10},{14,12},{3,1},{5,3},{7,5},{... | collective-permute-start | bytes 393224 | tf_op jit(solution)/shard_map/ppermute | solution.py:35
  280.5 4.3 %collective-permute-start.10 = (f32[128,64]{1,0:T(8,128)}, f32[128,64]{1,0:T(8,128)S(1)}, u32[]{:S(2)}, u32[]{:S(2)}) collective-permute-start(f32[128,64]{1,0:T(8,128)} %get-tuple-element.51), channel_id=1, source_target_pairs={{0,1},{2,3},{4,5},{6,7},{8,9},{10,11},{12,13},{14,15},{16,17},{18,... | collective-permute-start | bytes 98312 | tf_op jit(solution)/shard_map/ppermute | solution.py:36
  281.8 4.1 %collective-permute-start.11 = (f32[128,64]{1,0:T(8,128)}, f32[128,64]{1,0:T(8,128)S(1)}, u32[]{:S(2)}, u32[]{:S(2)}) collective-permute-start(f32[128,64]{1,0:T(8,128)} %get-tuple-element.52), channel_id=1, source_target_pairs={{1,0},{3,2},{5,4},{7,6},{9,8},{11,10},{13,12},{15,14},{17,16},{19,... | collective-permute-start | bytes 98312 | tf_op jit(solution)/shard_map/ppermute | solution.py:37
  284.9 1.1 copy-start.10
  286.0 0.7 copy-start.4
  286.0 0.7 copy-start.5
  (2 other events, 1.2 us)

commit v16 on v14

--- a/solution.py
+++ b/solution.py
@@ -14,7 +14,7 @@
 CAP_LOG = 1.5
 CHUNK_Z = 16
 EDGE_Z = 64
-DEPTH_X = 16
+DEPTH_X = 8
 
 
 def permeability(values):

time: 315 us -> 314 us (level)
  no operation moved by 1% of the time
where the time goes in v16:
time: 314 us; the launch traced here: 312 us
  waiting for transfers between devices  161 us (51%)
  Pallas kernels  95 us (30%)
  starting transfers between devices  46.9 us (15%)
  matrix products  6.74 us (2%)
    all_to_all x1, waiting for transfers between devices, body(): lax.all_to_all(outgoing, ('wide', 'narrow'), split_axis=0, concat_axis=0,...  79.8 us
    all_to_all x1, waiting for transfers between devices, body(): lax.all_to_all(first.reshape(groups, planes, rows_x, rows_y), ('wide', 'n...  79.5 us
    pallas_call x1, Pallas kernels, advance(): pl.pallas_call(first_step_kernel, out_shape=tuple(out_shape + [full, full...  36.3 us
    pallas_call x1, Pallas kernels, advance(): pl.pallas_call(later_step_kernel, out_shape=tuple(out_shape), grid=grid,...  27 us
    pallas_call x1, Pallas kernels, depth_transform(): pl.pallas_call(depth_kernel, out_shape=jax.ShapeDtypeStruct(noise.shape,...  13.2 us
    ppermute x3, starting transfers between devices, halos(): x_lo = lax.ppermute(last_x, 'wide', forward_w)  12.1 us
    pallas_call x1, Pallas kernels, line_transforms(): pl.pallas_call(functools.partial(line_kernel, count_w=count_w, count_n=co...  9.68 us
    ppermute x3, starting transfers between devices, halos(): y_hi = lax.ppermute(first_y, 'narrow', backward_n)  9.28 us
  transfers between devices with their start and end apart: 14, of which 4 were waited for; matrix products, arithmetic and copies ran while one was open for 2% of the time, Pallas kernels for 3%

profile of v16, /device:TPU:11, one launch (start us, length us, event | category | flops | bytes accessed | tf_op | source)
XLA Modules:
  0.0 312.5 jit_solution(7929962166111912215)
XLA Ops:
  0.6 13.2 %shard_map.104 = bf16[128,64,256]{2,1,0:T(8,128)(2,1)} custom-call(bf16[128,128]{1,0:T(8,128)(2,1)} %rz_ref.1, bf16[128,64,256]{2,1,0:T(8,128)(2,1)} %n_ref.1), custom_call_target="tpu_custom_call" | custom-call | tf_op jit(solution)/shard_map/pallas_call | solution.py:273
  13.9 6.8 %all-to-all-start = ((bf16[16,8,64,256]{3,2,1,0:T(8,128)(2,1)}), bf16[16,8,64,256]{3,2,1,0:T(8,128)(2,1)}, u32[]{:S(2)}, u32[]{:S(2)}) async-start(bf16[16,8,64,256]{3,2,1,0:T(8,128)(2,1)} %bitcast.9), calls=%async_computation | async-start | bytes 8388608 | tf_op jit(solution)/shard_map/all_to_all | solution.py:323
  20.6 4.0 %shard_map.105 = (f32[128,256]{1,0:T(8,128)}, f32[128,256]{1,0:T(8,128)}, f32[128,64]{1,0:T(8,128)}, f32[128,64]{1,0:T(8,128)}) custom-call(bf16[128,64,256]{2,1,0:T(8,128)(2,1)} %pa_ref.1), custom_call_target="tpu_custom_call" | custom-call | tf_op jit(solution)/shard_map/pallas_call | solution.py:111
  24.7 6.7 %fusion = f32[8192,256]{1,0:T(8,128)} fusion(f32[256]{0:T(256)S(1)} %get-tuple-element.54, s32[256]{0:T(256)S(1)} %multiply_add_fusion, s32[256]{0:T(256)S(1)} %get-tuple-element.55), kind=kOutput, calls=%fused_computation | convolution fusion | flops 6446710784 | bytes 8391680 | tf_op jit(solution)/shard_map/dot_general | solution.py:346
  31.4 79.5 %all-to-all-done.g_ref = bf16[16,8,64,256]{3,2,1,0:T(8,128)(2,1)} async-done(((bf16[16,8,64,256]{3,2,1,0:T(8,128)(2,1)}), bf16[16,8,64,256]{3,2,1,0:T(8,128)(2,1)}, u32[]{:S(2)}, u32[]{:S(2)}) %all-to-all-start) | async-done | bytes 4194336 | tf_op jit(solution)/shard_map/all_to_all | solution.py:323
  111.0 9.7 %shard_map.106 = bf16[16,8,64,256]{3,2,1,0:T(8,128)(2,1)} custom-call(bf16[16,8,64,256]{3,2,1,0:T(8,128)(2,1)} %all-to-all-done.g_ref, bf16[512,512]{1,0:T(8,128)(2,1)} %rx_ref.1, bf16[512,512]{1,0:T(8,128)(2,1)} %ry_ref.1), custom_call_target="tpu_custom_call" | custom-call | tf_op jit(solution)/shard_map/pallas_call | solution.py:306
  120.6 7.1 %all-to-all-start.1 = ((bf16[16,8,64,256]{3,2,1,0:T(8,128)(2,1)}), bf16[16,8,64,256]{3,2,1,0:T(8,128)(2,1)}, u32[]{:S(2)}, u32[]{:S(2)}) async-start(bf16[16,8,64,256]{3,2,1,0:T(8,128)(2,1)} %shard_map.106), calls=%async_computation.1 | async-start | bytes 8388608 | tf_op jit(solution)/shard_map/all_to_all | solution.py:356
  127.7 3.1 collective-permute-start.4
  130.8 1.3 collective-permute-start.6
  132.1 3.0 collective-permute-start.7
  135.2 3.1 collective-permute-start.5
  138.3 79.8 %all-to-all-done.1 = bf16[16,8,64,256]{3,2,1,0:T(8,128)(2,1)} async-done(((bf16[16,8,64,256]{3,2,1,0:T(8,128)(2,1)}), bf16[16,8,64,256]{3,2,1,0:T(8,128)(2,1)}, u32[]{:S(2)}, u32[]{:S(2)}) %all-to-all-start.1) | async-done | bytes 4194336 | tf_op jit(solution)/shard_map/all_to_all | solution.py:356
  218.1 4.7 %shard_map.107 = (f32[128,256]{1,0:T(8,128)}, f32[128,256]{1,0:T(8,128)}, f32[128,64]{1,0:T(8,128)}, f32[128,64]{1,0:T(8,128)}, bf16[128,64,256]{2,1,0:T(8,128)(2,1)}) custom-call(bf16[128,64,256]{2,1,0:T(8,128)(2,1)} %bitcast.2.block_ref), custom_call_target="tpu_custom_call" | custom-call | tf_op jit(solution)/shard_map/pallas_call | solution.py:111
  222.8 5.7 %collective-permute-start = (f32[128,256]{1,0:T(8,128)}, f32[128,256]{1,0:T(8,128)S(1)}, u32[]{:S(2)}, u32[]{:S(2)}) collective-permute-start(f32[128,256]{1,0:T(8,128)} %get-tuple-element.34), channel_id=1, source_target_pairs={{0,2},{2,4},{4,6},{6,8},{8,10},{10,12},{12,14},{1,3},{3,5},{5,7},{... | collective-permute-start | bytes 393224 | tf_op jit(solution)/shard_map/ppermute | solution.py:34
  228.5 1.9 collective-permute-start.1
  230.5 1.3 collective-permute-start.2
  231.8 3.0 collective-permute-start.3
  234.8 0.7 add_convert_fusion.inside_ref
  235.5 0.4 collective-permute-done.3.lyh_ref
  236.0 0.2 copy-done.1
  236.2 0.4 copy-done.9
  236.5 0.1 copy-done.2
  236.6 36.3 %shard_map.108 = (f32[128,64,256]{2,1,0:T(8,128)}, f32[128,256]{1,0:T(8,128)}, f32[128,256]{1,0:T(8,128)}, f32[128,64]{1,0:T(8,128)}, f32[128,64]{1,0:T(8,128)},...) custom-call(s32[4]{0:T(128)} %add_convert_fusion.inside_ref, ...), custom_call_target="tpu_custom_call" | custom-call | tf_op jit(solution)/shard_map/pallas_call | solution.py:240
  272.9 3.4 %collective-permute-start.8 = (f32[128,256]{1,0:T(8,128)}, f32[128,256]{1,0:T(8,128)S(1)}, u32[]{:S(2)}, u32[]{:S(2)}) collective-permute-start(f32[128,256]{1,0:T(8,128)} %get-tuple-element.49), channel_id=1, source_target_pairs={{0,2},{2,4},{4,6},{6,8},{8,10},{10,12},{12,14},{1,3},{3,5},{5,7},{... | collective-permute-start | bytes 393224 | tf_op jit(solution)/shard_map/ppermute | solution.py:34
  276.3 2.8 collective-permute-start.9
  279.1 1.3 collective-permute-start.10
  280.4 3.2 %collective-permute-start.11 = (f32[128,64]{1,0:T(8,128)}, f32[128,64]{1,0:T(8,128)S(1)}, u32[]{:S(2)}, u32[]{:S(2)}) collective-permute-start(f32[128,64]{1,0:T(8,128)} %get-tuple-element.52), channel_id=1, source_target_pairs={{1,0},{3,2},{5,4},{7,6},{9,8},{11,10},{13,12},{15,14},{17,16},{19,... | collective-permute-start | bytes 98312 | tf_op jit(solution)/shard_map/ppermute | solution.py:37
  283.7 0.9 collective-permute-done.11.qyh_ref
  284.6 0.6 copy-done.11
  285.2 0.1 copy-done.4
  285.2 0.1 copy-done.5
  285.3 27.0 %shard_map.109 = (f32[128,64,256]{2,1,0:T(8,128)}, f32[128,256]{1,0:T(8,128)}, f32[128,256]{1,0:T(8,128)}, f32[128,64]{1,0:T(8,128)}, f32[128,64]{1,0:T(8,128)}) custom-call(f32[128,64,256]{2,1,0:T(8,128)} %get-tuple-element.43.tzm_ref.tza_ref, f32[128,64,256]{2,1,0:T(8,128)} %get-tuple-element.43.tzm_ref.tza_ref, ...), custom_call_target="tpu_custom_call" | custom-call | tf_op jit(solution)/shard_map/pallas_call | solution.py:250
  (46 shorter events, 0.2 us)
Async XLA Ops:
  13.9 10.8 %copy-start.12 = (s32[256]{0:T(256)S(1)}, s32[256]{0:T(256)}, u32[]{:S(2)}) copy-start(s32[256]{0:T(256)} %param.14) | copy-start | bytes 3076
  13.9 10.8 %copy-start.13 = (s32[256]{0:T(256)S(1)}, s32[256]{0:T(256)}, u32[]{:S(2)}) copy-start(s32[256]{0:T(256)} %param.16) | copy-start | bytes 3076
  13.9 10.8 %copy-start.14 = (f32[256]{0:T(256)S(1)}, f32[256]{0:T(256)}, u32[]{:S(2)}) copy-start(f32[256]{0:T(256)} %param.17) | copy-start | bytes 3076
  13.9 10.8 %copy-start.15 = (s32[256]{0:T(256)S(1)}, s32[256]{0:T(256)}, u32[]{:S(2)}) copy-start(s32[256]{0:T(256)} %param.15) | copy-start | bytes 3076
  13.9 97.1 %all-to-all-start = ((bf16[16,8,64,256]{3,2,1,0:T(8,128)(2,1)}), bf16[16,8,64,256]{3,2,1,0:T(8,128)(2,1)}, u32[]{:S(2)}, u32[]{:S(2)}) async-start(bf16[16,8,64,256]{3,2,1,0:T(8,128)(2,1)} %bitcast.9), calls=%async_computation | async-start | bytes 8388608 | tf_op jit(solution)/shard_map/all_to_all | solution.py:323
  111.0 16.8 %copy-start.17 = (f32[128,256]{1,0:T(8,128)S(1)}, f32[128,256]{1,0:T(8,128)}, u32[]{:S(2)}) copy-start(f32[128,256]{1,0:T(8,128)} %get-tuple-element.38) | copy-start | bytes 393220
  111.0 19.9 %copy-start.19 = (f32[128,64]{1,0:T(8,128)S(1)}, f32[128,64]{1,0:T(8,128)}, u32[]{:S(2)}) copy-start(f32[128,64]{1,0:T(8,128)} %get-tuple-element.40) | copy-start | bytes 98308
  111.0 21.2 %copy-start.18 = (f32[128,64]{1,0:T(8,128)S(1)}, f32[128,64]{1,0:T(8,128)}, u32[]{:S(2)}) copy-start(f32[128,64]{1,0:T(8,128)} %get-tuple-element.41) | copy-start | bytes 98308
  111.0 24.2 %copy-start.16 = (f32[128,256]{1,0:T(8,128)S(1)}, f32[128,256]{1,0:T(8,128)}, u32[]{:S(2)}) copy-start(f32[128,256]{1,0:T(8,128)} %get-tuple-element.39) | copy-start | bytes 393220
  120.6 97.4 %all-to-all-start.1 = ((bf16[16,8,64,256]{3,2,1,0:T(8,128)(2,1)}), bf16[16,8,64,256]{3,2,1,0:T(8,128)(2,1)}, u32[]{:S(2)}, u32[]{:S(2)}) async-start(bf16[16,8,64,256]{3,2,1,0:T(8,128)(2,1)} %shard_map.106), calls=%async_computation.1 | async-start | bytes 8388608 | tf_op jit(solution)/shard_map/all_to_all | solution.py:356
  127.7 104.0 %collective-permute-start.4 = (f32[128,256]{1,0:T(8,128)S(1)}, f32[128,256]{1,0:T(8,128)S(1)}, u32[]{:S(2)}, u32[]{:S(2)}) collective-permute-start(f32[128,256]{1,0:T(8,128)S(1)} %copy-done.17), channel_id=1, source_target_pairs={{0,2},{2,4},{4,6},{6,8},{8,10},{10,12},{12,14},{1,3},{3,5},{5,7},{... | collective-permute-start | bytes 393224 | tf_op jit(solution)/shard_map/ppermute | solution.py:34
  130.8 97.6 %collective-permute-start.6 = (f32[128,64]{1,0:T(8,128)S(1)}, f32[128,64]{1,0:T(8,128)S(1)}, u32[]{:S(2)}, u32[]{:S(2)}) collective-permute-start(f32[128,64]{1,0:T(8,128)S(1)} %copy-done.19), channel_id=1, source_target_pairs={{0,1},{2,3},{4,5},{6,7},{8,9},{10,11},{12,13},{14,15},{16,17},{18,... | collective-permute-start | bytes 98312 | tf_op jit(solution)/shard_map/ppermute | solution.py:36
  132.1 98.3 %collective-permute-start.7 = (f32[128,64]{1,0:T(8,128)S(1)}, f32[128,64]{1,0:T(8,128)S(1)}, u32[]{:S(2)}, u32[]{:S(2)}) collective-permute-start(f32[128,64]{1,0:T(8,128)S(1)} %copy-done.18), channel_id=1, source_target_pairs={{1,0},{3,2},{5,4},{7,6},{9,8},{11,10},{13,12},{15,14},{17,16},{19,... | collective-permute-start | bytes 98312 | tf_op jit(solution)/shard_map/ppermute | solution.py:37
  135.2 100.3 %collective-permute-start.5 = (f32[128,256]{1,0:T(8,128)S(1)}, f32[128,256]{1,0:T(8,128)S(1)}, u32[]{:S(2)}, u32[]{:S(2)}) collective-permute-start(f32[128,256]{1,0:T(8,128)S(1)} %copy-done.16), channel_id=1, source_target_pairs={{2,0},{4,2},{6,4},{8,6},{10,8},{12,10},{14,12},{3,1},{5,3},{7,5},{... | collective-permute-start | bytes 393224 | tf_op jit(solution)/shard_map/ppermute | solution.py:35
  222.8 13.1 %collective-permute-start = (f32[128,256]{1,0:T(8,128)}, f32[128,256]{1,0:T(8,128)S(1)}, u32[]{:S(2)}, u32[]{:S(2)}) collective-permute-start(f32[128,256]{1,0:T(8,128)} %get-tuple-element.34), channel_id=1, source_target_pairs={{0,2},{2,4},{4,6},{6,8},{8,10},{10,12},{12,14},{1,3},{3,5},{5,7},{... | collective-permute-start | bytes 393224 | tf_op jit(solution)/shard_map/ppermute | solution.py:34
  228.5 7.5 %copy-start.6 = (f32[128,64]{1,0:T(8,128)}, f32[128,64]{1,0:T(8,128)S(1)}, u32[]{:S(2)}) copy-start(f32[128,64]{1,0:T(8,128)S(1)} %collective-permute-done.6.qyl_ref) | copy-start | bytes 98308
  228.5 7.4 %collective-permute-start.1 = (f32[128,256]{1,0:T(8,128)}, f32[128,256]{1,0:T(8,128)S(1)}, u32[]{:S(2)}, u32[]{:S(2)}) collective-permute-start(f32[128,256]{1,0:T(8,128)} %get-tuple-element.35), channel_id=1, source_target_pairs={{2,0},{4,2},{6,4},{8,6},{10,8},{12,10},{14,12},{3,1},{5,3},{7,5},{... | collective-permute-start | bytes 393224 | tf_op jit(solution)/shard_map/ppermute | solution.py:35
  230.4 5.5 %copy-start.7 = (f32[128,64]{1,0:T(8,128)}, f32[128,64]{1,0:T(8,128)S(1)}, u32[]{:S(2)}) copy-start(f32[128,64]{1,0:T(8,128)S(1)} %collective-permute-done.7.qyh_ref) | copy-start | bytes 98308
  230.5 5.0 %collective-permute-start.2 = (f32[128,64]{1,0:T(8,128)}, f32[128,64]{1,0:T(8,128)S(1)}, u32[]{:S(2)}, u32[]{:S(2)}) collective-permute-start(f32[128,64]{1,0:T(8,128)} %get-tuple-element.36), channel_id=1, source_target_pairs={{0,1},{2,3},{4,5},{6,7},{8,9},{10,11},{12,13},{14,15},{16,17},{18,... | collective-permute-start | bytes 98312 | tf_op jit(solution)/shard_map/ppermute | solution.py:36
  231.8 4.2 %copy-start = (f32[128,256]{1,0:T(8,128)}, f32[128,256]{1,0:T(8,128)S(1)}, u32[]{:S(2)}) copy-start(f32[128,256]{1,0:T(8,128)S(1)} %collective-permute-done.4.qxl_ref) | copy-start | bytes 393220
  231.8 4.1 %collective-permute-start.3 = (f32[128,64]{1,0:T(8,128)}, f32[128,64]{1,0:T(8,128)S(1)}, u32[]{:S(2)}, u32[]{:S(2)}) collective-permute-start(f32[128,64]{1,0:T(8,128)} %get-tuple-element.37), channel_id=1, source_target_pairs={{1,0},{3,2},{5,4},{7,6},{9,8},{11,10},{13,12},{15,14},{17,16},{19,... | collective-permute-start | bytes 98312 | tf_op jit(solution)/shard_map/ppermute | solution.py:37
  235.5 0.7 copy-start.1
  235.5 0.7 copy-start.8
  235.9 0.7 copy-start.2
  235.9 0.7 copy-start.3
  272.9 11.6 %collective-permute-start.8 = (f32[128,256]{1,0:T(8,128)}, f32[128,256]{1,0:T(8,128)S(1)}, u32[]{:S(2)}, u32[]{:S(2)}) collective-permute-start(f32[128,256]{1,0:T(8,128)} %get-tuple-element.49), channel_id=1, source_target_pairs={{0,2},{2,4},{4,6},{6,8},{8,10},{10,12},{12,14},{1,3},{3,5},{5,7},{... | collective-permute-start | bytes 393224 | tf_op jit(solution)/shard_map/ppermute | solution.py:34
  276.3 8.3 %collective-permute-start.9 = (f32[128,256]{1,0:T(8,128)}, f32[128,256]{1,0:T(8,128)S(1)}, u32[]{:S(2)}, u32[]{:S(2)}) collective-permute-start(f32[128,256]{1,0:T(8,128)} %get-tuple-element.50), channel_id=1, source_target_pairs={{2,0},{4,2},{6,4},{8,6},{10,8},{12,10},{14,12},{3,1},{5,3},{7,5},{... | collective-permute-start | bytes 393224 | tf_op jit(solution)/shard_map/ppermute | solution.py:35
  279.1 4.5 %collective-permute-start.10 = (f32[128,64]{1,0:T(8,128)}, f32[128,64]{1,0:T(8,128)S(1)}, u32[]{:S(2)}, u32[]{:S(2)}) collective-permute-start(f32[128,64]{1,0:T(8,128)} %get-tuple-element.51), channel_id=1, source_target_pairs={{0,1},{2,3},{4,5},{6,7},{8,9},{10,11},{12,13},{14,15},{16,17},{18,... | collective-permute-start | bytes 98312 | tf_op jit(solution)/shard_map/ppermute | solution.py:36
  280.4 4.1 %collective-permute-start.11 = (f32[128,64]{1,0:T(8,128)}, f32[128,64]{1,0:T(8,128)S(1)}, u32[]{:S(2)}, u32[]{:S(2)}) collective-permute-start(f32[128,64]{1,0:T(8,128)} %get-tuple-element.52), channel_id=1, source_target_pairs={{1,0},{3,2},{5,4},{7,6},{9,8},{11,10},{13,12},{15,14},{17,16},{19,... | collective-permute-start | bytes 98312 | tf_op jit(solution)/shard_map/ppermute | solution.py:37
  283.7 0.9 copy-start.10
  284.6 0.7 copy-start.4
  284.6 0.7 copy-start.5
  (2 other events, 1.2 us)

commit v17 on v14

--- a/solution.py
+++ b/solution.py
@@ -193,8 +193,47 @@
     )
 
 
+def trans_kernel(lpm_ref, lpb_ref, lpa_ref, tzm_ref, txm_ref, tym_ref, cx0_ref, cxl_ref, cy0_ref, cyl_ref):
+    c = pl.program_id(0)
+    last = pl.num_programs(0) - 1
+    tz, nx, ny = lpm_ref.shape
+    f32 = jnp.float32
+    below = jnp.where(c == 0, 0.0, permeability(lpb_ref[...].astype(f32)))
+    above = jnp.where(c == last, 0.0, permeability(lpa_ref[...].astype(f32)))
+    centre = permeability(lpm_ref[...].astype(f32))
+    ext = jnp.concatenate([below, centre, above], axis=0)
+    tzm_ref[...] = harmonic(ext[:-2], ext[1:-1])
+    txm_ref[...] = pltpu.roll(harmonic(centre, pltpu.roll(centre, nx - 1, 1)), 1, 1)
+    tym_ref[...] = pltpu.roll(harmonic(centre, pltpu.roll(centre, ny - 1, 2)), 1, 2)
+    store_x_rows(cx0_ref, centre[:, :1, :])
+    store_x_rows(cxl_ref, centre[:, nx - 1 :, :])
+    cy0_ref[...], cyl_ref[...] = to_rows(centre)
+
+
+def face_transmissibilities(log_perm):
+    depth, nx, ny = log_perm.shape
+    tz = CHUNK_Z
+    f32 = jnp.float32
+    main = pl.BlockSpec((tz, nx, ny), lambda c: (c, 0, 0))
+    below = pl.BlockSpec((1, nx, ny), lambda c: (jnp.maximum(c * tz - 1, 0), 0, 0))
+    above = pl.BlockSpec((1, nx, ny), lambda c: (jnp.minimum(c * tz + tz, depth - 1), 0, 0))
+    row = pl.BlockSpec((tz, ny), lambda c: (c, 0))
+    col = pl.BlockSpec((tz, nx), lambda c: (c, 0))
+    full = jax.ShapeDtypeStruct((depth, nx, ny), f32)
+    rows = jax.ShapeDtypeStruct((depth, ny), f32)
+    cols = jax.ShapeDtypeStruct((depth, nx), f32)
+    return pl.pallas_call(
+        trans_kernel,
+        out_shape=(full, full, full, rows, rows, cols, cols),
+        grid=(depth // tz,),
+        in_specs=[main, below, above],
+        out_specs=[main, main, main, row, row, col, col],
+        compiler_params=pltpu.CompilerParams(dimension_semantics=("arbitrary",)),
+    )(log_perm, log_perm, log_perm)
+
+
 def later_step_kernel(
-    tzm_ref, tza_ref, txm_ref, tym_ref, txp_ref, typ_ref,
+    tzm_ref, tza_ref, txm_ref, tym_ref, txp_ref, typ_ref, bxm_ref, bym_ref,
     pm_ref, pb_ref, pa_ref, qxl_ref, qxh_ref, qyl_ref, qyh_ref, f_ref,
     o_ref, exl_ref, exh_ref, eyl_ref, eyh_ref,
 ):
@@ -205,10 +244,12 @@
     yi = lax.broadcasted_iota(jnp.int32, (tz, nx, ny), 2)
     t_zm = tzm_ref[...]
     t_zp = jnp.concatenate([t_zm[1:], jnp.where(c == last, 0.0, tza_ref[...])], axis=0)
-    t_xm = txm_ref[...]
-    t_xp = jnp.where(xi == nx - 1, x_rows(txp_ref), pltpu.roll(t_xm, nx - 1, 1))
-    t_ym = tym_ref[...]
-    t_yp = jnp.where(yi == ny - 1, to_columns(typ_ref[...]), pltpu.roll(t_ym, ny - 1, 2))
+    raw_xm = txm_ref[...]
+    t_xp = jnp.where(xi == nx - 1, x_rows(txp_ref), pltpu.roll(raw_xm, nx - 1, 1))
+    t_xm = jnp.where(xi == 0, x_rows(bxm_ref), raw_xm)
+    raw_ym = tym_ref[...]
+    t_yp = jnp.where(yi == ny - 1, to_columns(typ_ref[...]), pltpu.roll(raw_ym, ny - 1, 2))
+    t_ym = jnp.where(yi == 0, to_columns(bym_ref[...]), raw_ym)
     update(
         (t_zp, t_zm, t_xp, t_xm, t_yp, t_ym),
         pm_ref, pb_ref, pa_ref, qxl_ref, qxh_ref, qyl_ref, qyh_ref, f_ref,
@@ -246,15 +287,15 @@
             compiler_params=params,
         )(inside, log_perm, log_perm, log_perm, *perm_halos, *pressure_args)
         return outs[0], outs[1:5], outs[5:]
-    t_zm, t_xm, t_ym, t_xp, t_yp = stored
+    t_zm, t_xm, t_ym, t_xp, t_yp, b_xm, b_ym = stored
     outs = pl.pallas_call(
         later_step_kernel,
         out_shape=tuple(out_shape),
         grid=grid,
-        in_specs=[main, above, main, main, row, col] + pressure_specs,
+        in_specs=[main, above, main, main, row, col, row, col] + pressure_specs,
         out_specs=out_specs,
         compiler_params=params,
-    )(t_zm, t_zm, t_xm, t_ym, t_xp, t_yp, *pressure_args)
+    )(t_zm, t_zm, t_xm, t_ym, t_xp, t_yp, b_xm, b_ym, *pressure_args)
     return outs[0], outs[1:5], stored
 
 
@@ -360,7 +401,17 @@
     *lp_edges, log_perm = block_edges(log_perm, keep=True)
     perm_halos = halos(lp_edges)
     pressure = pressure_start
-    stored = None
+    t_zm, t_xm, t_ym, c_x0, c_xl, c_y0, c_yl = face_transmissibilities(log_perm)
+    k_xl, k_xh, k_yl, k_yh = perm_halos
+    f32 = jnp.float32
+    k_xl = jnp.where(wide_at > 0, permeability(k_xl), 0.0)
+    k_xh = jnp.where(wide_at < last_w, permeability(k_xh), 0.0)
+    k_yl = jnp.where(narrow_at > 0, permeability(k_yl), 0.0)
+    k_yh = jnp.where(narrow_at < last_n, permeability(k_yh), 0.0)
+    stored = (
+        t_zm, t_xm, t_ym,
+        harmonic(c_xl, k_xh), harmonic(c_yl, k_yh), harmonic(c_x0, k_xl), harmonic(c_y0, k_yl),
+    )
     for step in range(STEPS):
         pressure, edges, stored = advance(
             stored, pressure, halos(edges), flow, inside, log_perm, perm_halos

time: 315 us -> 345 us (1.095)
  blocking collectives: 0 us -> 100 us
  waiting for transfers between devices: 161 us -> 88 us
  starting transfers between devices: 46.9 us -> 35.9 us
  Pallas kernels: 95.3 us -> 105 us
  other arithmetic: 0.69 us -> 6.32 us
    all_to_all x0 -> x1, blocking collectives: none -> 100 us  [body(): lax.all_to_all(outgoing, ('wide', 'narrow'), split_axis=0, concat_axis=0,...]
    all_to_all x1 -> x0, waiting for transfers between devices: 79.8 us -> none  [body(): lax.all_to_all(outgoing, ('wide', 'narrow'), split_axis=0, concat_axis=0,...]
    pallas_call x1 -> x2, Pallas kernels: 27 us -> 57.6 us  [advance(): pl.pallas_call(later_step_kernel, out_shape=tuple(out_shape), grid=grid,...]
    pallas_call x1, Pallas kernels: 36.3 us -> 15.2 us  [face_transmissibilities(): pl.pallas_call(trans_kernel, out_shape=(full, full, full, rows, rows, col...]
    all_to_all x1 -> x0, starting transfers between devices: 7.07 us -> none  [body(): lax.all_to_all(outgoing, ('wide', 'narrow'), split_axis=0, concat_axis=0,...]
    div x0 -> x4, other arithmetic: none -> 6.3 us  [harmonic(): return 2.0 * a * b / (a + b)]
    ppermute x3, starting transfers between devices: 12.1 us -> 6.58 us  [halos(): x_lo = lax.ppermute(last_x, 'wide', forward_w)]
    ppermute x3, waiting for transfers between devices: 0.01 us -> 4.7 us  [halos(): x_lo = lax.ppermute(last_x, 'wide', forward_w)]
  transfers between devices with their start and end apart: 14 -> 13, of which waited for: 4 -> 4; matrix products, arithmetic and copies ran while one was open for 2% -> 4% of each run, Pallas kernels for 3% -> 6%
where the time goes in v17:
time: 345 us; the launch traced here: 344 us
  Pallas kernels  105 us (30%)
  blocking collectives  100 us (29%)
  waiting for transfers between devices  88 us (26%)
  starting transfers between devices  35.9 us (10%)
  matrix products  6.73 us (2%)
  other arithmetic  6.32 us (2%)
    all_to_all x1, blocking collectives, body(): lax.all_to_all(outgoing, ('wide', 'narrow'), split_axis=0, concat_axis=0,...  100 us
    all_to_all x1, waiting for transfers between devices, body(): lax.all_to_all(first.reshape(groups, planes, rows_x, rows_y), ('wide', 'n...  79.5 us
    pallas_call x2, Pallas kernels, advance(): pl.pallas_call(later_step_kernel, out_shape=tuple(out_shape), grid=grid,...  57.6 us
    pallas_call x1, Pallas kernels, face_transmissibilities(): pl.pallas_call(trans_kernel, out_shape=(full, full, full, rows, rows, col...  15.2 us
    pallas_call x1, Pallas kernels, depth_transform(): pl.pallas_call(depth_kernel, out_shape=jax.ShapeDtypeStruct(noise.shape,...  13.6 us
    ppermute x3, starting transfers between devices, halos(): x_hi = lax.ppermute(first_x, 'wide', backward_w)  9.78 us
    pallas_call x1, Pallas kernels, line_transforms(): pl.pallas_call(functools.partial(line_kernel, count_w=count_w, count_n=co...  9.62 us
    ppermute x3, starting transfers between devices, halos(): y_hi = lax.ppermute(first_y, 'narrow', backward_n)  8.78 us
  transfers between devices with their start and end apart: 13, of which 4 were waited for; matrix products, arithmetic and copies ran while one was open for 4% of the time, Pallas kernels for 6%

profile of v17, /device:TPU:11, one launch (start us, length us, event | category | flops | bytes accessed | tf_op | source)
XLA Modules:
  0.0 344.2 jit_solution(7166221992640430959)
XLA Ops:
  0.6 13.6 %shard_map.104 = bf16[128,64,256]{2,1,0:T(8,128)(2,1)} custom-call(bf16[128,128]{1,0:T(8,128)(2,1)} %rz_ref.1, bf16[128,64,256]{2,1,0:T(8,128)(2,1)} %n_ref.1), custom_call_target="tpu_custom_call" | custom-call | tf_op jit(solution)/shard_map/pallas_call | solution.py:314
  14.2 6.8 %all-to-all-start = ((bf16[16,8,64,256]{3,2,1,0:T(8,128)(2,1)}), bf16[16,8,64,256]{3,2,1,0:T(8,128)(2,1)}, u32[]{:S(2)}, u32[]{:S(2)}) async-start(bf16[16,8,64,256]{3,2,1,0:T(8,128)(2,1)} %bitcast.5), calls=%async_computation | async-start | bytes 8388608 | tf_op jit(solution)/shard_map/all_to_all | solution.py:364
  21.0 4.0 %shard_map.105 = (f32[128,256]{1,0:T(8,128)}, f32[128,256]{1,0:T(8,128)}, f32[128,64]{1,0:T(8,128)}, f32[128,64]{1,0:T(8,128)}) custom-call(bf16[128,64,256]{2,1,0:T(8,128)(2,1)} %pa_ref.1), custom_call_target="tpu_custom_call" | custom-call | tf_op jit(solution)/shard_map/pallas_call | solution.py:111
  25.0 6.7 %fusion = f32[8192,256]{1,0:T(8,128)} fusion(f32[256]{0:T(256)S(1)} %get-tuple-element.58, s32[256]{0:T(256)S(1)} %multiply_add_fusion, s32[256]{0:T(256)S(1)} %get-tuple-element.59), kind=kOutput, calls=%fused_computation | convolution fusion | flops 6446710784 | bytes 8391680 | tf_op jit(solution)/shard_map/dot_general | solution.py:387
  31.7 79.5 %all-to-all-done.g_ref = bf16[16,8,64,256]{3,2,1,0:T(8,128)(2,1)} async-done(((bf16[16,8,64,256]{3,2,1,0:T(8,128)(2,1)}), bf16[16,8,64,256]{3,2,1,0:T(8,128)(2,1)}, u32[]{:S(2)}, u32[]{:S(2)}) %all-to-all-start) | async-done | bytes 4194336 | tf_op jit(solution)/shard_map/all_to_all | solution.py:364
  111.3 9.6 %shard_map.106 = bf16[16,8,64,256]{3,2,1,0:T(8,128)(2,1)} custom-call(bf16[16,8,64,256]{3,2,1,0:T(8,128)(2,1)} %all-to-all-done.g_ref, bf16[512,512]{1,0:T(8,128)(2,1)} %rx_ref.1, bf16[512,512]{1,0:T(8,128)(2,1)} %ry_ref.1), custom_call_target="tpu_custom_call" | custom-call | tf_op jit(solution)/shard_map/pallas_call | solution.py:347
  120.9 100.1 %all_to_all.10 = bf16[16,8,64,256]{3,2,1,0:T(8,128)(2,1)} all-to-all(bf16[16,8,64,256]{3,2,1,0:T(8,128)(2,1)} %shard_map.106), channel_id=1, replica_groups=mesh['member'=2,'wide'=8,'narrow'=2] {'wide','narrow'}, dimensions={0} | all-to-all | bytes 8388608 | tf_op jit(solution)/shard_map/all_to_all | solution.py:397
  221.0 4.7 %shard_map.107 = (f32[128,256]{1,0:T(8,128)}, f32[128,256]{1,0:T(8,128)}, f32[128,64]{1,0:T(8,128)}, f32[128,64]{1,0:T(8,128)}, bf16[128,64,256]{2,1,0:T(8,128)(2,1)}) custom-call(bf16[128,64,256]{2,1,0:T(8,128)(2,1)} %bitcast.6), custom_call_target="tpu_custom_call" | custom-call | tf_op jit(solution)/shard_map/pallas_call | solution.py:111
  225.8 1.4 collective-permute-start.3
  227.2 1.3 collective-permute-start.6
  228.5 3.0 collective-permute-start.7
  231.6 2.5 collective-permute-start.4
  234.2 3.6 %collective-permute-start.5 = (f32[128,256]{1,0:T(8,128)S(1)}, f32[128,256]{1,0:T(8,128)S(1)}, u32[]{:S(2)}, u32[]{:S(2)}) collective-permute-start(f32[128,256]{1,0:T(8,128)S(1)} %copy-done.12), channel_id=1, source_target_pairs={{2,0},{4,2},{6,4},{8,6},{10,8},{12,10},{14,12},{3,1},{5,3},{7,5},{... | collective-permute-start | bytes 393224 | tf_op jit(solution)/shard_map/ppermute | solution.py:35
  237.8 15.2 %shard_map.108 = (f32[128,64,256]{2,1,0:T(8,128)}, f32[128,64,256]{2,1,0:T(8,128)}, f32[128,64,256]{2,1,0:T(8,128)}, f32[128,256]{1,0:T(8,128)}, f32[128,256]{1,...) custom-call(bf16[128,64,256]{2,1,0:T(8,128)(2,1)} %get-tuple-element.28.lpm_ref.lpb_ref.lpa_ref, ...), custom_call_target="tpu_custom_call" | custom-call | tf_op jit(solution)/shard_map/pallas_call | solution.py:225
  253.0 1.9 collective-permute-start.1
  254.8 1.5 add_divide_fusion.2.bym_ref
  256.4 1.9 collective-permute-start.2
  258.3 1.5 add_divide_fusion.3.typ_ref
  259.8 4.7 %collective-permute-done.2 = f32[128,256]{1,0:T(8,128)S(1)} collective-permute-done((f32[128,256]{1,0:T(8,128)S(1)}, f32[128,256]{1,0:T(8,128)S(1)}, u32[]{:S(2)}, u32[]{:S(2)}) %collective-permute-start.2) | collective-permute-done | bytes 131104 | tf_op jit(solution)/shard_map/ppermute | solution.py:34
  264.5 2.1 collective-permute-start
  266.6 1.6 add_divide_fusion.bxm_ref
  268.2 2.6 collective-permute-done
  270.9 1.6 add_divide_fusion.1.txp_ref
  272.6 0.6 copy-done.4
  273.2 28.3 %shard_map.109 = (f32[128,64,256]{2,1,0:T(8,128)}, f32[128,256]{1,0:T(8,128)}, f32[128,256]{1,0:T(8,128)}, f32[128,64]{1,0:T(8,128)}, f32[128,64]{1,0:T(8,128)}) custom-call(f32[128,64,256]{2,1,0:T(8,128)} %get-tuple-element.36.tzm_ref.tza_ref, f32[128,64,256]{2,1,0:T(8,128)} %get-tuple-element.36.tzm_ref.tza_ref, ...), custom_call_target="tpu_custom_call" | custom-call | tf_op jit(solution)/shard_map/pallas_call | solution.py:291
  301.6 2.1 collective-permute-start.8
  303.7 4.1 %collective-permute-start.9 = (f32[128,256]{1,0:T(8,128)}, f32[128,256]{1,0:T(8,128)S(1)}, u32[]{:S(2)}, u32[]{:S(2)}) collective-permute-start(f32[128,256]{1,0:T(8,128)} %get-tuple-element.54), channel_id=1, source_target_pairs={{2,0},{4,2},{6,4},{8,6},{10,8},{12,10},{14,12},{3,1},{5,3},{7,5},{... | collective-permute-start | bytes 393224 | tf_op jit(solution)/shard_map/ppermute | solution.py:35
  307.8 1.3 collective-permute-start.10
  309.1 3.9 %collective-permute-start.11 = (f32[128,64]{1,0:T(8,128)}, f32[128,64]{1,0:T(8,128)S(1)}, u32[]{:S(2)}, u32[]{:S(2)}) collective-permute-start(f32[128,64]{1,0:T(8,128)} %get-tuple-element.56), channel_id=1, source_target_pairs={{1,0},{3,2},{5,4},{7,6},{9,8},{11,10},{13,12},{15,14},{17,16},{19,... | collective-permute-start | bytes 98312 | tf_op jit(solution)/shard_map/ppermute | solution.py:37
  313.0 1.1 collective-permute-done.11.qyh_ref
  314.1 0.6 copy-done.7
  314.8 29.3 %shard_map.110 = (f32[128,64,256]{2,1,0:T(8,128)}, f32[128,256]{1,0:T(8,128)}, f32[128,256]{1,0:T(8,128)}, f32[128,64]{1,0:T(8,128)}, f32[128,64]{1,0:T(8,128)}) custom-call(f32[128,64,256]{2,1,0:T(8,128)} %get-tuple-element.36.tzm_ref.tza_ref, f32[128,64,256]{2,1,0:T(8,128)} %get-tuple-element.36.tzm_ref.tza_ref, ...), custom_call_target="tpu_custom_call" | custom-call | tf_op jit(solution)/shard_map/pallas_call | solution.py:291
  (47 shorter events, 0.3 us)
Async XLA Ops:
  14.2 10.8 %copy-start.8 = (s32[256]{0:T(256)S(1)}, s32[256]{0:T(256)}, u32[]{:S(2)}) copy-start(s32[256]{0:T(256)} %param.14) | copy-start | bytes 3076
  14.2 10.8 %copy-start.9 = (s32[256]{0:T(256)S(1)}, s32[256]{0:T(256)}, u32[]{:S(2)}) copy-start(s32[256]{0:T(256)} %param.16) | copy-start | bytes 3076
  14.2 10.8 %copy-start.10 = (f32[256]{0:T(256)S(1)}, f32[256]{0:T(256)}, u32[]{:S(2)}) copy-start(f32[256]{0:T(256)} %param.17) | copy-start | bytes 3076
  14.2 10.8 %copy-start.11 = (s32[256]{0:T(256)S(1)}, s32[256]{0:T(256)}, u32[]{:S(2)}) copy-start(s32[256]{0:T(256)} %param.15) | copy-start | bytes 3076
  14.2 97.1 %all-to-all-start = ((bf16[16,8,64,256]{3,2,1,0:T(8,128)(2,1)}), bf16[16,8,64,256]{3,2,1,0:T(8,128)(2,1)}, u32[]{:S(2)}, u32[]{:S(2)}) async-start(bf16[16,8,64,256]{3,2,1,0:T(8,128)(2,1)} %bitcast.5), calls=%async_computation | async-start | bytes 8388608 | tf_op jit(solution)/shard_map/all_to_all | solution.py:364
  120.9 106.3 %copy-start.17 = (f32[128,64]{1,0:T(8,128)S(1)}, f32[128,64]{1,0:T(8,128)}, u32[]{:S(2)}) copy-start(f32[128,64]{1,0:T(8,128)} %get-tuple-element.49) | copy-start | bytes 98308
  120.9 107.6 %copy-start.16 = (f32[128,64]{1,0:T(8,128)S(1)}, f32[128,64]{1,0:T(8,128)}, u32[]{:S(2)}) copy-start(f32[128,64]{1,0:T(8,128)} %get-tuple-element.50) | copy-start | bytes 98308
  120.9 110.7 %copy-start.13 = (f32[128,256]{1,0:T(8,128)S(1)}, f32[128,256]{1,0:T(8,128)}, u32[]{:S(2)}) copy-start(f32[128,256]{1,0:T(8,128)} %get-tuple-element.47) | copy-start | bytes 393220
  120.9 113.2 %copy-start.12 = (f32[128,256]{1,0:T(8,128)S(1)}, f32[128,256]{1,0:T(8,128)}, u32[]{:S(2)}) copy-start(f32[128,256]{1,0:T(8,128)} %get-tuple-element.48) | copy-start | bytes 393220
  225.8 27.2 %copy-start.18 = (f32[128,64]{1,0:T(8,128)S(1)}, f32[128,64]{1,0:T(8,128)}, u32[]{:S(2)}) copy-start(f32[128,64]{1,0:T(8,128)} %get-tuple-element.42) | copy-start | bytes 98308
  225.8 30.6 %copy-start.15 = (f32[128,256]{1,0:T(8,128)S(1)}, f32[128,256]{1,0:T(8,128)}, u32[]{:S(2)}) copy-start(f32[128,256]{1,0:T(8,128)} %get-tuple-element.44) | copy-start | bytes 393220
  225.8 38.7 %copy-start.14 = (f32[128,256]{1,0:T(8,128)S(1)}, f32[128,256]{1,0:T(8,128)}, u32[]{:S(2)}) copy-start(f32[128,256]{1,0:T(8,128)} %get-tuple-element.40) | copy-start | bytes 393220
  225.8 27.2 %collective-permute-start.3 = (f32[128,64]{1,0:T(8,128)}, f32[128,64]{1,0:T(8,128)S(1)}, u32[]{:S(2)}, u32[]{:S(2)}) collective-permute-start(f32[128,64]{1,0:T(8,128)} %get-tuple-element.46), channel_id=1, source_target_pairs={{0,1},{2,3},{4,5},{6,7},{8,9},{10,11},{12,13},{14,15},{16,17},{18,... | collective-permute-start | bytes 98312 | tf_op jit(solution)/shard_map/ppermute | solution.py:36
  227.2 45.3 %collective-permute-start.6 = (f32[128,64]{1,0:T(8,128)S(1)}, f32[128,64]{1,0:T(8,128)S(1)}, u32[]{:S(2)}, u32[]{:S(2)}) collective-permute-start(f32[128,64]{1,0:T(8,128)S(1)} %copy-done.17), channel_id=1, source_target_pairs={{0,1},{2,3},{4,5},{6,7},{8,9},{10,11},{12,13},{14,15},{16,17},{18,... | collective-permute-start | bytes 98312 | tf_op jit(solution)/shard_map/ppermute | solution.py:36
  228.5 44.0 %collective-permute-start.7 = (f32[128,64]{1,0:T(8,128)S(1)}, f32[128,64]{1,0:T(8,128)S(1)}, u32[]{:S(2)}, u32[]{:S(2)}) collective-permute-start(f32[128,64]{1,0:T(8,128)S(1)} %copy-done.16), channel_id=1, source_target_pairs={{1,0},{3,2},{5,4},{7,6},{9,8},{11,10},{13,12},{15,14},{17,16},{19,... | collective-permute-start | bytes 98312 | tf_op jit(solution)/shard_map/ppermute | solution.py:37
  231.6 40.9 %collective-permute-start.4 = (f32[128,256]{1,0:T(8,128)S(1)}, f32[128,256]{1,0:T(8,128)S(1)}, u32[]{:S(2)}, u32[]{:S(2)}) collective-permute-start(f32[128,256]{1,0:T(8,128)S(1)} %copy-done.13), channel_id=1, source_target_pairs={{0,2},{2,4},{4,6},{6,8},{8,10},{10,12},{12,14},{1,3},{3,5},{5,7},{... | collective-permute-start | bytes 393224 | tf_op jit(solution)/shard_map/ppermute | solution.py:34
  234.2 38.4 %collective-permute-start.5 = (f32[128,256]{1,0:T(8,128)S(1)}, f32[128,256]{1,0:T(8,128)S(1)}, u32[]{:S(2)}, u32[]{:S(2)}) collective-permute-start(f32[128,256]{1,0:T(8,128)S(1)} %copy-done.12), channel_id=1, source_target_pairs={{2,0},{4,2},{6,4},{8,6},{10,8},{12,10},{14,12},{3,1},{5,3},{7,5},{... | collective-permute-start | bytes 393224 | tf_op jit(solution)/shard_map/ppermute | solution.py:35
  253.0 3.4 collective-permute-start.1
  256.4 8.1 %collective-permute-start.2 = (f32[128,256]{1,0:T(8,128)S(1)}, f32[128,256]{1,0:T(8,128)S(1)}, u32[]{:S(2)}, u32[]{:S(2)}) collective-permute-start(f32[128,256]{1,0:T(8,128)S(1)} %copy-done.15), channel_id=1, source_target_pairs={{0,2},{2,4},{4,6},{6,8},{8,10},{10,12},{12,14},{1,3},{3,5},{5,7},{... | collective-permute-start | bytes 393224 | tf_op jit(solution)/shard_map/ppermute | solution.py:34
  264.5 6.4 %collective-permute-start = (f32[128,256]{1,0:T(8,128)S(1)}, f32[128,256]{1,0:T(8,128)S(1)}, u32[]{:S(2)}, u32[]{:S(2)}) collective-permute-start(f32[128,256]{1,0:T(8,128)S(1)} %copy-done.14), channel_id=1, source_target_pairs={{2,0},{4,2},{6,4},{8,6},{10,8},{12,10},{14,12},{3,1},{5,3},{7,5},{... | collective-permute-start | bytes 393224 | tf_op jit(solution)/shard_map/ppermute | solution.py:35
  272.5 0.6 copy-start.4
  272.5 0.7 copy-start.5
  272.5 0.7 copy-start
  272.5 0.7 copy-start.1
  301.6 12.5 %collective-permute-start.8 = (f32[128,256]{1,0:T(8,128)}, f32[128,256]{1,0:T(8,128)S(1)}, u32[]{:S(2)}, u32[]{:S(2)}) collective-permute-start(f32[128,256]{1,0:T(8,128)} %get-tuple-element.53), channel_id=1, source_target_pairs={{0,2},{2,4},{4,6},{6,8},{8,10},{10,12},{12,14},{1,3},{3,5},{5,7},{... | collective-permute-start | bytes 393224 | tf_op jit(solution)/shard_map/ppermute | solution.py:34
  303.7 10.4 %collective-permute-start.9 = (f32[128,256]{1,0:T(8,128)}, f32[128,256]{1,0:T(8,128)S(1)}, u32[]{:S(2)}, u32[]{:S(2)}) collective-permute-start(f32[128,256]{1,0:T(8,128)} %get-tuple-element.54), channel_id=1, source_target_pairs={{2,0},{4,2},{6,4},{8,6},{10,8},{12,10},{14,12},{3,1},{5,3},{7,5},{... | collective-permute-start | bytes 393224 | tf_op jit(solution)/shard_map/ppermute | solution.py:35
  307.8 5.2 %collective-permute-start.10 = (f32[128,64]{1,0:T(8,128)}, f32[128,64]{1,0:T(8,128)S(1)}, u32[]{:S(2)}, u32[]{:S(2)}) collective-permute-start(f32[128,64]{1,0:T(8,128)} %get-tuple-element.55), channel_id=1, source_target_pairs={{0,1},{2,3},{4,5},{6,7},{8,9},{10,11},{12,13},{14,15},{16,17},{18,... | collective-permute-start | bytes 98312 | tf_op jit(solution)/shard_map/ppermute | solution.py:36
  309.1 5.0 %collective-permute-start.11 = (f32[128,64]{1,0:T(8,128)}, f32[128,64]{1,0:T(8,128)S(1)}, u32[]{:S(2)}, u32[]{:S(2)}) collective-permute-start(f32[128,64]{1,0:T(8,128)} %get-tuple-element.56), channel_id=1, source_target_pairs={{1,0},{3,2},{5,4},{7,6},{9,8},{11,10},{13,12},{15,14},{17,16},{19,... | collective-permute-start | bytes 98312 | tf_op jit(solution)/shard_map/ppermute | solution.py:37
  313.0 1.1 copy-start.6
  314.1 0.6 copy-start.7
  314.1 0.7 copy-start.2
  314.1 0.7 copy-start.3

commit v18 on v14

--- a/solution.py
+++ b/solution.py
@@ -60,7 +60,7 @@
         ref[k : k + 1, :] = rows[k]
 
 
-def to_rows(block):
+def to_rows(block, last_only=False):
     tz, nx, ny = block.shape
     lane = lax.broadcasted_iota(jnp.int32, (nx, 128), 1)
     pick = jnp.where(
@@ -68,7 +68,7 @@
         1.0, 0.0,
     )
     result = []
-    for column in (0, ny - 1):
+    for column in ((ny - 1,) if last_only else (0, ny - 1)):
         gathered = jnp.zeros((nx, 128), jnp.float32)
         for k in range(tz):
             gathered = jnp.where(lane == k, block[k, :, column : column + 1], gathered)
@@ -78,7 +78,7 @@
                 precision=lax.Precision.HIGHEST, preferred_element_type=jnp.float32,
             )
         )
-    return result[0], result[1]
+    return tuple(result)
 
 
 def edge_kernel(block_ref, xl_ref, xh_ref, yl_ref, yh_ref, *copy_ref):
@@ -185,7 +185,7 @@
     txm_ref[...] = t_xm
     tym_ref[...] = t_ym
     store_x_rows(txp_ref, t_xp[:, nx - 1 :, :])
-    typ_ref[...] = to_rows(t_yp)[1]
+    typ_ref[...] = to_rows(t_yp, last_only=True)[0]
     update(
         (t_zp, t_zm, t_xp, t_xm, t_yp, t_ym),
         pm_ref, pb_ref, pa_ref, qxl_ref, qxh_ref, qyl_ref, qyh_ref, f_ref,

time: 315 us -> 315 us (level)
  no operation moved by 1% of the time
where the time goes in v18:
time: 315 us; the launch traced here: 313 us
  waiting for transfers between devices  161 us (51%)
  Pallas kernels  95.3 us (30%)
  starting transfers between devices  46.9 us (15%)
  matrix products  6.74 us (2%)
    all_to_all x1, waiting for transfers between devices, body(): lax.all_to_all(outgoing, ('wide', 'narrow'), split_axis=0, concat_axis=0,...  79.8 us
    all_to_all x1, waiting for transfers between devices, body(): lax.all_to_all(first.reshape(groups, planes, rows_x, rows_y), ('wide', 'n...  79.5 us
    pallas_call x1, Pallas kernels, advance(): pl.pallas_call(first_step_kernel, out_shape=tuple(out_shape + [full, full...  36.3 us
    pallas_call x1, Pallas kernels, advance(): pl.pallas_call(later_step_kernel, out_shape=tuple(out_shape), grid=grid,...  27 us
    pallas_call x1, Pallas kernels, depth_transform(): pl.pallas_call(depth_kernel, out_shape=jax.ShapeDtypeStruct(noise.shape,...  13.6 us
    ppermute x3, starting transfers between devices, halos(): x_lo = lax.ppermute(last_x, 'wide', forward_w)  12.1 us
    pallas_call x1, Pallas kernels, line_transforms(): pl.pallas_call(functools.partial(line_kernel, count_w=count_w, count_n=co...  9.68 us
    ppermute x3, starting transfers between devices, halos(): y_hi = lax.ppermute(first_y, 'narrow', backward_n)  9.28 us
  transfers between devices with their start and end apart: 14, of which 4 were waited for; matrix products, arithmetic and copies ran while one was open for 2% of the time, Pallas kernels for 3%

profile of v18, /device:TPU:11, one launch (start us, length us, event | category | flops | bytes accessed | tf_op | source)
XLA Modules:
  0.0 312.8 jit_solution(13054475650408781063)
XLA Ops:
  0.6 13.6 %shard_map.104 = bf16[128,64,256]{2,1,0:T(8,128)(2,1)} custom-call(bf16[128,128]{1,0:T(8,128)(2,1)} %rz_ref.1, bf16[128,64,256]{2,1,0:T(8,128)(2,1)} %n_ref.1), custom_call_target="tpu_custom_call" | custom-call | tf_op jit(solution)/shard_map/pallas_call | solution.py:273
  14.2 6.8 %all-to-all-start = ((bf16[16,8,64,256]{3,2,1,0:T(8,128)(2,1)}), bf16[16,8,64,256]{3,2,1,0:T(8,128)(2,1)}, u32[]{:S(2)}, u32[]{:S(2)}) async-start(bf16[16,8,64,256]{3,2,1,0:T(8,128)(2,1)} %bitcast.9), calls=%async_computation | async-start | bytes 8388608 | tf_op jit(solution)/shard_map/all_to_all | solution.py:323
  21.0 4.0 %shard_map.105 = (f32[128,256]{1,0:T(8,128)}, f32[128,256]{1,0:T(8,128)}, f32[128,64]{1,0:T(8,128)}, f32[128,64]{1,0:T(8,128)}) custom-call(bf16[128,64,256]{2,1,0:T(8,128)(2,1)} %pa_ref.1), custom_call_target="tpu_custom_call" | custom-call | tf_op jit(solution)/shard_map/pallas_call | solution.py:111
  25.0 6.7 %fusion = f32[8192,256]{1,0:T(8,128)} fusion(f32[256]{0:T(256)S(1)} %get-tuple-element.54, s32[256]{0:T(256)S(1)} %multiply_add_fusion, s32[256]{0:T(256)S(1)} %get-tuple-element.55), kind=kOutput, calls=%fused_computation | convolution fusion | flops 6446710784 | bytes 8391680 | tf_op jit(solution)/shard_map/dot_general | solution.py:346
  31.8 79.5 %all-to-all-done.g_ref = bf16[16,8,64,256]{3,2,1,0:T(8,128)(2,1)} async-done(((bf16[16,8,64,256]{3,2,1,0:T(8,128)(2,1)}), bf16[16,8,64,256]{3,2,1,0:T(8,128)(2,1)}, u32[]{:S(2)}, u32[]{:S(2)}) %all-to-all-start) | async-done | bytes 4194336 | tf_op jit(solution)/shard_map/all_to_all | solution.py:323
  111.3 9.7 %shard_map.106 = bf16[16,8,64,256]{3,2,1,0:T(8,128)(2,1)} custom-call(bf16[16,8,64,256]{3,2,1,0:T(8,128)(2,1)} %all-to-all-done.g_ref, bf16[512,512]{1,0:T(8,128)(2,1)} %rx_ref.1, bf16[512,512]{1,0:T(8,128)(2,1)} %ry_ref.1), custom_call_target="tpu_custom_call" | custom-call | tf_op jit(solution)/shard_map/pallas_call | solution.py:306
  121.0 7.1 %all-to-all-start.1 = ((bf16[16,8,64,256]{3,2,1,0:T(8,128)(2,1)}), bf16[16,8,64,256]{3,2,1,0:T(8,128)(2,1)}, u32[]{:S(2)}, u32[]{:S(2)}) async-start(bf16[16,8,64,256]{3,2,1,0:T(8,128)(2,1)} %shard_map.106), calls=%async_computation.1 | async-start | bytes 8388608 | tf_op jit(solution)/shard_map/all_to_all | solution.py:356
  128.0 3.1 collective-permute-start.4
  131.2 1.3 collective-permute-start.6
  132.5 3.0 collective-permute-start.7
  135.5 3.1 collective-permute-start.5
  138.6 79.8 %all-to-all-done.1 = bf16[16,8,64,256]{3,2,1,0:T(8,128)(2,1)} async-done(((bf16[16,8,64,256]{3,2,1,0:T(8,128)(2,1)}), bf16[16,8,64,256]{3,2,1,0:T(8,128)(2,1)}, u32[]{:S(2)}, u32[]{:S(2)}) %all-to-all-start.1) | async-done | bytes 4194336 | tf_op jit(solution)/shard_map/all_to_all | solution.py:356
  218.4 4.7 %shard_map.107 = (f32[128,256]{1,0:T(8,128)}, f32[128,256]{1,0:T(8,128)}, f32[128,64]{1,0:T(8,128)}, f32[128,64]{1,0:T(8,128)}, bf16[128,64,256]{2,1,0:T(8,128)(2,1)}) custom-call(bf16[128,64,256]{2,1,0:T(8,128)(2,1)} %bitcast.2.block_ref), custom_call_target="tpu_custom_call" | custom-call | tf_op jit(solution)/shard_map/pallas_call | solution.py:111
  223.1 5.7 %collective-permute-start = (f32[128,256]{1,0:T(8,128)}, f32[128,256]{1,0:T(8,128)S(1)}, u32[]{:S(2)}, u32[]{:S(2)}) collective-permute-start(f32[128,256]{1,0:T(8,128)} %get-tuple-element.34), channel_id=1, source_target_pairs={{0,2},{2,4},{4,6},{6,8},{8,10},{10,12},{12,14},{1,3},{3,5},{5,7},{... | collective-permute-start | bytes 393224 | tf_op jit(solution)/shard_map/ppermute | solution.py:34
  228.8 1.9 collective-permute-start.1
  230.8 1.3 collective-permute-start.2
  232.1 3.2 %collective-permute-start.3 = (f32[128,64]{1,0:T(8,128)}, f32[128,64]{1,0:T(8,128)S(1)}, u32[]{:S(2)}, u32[]{:S(2)}) collective-permute-start(f32[128,64]{1,0:T(8,128)} %get-tuple-element.37), channel_id=1, source_target_pairs={{1,0},{3,2},{5,4},{7,6},{9,8},{11,10},{13,12},{15,14},{17,16},{19,... | collective-permute-start | bytes 98312 | tf_op jit(solution)/shard_map/ppermute | solution.py:37
  235.3 0.7 add_convert_fusion.inside_ref
  236.0 0.2 collective-permute-done.3.lyh_ref
  236.3 0.4 copy-done.1
  236.7 0.2 copy-done.9
  236.9 0.1 copy-done.2
  237.0 36.3 %shard_map.108 = (f32[128,64,256]{2,1,0:T(8,128)}, f32[128,256]{1,0:T(8,128)}, f32[128,256]{1,0:T(8,128)}, f32[128,64]{1,0:T(8,128)}, f32[128,64]{1,0:T(8,128)},...) custom-call(s32[4]{0:T(128)} %add_convert_fusion.inside_ref, ...), custom_call_target="tpu_custom_call" | custom-call | tf_op jit(solution)/shard_map/pallas_call | solution.py:240
  273.3 3.4 %collective-permute-start.8 = (f32[128,256]{1,0:T(8,128)}, f32[128,256]{1,0:T(8,128)S(1)}, u32[]{:S(2)}, u32[]{:S(2)}) collective-permute-start(f32[128,256]{1,0:T(8,128)} %get-tuple-element.49), channel_id=1, source_target_pairs={{0,2},{2,4},{4,6},{6,8},{8,10},{10,12},{12,14},{1,3},{3,5},{5,7},{... | collective-permute-start | bytes 393224 | tf_op jit(solution)/shard_map/ppermute | solution.py:34
  276.6 2.8 collective-permute-start.9
  279.4 1.3 collective-permute-start.10
  280.7 3.0 collective-permute-start.11
  283.8 1.1 collective-permute-done.11.qyh_ref
  284.9 0.6 copy-done.11
  285.5 0.1 copy-done.4
  285.6 0.1 copy-done.5
  285.6 27.0 %shard_map.109 = (f32[128,64,256]{2,1,0:T(8,128)}, f32[128,256]{1,0:T(8,128)}, f32[128,256]{1,0:T(8,128)}, f32[128,64]{1,0:T(8,128)}, f32[128,64]{1,0:T(8,128)}) custom-call(f32[128,64,256]{2,1,0:T(8,128)} %get-tuple-element.43.tzm_ref.tza_ref, f32[128,64,256]{2,1,0:T(8,128)} %get-tuple-element.43.tzm_ref.tza_ref, ...), custom_call_target="tpu_custom_call" | custom-call | tf_op jit(solution)/shard_map/pallas_call | solution.py:250
  (46 shorter events, 0.2 us)
Async XLA Ops:
  14.2 10.8 %copy-start.12 = (s32[256]{0:T(256)S(1)}, s32[256]{0:T(256)}, u32[]{:S(2)}) copy-start(s32[256]{0:T(256)} %param.14) | copy-start | bytes 3076
  14.2 10.8 %copy-start.13 = (s32[256]{0:T(256)S(1)}, s32[256]{0:T(256)}, u32[]{:S(2)}) copy-start(s32[256]{0:T(256)} %param.16) | copy-start | bytes 3076
  14.2 10.8 %copy-start.14 = (f32[256]{0:T(256)S(1)}, f32[256]{0:T(256)}, u32[]{:S(2)}) copy-start(f32[256]{0:T(256)} %param.17) | copy-start | bytes 3076
  14.2 10.8 %copy-start.15 = (s32[256]{0:T(256)S(1)}, s32[256]{0:T(256)}, u32[]{:S(2)}) copy-start(s32[256]{0:T(256)} %param.15) | copy-start | bytes 3076
  14.2 97.1 %all-to-all-start = ((bf16[16,8,64,256]{3,2,1,0:T(8,128)(2,1)}), bf16[16,8,64,256]{3,2,1,0:T(8,128)(2,1)}, u32[]{:S(2)}, u32[]{:S(2)}) async-start(bf16[16,8,64,256]{3,2,1,0:T(8,128)(2,1)} %bitcast.9), calls=%async_computation | async-start | bytes 8388608 | tf_op jit(solution)/shard_map/all_to_all | solution.py:323
  111.3 16.8 %copy-start.17 = (f32[128,256]{1,0:T(8,128)S(1)}, f32[128,256]{1,0:T(8,128)}, u32[]{:S(2)}) copy-start(f32[128,256]{1,0:T(8,128)} %get-tuple-element.38) | copy-start | bytes 393220
  111.3 19.9 %copy-start.19 = (f32[128,64]{1,0:T(8,128)S(1)}, f32[128,64]{1,0:T(8,128)}, u32[]{:S(2)}) copy-start(f32[128,64]{1,0:T(8,128)} %get-tuple-element.40) | copy-start | bytes 98308
  111.3 21.2 %copy-start.18 = (f32[128,64]{1,0:T(8,128)S(1)}, f32[128,64]{1,0:T(8,128)}, u32[]{:S(2)}) copy-start(f32[128,64]{1,0:T(8,128)} %get-tuple-element.41) | copy-start | bytes 98308
  111.3 24.2 %copy-start.16 = (f32[128,256]{1,0:T(8,128)S(1)}, f32[128,256]{1,0:T(8,128)}, u32[]{:S(2)}) copy-start(f32[128,256]{1,0:T(8,128)} %get-tuple-element.39) | copy-start | bytes 393220
  121.0 97.4 %all-to-all-start.1 = ((bf16[16,8,64,256]{3,2,1,0:T(8,128)(2,1)}), bf16[16,8,64,256]{3,2,1,0:T(8,128)(2,1)}, u32[]{:S(2)}, u32[]{:S(2)}) async-start(bf16[16,8,64,256]{3,2,1,0:T(8,128)(2,1)} %shard_map.106), calls=%async_computation.1 | async-start | bytes 8388608 | tf_op jit(solution)/shard_map/all_to_all | solution.py:356
  128.0 104.0 %collective-permute-start.4 = (f32[128,256]{1,0:T(8,128)S(1)}, f32[128,256]{1,0:T(8,128)S(1)}, u32[]{:S(2)}, u32[]{:S(2)}) collective-permute-start(f32[128,256]{1,0:T(8,128)S(1)} %copy-done.17), channel_id=1, source_target_pairs={{0,2},{2,4},{4,6},{6,8},{8,10},{10,12},{12,14},{1,3},{3,5},{5,7},{... | collective-permute-start | bytes 393224 | tf_op jit(solution)/shard_map/ppermute | solution.py:34
  131.2 97.6 %collective-permute-start.6 = (f32[128,64]{1,0:T(8,128)S(1)}, f32[128,64]{1,0:T(8,128)S(1)}, u32[]{:S(2)}, u32[]{:S(2)}) collective-permute-start(f32[128,64]{1,0:T(8,128)S(1)} %copy-done.19), channel_id=1, source_target_pairs={{0,1},{2,3},{4,5},{6,7},{8,9},{10,11},{12,13},{14,15},{16,17},{18,... | collective-permute-start | bytes 98312 | tf_op jit(solution)/shard_map/ppermute | solution.py:36
  132.5 98.3 %collective-permute-start.7 = (f32[128,64]{1,0:T(8,128)S(1)}, f32[128,64]{1,0:T(8,128)S(1)}, u32[]{:S(2)}, u32[]{:S(2)}) collective-permute-start(f32[128,64]{1,0:T(8,128)S(1)} %copy-done.18), channel_id=1, source_target_pairs={{1,0},{3,2},{5,4},{7,6},{9,8},{11,10},{13,12},{15,14},{17,16},{19,... | collective-permute-start | bytes 98312 | tf_op jit(solution)/shard_map/ppermute | solution.py:37
  135.5 100.5 %collective-permute-start.5 = (f32[128,256]{1,0:T(8,128)S(1)}, f32[128,256]{1,0:T(8,128)S(1)}, u32[]{:S(2)}, u32[]{:S(2)}) collective-permute-start(f32[128,256]{1,0:T(8,128)S(1)} %copy-done.16), channel_id=1, source_target_pairs={{2,0},{4,2},{6,4},{8,6},{10,8},{12,10},{14,12},{3,1},{5,3},{7,5},{... | collective-permute-start | bytes 393224 | tf_op jit(solution)/shard_map/ppermute | solution.py:35
  223.1 13.1 %collective-permute-start = (f32[128,256]{1,0:T(8,128)}, f32[128,256]{1,0:T(8,128)S(1)}, u32[]{:S(2)}, u32[]{:S(2)}) collective-permute-start(f32[128,256]{1,0:T(8,128)} %get-tuple-element.34), channel_id=1, source_target_pairs={{0,2},{2,4},{4,6},{6,8},{8,10},{10,12},{12,14},{1,3},{3,5},{5,7},{... | collective-permute-start | bytes 393224 | tf_op jit(solution)/shard_map/ppermute | solution.py:34
  228.8 7.5 %copy-start.6 = (f32[128,64]{1,0:T(8,128)}, f32[128,64]{1,0:T(8,128)S(1)}, u32[]{:S(2)}) copy-start(f32[128,64]{1,0:T(8,128)S(1)} %collective-permute-done.6.qyl_ref) | copy-start | bytes 98308
  228.8 7.4 %collective-permute-start.1 = (f32[128,256]{1,0:T(8,128)}, f32[128,256]{1,0:T(8,128)S(1)}, u32[]{:S(2)}, u32[]{:S(2)}) collective-permute-start(f32[128,256]{1,0:T(8,128)} %get-tuple-element.35), channel_id=1, source_target_pairs={{2,0},{4,2},{6,4},{8,6},{10,8},{12,10},{14,12},{3,1},{5,3},{7,5},{... | collective-permute-start | bytes 393224 | tf_op jit(solution)/shard_map/ppermute | solution.py:35
  230.8 5.5 %copy-start.7 = (f32[128,64]{1,0:T(8,128)}, f32[128,64]{1,0:T(8,128)S(1)}, u32[]{:S(2)}) copy-start(f32[128,64]{1,0:T(8,128)S(1)} %collective-permute-done.7.qyh_ref) | copy-start | bytes 98308
  230.8 5.2 %collective-permute-start.2 = (f32[128,64]{1,0:T(8,128)}, f32[128,64]{1,0:T(8,128)S(1)}, u32[]{:S(2)}, u32[]{:S(2)}) collective-permute-start(f32[128,64]{1,0:T(8,128)} %get-tuple-element.36), channel_id=1, source_target_pairs={{0,1},{2,3},{4,5},{6,7},{8,9},{10,11},{12,13},{14,15},{16,17},{18,... | collective-permute-start | bytes 98312 | tf_op jit(solution)/shard_map/ppermute | solution.py:36
  232.1 4.2 %copy-start = (f32[128,256]{1,0:T(8,128)}, f32[128,256]{1,0:T(8,128)S(1)}, u32[]{:S(2)}) copy-start(f32[128,256]{1,0:T(8,128)S(1)} %collective-permute-done.4.qxl_ref) | copy-start | bytes 393220
  232.1 4.1 %collective-permute-start.3 = (f32[128,64]{1,0:T(8,128)}, f32[128,64]{1,0:T(8,128)S(1)}, u32[]{:S(2)}, u32[]{:S(2)}) collective-permute-start(f32[128,64]{1,0:T(8,128)} %get-tuple-element.37), channel_id=1, source_target_pairs={{1,0},{3,2},{5,4},{7,6},{9,8},{11,10},{13,12},{15,14},{17,16},{19,... | collective-permute-start | bytes 98312 | tf_op jit(solution)/shard_map/ppermute | solution.py:37
  236.0 0.7 copy-start.1
  236.0 0.7 copy-start.8
  236.2 0.7 copy-start.2
  236.3 0.7 copy-start.3
  273.3 11.6 %collective-permute-start.8 = (f32[128,256]{1,0:T(8,128)}, f32[128,256]{1,0:T(8,128)S(1)}, u32[]{:S(2)}, u32[]{:S(2)}) collective-permute-start(f32[128,256]{1,0:T(8,128)} %get-tuple-element.49), channel_id=1, source_target_pairs={{0,2},{2,4},{4,6},{6,8},{8,10},{10,12},{12,14},{1,3},{3,5},{5,7},{... | collective-permute-start | bytes 393224 | tf_op jit(solution)/shard_map/ppermute | solution.py:34
  276.6 8.3 %collective-permute-start.9 = (f32[128,256]{1,0:T(8,128)}, f32[128,256]{1,0:T(8,128)S(1)}, u32[]{:S(2)}, u32[]{:S(2)}) collective-permute-start(f32[128,256]{1,0:T(8,128)} %get-tuple-element.50), channel_id=1, source_target_pairs={{2,0},{4,2},{6,4},{8,6},{10,8},{12,10},{14,12},{3,1},{5,3},{7,5},{... | collective-permute-start | bytes 393224 | tf_op jit(solution)/shard_map/ppermute | solution.py:35
  279.4 4.3 %collective-permute-start.10 = (f32[128,64]{1,0:T(8,128)}, f32[128,64]{1,0:T(8,128)S(1)}, u32[]{:S(2)}, u32[]{:S(2)}) collective-permute-start(f32[128,64]{1,0:T(8,128)} %get-tuple-element.51), channel_id=1, source_target_pairs={{0,1},{2,3},{4,5},{6,7},{8,9},{10,11},{12,13},{14,15},{16,17},{18,... | collective-permute-start | bytes 98312 | tf_op jit(solution)/shard_map/ppermute | solution.py:36
  280.7 4.1 %collective-permute-start.11 = (f32[128,64]{1,0:T(8,128)}, f32[128,64]{1,0:T(8,128)S(1)}, u32[]{:S(2)}, u32[]{:S(2)}) collective-permute-start(f32[128,64]{1,0:T(8,128)} %get-tuple-element.52), channel_id=1, source_target_pairs={{1,0},{3,2},{5,4},{7,6},{9,8},{11,10},{13,12},{15,14},{17,16},{19,... | collective-permute-start | bytes 98312 | tf_op jit(solution)/shard_map/ppermute | solution.py:37
  283.8 1.1 copy-start.10
  284.9 0.7 copy-start.4
  284.9 0.7 copy-start.5
  (2 other events, 1.2 us)

commit v19 on v14

--- a/solution.py
+++ b/solution.py
@@ -285,28 +285,30 @@
     nx = g_ref.shape[2]
     ny = g_ref.shape[3]
     rx = rx_ref[...]
-    halves = []
-    for n in range(count_n):
-        lines = jnp.concatenate([g_ref[w * count_n + n, 0] for w in range(count_w)], axis=0)
-        halves.append(jnp.dot(rx, lines, preferred_element_type=f32).astype(jnp.bfloat16))
-    second = jnp.concatenate(halves, axis=1)
-    third = lax.dot_general(
-        second, ry_ref[...], (((1,), (1,)), ((), ())), preferred_element_type=f32
-    ).astype(jnp.bfloat16)
-    for w in range(count_w):
+    for z in range(g_ref.shape[1]):
+        halves = []
         for n in range(count_n):
-            o_ref[w * count_n + n, 0] = third[w * nx : (w + 1) * nx, n * ny : (n + 1) * ny]
+            lines = jnp.concatenate([g_ref[w * count_n + n, z] for w in range(count_w)], axis=0)
+            halves.append(jnp.dot(rx, lines, preferred_element_type=f32).astype(jnp.bfloat16))
+        second = jnp.concatenate(halves, axis=1)
+        third = lax.dot_general(
+            second, ry_ref[...], (((1,), (1,)), ((), ())), preferred_element_type=f32
+        ).astype(jnp.bfloat16)
+        for w in range(count_w):
+            for n in range(count_n):
+                o_ref[w * count_n + n, z] = third[w * nx : (w + 1) * nx, n * ny : (n + 1) * ny]
 
 
 def line_transforms(gathered, root_x, root_y, count_w, count_n):
     groups, planes, nx, ny = gathered.shape
-    block = pl.BlockSpec((groups, 1, nx, ny), lambda z: (0, z, 0, 0))
+    step = 2 if planes % 2 == 0 else 1
+    block = pl.BlockSpec((groups, step, nx, ny), lambda z: (0, z, 0, 0))
     whole_x = pl.BlockSpec(root_x.shape, lambda z: (0, 0))
     whole_y = pl.BlockSpec(root_y.shape, lambda z: (0, 0))
     return pl.pallas_call(
         functools.partial(line_kernel, count_w=count_w, count_n=count_n),
         out_shape=jax.ShapeDtypeStruct(gathered.shape, jnp.bfloat16),
-        grid=(planes,),
+        grid=(planes // step,),
         in_specs=[block, whole_x, whole_y],
         out_specs=block,
         compiler_params=pltpu.CompilerParams(dimension_semantics=("arbitrary",)),

time: 315 us -> 313 us (level)
  no operation moved by 1% of the time
where the time goes in v19:
time: 313 us; the launch traced here: 311 us
  waiting for transfers between devices  161 us (51%)
  Pallas kernels  93.7 us (30%)
  starting transfers between devices  46.9 us (15%)
  matrix products  6.74 us (2%)
    all_to_all x1, waiting for transfers between devices, body(): lax.all_to_all(outgoing, ('wide', 'narrow'), split_axis=0, concat_axis=0,...  79.8 us
    all_to_all x1, waiting for transfers between devices, body(): lax.all_to_all(first.reshape(groups, planes, rows_x, rows_y), ('wide', 'n...  79.5 us
    pallas_call x1, Pallas kernels, advance(): pl.pallas_call(first_step_kernel, out_shape=tuple(out_shape + [full, full...  36.3 us
    pallas_call x1, Pallas kernels, advance(): pl.pallas_call(later_step_kernel, out_shape=tuple(out_shape), grid=grid,...  27 us
    pallas_call x1, Pallas kernels, depth_transform(): pl.pallas_call(depth_kernel, out_shape=jax.ShapeDtypeStruct(noise.shape,...  13.6 us
    ppermute x3, starting transfers between devices, halos(): x_lo = lax.ppermute(last_x, 'wide', forward_w)  12.1 us
    ppermute x3, starting transfers between devices, halos(): y_hi = lax.ppermute(first_y, 'narrow', backward_n)  9.28 us
    pallas_call x2, Pallas kernels, block_edges(): pl.pallas_call(edge_kernel, out_shape=tuple(out_shape), grid=(depth // tz...  8.71 us
  transfers between devices with their start and end apart: 14, of which 4 were waited for; matrix products, arithmetic and copies ran while one was open for 2% of the time, Pallas kernels for 3%

profile of v19, /device:TPU:11, one launch (start us, length us, event | category | flops | bytes accessed | tf_op | source)
XLA Modules:
  0.0 311.2 jit_solution(363311313268159191)
XLA Ops:
  0.6 13.6 %shard_map.104 = bf16[128,64,256]{2,1,0:T(8,128)(2,1)} custom-call(bf16[128,128]{1,0:T(8,128)(2,1)} %rz_ref.1, bf16[128,64,256]{2,1,0:T(8,128)(2,1)} %n_ref.1), custom_call_target="tpu_custom_call" | custom-call | tf_op jit(solution)/shard_map/pallas_call | solution.py:273
  14.2 6.8 %all-to-all-start = ((bf16[16,8,64,256]{3,2,1,0:T(8,128)(2,1)}), bf16[16,8,64,256]{3,2,1,0:T(8,128)(2,1)}, u32[]{:S(2)}, u32[]{:S(2)}) async-start(bf16[16,8,64,256]{3,2,1,0:T(8,128)(2,1)} %bitcast.9), calls=%async_computation | async-start | bytes 8388608 | tf_op jit(solution)/shard_map/all_to_all | solution.py:325
  21.0 4.0 %shard_map.105 = (f32[128,256]{1,0:T(8,128)}, f32[128,256]{1,0:T(8,128)}, f32[128,64]{1,0:T(8,128)}, f32[128,64]{1,0:T(8,128)}) custom-call(bf16[128,64,256]{2,1,0:T(8,128)(2,1)} %pa_ref.1), custom_call_target="tpu_custom_call" | custom-call | tf_op jit(solution)/shard_map/pallas_call | solution.py:111
  25.0 6.7 %fusion = f32[8192,256]{1,0:T(8,128)} fusion(f32[256]{0:T(256)S(1)} %get-tuple-element.54, s32[256]{0:T(256)S(1)} %multiply_add_fusion, s32[256]{0:T(256)S(1)} %get-tuple-element.55), kind=kOutput, calls=%fused_computation | convolution fusion | flops 6446710784 | bytes 8391680 | tf_op jit(solution)/shard_map/dot_general | solution.py:348
  31.8 79.5 %all-to-all-done.g_ref = bf16[16,8,64,256]{3,2,1,0:T(8,128)(2,1)} async-done(((bf16[16,8,64,256]{3,2,1,0:T(8,128)(2,1)}), bf16[16,8,64,256]{3,2,1,0:T(8,128)(2,1)}, u32[]{:S(2)}, u32[]{:S(2)}) %all-to-all-start) | async-done | bytes 4194336 | tf_op jit(solution)/shard_map/all_to_all | solution.py:325
  111.3 8.1 %shard_map.106 = bf16[16,8,64,256]{3,2,1,0:T(8,128)(2,1)} custom-call(bf16[16,8,64,256]{3,2,1,0:T(8,128)(2,1)} %all-to-all-done.g_ref, bf16[512,512]{1,0:T(8,128)(2,1)} %rx_ref.1, bf16[512,512]{1,0:T(8,128)(2,1)} %ry_ref.1), custom_call_target="tpu_custom_call" | custom-call | tf_op jit(solution)/shard_map/pallas_call | solution.py:308
  119.3 7.1 %all-to-all-start.1 = ((bf16[16,8,64,256]{3,2,1,0:T(8,128)(2,1)}), bf16[16,8,64,256]{3,2,1,0:T(8,128)(2,1)}, u32[]{:S(2)}, u32[]{:S(2)}) async-start(bf16[16,8,64,256]{3,2,1,0:T(8,128)(2,1)} %shard_map.106), calls=%async_computation.1 | async-start | bytes 8388608 | tf_op jit(solution)/shard_map/all_to_all | solution.py:358
  126.4 3.1 collective-permute-start.4
  129.5 1.3 collective-permute-start.6
  130.8 3.0 collective-permute-start.7
  133.9 3.1 collective-permute-start.5
  137.0 79.8 %all-to-all-done.1 = bf16[16,8,64,256]{3,2,1,0:T(8,128)(2,1)} async-done(((bf16[16,8,64,256]{3,2,1,0:T(8,128)(2,1)}), bf16[16,8,64,256]{3,2,1,0:T(8,128)(2,1)}, u32[]{:S(2)}, u32[]{:S(2)}) %all-to-all-start.1) | async-done | bytes 4194336 | tf_op jit(solution)/shard_map/all_to_all | solution.py:358
  216.8 4.7 %shard_map.107 = (f32[128,256]{1,0:T(8,128)}, f32[128,256]{1,0:T(8,128)}, f32[128,64]{1,0:T(8,128)}, f32[128,64]{1,0:T(8,128)}, bf16[128,64,256]{2,1,0:T(8,128)(2,1)}) custom-call(bf16[128,64,256]{2,1,0:T(8,128)(2,1)} %bitcast.2.block_ref), custom_call_target="tpu_custom_call" | custom-call | tf_op jit(solution)/shard_map/pallas_call | solution.py:111
  221.5 5.7 %collective-permute-start = (f32[128,256]{1,0:T(8,128)}, f32[128,256]{1,0:T(8,128)S(1)}, u32[]{:S(2)}, u32[]{:S(2)}) collective-permute-start(f32[128,256]{1,0:T(8,128)} %get-tuple-element.34), channel_id=1, source_target_pairs={{0,2},{2,4},{4,6},{6,8},{8,10},{10,12},{12,14},{1,3},{3,5},{5,7},{... | collective-permute-start | bytes 393224 | tf_op jit(solution)/shard_map/ppermute | solution.py:34
  227.2 1.9 collective-permute-start.1
  229.2 1.3 collective-permute-start.2
  230.5 3.2 %collective-permute-start.3 = (f32[128,64]{1,0:T(8,128)}, f32[128,64]{1,0:T(8,128)S(1)}, u32[]{:S(2)}, u32[]{:S(2)}) collective-permute-start(f32[128,64]{1,0:T(8,128)} %get-tuple-element.37), channel_id=1, source_target_pairs={{1,0},{3,2},{5,4},{7,6},{9,8},{11,10},{13,12},{15,14},{17,16},{19,... | collective-permute-start | bytes 98312 | tf_op jit(solution)/shard_map/ppermute | solution.py:37
  233.7 0.7 add_convert_fusion.inside_ref
  234.4 0.2 collective-permute-done.3.lyh_ref
  234.7 0.4 copy-done.1
  235.1 0.2 copy-done.9
  235.2 0.1 copy-done.2
  235.3 36.3 %shard_map.108 = (f32[128,64,256]{2,1,0:T(8,128)}, f32[128,256]{1,0:T(8,128)}, f32[128,256]{1,0:T(8,128)}, f32[128,64]{1,0:T(8,128)}, f32[128,64]{1,0:T(8,128)},...) custom-call(s32[4]{0:T(128)} %add_convert_fusion.inside_ref, ...), custom_call_target="tpu_custom_call" | custom-call | tf_op jit(solution)/shard_map/pallas_call | solution.py:240
  271.6 3.4 %collective-permute-start.8 = (f32[128,256]{1,0:T(8,128)}, f32[128,256]{1,0:T(8,128)S(1)}, u32[]{:S(2)}, u32[]{:S(2)}) collective-permute-start(f32[128,256]{1,0:T(8,128)} %get-tuple-element.49), channel_id=1, source_target_pairs={{0,2},{2,4},{4,6},{6,8},{8,10},{10,12},{12,14},{1,3},{3,5},{5,7},{... | collective-permute-start | bytes 393224 | tf_op jit(solution)/shard_map/ppermute | solution.py:34
  275.0 2.8 collective-permute-start.9
  277.8 1.3 collective-permute-start.10
  279.1 3.0 collective-permute-start.11
  282.2 1.1 collective-permute-done.11.qyh_ref
  283.3 0.6 copy-done.11
  283.9 0.1 copy-done.4
  283.9 0.1 copy-done.5
  284.0 27.0 %shard_map.109 = (f32[128,64,256]{2,1,0:T(8,128)}, f32[128,256]{1,0:T(8,128)}, f32[128,256]{1,0:T(8,128)}, f32[128,64]{1,0:T(8,128)}, f32[128,64]{1,0:T(8,128)}) custom-call(f32[128,64,256]{2,1,0:T(8,128)} %get-tuple-element.43.tzm_ref.tza_ref, f32[128,64,256]{2,1,0:T(8,128)} %get-tuple-element.43.tzm_ref.tza_ref, ...), custom_call_target="tpu_custom_call" | custom-call | tf_op jit(solution)/shard_map/pallas_call | solution.py:250
  (46 shorter events, 0.2 us)
Async XLA Ops:
  14.2 10.8 %copy-start.12 = (s32[256]{0:T(256)S(1)}, s32[256]{0:T(256)}, u32[]{:S(2)}) copy-start(s32[256]{0:T(256)} %param.14) | copy-start | bytes 3076
  14.2 10.8 %copy-start.13 = (s32[256]{0:T(256)S(1)}, s32[256]{0:T(256)}, u32[]{:S(2)}) copy-start(s32[256]{0:T(256)} %param.16) | copy-start | bytes 3076
  14.2 10.8 %copy-start.14 = (f32[256]{0:T(256)S(1)}, f32[256]{0:T(256)}, u32[]{:S(2)}) copy-start(f32[256]{0:T(256)} %param.17) | copy-start | bytes 3076
  14.2 10.8 %copy-start.15 = (s32[256]{0:T(256)S(1)}, s32[256]{0:T(256)}, u32[]{:S(2)}) copy-start(s32[256]{0:T(256)} %param.15) | copy-start | bytes 3076
  14.2 97.1 %all-to-all-start = ((bf16[16,8,64,256]{3,2,1,0:T(8,128)(2,1)}), bf16[16,8,64,256]{3,2,1,0:T(8,128)(2,1)}, u32[]{:S(2)}, u32[]{:S(2)}) async-start(bf16[16,8,64,256]{3,2,1,0:T(8,128)(2,1)} %bitcast.9), calls=%async_computation | async-start | bytes 8388608 | tf_op jit(solution)/shard_map/all_to_all | solution.py:325
  111.3 15.1 %copy-start.17 = (f32[128,256]{1,0:T(8,128)S(1)}, f32[128,256]{1,0:T(8,128)}, u32[]{:S(2)}) copy-start(f32[128,256]{1,0:T(8,128)} %get-tuple-element.38) | copy-start | bytes 393220
  111.3 18.2 %copy-start.19 = (f32[128,64]{1,0:T(8,128)S(1)}, f32[128,64]{1,0:T(8,128)}, u32[]{:S(2)}) copy-start(f32[128,64]{1,0:T(8,128)} %get-tuple-element.40) | copy-start | bytes 98308
  111.3 19.5 %copy-start.18 = (f32[128,64]{1,0:T(8,128)S(1)}, f32[128,64]{1,0:T(8,128)}, u32[]{:S(2)}) copy-start(f32[128,64]{1,0:T(8,128)} %get-tuple-element.41) | copy-start | bytes 98308
  111.3 22.6 %copy-start.16 = (f32[128,256]{1,0:T(8,128)S(1)}, f32[128,256]{1,0:T(8,128)}, u32[]{:S(2)}) copy-start(f32[128,256]{1,0:T(8,128)} %get-tuple-element.39) | copy-start | bytes 393220
  119.3 97.4 %all-to-all-start.1 = ((bf16[16,8,64,256]{3,2,1,0:T(8,128)(2,1)}), bf16[16,8,64,256]{3,2,1,0:T(8,128)(2,1)}, u32[]{:S(2)}, u32[]{:S(2)}) async-start(bf16[16,8,64,256]{3,2,1,0:T(8,128)(2,1)} %shard_map.106), calls=%async_computation.1 | async-start | bytes 8388608 | tf_op jit(solution)/shard_map/all_to_all | solution.py:358
  126.4 104.0 %collective-permute-start.4 = (f32[128,256]{1,0:T(8,128)S(1)}, f32[128,256]{1,0:T(8,128)S(1)}, u32[]{:S(2)}, u32[]{:S(2)}) collective-permute-start(f32[128,256]{1,0:T(8,128)S(1)} %copy-done.17), channel_id=1, source_target_pairs={{0,2},{2,4},{4,6},{6,8},{8,10},{10,12},{12,14},{1,3},{3,5},{5,7},{... | collective-permute-start | bytes 393224 | tf_op jit(solution)/shard_map/ppermute | solution.py:34
  129.5 97.6 %collective-permute-start.6 = (f32[128,64]{1,0:T(8,128)S(1)}, f32[128,64]{1,0:T(8,128)S(1)}, u32[]{:S(2)}, u32[]{:S(2)}) collective-permute-start(f32[128,64]{1,0:T(8,128)S(1)} %copy-done.19), channel_id=1, source_target_pairs={{0,1},{2,3},{4,5},{6,7},{8,9},{10,11},{12,13},{14,15},{16,17},{18,... | collective-permute-start | bytes 98312 | tf_op jit(solution)/shard_map/ppermute | solution.py:36
  130.8 98.3 %collective-permute-start.7 = (f32[128,64]{1,0:T(8,128)S(1)}, f32[128,64]{1,0:T(8,128)S(1)}, u32[]{:S(2)}, u32[]{:S(2)}) collective-permute-start(f32[128,64]{1,0:T(8,128)S(1)} %copy-done.18), channel_id=1, source_target_pairs={{1,0},{3,2},{5,4},{7,6},{9,8},{11,10},{13,12},{15,14},{17,16},{19,... | collective-permute-start | bytes 98312 | tf_op jit(solution)/shard_map/ppermute | solution.py:37
  133.9 100.5 %collective-permute-start.5 = (f32[128,256]{1,0:T(8,128)S(1)}, f32[128,256]{1,0:T(8,128)S(1)}, u32[]{:S(2)}, u32[]{:S(2)}) collective-permute-start(f32[128,256]{1,0:T(8,128)S(1)} %copy-done.16), channel_id=1, source_target_pairs={{2,0},{4,2},{6,4},{8,6},{10,8},{12,10},{14,12},{3,1},{5,3},{7,5},{... | collective-permute-start | bytes 393224 | tf_op jit(solution)/shard_map/ppermute | solution.py:35
  221.5 13.1 %collective-permute-start = (f32[128,256]{1,0:T(8,128)}, f32[128,256]{1,0:T(8,128)S(1)}, u32[]{:S(2)}, u32[]{:S(2)}) collective-permute-start(f32[128,256]{1,0:T(8,128)} %get-tuple-element.34), channel_id=1, source_target_pairs={{0,2},{2,4},{4,6},{6,8},{8,10},{10,12},{12,14},{1,3},{3,5},{5,7},{... | collective-permute-start | bytes 393224 | tf_op jit(solution)/shard_map/ppermute | solution.py:34
  227.2 7.5 %copy-start.6 = (f32[128,64]{1,0:T(8,128)}, f32[128,64]{1,0:T(8,128)S(1)}, u32[]{:S(2)}) copy-start(f32[128,64]{1,0:T(8,128)S(1)} %collective-permute-done.6.qyl_ref) | copy-start | bytes 98308
  227.2 7.4 %collective-permute-start.1 = (f32[128,256]{1,0:T(8,128)}, f32[128,256]{1,0:T(8,128)S(1)}, u32[]{:S(2)}, u32[]{:S(2)}) collective-permute-start(f32[128,256]{1,0:T(8,128)} %get-tuple-element.35), channel_id=1, source_target_pairs={{2,0},{4,2},{6,4},{8,6},{10,8},{12,10},{14,12},{3,1},{5,3},{7,5},{... | collective-permute-start | bytes 393224 | tf_op jit(solution)/shard_map/ppermute | solution.py:35
  229.2 5.5 %copy-start.7 = (f32[128,64]{1,0:T(8,128)}, f32[128,64]{1,0:T(8,128)S(1)}, u32[]{:S(2)}) copy-start(f32[128,64]{1,0:T(8,128)S(1)} %collective-permute-done.7.qyh_ref) | copy-start | bytes 98308
  229.2 5.2 %collective-permute-start.2 = (f32[128,64]{1,0:T(8,128)}, f32[128,64]{1,0:T(8,128)S(1)}, u32[]{:S(2)}, u32[]{:S(2)}) collective-permute-start(f32[128,64]{1,0:T(8,128)} %get-tuple-element.36), channel_id=1, source_target_pairs={{0,1},{2,3},{4,5},{6,7},{8,9},{10,11},{12,13},{14,15},{16,17},{18,... | collective-permute-start | bytes 98312 | tf_op jit(solution)/shard_map/ppermute | solution.py:36
  230.5 4.2 %copy-start = (f32[128,256]{1,0:T(8,128)}, f32[128,256]{1,0:T(8,128)S(1)}, u32[]{:S(2)}) copy-start(f32[128,256]{1,0:T(8,128)S(1)} %collective-permute-done.4.qxl_ref) | copy-start | bytes 393220
  230.5 4.1 %collective-permute-start.3 = (f32[128,64]{1,0:T(8,128)}, f32[128,64]{1,0:T(8,128)S(1)}, u32[]{:S(2)}, u32[]{:S(2)}) collective-permute-start(f32[128,64]{1,0:T(8,128)} %get-tuple-element.37), channel_id=1, source_target_pairs={{1,0},{3,2},{5,4},{7,6},{9,8},{11,10},{13,12},{15,14},{17,16},{19,... | collective-permute-start | bytes 98312 | tf_op jit(solution)/shard_map/ppermute | solution.py:37
  234.4 0.7 copy-start.1
  234.4 0.7 copy-start.8
  234.6 0.7 copy-start.2
  234.6 0.7 copy-start.3
  271.6 11.6 %collective-permute-start.8 = (f32[128,256]{1,0:T(8,128)}, f32[128,256]{1,0:T(8,128)S(1)}, u32[]{:S(2)}, u32[]{:S(2)}) collective-permute-start(f32[128,256]{1,0:T(8,128)} %get-tuple-element.49), channel_id=1, source_target_pairs={{0,2},{2,4},{4,6},{6,8},{8,10},{10,12},{12,14},{1,3},{3,5},{5,7},{... | collective-permute-start | bytes 393224 | tf_op jit(solution)/shard_map/ppermute | solution.py:34
  275.0 8.3 %collective-permute-start.9 = (f32[128,256]{1,0:T(8,128)}, f32[128,256]{1,0:T(8,128)S(1)}, u32[]{:S(2)}, u32[]{:S(2)}) collective-permute-start(f32[128,256]{1,0:T(8,128)} %get-tuple-element.50), channel_id=1, source_target_pairs={{2,0},{4,2},{6,4},{8,6},{10,8},{12,10},{14,12},{3,1},{5,3},{7,5},{... | collective-permute-start | bytes 393224 | tf_op jit(solution)/shard_map/ppermute | solution.py:35
  277.8 4.3 %collective-permute-start.10 = (f32[128,64]{1,0:T(8,128)}, f32[128,64]{1,0:T(8,128)S(1)}, u32[]{:S(2)}, u32[]{:S(2)}) collective-permute-start(f32[128,64]{1,0:T(8,128)} %get-tuple-element.51), channel_id=1, source_target_pairs={{0,1},{2,3},{4,5},{6,7},{8,9},{10,11},{12,13},{14,15},{16,17},{18,... | collective-permute-start | bytes 98312 | tf_op jit(solution)/shard_map/ppermute | solution.py:36
  279.1 4.1 %collective-permute-start.11 = (f32[128,64]{1,0:T(8,128)}, f32[128,64]{1,0:T(8,128)S(1)}, u32[]{:S(2)}, u32[]{:S(2)}) collective-permute-start(f32[128,64]{1,0:T(8,128)} %get-tuple-element.52), channel_id=1, source_target_pairs={{1,0},{3,2},{5,4},{7,6},{9,8},{11,10},{13,12},{15,14},{17,16},{19,... | collective-permute-start | bytes 98312 | tf_op jit(solution)/shard_map/ppermute | solution.py:37
  282.2 1.1 copy-start.10
  283.3 0.7 copy-start.4
  283.3 0.7 copy-start.5
  (2 other events, 1.2 us)

commit v20 on v19

--- a/solution.py
+++ b/solution.py
@@ -301,7 +301,7 @@
 
 def line_transforms(gathered, root_x, root_y, count_w, count_n):
     groups, planes, nx, ny = gathered.shape
-    step = 2 if planes % 2 == 0 else 1
+    step = 4 if planes % 4 == 0 else (2 if planes % 2 == 0 else 1)
     block = pl.BlockSpec((groups, step, nx, ny), lambda z: (0, z, 0, 0))
     whole_x = pl.BlockSpec(root_x.shape, lambda z: (0, 0))
     whole_y = pl.BlockSpec(root_y.shape, lambda z: (0, 0))

time: 313 us -> 313 us (level)
  no operation moved by 1% of the time
where the time goes in v20:
time: 313 us; the launch traced here: 311 us
  waiting for transfers between devices  161 us (51%)
  Pallas kernels  93.5 us (30%)
  starting transfers between devices  46.9 us (15%)
  matrix products  6.74 us (2%)
    all_to_all x1, waiting for transfers between devices, body(): lax.all_to_all(outgoing, ('wide', 'narrow'), split_axis=0, concat_axis=0,...  79.8 us
    all_to_all x1, waiting for transfers between devices, body(): lax.all_to_all(first.reshape(groups, planes, rows_x, rows_y), ('wide', 'n...  79.5 us
    pallas_call x1, Pallas kernels, advance(): pl.pallas_call(first_step_kernel, out_shape=tuple(out_shape + [full, full...  36.3 us
    pallas_call x1, Pallas kernels, advance(): pl.pallas_call(later_step_kernel, out_shape=tuple(out_shape), grid=grid,...  27 us
    pallas_call x1, Pallas kernels, depth_transform(): pl.pallas_call(depth_kernel, out_shape=jax.ShapeDtypeStruct(noise.shape,...  13.6 us
    ppermute x3, starting transfers between devices, halos(): x_lo = lax.ppermute(last_x, 'wide', forward_w)  12.1 us
    ppermute x3, starting transfers between devices, halos(): y_hi = lax.ppermute(first_y, 'narrow', backward_n)  9.28 us
    pallas_call x2, Pallas kernels, block_edges(): pl.pallas_call(edge_kernel, out_shape=tuple(out_shape), grid=(depth // tz...  8.71 us
  transfers between devices with their start and end apart: 14, of which 4 were waited for; matrix products, arithmetic and copies ran while one was open for 2% of the time, Pallas kernels for 3%

profile of v20, /device:TPU:11, one launch (start us, length us, event | category | flops | bytes accessed | tf_op | source)
XLA Modules:
  0.0 311.1 jit_solution(16697789532724161803)
XLA Ops:
  0.6 13.6 %shard_map.104 = bf16[128,64,256]{2,1,0:T(8,128)(2,1)} custom-call(bf16[128,128]{1,0:T(8,128)(2,1)} %rz_ref.1, bf16[128,64,256]{2,1,0:T(8,128)(2,1)} %n_ref.1), custom_call_target="tpu_custom_call" | custom-call | tf_op jit(solution)/shard_map/pallas_call | solution.py:273
  14.2 6.8 %all-to-all-start = ((bf16[16,8,64,256]{3,2,1,0:T(8,128)(2,1)}), bf16[16,8,64,256]{3,2,1,0:T(8,128)(2,1)}, u32[]{:S(2)}, u32[]{:S(2)}) async-start(bf16[16,8,64,256]{3,2,1,0:T(8,128)(2,1)} %bitcast.9), calls=%async_computation | async-start | bytes 8388608 | tf_op jit(solution)/shard_map/all_to_all | solution.py:325
  21.0 4.0 %shard_map.105 = (f32[128,256]{1,0:T(8,128)}, f32[128,256]{1,0:T(8,128)}, f32[128,64]{1,0:T(8,128)}, f32[128,64]{1,0:T(8,128)}) custom-call(bf16[128,64,256]{2,1,0:T(8,128)(2,1)} %pa_ref.1), custom_call_target="tpu_custom_call" | custom-call | tf_op jit(solution)/shard_map/pallas_call | solution.py:111
  25.0 6.7 %fusion = f32[8192,256]{1,0:T(8,128)} fusion(f32[256]{0:T(256)S(1)} %get-tuple-element.54, s32[256]{0:T(256)S(1)} %multiply_add_fusion, s32[256]{0:T(256)S(1)} %get-tuple-element.55), kind=kOutput, calls=%fused_computation | convolution fusion | flops 6446710784 | bytes 8391680 | tf_op jit(solution)/shard_map/dot_general | solution.py:348
  31.8 79.5 %all-to-all-done.g_ref = bf16[16,8,64,256]{3,2,1,0:T(8,128)(2,1)} async-done(((bf16[16,8,64,256]{3,2,1,0:T(8,128)(2,1)}), bf16[16,8,64,256]{3,2,1,0:T(8,128)(2,1)}, u32[]{:S(2)}, u32[]{:S(2)}) %all-to-all-start) | async-done | bytes 4194336 | tf_op jit(solution)/shard_map/all_to_all | solution.py:325
  111.3 7.9 %shard_map.106 = bf16[16,8,64,256]{3,2,1,0:T(8,128)(2,1)} custom-call(bf16[16,8,64,256]{3,2,1,0:T(8,128)(2,1)} %all-to-all-done.g_ref, bf16[512,512]{1,0:T(8,128)(2,1)} %rx_ref.1, bf16[512,512]{1,0:T(8,128)(2,1)} %ry_ref.1), custom_call_target="tpu_custom_call" | custom-call | tf_op jit(solution)/shard_map/pallas_call | solution.py:308
  119.2 7.1 %all-to-all-start.1 = ((bf16[16,8,64,256]{3,2,1,0:T(8,128)(2,1)}), bf16[16,8,64,256]{3,2,1,0:T(8,128)(2,1)}, u32[]{:S(2)}, u32[]{:S(2)}) async-start(bf16[16,8,64,256]{3,2,1,0:T(8,128)(2,1)} %shard_map.106), calls=%async_computation.1 | async-start | bytes 8388608 | tf_op jit(solution)/shard_map/all_to_all | solution.py:358
  126.3 3.1 collective-permute-start.4
  129.4 1.3 collective-permute-start.6
  130.7 3.0 collective-permute-start.7
  133.8 3.1 collective-permute-start.5
  136.9 79.8 %all-to-all-done.1 = bf16[16,8,64,256]{3,2,1,0:T(8,128)(2,1)} async-done(((bf16[16,8,64,256]{3,2,1,0:T(8,128)(2,1)}), bf16[16,8,64,256]{3,2,1,0:T(8,128)(2,1)}, u32[]{:S(2)}, u32[]{:S(2)}) %all-to-all-start.1) | async-done | bytes 4194336 | tf_op jit(solution)/shard_map/all_to_all | solution.py:358
  216.7 4.7 %shard_map.107 = (f32[128,256]{1,0:T(8,128)}, f32[128,256]{1,0:T(8,128)}, f32[128,64]{1,0:T(8,128)}, f32[128,64]{1,0:T(8,128)}, bf16[128,64,256]{2,1,0:T(8,128)(2,1)}) custom-call(bf16[128,64,256]{2,1,0:T(8,128)(2,1)} %bitcast.2.block_ref), custom_call_target="tpu_custom_call" | custom-call | tf_op jit(solution)/shard_map/pallas_call | solution.py:111
  221.4 5.7 %collective-permute-start = (f32[128,256]{1,0:T(8,128)}, f32[128,256]{1,0:T(8,128)S(1)}, u32[]{:S(2)}, u32[]{:S(2)}) collective-permute-start(f32[128,256]{1,0:T(8,128)} %get-tuple-element.34), channel_id=1, source_target_pairs={{0,2},{2,4},{4,6},{6,8},{8,10},{10,12},{12,14},{1,3},{3,5},{5,7},{... | collective-permute-start | bytes 393224 | tf_op jit(solution)/shard_map/ppermute | solution.py:34
  227.1 1.9 collective-permute-start.1
  229.0 1.3 collective-permute-start.2
  230.4 3.2 %collective-permute-start.3 = (f32[128,64]{1,0:T(8,128)}, f32[128,64]{1,0:T(8,128)S(1)}, u32[]{:S(2)}, u32[]{:S(2)}) collective-permute-start(f32[128,64]{1,0:T(8,128)} %get-tuple-element.37), channel_id=1, source_target_pairs={{1,0},{3,2},{5,4},{7,6},{9,8},{11,10},{13,12},{15,14},{17,16},{19,... | collective-permute-start | bytes 98312 | tf_op jit(solution)/shard_map/ppermute | solution.py:37
  233.6 0.7 add_convert_fusion.inside_ref
  234.3 0.2 collective-permute-done.3.lyh_ref
  234.5 0.4 copy-done.1
  234.9 0.2 copy-done.9
  235.1 0.1 copy-done.2
  235.2 36.3 %shard_map.108 = (f32[128,64,256]{2,1,0:T(8,128)}, f32[128,256]{1,0:T(8,128)}, f32[128,256]{1,0:T(8,128)}, f32[128,64]{1,0:T(8,128)}, f32[128,64]{1,0:T(8,128)},...) custom-call(s32[4]{0:T(128)} %add_convert_fusion.inside_ref, ...), custom_call_target="tpu_custom_call" | custom-call | tf_op jit(solution)/shard_map/pallas_call | solution.py:240
  271.5 3.4 %collective-permute-start.8 = (f32[128,256]{1,0:T(8,128)}, f32[128,256]{1,0:T(8,128)S(1)}, u32[]{:S(2)}, u32[]{:S(2)}) collective-permute-start(f32[128,256]{1,0:T(8,128)} %get-tuple-element.49), channel_id=1, source_target_pairs={{0,2},{2,4},{4,6},{6,8},{8,10},{10,12},{12,14},{1,3},{3,5},{5,7},{... | collective-permute-start | bytes 393224 | tf_op jit(solution)/shard_map/ppermute | solution.py:34
  274.9 2.8 collective-permute-start.9
  277.7 1.3 collective-permute-start.10
  279.0 3.0 collective-permute-start.11
  282.1 1.1 collective-permute-done.11.qyh_ref
  283.2 0.6 copy-done.11
  283.8 0.1 copy-done.4
  283.8 0.1 copy-done.5
  283.9 27.0 %shard_map.109 = (f32[128,64,256]{2,1,0:T(8,128)}, f32[128,256]{1,0:T(8,128)}, f32[128,256]{1,0:T(8,128)}, f32[128,64]{1,0:T(8,128)}, f32[128,64]{1,0:T(8,128)}) custom-call(f32[128,64,256]{2,1,0:T(8,128)} %get-tuple-element.43.tzm_ref.tza_ref, f32[128,64,256]{2,1,0:T(8,128)} %get-tuple-element.43.tzm_ref.tza_ref, ...), custom_call_target="tpu_custom_call" | custom-call | tf_op jit(solution)/shard_map/pallas_call | solution.py:250
  (46 shorter events, 0.2 us)
Async XLA Ops:
  14.2 10.8 %copy-start.12 = (s32[256]{0:T(256)S(1)}, s32[256]{0:T(256)}, u32[]{:S(2)}) copy-start(s32[256]{0:T(256)} %param.14) | copy-start | bytes 3076
  14.2 10.8 %copy-start.13 = (s32[256]{0:T(256)S(1)}, s32[256]{0:T(256)}, u32[]{:S(2)}) copy-start(s32[256]{0:T(256)} %param.16) | copy-start | bytes 3076
  14.2 10.8 %copy-start.14 = (f32[256]{0:T(256)S(1)}, f32[256]{0:T(256)}, u32[]{:S(2)}) copy-start(f32[256]{0:T(256)} %param.17) | copy-start | bytes 3076
  14.2 10.8 %copy-start.15 = (s32[256]{0:T(256)S(1)}, s32[256]{0:T(256)}, u32[]{:S(2)}) copy-start(s32[256]{0:T(256)} %param.15) | copy-start | bytes 3076
  14.2 97.1 %all-to-all-start = ((bf16[16,8,64,256]{3,2,1,0:T(8,128)(2,1)}), bf16[16,8,64,256]{3,2,1,0:T(8,128)(2,1)}, u32[]{:S(2)}, u32[]{:S(2)}) async-start(bf16[16,8,64,256]{3,2,1,0:T(8,128)(2,1)} %bitcast.9), calls=%async_computation | async-start | bytes 8388608 | tf_op jit(solution)/shard_map/all_to_all | solution.py:325
  111.3 15.0 %copy-start.17 = (f32[128,256]{1,0:T(8,128)S(1)}, f32[128,256]{1,0:T(8,128)}, u32[]{:S(2)}) copy-start(f32[128,256]{1,0:T(8,128)} %get-tuple-element.38) | copy-start | bytes 393220
  111.3 18.1 %copy-start.19 = (f32[128,64]{1,0:T(8,128)S(1)}, f32[128,64]{1,0:T(8,128)}, u32[]{:S(2)}) copy-start(f32[128,64]{1,0:T(8,128)} %get-tuple-element.40) | copy-start | bytes 98308
  111.3 19.4 %copy-start.18 = (f32[128,64]{1,0:T(8,128)S(1)}, f32[128,64]{1,0:T(8,128)}, u32[]{:S(2)}) copy-start(f32[128,64]{1,0:T(8,128)} %get-tuple-element.41) | copy-start | bytes 98308
  111.3 22.5 %copy-start.16 = (f32[128,256]{1,0:T(8,128)S(1)}, f32[128,256]{1,0:T(8,128)}, u32[]{:S(2)}) copy-start(f32[128,256]{1,0:T(8,128)} %get-tuple-element.39) | copy-start | bytes 393220
  119.2 97.4 %all-to-all-start.1 = ((bf16[16,8,64,256]{3,2,1,0:T(8,128)(2,1)}), bf16[16,8,64,256]{3,2,1,0:T(8,128)(2,1)}, u32[]{:S(2)}, u32[]{:S(2)}) async-start(bf16[16,8,64,256]{3,2,1,0:T(8,128)(2,1)} %shard_map.106), calls=%async_computation.1 | async-start | bytes 8388608 | tf_op jit(solution)/shard_map/all_to_all | solution.py:358
  126.3 104.0 %collective-permute-start.4 = (f32[128,256]{1,0:T(8,128)S(1)}, f32[128,256]{1,0:T(8,128)S(1)}, u32[]{:S(2)}, u32[]{:S(2)}) collective-permute-start(f32[128,256]{1,0:T(8,128)S(1)} %copy-done.17), channel_id=1, source_target_pairs={{0,2},{2,4},{4,6},{6,8},{8,10},{10,12},{12,14},{1,3},{3,5},{5,7},{... | collective-permute-start | bytes 393224 | tf_op jit(solution)/shard_map/ppermute | solution.py:34
  129.4 97.6 %collective-permute-start.6 = (f32[128,64]{1,0:T(8,128)S(1)}, f32[128,64]{1,0:T(8,128)S(1)}, u32[]{:S(2)}, u32[]{:S(2)}) collective-permute-start(f32[128,64]{1,0:T(8,128)S(1)} %copy-done.19), channel_id=1, source_target_pairs={{0,1},{2,3},{4,5},{6,7},{8,9},{10,11},{12,13},{14,15},{16,17},{18,... | collective-permute-start | bytes 98312 | tf_op jit(solution)/shard_map/ppermute | solution.py:36
  130.7 98.3 %collective-permute-start.7 = (f32[128,64]{1,0:T(8,128)S(1)}, f32[128,64]{1,0:T(8,128)S(1)}, u32[]{:S(2)}, u32[]{:S(2)}) collective-permute-start(f32[128,64]{1,0:T(8,128)S(1)} %copy-done.18), channel_id=1, source_target_pairs={{1,0},{3,2},{5,4},{7,6},{9,8},{11,10},{13,12},{15,14},{17,16},{19,... | collective-permute-start | bytes 98312 | tf_op jit(solution)/shard_map/ppermute | solution.py:37
  133.8 100.5 %collective-permute-start.5 = (f32[128,256]{1,0:T(8,128)S(1)}, f32[128,256]{1,0:T(8,128)S(1)}, u32[]{:S(2)}, u32[]{:S(2)}) collective-permute-start(f32[128,256]{1,0:T(8,128)S(1)} %copy-done.16), channel_id=1, source_target_pairs={{2,0},{4,2},{6,4},{8,6},{10,8},{12,10},{14,12},{3,1},{5,3},{7,5},{... | collective-permute-start | bytes 393224 | tf_op jit(solution)/shard_map/ppermute | solution.py:35
  221.4 13.1 %collective-permute-start = (f32[128,256]{1,0:T(8,128)}, f32[128,256]{1,0:T(8,128)S(1)}, u32[]{:S(2)}, u32[]{:S(2)}) collective-permute-start(f32[128,256]{1,0:T(8,128)} %get-tuple-element.34), channel_id=1, source_target_pairs={{0,2},{2,4},{4,6},{6,8},{8,10},{10,12},{12,14},{1,3},{3,5},{5,7},{... | collective-permute-start | bytes 393224 | tf_op jit(solution)/shard_map/ppermute | solution.py:34
  227.1 7.5 %copy-start.6 = (f32[128,64]{1,0:T(8,128)}, f32[128,64]{1,0:T(8,128)S(1)}, u32[]{:S(2)}) copy-start(f32[128,64]{1,0:T(8,128)S(1)} %collective-permute-done.6.qyl_ref) | copy-start | bytes 98308
  227.1 7.4 %collective-permute-start.1 = (f32[128,256]{1,0:T(8,128)}, f32[128,256]{1,0:T(8,128)S(1)}, u32[]{:S(2)}, u32[]{:S(2)}) collective-permute-start(f32[128,256]{1,0:T(8,128)} %get-tuple-element.35), channel_id=1, source_target_pairs={{2,0},{4,2},{6,4},{8,6},{10,8},{12,10},{14,12},{3,1},{5,3},{7,5},{... | collective-permute-start | bytes 393224 | tf_op jit(solution)/shard_map/ppermute | solution.py:35
  229.0 5.5 %copy-start.7 = (f32[128,64]{1,0:T(8,128)}, f32[128,64]{1,0:T(8,128)S(1)}, u32[]{:S(2)}) copy-start(f32[128,64]{1,0:T(8,128)S(1)} %collective-permute-done.7.qyh_ref) | copy-start | bytes 98308
  229.0 5.2 %collective-permute-start.2 = (f32[128,64]{1,0:T(8,128)}, f32[128,64]{1,0:T(8,128)S(1)}, u32[]{:S(2)}, u32[]{:S(2)}) collective-permute-start(f32[128,64]{1,0:T(8,128)} %get-tuple-element.36), channel_id=1, source_target_pairs={{0,1},{2,3},{4,5},{6,7},{8,9},{10,11},{12,13},{14,15},{16,17},{18,... | collective-permute-start | bytes 98312 | tf_op jit(solution)/shard_map/ppermute | solution.py:36
  230.4 4.2 %copy-start = (f32[128,256]{1,0:T(8,128)}, f32[128,256]{1,0:T(8,128)S(1)}, u32[]{:S(2)}) copy-start(f32[128,256]{1,0:T(8,128)S(1)} %collective-permute-done.4.qxl_ref) | copy-start | bytes 393220
  230.4 4.1 %collective-permute-start.3 = (f32[128,64]{1,0:T(8,128)}, f32[128,64]{1,0:T(8,128)S(1)}, u32[]{:S(2)}, u32[]{:S(2)}) collective-permute-start(f32[128,64]{1,0:T(8,128)} %get-tuple-element.37), channel_id=1, source_target_pairs={{1,0},{3,2},{5,4},{7,6},{9,8},{11,10},{13,12},{15,14},{17,16},{19,... | collective-permute-start | bytes 98312 | tf_op jit(solution)/shard_map/ppermute | solution.py:37
  234.3 0.7 copy-start.1
  234.3 0.7 copy-start.8
  234.5 0.7 copy-start.2
  234.5 0.7 copy-start.3
  271.5 11.6 %collective-permute-start.8 = (f32[128,256]{1,0:T(8,128)}, f32[128,256]{1,0:T(8,128)S(1)}, u32[]{:S(2)}, u32[]{:S(2)}) collective-permute-start(f32[128,256]{1,0:T(8,128)} %get-tuple-element.49), channel_id=1, source_target_pairs={{0,2},{2,4},{4,6},{6,8},{8,10},{10,12},{12,14},{1,3},{3,5},{5,7},{... | collective-permute-start | bytes 393224 | tf_op jit(solution)/shard_map/ppermute | solution.py:34
  274.9 8.3 %collective-permute-start.9 = (f32[128,256]{1,0:T(8,128)}, f32[128,256]{1,0:T(8,128)S(1)}, u32[]{:S(2)}, u32[]{:S(2)}) collective-permute-start(f32[128,256]{1,0:T(8,128)} %get-tuple-element.50), channel_id=1, source_target_pairs={{2,0},{4,2},{6,4},{8,6},{10,8},{12,10},{14,12},{3,1},{5,3},{7,5},{... | collective-permute-start | bytes 393224 | tf_op jit(solution)/shard_map/ppermute | solution.py:35
  277.7 4.3 %collective-permute-start.10 = (f32[128,64]{1,0:T(8,128)}, f32[128,64]{1,0:T(8,128)S(1)}, u32[]{:S(2)}, u32[]{:S(2)}) collective-permute-start(f32[128,64]{1,0:T(8,128)} %get-tuple-element.51), channel_id=1, source_target_pairs={{0,1},{2,3},{4,5},{6,7},{8,9},{10,11},{12,13},{14,15},{16,17},{18,... | collective-permute-start | bytes 98312 | tf_op jit(solution)/shard_map/ppermute | solution.py:36
  279.0 4.1 %collective-permute-start.11 = (f32[128,64]{1,0:T(8,128)}, f32[128,64]{1,0:T(8,128)S(1)}, u32[]{:S(2)}, u32[]{:S(2)}) collective-permute-start(f32[128,64]{1,0:T(8,128)} %get-tuple-element.52), channel_id=1, source_target_pairs={{1,0},{3,2},{5,4},{7,6},{9,8},{11,10},{13,12},{15,14},{17,16},{19,... | collective-permute-start | bytes 98312 | tf_op jit(solution)/shard_map/ppermute | solution.py:37
  282.1 1.1 copy-start.10
  283.1 0.7 copy-start.4
  283.1 0.7 copy-start.5
  (2 other events, 1.2 us)
